TPU v7x, 512 devices: a whole 4x8x8 slice. The times are simulated.
512 devices in a mesh: req: 8 (over z), blk: 64 (over x, y, core).
Axes of the slice: x: 4, y: 8, z: 8, core: 2. Of those that a mesh axis runs over, the one named last changes fastest.
Arguments:
- tokens: bfloat16 [8, 512, 2048], P('req'), may hold values from -6 to 6
- cache_entries: bfloat16 [8, 64, 2048, 2, 128], P('req', 'blk'), may hold values from -1400 to 1400
- cache_tenants: int32 [8, 8192], P('req'), may hold values from 0 to 7
- cached_length: int32 [8], P('req'), may hold values from 2048 to 8192, as said below
- tenant_bounds: int32 [8, 2], P('req'), may hold values from 0 to 8, as said below
- qkv_weight: bfloat16 [2048, 3, 2048], P('req', None, 'blk'), may hold values from -0.125 to 0.125
- qkv_bias: float32 [3, 2048], P(None, 'blk'), may hold values from -3 to 3
- out_weight: bfloat16 [2048, 2048], P('req', 'blk'), may hold values from -0.125 to 0.125
- in_weight: bfloat16 [2048, 8192], P('req', 'blk'), may hold values from -0.125 to 0.125
- in_bias: float32 [8192], replicated, may hold values from -3 to 3
- down_weight: bfloat16 [2048, 8192], P('req', 'blk'), may hold values from -0.0625 to 0.0625
- out_biases: float32 [2, 2048], replicated, may hold values from -3 to 3
- norm_gains: float32 [2, 2048], replicated, may hold values from 0.5 to 1.5
- norm_biases: float32 [2, 2048], replicated, may hold values from -1.2 to 1.2
Outputs:
- layer_output: bfloat16 [8, 512, 2048], P('req', 'blk')
- appended: bfloat16 [8, 512, 2, 2048], P('req', None, None, 'blk')
Inputs may be any that keep to these rules, and one draw needn't show every extreme that they name: `cached_length`: at least one request has exactly 8192 cached positions. `tenant_bounds`: the lower bound is below the upper one; some request's upper bound is 8 and some request's lower bound is 0.
All inputs are finite; a program needn't handle non-finite values.
Results may differ from a plain program's by a relative error of at most 0.015.
The roundings to bfloat16 on the way count: a program that leaves them out, or rounds other values in their place, can miss the bound.
Values may be sent and summed in bfloat16 or wider, within the bound.
No kernel may reach another device: no remote copies, remote signals or barrier semaphores. Data moves between devices by JAX's collectives and lax.ppermute only.
A program may use at most 64 MiB of HBM per device.

v0:
```python
import math

import jax
import jax.numpy as jnp
from jax import lax
from jax.sharding import PartitionSpec as P

HEADS = 16
HEAD_DIM = 128


MASKED = -1e30


def from_partner(value, axis, distance):
    return lax.ppermute(value, axis, [(i, i ^ 1 << distance) for i in range(lax.axis_size(axis))])


def layer_norm(values, gain_row, shift_row):
    centered = values - jnp.mean(values, axis=-1, keepdims=True)
    variance = jnp.mean(centered * centered, axis=-1, keepdims=True)
    return centered * lax.rsqrt(variance + 1e-06) * gain_row + shift_row


def partial_block(queries, key_rows, value_rows, visible):
    scores = jnp.einsum("qd,kd->qk", queries, key_rows, preferred_element_type=jnp.float32) * (
        1.0 / math.sqrt(HEAD_DIM)
    )
    scores = jnp.where(visible, scores, MASKED)
    row_max = jnp.max(scores, axis=1)
    weights = jnp.where(visible, jnp.exp(scores - row_max[:, None]), 0.0)
    row_total = jnp.sum(weights, axis=1)
    numerator = jnp.dot(
        weights.astype(jnp.bfloat16), value_rows, preferred_element_type=jnp.float32
    )
    return (numerator, row_max, row_total)


def merge_blocks(earlier_part, later_part):
    joined = jnp.maximum(earlier_part[1], later_part[1])
    scale_earlier = jnp.exp(earlier_part[1] - joined)
    scale_later = jnp.exp(later_part[1] - joined)
    numerator = earlier_part[0] * scale_earlier[:, None] + later_part[0] * scale_later[:, None]
    return (numerator, joined, earlier_part[2] * scale_earlier + later_part[2] * scale_later)


def local(
    tokens,
    cache_entries,
    cache_tenants,
    cached_length,
    tenant_bounds,
    qkv_weight,
    qkv_bias,
    out_weight,
    in_weight,
    in_bias,
    down_weight,
    out_biases,
    norm_gains,
    norm_biases,
):
    full_qkv, full_out, full_in, full_down = (
        lax.all_gather(qkv_weight, "req", axis=0, tiled=True),
        lax.all_gather(out_weight, "req", axis=0, tiled=True),
        lax.all_gather(in_weight, "req", axis=0, tiled=True),
        lax.all_gather(down_weight, "req", axis=0, tiled=True),
    )
    group_size = lax.axis_size("blk")
    groups = group_size // HEADS
    low_bits = groups.bit_length() - 1
    block_index = lax.axis_index("blk")
    group_index = block_index % groups
    query_total = tokens.shape[1]
    own_rows = query_total // group_size
    column_width = full_qkv.shape[2]
    token_rows = tokens[0]
    qkv_columns = (
        jnp.einsum("td,dce->tce", token_rows, full_qkv, preferred_element_type=jnp.float32)
        + qkv_bias
    ).astype(jnp.bfloat16)
    appended = qkv_columns[None, :, 1:]
    head_qkv = qkv_columns
    for bit_level in range(low_bits):
        partner = from_partner(head_qkv, "blk", bit_level)
        upper_bit = group_index >> bit_level & 1
        head_qkv = jnp.where(
            upper_bit == 1,
            jnp.concatenate([partner, head_qkv], axis=2),
            jnp.concatenate([head_qkv, partner], axis=2),
        )
    queries = head_qkv[:, 0]
    fresh_count = query_total // groups
    fresh_start = group_index * fresh_count
    fresh_keys = lax.dynamic_slice_in_dim(head_qkv[:, 1], fresh_start, fresh_count, 0)
    fresh_values = lax.dynamic_slice_in_dim(head_qkv[:, 2], fresh_start, fresh_count, 0)
    cache_count = cache_entries.shape[2]
    cache_keys = cache_entries[0, 0, :, 0]
    cache_values = cache_entries[0, 0, :, 1]
    cache_position = group_index * cache_count + jnp.arange(cache_count, dtype=jnp.int32)
    tenant_slice = lax.dynamic_slice_in_dim(
        cache_tenants[0], group_index * cache_count, cache_count, 0
    )
    readable = (
        (cache_position < cached_length[0])
        & (tenant_slice >= tenant_bounds[0, 0])
        & (tenant_slice < tenant_bounds[0, 1])
    )
    query_position = jnp.arange(query_total, dtype=jnp.int32)
    fresh_position = fresh_start + jnp.arange(fresh_count, dtype=jnp.int32)
    fresh_visible = fresh_position[None, :] <= query_position[:, None]
    cache_visible = jnp.broadcast_to(readable[None, :], (query_total, cache_count))
    partial_value = partial_block(
        queries,
        jnp.concatenate([cache_keys, fresh_keys], axis=0),
        jnp.concatenate([cache_values, fresh_values], axis=0),
        jnp.concatenate([cache_visible, fresh_visible], axis=1),
    )
    numerator, row_max, row_total = partial_value
    for bit_level in reversed(range(low_bits)):
        halves = numerator.reshape(query_total, 2, -1)
        upper_bit = group_index >> bit_level & 1
        kept_half = jnp.where(upper_bit == 1, halves[:, 1], halves[:, 0])
        sent_half = jnp.where(upper_bit == 1, halves[:, 0], halves[:, 1])
        other_sum, other_max, other_total = from_partner(
            (sent_half, row_max, row_total), "blk", bit_level
        )
        numerator, row_max, row_total = merge_blocks(
            (kept_half, row_max, row_total), (other_sum, other_max, other_total)
        )
    context_columns = (numerator / row_total[:, None]).astype(jnp.bfloat16)
    out_sum = jnp.dot(
        lax.all_gather(context_columns, "blk", axis=1, tiled=True),
        full_out,
        preferred_element_type=jnp.float32,
    )
    column_bias = lax.dynamic_slice_in_dim(out_biases[0], block_index * column_width, column_width)
    projected_part = (out_sum + column_bias).astype(jnp.bfloat16)
    projected = lax.all_gather(projected_part, "blk", axis=1, tiled=True)
    normed = layer_norm(
        token_rows.astype(jnp.float32) + projected.astype(jnp.float32),
        norm_gains[0],
        norm_biases[0],
    ).astype(jnp.bfloat16)
    hidden_width = full_in.shape[1]
    bias_slice = lax.dynamic_slice_in_dim(in_bias, block_index * hidden_width, hidden_width)
    inner = jax.nn.gelu(
        jnp.dot(normed, full_in, preferred_element_type=jnp.float32) + bias_slice, approximate=True
    ).astype(jnp.bfloat16)
    mixed_rows = lax.psum_scatter(
        jnp.einsum("rf,df->rd", inner, full_down, preferred_element_type=jnp.float32),
        "blk",
        scatter_dimension=0,
        tiled=True,
    )
    own_normed = lax.dynamic_slice_in_dim(normed, block_index * own_rows, own_rows, 0)
    layer_output = layer_norm(
        own_normed.astype(jnp.float32) + mixed_rows + out_biases[1], norm_gains[1], norm_biases[1]
    ).astype(jnp.bfloat16)
    return (layer_output[None], appended)


def solution(mesh):
    return jax.shard_map(
        local,
        mesh=mesh,
        in_specs=(
            P("req", None, None),
            P("req", "blk", None, None, None),
            P("req", None),
            P("req"),
            P("req", None),
            P("req", None, "blk"),
            P(None, "blk"),
            P("req", "blk"),
            P("req", "blk"),
            P(),
            P("req", "blk"),
            P(),
            P(),
            P(),
        ),
        out_specs=(P("req", "blk", None), P("req", None, None, "blk")),
        check_vma=False,
    )
```

profile of v0, /device:TPU:16, one launch (start us, length us, event | category | flops | bytes accessed | tf_op | source)
XLA Modules:
  0.0 417.9 jit_solution(15506608542563348457)
XLA Ops:
  7.2 31.7 %all_gather.18 = bf16[2048,3,32]{0,2,1:T(8,128)(2,1)S(1)} all-gather(bf16[256,3,32]{0,2,1:T(8,128)(2,1)} %param.19), channel_id=1, replica_groups=mesh['req'=8,'blk'=64] {'req'}, dimensions={0}, use_global_device_ids=true | all-gather | bytes 442368 | tf_op jit(solution)/shard_map/all_gather | solution.py:64
  39.0 2.4 fusion.8
  41.4 1.9 collective-permute-start
  44.6 1.5 fusion.50
  46.3 2.0 and_reduce_fusion
  48.4 3.5 collective-permute-start.1
  51.9 5.7 %collective-permute-done.1 = bf16[512,3,64]{0,2,1:T(8,128)(2,1)S(1)} collective-permute-done((bf16[512,3,64]{0,2,1:T(8,128)(2,1)S(1)}, bf16[512,3,64]{0,2,1:T(8,128)(2,1)S(1)}, u32[]{:S(2)}, u32[]{:S(2)}) %collective-permute-start.1) | collective-permute-done | bytes 196640 | tf_op jit(solution)/shard_map/ppermute | solution.py:16
  58.0 1.1 fusion.56
  59.1 3.5 collective-permute-start.2
  62.6 0.9 fusion.3
  63.5 2.4 collective-permute-start.6
  65.9 1.0 fusion.5
  67.0 3.6 collective-permute-start.3
  70.6 1.9 collective-permute-start.7
  72.5 2.4 collective-permute-start.4
  75.1 1.9 collective-permute-start.5
  77.0 1.2 collective-permute-done.5
  78.9 24.6 %all_gather.20 = bf16[2048,32]{0,1:T(8,128)(2,1)S(1)} all-gather(bf16[256,32]{0,1:T(8,128)(2,1)S(1)} %copy-done.5), channel_id=1, replica_groups=mesh['req'=8,'blk'=64] {'req'}, dimensions={0}, use_global_device_ids=true | all-gather | bytes 147456 | tf_op jit(solution)/shard_map/all_gather | solution.py:65
  103.6 55.2 %all-gather.3.cloned.1.call-done = bf16[512,2048]{0,1:T(8,128)(2,1)} async-done(((bf16[512,32]{0,1:T(8,128)(2,1)}), bf16[512,2048]{0,1:T(8,128)(2,1)}) %all-gather.3.cloned.1.call-update) | async-done | bytes 2097168 | tf_op jit(solution)/shard_map/all_gather | solution.py:133
  158.8 2.7 fusion.10
  162.3 27.3 %all_gather.22 = bf16[2048,128]{1,0:T(8,128)(2,1)S(1)} all-gather(bf16[256,128]{1,0:T(8,128)(2,1)S(1)} %copy-done.3), channel_id=1, replica_groups=mesh['req'=8,'blk'=64] {'req'}, dimensions={0}, use_global_device_ids=true | all-gather | bytes 589824 | tf_op jit(solution)/shard_map/all_gather | solution.py:66
  189.6 25.3 %all_gather.23 = bf16[2048,128]{1,0:T(8,128)(2,1)S(1)} all-gather(bf16[256,128]{1,0:T(8,128)(2,1)S(1)} %copy-done.4), channel_id=1, replica_groups=mesh['req'=8,'blk'=64] {'req'}, dimensions={0}, use_global_device_ids=true | all-gather | bytes 589824 | tf_op jit(solution)/shard_map/all_gather | solution.py:67
  214.9 28.3 %all-gather.5.cloned.1.call-done = bf16[512,2048]{0,1:T(8,128)(2,1)} async-done(((bf16[512,32]{0,1:T(8,128)(2,1)}), bf16[512,2048]{0,1:T(8,128)(2,1)}) %all-gather.5.cloned.1.call-update) | async-done | bytes 2097168 | tf_op jit(solution)/shard_map/all_gather | solution.py:139
  243.3 4.0 copy.47
  247.2 2.4 fusion.2
  249.6 0.9 multiply_reduce_fusion
  250.5 2.4 add_convert_fusion
  252.9 4.8 %fusion.25 = f32[512,2048]{1,0:T(8,128)} fusion(bf16[2048,128]{1,0:T(8,128)(2,1)S(1)} %all_gather.23, bf16[512,2048]{1,0:T(8,128)(2,1)} %add_convert_fusion, bf16[2048,128]{1,0:T(8,128)(2,1)S(1)} %all_gather.22, f32[128]{0:T(128)S(1)} %dynamic_slice.29), kind=kOutput, calls=%fused_computation.36 | convolution fusion | flops 537526272 | bytes 7340544
  258.4 149.4 %reduce-scatter.4.cloned.1.call-done = f32[8,2048]{1,0:T(8,128)} async-done(((f32[512,2048]{1,0:T(8,128)}), f32[8,2048]{1,0:T(8,128)}) %reduce-scatter.4.cloned.1.call-update) | async-done | bytes 65552 | tf_op jit(solution)/shard_map/reduce_scatter | solution.py:150
  407.8 1.0 fusion.38
  408.8 1.0 multiply_reduce_fusion.1
  409.8 1.5 fusion.35
  (64 shorter events, 3.8 us)
Async XLA Ops:
  7.2 34.2 %copy-start.9 = (f32[3,32]{1,0:T(4,128)S(1)}, f32[3,32]{1,0:T(4,128)}, u32[]{:S(2)}) copy-start(f32[3,32]{1,0:T(4,128)} %param.20) | copy-start | bytes 1156
  7.2 36.9 %copy-start.10 = (s32[1,2]{1,0:T(1,128)S(1)}, s32[1,2]{1,0:T(1,128)}, u32[]{:S(2)}) copy-start(s32[1,2]{1,0:T(1,128)} %param.18) | copy-start | bytes 28
  7.2 37.4 %copy-start.2 = (bf16[1,1,2048,2,128]{4,3,2,1,0:T(2,128)(2,1)S(1)}, bf16[1,1,2048,2,128]{4,3,2,1,0:T(2,128)(2,1)}, u32[]{:S(2)}) copy-start(bf16[1,1,2048,2,128]{4,3,2,1,0:T(2,128)(2,1)} %param.15) | copy-start | bytes 3145732
  7.2 151.6 %all-gather.3.cloned.1.call-start = ((), (), s32[]{:S(2)}) async-start(), calls=%async_computation.1 | async-start | bytes 2129920 | tf_op jit(solution)/shard_map/all_gather | solution.py:133
  41.4 6.9 %collective-permute-start = (bf16[512,3,32]{0,2,1:T(8,128)(2,1)S(1)}, bf16[512,3,32]{0,2,1:T(8,128)(2,1)S(1)}, u32[]{:S(2)}, u32[]{:S(2)}) collective-permute-start(bf16[512,3,32]{0,2,1:T(8,128)(2,1)S(1)} %add_convert_fusion.1), channel_id=1, source_target_pairs={{0,1},{1,0},{2,3},{3,2},{4,5},{5,4},{6,7},{7,6},{8,9},{9,8},{10,11... | collective-permute-start | bytes 294920 | tf_op jit(solution)/shard_map/ppermute | solution.py:16
  48.4 9.2 %collective-permute-start.1 = (bf16[512,3,64]{0,2,1:T(8,128)(2,1)S(1)}, bf16[512,3,64]{0,2,1:T(8,128)(2,1)S(1)}, u32[]{:S(2)}, u32[]{:S(2)}) collective-permute-start(bf16[512,3,64]{0,2,1:T(8,128)(2,1)S(1)} %maximum_select_fusion.1), channel_id=1, source_target_pairs={{0,2},{1,3},{2,0},{3,1},{4,6},{5,7},{6,4},{7,5},{8,10},{9,11},{10,... | collective-permute-start | bytes 589832 | tf_op jit(solution)/shard_map/ppermute | solution.py:16
  59.1 11.5 %collective-permute-start.2 = (f32[512]{0:T(512)S(1)}, f32[512]{0:T(512)S(1)}, u32[]{:S(2)}, u32[]{:S(2)}) collective-permute-start(f32[512]{0:T(512)S(1)} %get-tuple-element.27), channel_id=1, source_target_pairs={{0,2},{1,3},{2,0},{3,1},{4,6},{5,7},{6,4},{7,5},{8,10},{9,11},{10,... | collective-permute-start | bytes 6152 | tf_op jit(solution)/shard_map/ppermute | solution.py:16
  63.5 7.1 %collective-permute-start.6 = (f32[512]{0:T(512)S(1)}, f32[512]{0:T(512)S(1)}, u32[]{:S(2)}, u32[]{:S(2)}) collective-permute-start(f32[512]{0:T(512)S(1)} %fusion.3), channel_id=1, source_target_pairs={{0,2},{1,3},{2,0},{3,1},{4,6},{5,7},{6,4},{7,5},{8,10},{9,11},{10,... | collective-permute-start | bytes 6152 | tf_op jit(solution)/shard_map/ppermute | solution.py:16
  65.9 13.0 %copy-start.5 = (bf16[256,32]{0,1:T(8,128)(2,1)S(1)}, bf16[256,32]{0,1:T(8,128)(2,1)}, u32[]{:S(2)}) copy-start(bf16[256,32]{0,1:T(8,128)(2,1)} %param.21) | copy-start | bytes 49156
  65.9 37.6 %copy-start.6 = (f32[2,2048]{1,0:T(2,128)S(1)}, f32[2,2048]{1,0:T(2,128)}, u32[]{:S(2)}) copy-start(f32[2,2048]{1,0:T(2,128)} %param.25) | copy-start | bytes 49156
  66.9 95.4 %copy-start.3 = (bf16[256,128]{1,0:T(8,128)(2,1)S(1)}, bf16[256,128]{1,0:T(8,128)(2,1)}, u32[]{:S(2)}) copy-start(bf16[256,128]{1,0:T(8,128)(2,1)} %param.22) | copy-start | bytes 196612
  66.9 122.7 %copy-start.4 = (bf16[256,128]{1,0:T(8,128)(2,1)S(1)}, bf16[256,128]{1,0:T(8,128)(2,1)}, u32[]{:S(2)}) copy-start(bf16[256,128]{1,0:T(8,128)(2,1)} %param.24) | copy-start | bytes 196612
  67.0 8.0 %collective-permute-start.3 = (f32[512,64]{0,1:T(8,128)S(1)}, f32[512,64]{0,1:T(8,128)S(1)}, u32[]{:S(2)}, u32[]{:S(2)}) collective-permute-start(f32[512,64]{0,1:T(8,128)S(1)} %select_bitcast_fusion), channel_id=1, source_target_pairs={{0,2},{1,3},{2,0},{3,1},{4,6},{5,7},{6,4},{7,5},{8,10},{9,11},{10,... | collective-permute-start | bytes 393224 | tf_op jit(solution)/shard_map/ppermute | solution.py:16
  70.6 6.4 %collective-permute-start.7 = (f32[512]{0:T(512)S(1)}, f32[512]{0:T(512)S(1)}, u32[]{:S(2)}, u32[]{:S(2)}) collective-permute-start(f32[512]{0:T(512)S(1)} %get-tuple-element.11), channel_id=1, source_target_pairs={{0,1},{1,0},{2,3},{3,2},{4,5},{5,4},{6,7},{7,6},{8,9},{9,8},{10,11... | collective-permute-start | bytes 6152 | tf_op jit(solution)/shard_map/ppermute | solution.py:16
  72.5 4.5 %collective-permute-start.4 = (f32[512]{0:T(512)S(1)}, f32[512]{0:T(512)S(1)}, u32[]{:S(2)}, u32[]{:S(2)}) collective-permute-start(f32[512]{0:T(512)S(1)} %get-tuple-element.14), channel_id=1, source_target_pairs={{0,1},{1,0},{2,3},{3,2},{4,5},{5,4},{6,7},{7,6},{8,9},{9,8},{10,11... | collective-permute-start | bytes 6152 | tf_op jit(solution)/shard_map/ppermute | solution.py:16
  75.0 139.9 %copy-start.7 = (f32[2,2048]{1,0:T(2,128)S(1)}, f32[2,2048]{1,0:T(2,128)}, u32[]{:S(2)}) copy-start(f32[2,2048]{1,0:T(2,128)} %param.26) | copy-start | bytes 49156
  75.0 139.9 %copy-start.8 = (f32[2,2048]{1,0:T(2,128)S(1)}, f32[2,2048]{1,0:T(2,128)}, u32[]{:S(2)}) copy-start(f32[2,2048]{1,0:T(2,128)} %param.27) | copy-start | bytes 49156
  75.1 3.1 collective-permute-start.5
  78.9 164.4 %all-gather.5.cloned.1.call-start = ((), (), s32[]{:S(2)}) async-start(), calls=%async_computation.2 | async-start | bytes 2129920 | tf_op jit(solution)/shard_map/all_gather | solution.py:139
  161.5 246.3 %reduce-scatter.4.cloned.1.call-start = ((), (), s32[]{:S(2)}) async-start(), calls=%async_computation.3 | async-start | bytes 4259840 | tf_op jit(solution)/shard_map/reduce_scatter | solution.py:150
  214.9 32.4 %copy-start = (bf16[1,512,2048]{2,1,0:T(8,128)(2,1)S(1)}, bf16[1,512,2048]{2,1,0:T(8,128)(2,1)}, u32[]{:S(2)}) copy-start(bf16[1,512,2048]{2,1,0:T(8,128)(2,1)} %param.14) | copy-start | bytes 6291460
  247.2 2.4 copy-start.1
Sparse Core Ops, SparseCore 0:
  79.0 79.7 all-gather.2
  162.7 80.5 all-gather.4
  257.9 149.8 reduce-scatter.3
where the time goes:
time: 419 us; the launch traced here: 418 us
  waiting for transfers between devices  240 us (57%)
  blocking collectives  109 us (26%)
  starting transfers between devices  21.2 us (5%)
  between operations  14.8 us (4%)
  other arithmetic  13.2 us (3%)
  matrix products  11.9 us (3%)
  local copies, waits for them, and re-layouts  8.04 us (2%)
    reduce_scatter x1, waiting for transfers between devices, local(): lax.psum_scatter(jnp.einsum('rf,df->rd', inner, full_down, preferred_elem...  149 us
    all_gather x1, waiting for transfers between devices, local(): lax.all_gather(context_columns, 'blk', axis=1, tiled=True)  55.2 us
    all_gather x1, blocking collectives, local(): lax.all_gather(qkv_weight, 'req', axis=0, tiled=True)  31.7 us
    all_gather x1, waiting for transfers between devices, local(): projected = lax.all_gather(projected_part, 'blk', axis=1, tiled=True)  28.3 us
    all_gather x1, blocking collectives, local(): lax.all_gather(in_weight, 'req', axis=0, tiled=True)  27.3 us
    all_gather x1, blocking collectives, local(): lax.all_gather(down_weight, 'req', axis=0, tiled=True)  25.3 us
    all_gather x1, blocking collectives, local(): lax.all_gather(out_weight, 'req', axis=0, tiled=True)  24.6 us
    ppermute x8, starting transfers between devices, from_partner(): lax.ppermute(value, axis, [(i, i ^ 1 << distance) for i in range(lax.axis...  21.1 us
  transfers between devices with their start and end apart: 11, of which 5 were waited for; matrix products, arithmetic and copies ran while one was open for 2% of the time, Pallas kernels for 0%

commit v1 on v0

--- a/solution.py
+++ b/solution.py
@@ -3,6 +3,7 @@
 import jax
 import jax.numpy as jnp
 from jax import lax
+from jax.sharding import Mesh
 from jax.sharding import PartitionSpec as P
 
 HEADS = 16
@@ -10,10 +11,12 @@
 
 
 MASKED = -1e30
-
-
-def from_partner(value, axis, distance):
-    return lax.ppermute(value, axis, [(i, i ^ 1 << distance) for i in range(lax.axis_size(axis))])
+PLANE = ("bx", "by")
+BLK = ("bx", "by", "bc")
+
+
+def swap(axis, n):
+    return [(i, i ^ 1) for i in range(n)]
 
 
 def layer_norm(values, gain_row, shift_row):
@@ -42,6 +45,14 @@
     scale_later = jnp.exp(later_part[1] - joined)
     numerator = earlier_part[0] * scale_earlier[:, None] + later_part[0] * scale_later[:, None]
     return (numerator, joined, earlier_part[2] * scale_earlier + later_part[2] * scale_later)
+
+
+def core_pair(own, other, core, axis):
+    return jnp.where(
+        core == 0,
+        jnp.concatenate([own, other], axis=axis),
+        jnp.concatenate([other, own], axis=axis),
+    )
 
 
 def local(
@@ -60,29 +71,56 @@
     norm_gains,
     norm_biases,
 ):
-    full_qkv, full_out, full_in, full_down = (
-        lax.all_gather(qkv_weight, "req", axis=0, tiled=True),
-        lax.all_gather(out_weight, "req", axis=0, tiled=True),
-        lax.all_gather(in_weight, "req", axis=0, tiled=True),
-        lax.all_gather(down_weight, "req", axis=0, tiled=True),
-    )
-    group_size = lax.axis_size("blk")
+    nx, ny, nc = lax.axis_size("bx"), lax.axis_size("by"), lax.axis_size("bc")
+    core = lax.axis_index("bc")
+    chip = lax.axis_index("bx") * ny + lax.axis_index("by")
+    block_index = chip * nc + core
+    group_size = nx * ny * nc
     groups = group_size // HEADS
     low_bits = groups.bit_length() - 1
-    block_index = lax.axis_index("blk")
     group_index = block_index % groups
+
+    rows, _, column_width = qkv_weight.shape
+    qkv_flat = qkv_weight.reshape(rows, 3 * column_width)
+    hidden_width = in_weight.shape[1]
+    packed = jnp.concatenate([qkv_flat, out_weight, in_weight, down_weight], axis=1)
+    full = lax.all_gather(packed, "req", axis=0, tiled=True)
+    edges = [0, 3 * column_width, 4 * column_width, 4 * column_width + hidden_width]
+    full_qkv = full[:, : edges[1]].reshape(-1, 3, column_width)
+    late = full[:, edges[1] :]
+    sibling = lax.ppermute(late, "bc", swap("bc", nc))
+    chip_out = core_pair(late[:, :column_width], sibling[:, :column_width], core, 1)
+    chip_in = jnp.concatenate(
+        [late[:, column_width : column_width + hidden_width], sibling[:, column_width : column_width + hidden_width]],
+        axis=1,
+    )
+    chip_down = jnp.concatenate(
+        [late[:, column_width + hidden_width :], sibling[:, column_width + hidden_width :]], axis=1
+    )
+    sibling_block = block_index ^ 1
+    chip_in_bias = jnp.concatenate(
+        [
+            lax.dynamic_slice_in_dim(in_bias, block_index * hidden_width, hidden_width),
+            lax.dynamic_slice_in_dim(in_bias, sibling_block * hidden_width, hidden_width),
+        ]
+    )
+
     query_total = tokens.shape[1]
-    own_rows = query_total // group_size
-    column_width = full_qkv.shape[2]
     token_rows = tokens[0]
     qkv_columns = (
         jnp.einsum("td,dce->tce", token_rows, full_qkv, preferred_element_type=jnp.float32)
         + qkv_bias
     ).astype(jnp.bfloat16)
     appended = qkv_columns[None, :, 1:]
+
+    def from_partner(value, bit_level):
+        if bit_level == 0:
+            return lax.ppermute(value, "bc", swap("bc", nc))
+        return lax.ppermute(value, "by", [(i, i ^ (1 << (bit_level - 1))) for i in range(ny)])
+
     head_qkv = qkv_columns
     for bit_level in range(low_bits):
-        partner = from_partner(head_qkv, "blk", bit_level)
+        partner = from_partner(head_qkv, bit_level)
         upper_bit = group_index >> bit_level & 1
         head_qkv = jnp.where(
             upper_bit == 1,
@@ -122,38 +160,44 @@
         upper_bit = group_index >> bit_level & 1
         kept_half = jnp.where(upper_bit == 1, halves[:, 1], halves[:, 0])
         sent_half = jnp.where(upper_bit == 1, halves[:, 0], halves[:, 1])
-        other_sum, other_max, other_total = from_partner(
-            (sent_half, row_max, row_total), "blk", bit_level
-        )
+        other_sum, other_max, other_total = from_partner((sent_half, row_max, row_total), bit_level)
         numerator, row_max, row_total = merge_blocks(
             (kept_half, row_max, row_total), (other_sum, other_max, other_total)
         )
     context_columns = (numerator / row_total[:, None]).astype(jnp.bfloat16)
-    out_sum = jnp.dot(
-        lax.all_gather(context_columns, "blk", axis=1, tiled=True),
-        full_out,
-        preferred_element_type=jnp.float32,
-    )
-    column_bias = lax.dynamic_slice_in_dim(out_biases[0], block_index * column_width, column_width)
-    projected_part = (out_sum + column_bias).astype(jnp.bfloat16)
-    projected = lax.all_gather(projected_part, "blk", axis=1, tiled=True)
+
+    block_rows = query_total // (group_size)
+    chips = nx * ny
+    by_core = context_columns.reshape(chips, nc, block_rows, column_width)
+    mine = lax.dynamic_index_in_dim(by_core, core, axis=1, keepdims=False)
+    theirs = lax.dynamic_index_in_dim(by_core, 1 - core, axis=1, keepdims=False)
+    got = lax.ppermute(theirs, "bc", swap("bc", nc))
+    chip_context = core_pair(mine, got, core, 2).reshape(chips * block_rows, nc * column_width)
+    core_context = lax.all_gather(chip_context, PLANE, axis=1, tiled=True)
+    chip_width = nc * column_width
+    column_bias = lax.dynamic_slice_in_dim(out_biases[0], chip * chip_width, chip_width)
+    projected_part = (
+        jnp.dot(core_context, chip_out, preferred_element_type=jnp.float32) + column_bias
+    ).astype(jnp.bfloat16)
+    projected = lax.all_gather(projected_part, PLANE, axis=1, tiled=True)
+    core_tokens = lax.dynamic_index_in_dim(
+        token_rows.reshape(chips, nc, block_rows, -1), core, axis=1, keepdims=False
+    ).reshape(chips * block_rows, -1)
     normed = layer_norm(
-        token_rows.astype(jnp.float32) + projected.astype(jnp.float32),
+        core_tokens.astype(jnp.float32) + projected.astype(jnp.float32),
         norm_gains[0],
         norm_biases[0],
     ).astype(jnp.bfloat16)
-    hidden_width = full_in.shape[1]
-    bias_slice = lax.dynamic_slice_in_dim(in_bias, block_index * hidden_width, hidden_width)
     inner = jax.nn.gelu(
-        jnp.dot(normed, full_in, preferred_element_type=jnp.float32) + bias_slice, approximate=True
+        jnp.dot(normed, chip_in, preferred_element_type=jnp.float32) + chip_in_bias, approximate=True
     ).astype(jnp.bfloat16)
     mixed_rows = lax.psum_scatter(
-        jnp.einsum("rf,df->rd", inner, full_down, preferred_element_type=jnp.float32),
-        "blk",
+        jnp.einsum("rf,df->rd", inner, chip_down, preferred_element_type=jnp.float32),
+        PLANE,
         scatter_dimension=0,
         tiled=True,
     )
-    own_normed = lax.dynamic_slice_in_dim(normed, block_index * own_rows, own_rows, 0)
+    own_normed = lax.dynamic_slice_in_dim(normed, chip * block_rows, block_rows, 0)
     layer_output = layer_norm(
         own_normed.astype(jnp.float32) + mixed_rows + out_biases[1], norm_gains[1], norm_biases[1]
     ).astype(jnp.bfloat16)
@@ -161,25 +205,27 @@
 
 
 def solution(mesh):
+    req, blk = mesh.devices.shape
+    fine = Mesh(mesh.devices.reshape(req, 4, blk // 8, 2), ("req",) + BLK)
     return jax.shard_map(
         local,
-        mesh=mesh,
+        mesh=fine,
         in_specs=(
             P("req", None, None),
-            P("req", "blk", None, None, None),
+            P("req", BLK, None, None, None),
             P("req", None),
             P("req"),
             P("req", None),
-            P("req", None, "blk"),
-            P(None, "blk"),
-            P("req", "blk"),
-            P("req", "blk"),
-            P(),
-            P("req", "blk"),
+            P("req", None, BLK),
+            P(None, BLK),
+            P("req", BLK),
+            P("req", BLK),
+            P(),
+            P("req", BLK),
             P(),
             P(),
             P(),
         ),
-        out_specs=(P("req", "blk", None), P("req", None, None, "blk")),
+        out_specs=(P("req", BLK, None), P("req", None, None, BLK)),
         check_vma=False,
     )

time: 419 us -> 506 us (1.21)
  waiting for transfers between devices: 240 us -> 421 us
  blocking collectives: 109 us -> 0 us
  local copies, waits for them, and re-layouts: 8.04 us -> 19.3 us
    all_gather x4 -> x0, blocking collectives: 109 us -> none  [the longest x1 31.7 us: local(): lax.all_gather(qkv_weight, 'req', axis=0, tiled=True)]
    all_gather x2 -> x3, waiting for transfers between devices: 83.5 us -> 190 us  [the longest x1 75.2 us: local(): projected = lax.all_gather(projected_part, PLANE, axis=1, tiled=True)]
    reduce_scatter x1, waiting for transfers between devices: 149 us -> 219 us  [local(): lax.psum_scatter(jnp.einsum('rf,df->rd', inner, chip_down, preferred_elem...]
    slice x0 -> x7, local copies, waits for them, and re-layouts: none -> 7.48 us  [the longest x1 2.44 us: local(): late = full[:, edges[1]:]]
    ppermute x8 -> x10, waiting for transfers between devices: 6.85 us -> 11.7 us  [the longest x4 5.4 us: from_partner(): lax.ppermute(value, 'by', [(i, i ^ 1 << bit_level - 1) for i in range(ny)])]
    ppermute x8 -> x10, starting transfers between devices: 21.1 us -> 25.1 us  [the longest x4 12.6 us: from_partner(): lax.ppermute(value, 'by', [(i, i ^ 1 << bit_level - 1) for i in range(ny)])]
  transfers between devices with their start and end apart: 11 -> 14, of which waited for: 5 -> 9; matrix products, arithmetic and copies ran while one was open for 2% -> 4% of each run, Pallas kernels for 0% -> 0%
where the time goes in v1:
time: 506 us; the launch traced here: 504 us
  waiting for transfers between devices  421 us (83%)
  starting transfers between devices  25.2 us (5%)
  local copies, waits for them, and re-layouts  19.3 us (4%)
  between operations  14.9 us (3%)
  matrix products  12.9 us (3%)
  other arithmetic  11.4 us (2%)
    reduce_scatter x1, waiting for transfers between devices, local(): lax.psum_scatter(jnp.einsum('rf,df->rd', inner, chip_down, preferred_elem...  219 us
    all_gather x1, waiting for transfers between devices, local(): projected = lax.all_gather(projected_part, PLANE, axis=1, tiled=True)  75.2 us
    all_gather x1, waiting for transfers between devices, local(): core_context = lax.all_gather(chip_context, PLANE, axis=1, tiled=True)  71.1 us
    all_gather x1, waiting for transfers between devices, local(): full = lax.all_gather(packed, 'req', axis=0, tiled=True)  43.7 us
    ppermute x4, starting transfers between devices, from_partner(): lax.ppermute(value, 'by', [(i, i ^ 1 << bit_level - 1) for i in range(ny)])  12.6 us
  transfers between devices with their start and end apart: 14, of which 9 were waited for; matrix products, arithmetic and copies ran while one was open for 4% of the time, Pallas kernels for 0%

profile of v1, /device:TPU:16, one launch (start us, length us, event | category | flops | bytes accessed | tf_op | source)
XLA Modules:
  0.0 504.4 jit_solution(17972534868358181991)
XLA Ops:
  9.1 1.5 pad_maximum_fusion
  11.4 3.3 fusion.82
  16.3 2.0 and_reduce_fusion
  18.3 43.7 %all-gather.4.cloned.1.call-done = bf16[2048,384]{0,1:T(8,128)(2,1)} async-done(((bf16[256,384]{0,1:T(8,128)(2,1)}), bf16[2048,384]{0,1:T(8,128)(2,1)}) %all-gather.4.cloned.1.call-update) | async-done | bytes 1572880 | tf_op jit(solution)/shard_map/all_gather | solution.py:87
  63.9 1.9 collective-permute-start
  65.8 1.3 collective-permute-done
  67.1 3.4 collective-permute-start.1
  70.6 5.4 %collective-permute-done.1 = bf16[512,3,64]{0,2,1:T(8,128)(2,1)S(1)} collective-permute-done((bf16[512,3,64]{0,2,1:T(8,128)(2,1)S(1)}, bf16[512,3,64]{0,2,1:T(8,128)(2,1)S(1)}, u32[]{:S(2)}, u32[]{:S(2)}) %collective-permute-start.1) | collective-permute-done | bytes 196640 | tf_op jit(solution)/shard_map/ppermute | solution.py:119
  76.3 2.1 fusion.89
  78.4 3.4 collective-permute-start.2
  82.7 2.4 collective-permute-start.6
  85.3 3.2 fusion.3
  88.6 3.4 collective-permute-start.3
  92.0 1.9 collective-permute-start.4
  94.0 2.4 collective-permute-start.7
  96.5 2.1 collective-permute-start.5
  98.6 1.2 collective-permute-done.5
  99.9 2.1 collective-permute-start.8
  102.0 1.1 collective-permute-done.8
  104.0 2.4 slice.112
  106.4 2.1 collective-permute-start.9
  108.6 2.8 collective-permute-done.9
  112.0 71.1 %all-gather.6.cloned.1.call-done = bf16[256,2048]{0,1:T(8,128)(2,1)} async-done(((bf16[256,64]{0,1:T(8,128)(2,1)}), bf16[256,2048]{0,1:T(8,128)(2,1)}) %all-gather.6.cloned.1.call-update) | async-done | bytes 1048592 | tf_op jit(solution)/shard_map/all_gather | solution.py:176
  183.1 2.3 fusion.19
  187.7 2.3 fusion.80
  190.0 1.0 fusion.81
  191.1 75.2 %all-gather.8.cloned.1.call-done = bf16[256,2048]{0,1:T(8,128)(2,1)} async-done(((bf16[256,64]{0,1:T(8,128)(2,1)}), bf16[256,2048]{0,1:T(8,128)(2,1)}) %all-gather.8.cloned.1.call-update) | async-done | bytes 1048592 | tf_op jit(solution)/shard_map/all_gather | solution.py:182
  266.3 1.5 copy.73
  268.7 1.5 add_convert_fusion
  270.2 4.5 fusion.23
  275.4 218.9 %reduce-scatter.4.cloned.1.call-done = f32[8,2048]{1,0:T(8,128)} async-done(((f32[256,2048]{1,0:T(8,128)}), f32[8,2048]{1,0:T(8,128)}) %reduce-scatter.4.cloned.1.call-update) | async-done | bytes 65552 | tf_op jit(solution)/shard_map/reduce_scatter | solution.py:194
  496.3 1.5 fusion.62
  (73 shorter events, 14.5 us)
Async XLA Ops:
  7.2 54.9 %all-gather.4.cloned.1.call-start = ((), (), s32[]{:S(2)}) async-start(), calls=%async_computation.1 | async-start | bytes 1769472 | tf_op jit(solution)/shard_map/all_gather | solution.py:87
  10.6 172.5 %all-gather.6.cloned.1.call-start = ((), (), s32[]{:S(2)}) async-start(), calls=%async_computation.2 | async-start | bytes 1081344 | tf_op jit(solution)/shard_map/all_gather | solution.py:176
  14.7 1.0 copy-start.4
  14.7 48.4 %copy-start = (bf16[1,512,2048]{2,1,0:T(8,128)(2,1)S(1)}, bf16[1,512,2048]{2,1,0:T(8,128)(2,1)}, u32[]{:S(2)}) copy-start(bf16[1,512,2048]{2,1,0:T(8,128)(2,1)} %param.14) | copy-start | bytes 6291460
  14.7 48.3 %copy-start.5 = (f32[3,32]{1,0:T(4,128)S(1)}, f32[3,32]{1,0:T(4,128)}, u32[]{:S(2)}) copy-start(f32[3,32]{1,0:T(4,128)} %param.20) | copy-start | bytes 1156
  63.9 3.2 collective-permute-start
  67.1 8.9 %collective-permute-start.1 = (bf16[512,3,64]{0,2,1:T(8,128)(2,1)S(1)}, bf16[512,3,64]{0,2,1:T(8,128)(2,1)S(1)}, u32[]{:S(2)}, u32[]{:S(2)}) collective-permute-start(bf16[512,3,64]{0,2,1:T(8,128)(2,1)S(1)} %maximum_select_fusion.3), channel_id=1, source_target_pairs={{0,2},{2,0},{4,6},{6,4},{8,10},{10,8},{12,14},{14,12},{1,3},{3,1},... | collective-permute-start | bytes 589832 | tf_op jit(solution)/shard_map/ppermute | solution.py:119
  78.4 4.3 copy-start.1
  78.4 13.6 %collective-permute-start.2 = (f32[512]{0:T(512)S(1)}, f32[512]{0:T(512)S(1)}, u32[]{:S(2)}, u32[]{:S(2)}) collective-permute-start(f32[512]{0:T(512)S(1)} %get-tuple-element.37), channel_id=1, source_target_pairs={{0,2},{2,0},{4,6},{6,4},{8,10},{10,8},{12,14},{14,12},{1,3},{3,1},... | collective-permute-start | bytes 6152 | tf_op jit(solution)/shard_map/ppermute | solution.py:119
  82.7 9.3 %collective-permute-start.6 = (f32[512]{0:T(512)S(1)}, f32[512]{0:T(512)S(1)}, u32[]{:S(2)}, u32[]{:S(2)}) collective-permute-start(f32[512]{0:T(512)S(1)} %fusion.1), channel_id=1, source_target_pairs={{0,2},{2,0},{4,6},{6,4},{8,10},{10,8},{12,14},{14,12},{1,3},{3,1},... | collective-permute-start | bytes 6152 | tf_op jit(solution)/shard_map/ppermute | solution.py:119
  88.6 19.9 %copy-start.2 = (f32[2,2048]{1,0:T(2,128)S(1)}, f32[2,2048]{1,0:T(2,128)}, u32[]{:S(2)}) copy-start(f32[2,2048]{1,0:T(2,128)} %param.25) | copy-start | bytes 49156
  88.6 7.8 %collective-permute-start.3 = (f32[512,64]{0,1:T(8,128)S(1)}, f32[512,64]{0,1:T(8,128)S(1)}, u32[]{:S(2)}, u32[]{:S(2)}) collective-permute-start(f32[512,64]{0,1:T(8,128)S(1)} %select_bitcast_fusion), channel_id=1, source_target_pairs={{0,2},{2,0},{4,6},{6,4},{8,10},{10,8},{12,14},{14,12},{1,3},{3,1},... | collective-permute-start | bytes 393224 | tf_op jit(solution)/shard_map/ppermute | solution.py:119
  92.0 6.5 %collective-permute-start.4 = (f32[512]{0:T(512)S(1)}, f32[512]{0:T(512)S(1)}, u32[]{:S(2)}, u32[]{:S(2)}) collective-permute-start(f32[512]{0:T(512)S(1)} %get-tuple-element.16), channel_id=1, source_target_pairs={{0,1},{1,0},{2,3},{3,2},{4,5},{5,4},{6,7},{7,6},{8,9},{9,8},{10,11... | collective-permute-start | bytes 6152 | tf_op jit(solution)/shard_map/ppermute | solution.py:118
  94.0 4.6 collective-permute-start.7
  96.4 86.7 %slice-start = ((bf16[2048,384]{0,1:T(8,128)(2,1)}), bf16[2048,32]{0,1:T(8,128)(2,1)S(1)}, s32[]{:S(2)}) async-start(bf16[2048,384]{0,1:T(8,128)(2,1)} %all-gather.4.cloned.1.call-done), calls=%async_computation.5 | async-start | bytes 262144 | tf_op jit(solution)/shard_map/slice | solution.py:92
  96.5 3.3 collective-permute-start.5
  99.9 3.1 collective-permute-start.8
  103.9 83.0 %copy-start.3 = (f32[2,2048]{1,0:T(2,128)S(1)}, f32[2,2048]{1,0:T(2,128)}, u32[]{:S(2)}) copy-start(f32[2,2048]{1,0:T(2,128)} %param.26) | copy-start | bytes 49156
  103.9 162.4 %all-gather.8.cloned.1.call-start = ((), (), s32[]{:S(2)}) async-start(), calls=%async_computation.3 | async-start | bytes 1081344 | tf_op jit(solution)/shard_map/all_gather | solution.py:182
  106.4 4.9 collective-permute-start.9
  185.4 308.9 %reduce-scatter.4.cloned.1.call-start = ((), (), s32[]{:S(2)}) async-start(), calls=%async_computation.4 | async-start | bytes 2162688 | tf_op jit(solution)/shard_map/reduce_scatter | solution.py:194
  268.7 1.6 copy-start.6
Sparse Core Ops, SparseCore 0:
  10.8 51.2 all-gather.3
  104.0 79.0 all-gather.5
  186.9 79.3 all-gather.7
  274.9 219.3 reduce-scatter.3

commit v2 on v1

--- a/solution.py
+++ b/solution.py
@@ -83,11 +83,9 @@
     rows, _, column_width = qkv_weight.shape
     qkv_flat = qkv_weight.reshape(rows, 3 * column_width)
     hidden_width = in_weight.shape[1]
-    packed = jnp.concatenate([qkv_flat, out_weight, in_weight, down_weight], axis=1)
-    full = lax.all_gather(packed, "req", axis=0, tiled=True)
-    edges = [0, 3 * column_width, 4 * column_width, 4 * column_width + hidden_width]
-    full_qkv = full[:, : edges[1]].reshape(-1, 3, column_width)
-    late = full[:, edges[1] :]
+    full_qkv = lax.all_gather(qkv_flat, "req", axis=0, tiled=True).reshape(-1, 3, column_width)
+    packed = jnp.concatenate([out_weight, in_weight, down_weight], axis=1)
+    late = lax.all_gather(packed, "req", axis=0, tiled=True)
     sibling = lax.ppermute(late, "bc", swap("bc", nc))
     chip_out = core_pair(late[:, :column_width], sibling[:, :column_width], core, 1)
     chip_in = jnp.concatenate(
@@ -160,7 +158,9 @@
         upper_bit = group_index >> bit_level & 1
         kept_half = jnp.where(upper_bit == 1, halves[:, 1], halves[:, 0])
         sent_half = jnp.where(upper_bit == 1, halves[:, 0], halves[:, 1])
-        other_sum, other_max, other_total = from_partner((sent_half, row_max, row_total), bit_level)
+        sent = jnp.concatenate([sent_half, row_max[:, None], row_total[:, None]], axis=1)
+        got_back = from_partner(sent, bit_level)
+        other_sum, other_max, other_total = got_back[:, :-2], got_back[:, -2], got_back[:, -1]
         numerator, row_max, row_total = merge_blocks(
             (kept_half, row_max, row_total), (other_sum, other_max, other_total)
         )
@@ -169,17 +169,23 @@
     block_rows = query_total // (group_size)
     chips = nx * ny
     by_core = context_columns.reshape(chips, nc, block_rows, column_width)
-    mine = lax.dynamic_index_in_dim(by_core, core, axis=1, keepdims=False)
-    theirs = lax.dynamic_index_in_dim(by_core, 1 - core, axis=1, keepdims=False)
-    got = lax.ppermute(theirs, "bc", swap("bc", nc))
-    chip_context = core_pair(mine, got, core, 2).reshape(chips * block_rows, nc * column_width)
-    core_context = lax.all_gather(chip_context, PLANE, axis=1, tiled=True)
+    halves = by_core.transpose(1, 0, 2, 3).reshape(nc, chips * block_rows, column_width)
+    outgoing = jnp.broadcast_to(halves[None], (chips, nc, chips * block_rows, column_width))
+    incoming = lax.all_to_all(
+        outgoing.reshape(group_size, chips * block_rows, column_width), BLK, 0, 0, tiled=True
+    )
+    core_context = incoming.transpose(1, 0, 2).reshape(chips * block_rows, group_size * column_width)
     chip_width = nc * column_width
     column_bias = lax.dynamic_slice_in_dim(out_biases[0], chip * chip_width, chip_width)
     projected_part = (
         jnp.dot(core_context, chip_out, preferred_element_type=jnp.float32) + column_bias
     ).astype(jnp.bfloat16)
-    projected = lax.all_gather(projected_part, PLANE, axis=1, tiled=True)
+    spread = jnp.broadcast_to(projected_part[None], (chips,) + projected_part.shape)
+    projected = (
+        lax.all_to_all(spread, PLANE, 0, 0, tiled=True)
+        .transpose(1, 0, 2)
+        .reshape(projected_part.shape[0], chips * chip_width)
+    )
     core_tokens = lax.dynamic_index_in_dim(
         token_rows.reshape(chips, nc, block_rows, -1), core, axis=1, keepdims=False
     ).reshape(chips * block_rows, -1)
@@ -191,12 +197,10 @@
     inner = jax.nn.gelu(
         jnp.dot(normed, chip_in, preferred_element_type=jnp.float32) + chip_in_bias, approximate=True
     ).astype(jnp.bfloat16)
-    mixed_rows = lax.psum_scatter(
-        jnp.einsum("rf,df->rd", inner, chip_down, preferred_element_type=jnp.float32),
-        PLANE,
-        scatter_dimension=0,
-        tiled=True,
-    )
+    mixed_parts = jnp.einsum("rf,df->rd", inner, chip_down, preferred_element_type=jnp.float32)
+    mixed_rows = lax.all_to_all(
+        mixed_parts.reshape(chips, block_rows, -1), PLANE, 0, 0, tiled=True
+    ).sum(axis=0)
     own_normed = lax.dynamic_slice_in_dim(normed, chip * block_rows, block_rows, 0)
     layer_output = layer_norm(
         own_normed.astype(jnp.float32) + mixed_rows + out_biases[1], norm_gains[1], norm_biases[1]

time: 506 us -> 238 us (0.47)
  the two profiles are of different devices: /device:TPU:16 before, /device:TPU:8 now
where the time goes in v2:
time: 238 us; the launch traced here: 237 us
  waiting for transfers between devices  110 us (46%)
  starting transfers between devices  36.2 us (15%)
  blocking collectives  31.7 us (13%)
  local copies, waits for them, and re-layouts  23.7 us (10%)
  between operations  15.2 us (6%)
  other arithmetic  11.4 us (5%)
  matrix products  8.95 us (4%)
    all_to_all x1, waiting for transfers between devices, local(): lax.all_to_all(mixed_parts.reshape(chips, block_rows, -1), PLANE, 0, 0, t...  48.7 us
    all_gather x1, blocking collectives, local(): lax.all_gather(qkv_flat, 'req', axis=0, tiled=True)  31.7 us
    all_to_all x1, waiting for transfers between devices, local(): lax.all_to_all(spread, PLANE, 0, 0, tiled=True).transpose(1, 0, 2)  24.4 us
    all_gather x1, waiting for transfers between devices, local(): late = lax.all_gather(packed, 'req', axis=0, tiled=True)  23.1 us
    convert_element_type x3, local copies, waits for them, and re-layouts, local(): projected.astype(jnp.float32)  11.1 us
    ppermute x2, waiting for transfers between devices, from_partner(): lax.ppermute(value, 'by', [(i, i ^ 1 << bit_level - 1) for i in range(ny)])  10.8 us
    all_to_all x1, starting transfers between devices, local(): lax.all_to_all(outgoing.reshape(group_size, chips * block_rows, column_wi...  10.6 us
    all_to_all x1, starting transfers between devices, local(): lax.all_to_all(spread, PLANE, 0, 0, tiled=True).transpose(1, 0, 2)  9.85 us
  transfers between devices with their start and end apart: 9, of which 7 were waited for; matrix products, arithmetic and copies ran while one was open for 5% of the time, Pallas kernels for 0%

profile of v2, /device:TPU:8, one launch (start us, length us, event | category | flops | bytes accessed | tf_op | source)
XLA Modules:
  0.0 237.4 jit_solution(12036210565771078719)
XLA Ops:
  7.2 31.7 %all_gather.6 = bf16[2048,96]{0,1:T(8,128)(2,1)S(1)} all-gather(bf16[256,96]{0,1:T(8,128)(2,1)} %bitcast.116), channel_id=1, replica_groups=mesh['req'=8,'bx'=4,'by'=8,'bc'=2] {'req'}, dimensions={0}, use_global_device_ids=true | all-gather | bytes 442368 | tf_op jit(solution)/shard_map/all_gather | solution.py:86
  39.0 2.4 fusion.12
  41.4 1.9 collective-permute-start
  44.6 1.5 fusion.79
  46.3 2.0 and_reduce_fusion
  48.4 2.4 collective-permute-start.1
  50.8 6.8 %collective-permute-done.1 = bf16[512,3,64]{0,2,1:T(8,128)(2,1)S(1)} collective-permute-done((bf16[512,3,64]{0,2,1:T(8,128)(2,1)S(1)}, bf16[512,3,64]{0,2,1:T(8,128)(2,1)S(1)}, u32[]{:S(2)}, u32[]{:S(2)}) %collective-permute-start.1) | collective-permute-done | bytes 196640 | tf_op jit(solution)/shard_map/ppermute | solution.py:117
  58.0 1.1 fusion.86
  61.1 2.4 collective-permute-start.2
  64.4 4.0 %collective-permute-done.2 = f32[512,66]{0,1:T(8,128)S(1)} collective-permute-done((f32[512,66]{0,1:T(8,128)S(1)}, f32[512,66]{0,1:T(8,128)S(1)}, u32[]{:S(2)}, u32[]{:S(2)}) %collective-permute-start.2) | collective-permute-done | bytes 135200 | tf_op jit(solution)/shard_map/ppermute | solution.py:117
  68.6 1.9 collective-permute-start.3
  70.5 1.2 collective-permute-done.3
  72.0 1.1 broadcast_in_dim.29
  73.2 10.6 %all-to-all-start = ((bf16[64,256,32]{1,2,0:T(8,128)(2,1)}), bf16[64,256,32]{1,2,0:T(8,128)(2,1)S(1)}, u32[]{:S(2)}, u32[]{:S(2)}) async-start(bf16[64,256,32]{1,2,0:T(8,128)(2,1)} %bitcast.31), calls=%async_computation | async-start | bytes 2097152 | tf_op jit(solution)/shard_map/all_to_all | solution.py:174
  83.7 23.1 %all-gather.2.cloned.1.call-done = bf16[2048,288]{0,1:T(8,128)(2,1)} async-done(((bf16[256,288]{0,1:T(8,128)(2,1)}), bf16[2048,288]{0,1:T(8,128)(2,1)}) %all-gather.2.cloned.1.call-update) | async-done | bytes 1179664 | tf_op jit(solution)/shard_map/all_gather | solution.py:88
  106.8 1.9 collective-permute-start.4
  109.8 2.0 collective-permute-done.4
  111.8 1.0 copy-done.4
  113.1 1.1 broadcast_in_dim.30
  114.2 9.9 %all-to-all-start.1 = ((bf16[32,256,64]{1,2,0:T(8,128)(2,1)}), bf16[32,256,64]{1,2,0:T(8,128)(2,1)S(1)}, u32[]{:S(2)}, u32[]{:S(2)}) async-start(bf16[32,256,64]{1,2,0:T(8,128)(2,1)} %broadcast_in_dim.30), calls=%async_computation.1 | async-start | bytes 2097152 | tf_op jit(solution)/shard_map/all_to_all | solution.py:185
  125.0 1.1 fusion.77
  126.1 2.3 fusion.78
  128.4 24.4 %all-to-all-done.1 = bf16[32,256,64]{1,2,0:T(8,128)(2,1)S(1)} async-done(((bf16[32,256,64]{1,2,0:T(8,128)(2,1)}), bf16[32,256,64]{1,2,0:T(8,128)(2,1)S(1)}, u32[]{:S(2)}, u32[]{:S(2)}) %all-to-all-start.1) | async-done | bytes 1048608 | tf_op jit(solution)/shard_map/all_to_all | solution.py:185
  152.8 1.9 convert_bitcast_fusion.1
  154.7 4.5 %copy.54 = f32[256,32,64]{2,1,0:T(8,128)} copy(f32[256,32,64]{0,2,1:T(8,128)S(1)} %get-tuple-element.15) | data formatting | bytes 4194304 | tf_op jit(solution)/shard_map/convert_element_type | solution.py:193
  159.2 3.6 %reshape.149 = f32[32,1,8,2048]{3,2,0,1:T(8,128)S(1)} reshape(f32[256,32,64]{2,1,0:T(8,128)} %copy.54) | data formatting | bytes 4194304 | tf_op jit(solution)/shard_map/convert_element_type | solution.py:193
  162.8 1.7 fusion.14
  165.2 3.1 %copy.53 = f32[256,2048]{1,0:T(8,128)} copy(f32[256,2048]{0,1:T(8,128)} %bitcast.102) | data formatting | bytes 4194304 | tf_op jit(solution)/shard_map/convert_element_type | solution.py:193
  168.4 2.1 fusion.11
  170.5 4.2 %convolution_bitcast_fusion = f32[32,8,2048]{2,1,0:T(8,128)} fusion(bf16[2048,128]{0,1:T(8,128)(2,1)} %get-tuple-element.14, bf16[2048,128]{0,1:T(8,128)(2,1)} %get-tuple-element.12, bf16[256,2048]{1,0:T(8,128)(2,1)S(1)} %fusion.11, bf16[2048,128]{0,1:T(8,128)(2,1)} %get-tuple-element.13, bf16[2048,128]{0,1:T(8,128)(2,1)} %get-tuple-element.11, ...), kind=kOutput, calls=%fused_computation.6 | convolution fusion | flops 541720576 | bytes 5243904 | tf_op jit(solution)/shard_map/rf,df->rd/dot_general | solution.py:200
  174.8 5.2 %all-to-all-start.2 = ((f32[32,8,2048]{2,1,0:T(8,128)}), f32[32,8,2048]{2,1,0:T(8,128)S(1)}, u32[]{:S(2)}, u32[]{:S(2)}) async-start(f32[32,8,2048]{2,1,0:T(8,128)} %convolution_bitcast_fusion), calls=%async_computation.2 | async-start | bytes 4194304 | tf_op jit(solution)/shard_map/all_to_all | solution.py:201
  180.6 48.7 %all-to-all-done.2 = f32[32,8,2048]{2,1,0:T(8,128)S(1)} async-done(((f32[32,8,2048]{2,1,0:T(8,128)}), f32[32,8,2048]{2,1,0:T(8,128)S(1)}, u32[]{:S(2)}, u32[]{:S(2)}) %all-to-all-start.2) | async-done | bytes 2097184 | tf_op jit(solution)/shard_map/all_to_all | solution.py:201
  (79 shorter events, 9.5 us)
Async XLA Ops:
  7.2 34.2 %copy-start.11 = (f32[3,32]{1,0:T(4,128)S(1)}, f32[3,32]{1,0:T(4,128)}, u32[]{:S(2)}) copy-start(f32[3,32]{1,0:T(4,128)} %param.20) | copy-start | bytes 1156
  7.2 36.9 %copy-start.12 = (s32[1,2]{1,0:T(1,128)S(1)}, s32[1,2]{1,0:T(1,128)}, u32[]{:S(2)}) copy-start(s32[1,2]{1,0:T(1,128)} %param.18) | copy-start | bytes 28
  7.2 37.4 %copy-start.2 = (bf16[1,1,2048,2,128]{4,3,2,1,0:T(2,128)(2,1)S(1)}, bf16[1,1,2048,2,128]{4,3,2,1,0:T(2,128)(2,1)}, u32[]{:S(2)}) copy-start(bf16[1,1,2048,2,128]{4,3,2,1,0:T(2,128)(2,1)} %param.15) | copy-start | bytes 3145732
  7.2 99.6 %all-gather.2.cloned.1.call-start = ((), (), s32[]{:S(2)}) async-start(), calls=%async_computation.3 | async-start | bytes 1327104 | tf_op jit(solution)/shard_map/all_gather | solution.py:88
  41.4 6.9 %collective-permute-start = (bf16[512,3,32]{0,2,1:T(8,128)(2,1)S(1)}, bf16[512,3,32]{0,2,1:T(8,128)(2,1)S(1)}, u32[]{:S(2)}, u32[]{:S(2)}) collective-permute-start(bf16[512,3,32]{0,2,1:T(8,128)(2,1)S(1)} %add_convert_fusion), channel_id=1, source_target_pairs={{0,1},{1,0},{2,3},{3,2},{4,5},{5,4},{6,7},{7,6},{8,9},{9,8},{10,11... | collective-permute-start | bytes 294920 | tf_op jit(solution)/shard_map/ppermute | solution.py:116
  48.4 9.2 %collective-permute-start.1 = (bf16[512,3,64]{0,2,1:T(8,128)(2,1)S(1)}, bf16[512,3,64]{0,2,1:T(8,128)(2,1)S(1)}, u32[]{:S(2)}, u32[]{:S(2)}) collective-permute-start(bf16[512,3,64]{0,2,1:T(8,128)(2,1)S(1)} %maximum_select_fusion.3), channel_id=1, source_target_pairs={{0,2},{2,0},{4,6},{6,4},{8,10},{10,8},{12,14},{14,12},{1,3},{3,1},... | collective-permute-start | bytes 589832 | tf_op jit(solution)/shard_map/ppermute | solution.py:117
  60.0 3.5 %copy-start.5 = (bf16[256,128]{1,0:T(8,128)(2,1)S(1)}, bf16[256,128]{1,0:T(8,128)(2,1)}, u32[]{:S(2)}) copy-start(bf16[256,128]{1,0:T(8,128)(2,1)} %param.22) | copy-start | bytes 196612
  60.0 3.6 %copy-start.6 = (bf16[256,128]{1,0:T(8,128)(2,1)S(1)}, bf16[256,128]{1,0:T(8,128)(2,1)}, u32[]{:S(2)}) copy-start(bf16[256,128]{1,0:T(8,128)(2,1)} %param.24) | copy-start | bytes 196612
  60.0 3.7 %copy-start.7 = (bf16[256,32]{0,1:T(8,128)(2,1)S(1)}, bf16[256,32]{0,1:T(8,128)(2,1)}, u32[]{:S(2)}) copy-start(bf16[256,32]{0,1:T(8,128)(2,1)} %param.21) | copy-start | bytes 49156
  61.1 7.4 %collective-permute-start.2 = (f32[512,66]{0,1:T(8,128)S(1)}, f32[512,66]{0,1:T(8,128)S(1)}, u32[]{:S(2)}, u32[]{:S(2)}) collective-permute-start(f32[512,66]{0,1:T(8,128)S(1)} %pad_maximum_fusion.1), channel_id=1, source_target_pairs={{0,2},{2,0},{4,6},{6,4},{8,10},{10,8},{12,14},{14,12},{1,3},{3,1},... | collective-permute-start | bytes 405512 | tf_op jit(solution)/shard_map/ppermute | solution.py:117
  68.5 40.2 %copy-start.8 = (f32[2,2048]{1,0:T(2,128)S(1)}, f32[2,2048]{1,0:T(2,128)}, u32[]{:S(2)}) copy-start(f32[2,2048]{1,0:T(2,128)} %param.25) | copy-start | bytes 49156
  68.6 3.2 %collective-permute-start.3 = (f32[512,34]{0,1:T(8,128)S(1)}, f32[512,34]{0,1:T(8,128)S(1)}, u32[]{:S(2)}, u32[]{:S(2)}) collective-permute-start(f32[512,34]{0,1:T(8,128)S(1)} %pad_maximum_fusion.2), channel_id=1, source_target_pairs={{0,1},{1,0},{2,3},{3,2},{4,5},{5,4},{6,7},{7,6},{8,9},{9,8},{10,11... | collective-permute-start | bytes 208904 | tf_op jit(solution)/shard_map/ppermute | solution.py:116
  73.2 38.6 %all-to-all-start = ((bf16[64,256,32]{1,2,0:T(8,128)(2,1)}), bf16[64,256,32]{1,2,0:T(8,128)(2,1)S(1)}, u32[]{:S(2)}, u32[]{:S(2)}) async-start(bf16[64,256,32]{1,2,0:T(8,128)(2,1)} %bitcast.31), calls=%async_computation | async-start | bytes 2097152 | tf_op jit(solution)/shard_map/all_to_all | solution.py:174
  106.8 4.9 %collective-permute-start.4 = (bf16[2048,288]{0,1:T(8,128)(2,1)}, bf16[2048,288]{0,1:T(8,128)(2,1)S(1)}, u32[]{:S(2)}, u32[]{:S(2)}) collective-permute-start(bf16[2048,288]{0,1:T(8,128)(2,1)} %all-gather.2.cloned.1.call-done), channel_id=1, source_target_pairs={{0,1},{1,0},{2,3},{3,2},{4,5},{5,4},{6,7},{7,6},{8,9},{9,8},{10,11... | collective-permute-start | bytes 3538952 | tf_op jit(solution)/shard_map/ppermute | solution.py:89
  111.7 1.0 copy-start.4
  112.8 12.1 %copy-start.9 = (f32[2,2048]{1,0:T(2,128)S(1)}, f32[2,2048]{1,0:T(2,128)}, u32[]{:S(2)}) copy-start(f32[2,2048]{1,0:T(2,128)} %param.26) | copy-start | bytes 49156
  112.8 12.2 %copy-start.10 = (f32[2,2048]{1,0:T(2,128)S(1)}, f32[2,2048]{1,0:T(2,128)}, u32[]{:S(2)}) copy-start(f32[2,2048]{1,0:T(2,128)} %param.27) | copy-start | bytes 49156
  112.8 12.2 %copy-start.3 = (bf16[2048,288]{0,1:T(8,128)(2,1)S(1)}, bf16[2048,288]{0,1:T(8,128)(2,1)}, u32[]{:S(2)}) copy-start(bf16[2048,288]{0,1:T(8,128)(2,1)} %all-gather.2.cloned.1.call-done) | copy-start | bytes 3538948
  114.2 38.6 %all-to-all-start.1 = ((bf16[32,256,64]{1,2,0:T(8,128)(2,1)}), bf16[32,256,64]{1,2,0:T(8,128)(2,1)S(1)}, u32[]{:S(2)}, u32[]{:S(2)}) async-start(bf16[32,256,64]{1,2,0:T(8,128)(2,1)} %broadcast_in_dim.30), calls=%async_computation.1 | async-start | bytes 2097152 | tf_op jit(solution)/shard_map/all_to_all | solution.py:185
  162.8 1.9 copy-start
  165.2 3.2 %copy-start.1 = (bf16[1,512,2048]{2,1,0:T(8,128)(2,1)S(1)}, bf16[1,512,2048]{2,1,0:T(8,128)(2,1)}, u32[]{:S(2)}) copy-start(bf16[1,512,2048]{2,1,0:T(8,128)(2,1)} %param.14) | copy-start | bytes 6291460
  174.8 54.6 %all-to-all-start.2 = ((f32[32,8,2048]{2,1,0:T(8,128)}), f32[32,8,2048]{2,1,0:T(8,128)S(1)}, u32[]{:S(2)}, u32[]{:S(2)}) async-start(f32[32,8,2048]{2,1,0:T(8,128)} %convolution_bitcast_fusion), calls=%async_computation.2 | async-start | bytes 4194304 | tf_op jit(solution)/shard_map/all_to_all | solution.py:201
Sparse Core Ops, SparseCore 0:
  64.6 42.2 all-gather.1

commit v3 on v2

--- a/solution.py
+++ b/solution.py
@@ -33,8 +33,8 @@
     row_max = jnp.max(scores, axis=1)
     weights = jnp.where(visible, jnp.exp(scores - row_max[:, None]), 0.0)
     row_total = jnp.sum(weights, axis=1)
-    numerator = jnp.dot(
-        weights.astype(jnp.bfloat16), value_rows, preferred_element_type=jnp.float32
+    numerator = jnp.einsum(
+        "qk,kd->dq", weights.astype(jnp.bfloat16), value_rows, preferred_element_type=jnp.float32
     )
     return (numerator, row_max, row_total)
 
@@ -45,6 +45,12 @@
     scale_later = jnp.exp(later_part[1] - joined)
     numerator = earlier_part[0] * scale_earlier[:, None] + later_part[0] * scale_later[:, None]
     return (numerator, joined, earlier_part[2] * scale_earlier + later_part[2] * scale_later)
+
+
+def gather_rows(block):
+    reqs = lax.axis_size("req")
+    spread = jnp.broadcast_to(block[None], (reqs,) + block.shape)
+    return lax.all_to_all(spread, "req", 0, 0, tiled=True).reshape(reqs * block.shape[0], -1)
 
 
 def core_pair(own, other, core, axis):
@@ -83,9 +89,9 @@
     rows, _, column_width = qkv_weight.shape
     qkv_flat = qkv_weight.reshape(rows, 3 * column_width)
     hidden_width = in_weight.shape[1]
-    full_qkv = lax.all_gather(qkv_flat, "req", axis=0, tiled=True).reshape(-1, 3, column_width)
     packed = jnp.concatenate([out_weight, in_weight, down_weight], axis=1)
-    late = lax.all_gather(packed, "req", axis=0, tiled=True)
+    full_qkv = gather_rows(qkv_flat).reshape(-1, 3, column_width)
+    late = gather_rows(packed)
     sibling = lax.ppermute(late, "bc", swap("bc", nc))
     chip_out = core_pair(late[:, :column_width], sibling[:, :column_width], core, 1)
     chip_in = jnp.concatenate(
@@ -106,10 +112,10 @@
     query_total = tokens.shape[1]
     token_rows = tokens[0]
     qkv_columns = (
-        jnp.einsum("td,dce->tce", token_rows, full_qkv, preferred_element_type=jnp.float32)
-        + qkv_bias
-    ).astype(jnp.bfloat16)
-    appended = qkv_columns[None, :, 1:]
+        jnp.einsum("td,dce->cet", token_rows, full_qkv, preferred_element_type=jnp.float32)
+        + qkv_bias[:, :, None]
+    ).astype(jnp.bfloat16)
+    appended = qkv_columns[1:].transpose(2, 0, 1)[None]
 
     def from_partner(value, bit_level):
         if bit_level == 0:
@@ -122,14 +128,14 @@
         upper_bit = group_index >> bit_level & 1
         head_qkv = jnp.where(
             upper_bit == 1,
-            jnp.concatenate([partner, head_qkv], axis=2),
-            jnp.concatenate([head_qkv, partner], axis=2),
+            jnp.concatenate([partner, head_qkv], axis=1),
+            jnp.concatenate([head_qkv, partner], axis=1),
         )
-    queries = head_qkv[:, 0]
+    queries = head_qkv[0].T
     fresh_count = query_total // groups
     fresh_start = group_index * fresh_count
-    fresh_keys = lax.dynamic_slice_in_dim(head_qkv[:, 1], fresh_start, fresh_count, 0)
-    fresh_values = lax.dynamic_slice_in_dim(head_qkv[:, 2], fresh_start, fresh_count, 0)
+    fresh_keys = lax.dynamic_slice_in_dim(head_qkv[1], fresh_start, fresh_count, 1).T
+    fresh_values = lax.dynamic_slice_in_dim(head_qkv[2], fresh_start, fresh_count, 1).T
     cache_count = cache_entries.shape[2]
     cache_keys = cache_entries[0, 0, :, 0]
     cache_values = cache_entries[0, 0, :, 1]
@@ -146,46 +152,47 @@
     fresh_position = fresh_start + jnp.arange(fresh_count, dtype=jnp.int32)
     fresh_visible = fresh_position[None, :] <= query_position[:, None]
     cache_visible = jnp.broadcast_to(readable[None, :], (query_total, cache_count))
-    partial_value = partial_block(
+    numerator, row_max, row_total = partial_block(
         queries,
         jnp.concatenate([cache_keys, fresh_keys], axis=0),
         jnp.concatenate([cache_values, fresh_values], axis=0),
         jnp.concatenate([cache_visible, fresh_visible], axis=1),
     )
-    numerator, row_max, row_total = partial_value
     for bit_level in reversed(range(low_bits)):
-        halves = numerator.reshape(query_total, 2, -1)
+        halves = numerator.reshape(2, -1, query_total)
         upper_bit = group_index >> bit_level & 1
-        kept_half = jnp.where(upper_bit == 1, halves[:, 1], halves[:, 0])
-        sent_half = jnp.where(upper_bit == 1, halves[:, 0], halves[:, 1])
-        sent = jnp.concatenate([sent_half, row_max[:, None], row_total[:, None]], axis=1)
+        kept_half = jnp.where(upper_bit == 1, halves[1], halves[0])
+        sent_half = jnp.where(upper_bit == 1, halves[0], halves[1])
+        sent = jnp.concatenate([sent_half, row_max[None], row_total[None]], axis=0)
         got_back = from_partner(sent, bit_level)
-        other_sum, other_max, other_total = got_back[:, :-2], got_back[:, -2], got_back[:, -1]
-        numerator, row_max, row_total = merge_blocks(
-            (kept_half, row_max, row_total), (other_sum, other_max, other_total)
-        )
-    context_columns = (numerator / row_total[:, None]).astype(jnp.bfloat16)
+        other_sum, other_max, other_total = got_back[:-2], got_back[-2], got_back[-1]
+        joined = jnp.maximum(row_max, other_max)
+        scale_kept = jnp.exp(row_max - joined)
+        scale_other = jnp.exp(other_max - joined)
+        numerator = kept_half * scale_kept[None] + other_sum * scale_other[None]
+        row_max, row_total = joined, row_total * scale_kept + other_total * scale_other
+    context_columns = (numerator / row_total[None]).astype(jnp.bfloat16)
 
     block_rows = query_total // (group_size)
     chips = nx * ny
-    by_core = context_columns.reshape(chips, nc, block_rows, column_width)
-    halves = by_core.transpose(1, 0, 2, 3).reshape(nc, chips * block_rows, column_width)
-    outgoing = jnp.broadcast_to(halves[None], (chips, nc, chips * block_rows, column_width))
-    incoming = lax.all_to_all(
-        outgoing.reshape(group_size, chips * block_rows, column_width), BLK, 0, 0, tiled=True
-    )
-    core_context = incoming.transpose(1, 0, 2).reshape(chips * block_rows, group_size * column_width)
+    core_rows = chips * block_rows
+    halves = (
+        context_columns.reshape(column_width, chips, nc, block_rows)
+        .transpose(2, 0, 1, 3)
+        .reshape(nc, column_width, core_rows)
+    )
+    outgoing = jnp.broadcast_to(halves[None], (chips, nc, column_width, core_rows))
+    core_context = lax.all_to_all(
+        outgoing.reshape(group_size, column_width, core_rows), BLK, 0, 0, tiled=True
+    ).reshape(group_size * column_width, core_rows)
     chip_width = nc * column_width
     column_bias = lax.dynamic_slice_in_dim(out_biases[0], chip * chip_width, chip_width)
     projected_part = (
-        jnp.dot(core_context, chip_out, preferred_element_type=jnp.float32) + column_bias
+        jnp.einsum("ct,cd->dt", core_context, chip_out, preferred_element_type=jnp.float32)
+        + column_bias[:, None]
     ).astype(jnp.bfloat16)
     spread = jnp.broadcast_to(projected_part[None], (chips,) + projected_part.shape)
-    projected = (
-        lax.all_to_all(spread, PLANE, 0, 0, tiled=True)
-        .transpose(1, 0, 2)
-        .reshape(projected_part.shape[0], chips * chip_width)
-    )
+    projected = lax.all_to_all(spread, PLANE, 0, 0, tiled=True).reshape(chips * chip_width, core_rows).T
     core_tokens = lax.dynamic_index_in_dim(
         token_rows.reshape(chips, nc, block_rows, -1), core, axis=1, keepdims=False
     ).reshape(chips * block_rows, -1)

time: 238 us -> 211 us (0.89)
  blocking collectives: 31.7 us -> 0 us
  between operations: 15.2 us -> 1.78 us
  starting transfers between devices: 36.2 us -> 47.2 us
  waiting for transfers between devices: 110 us -> 118 us
    all_gather x1 -> x0, blocking collectives: 31.7 us -> none  [local(): lax.all_gather(qkv_flat, 'req', axis=0, tiled=True)]
    all_to_all x2 -> x4, waiting for transfers between devices: 24.4 us -> 54.4 us  [the longest x1 23.9 us: local(): lax.all_to_all(spread, PLANE, 0, 0, tiled=True)]
    all_gather x1 -> x0, waiting for transfers between devices: 23.1 us -> none  [local(): late = lax.all_gather(packed, 'req', axis=0, tiled=True)]
    all_to_all x2 -> x4, starting transfers between devices: 20.4 us -> 31.2 us  [the longest x2 14 us: gather_rows(): lax.all_to_all(spread, 'req', 0, 0, tiled=True)]
    convert_element_type x3 -> x1, local copies, waits for them, and re-layouts: 11.1 us -> 1.92 us  [local(): projected.astype(jnp.float32)]
    dot_general x2 -> x3, matrix products: 1.29 us -> 4.33 us  [the longest x1 1.77 us: local(): jnp.einsum('td,dce->cet', token_rows, full_qkv, preferred_element_type=jn...]
    broadcast_in_dim x3 -> x5, local copies, waits for them, and re-layouts: 1.83 us -> 4.59 us  [the longest x2 2.78 us: gather_rows(): spread = jnp.broadcast_to(block[None], (reqs,) + block.shape)]
  transfers between devices with their start and end apart: 9 -> 10, of which waited for: 7 -> 9; matrix products, arithmetic and copies ran while one was open for 5% -> 11% of each run, Pallas kernels for 0% -> 0%
where the time goes in v3:
time: 211 us; the launch traced here: 210 us
  waiting for transfers between devices  118 us (56%)
  starting transfers between devices  47.2 us (22%)
  local copies, waits for them, and re-layouts  22.4 us (11%)
  matrix products  10.7 us (5%)
  other arithmetic  9.44 us (4%)
    all_to_all x1, waiting for transfers between devices, local(): lax.all_to_all(mixed_parts.reshape(chips, block_rows, -1), PLANE, 0, 0, t...  48.7 us
    all_to_all x1, waiting for transfers between devices, local(): lax.all_to_all(spread, PLANE, 0, 0, tiled=True)  23.9 us
    all_to_all x1, waiting for transfers between devices, local(): lax.all_to_all(outgoing.reshape(group_size, column_width, core_rows), BLK...  22.9 us
    all_to_all x2, starting transfers between devices, gather_rows(): lax.all_to_all(spread, 'req', 0, 0, tiled=True)  14 us
    ppermute x2, waiting for transfers between devices, from_partner(): lax.ppermute(value, 'by', [(i, i ^ 1 << bit_level - 1) for i in range(ny)])  11.1 us
    all_to_all x1, starting transfers between devices, local(): lax.all_to_all(outgoing.reshape(group_size, column_width, core_rows), BLK...  10.8 us
    all_to_all x2, waiting for transfers between devices, gather_rows(): lax.all_to_all(spread, 'req', 0, 0, tiled=True)  7.65 us
    all_to_all x1, starting transfers between devices, local(): lax.all_to_all(spread, PLANE, 0, 0, tiled=True)  6.47 us
  transfers between devices with their start and end apart: 10, of which 9 were waited for; matrix products, arithmetic and copies ran while one was open for 11% of the time, Pallas kernels for 0%

profile of v3, /device:TPU:8, one launch (start us, length us, event | category | flops | bytes accessed | tf_op | source)
XLA Modules:
  0.0 210.0 jit_solution(8517659452125142832)
XLA Ops:
  0.6 1.7 broadcast_in_dim.31
  2.3 10.3 %all-to-all-start.1 = ((bf16[8,256,96]{1,2,0:T(8,128)(2,1)}), bf16[8,256,96]{1,2,0:T(8,128)(2,1)S(1)}, u32[]{:S(2)}, u32[]{:S(2)}) async-start(bf16[8,256,96]{1,2,0:T(8,128)(2,1)} %broadcast_in_dim.31), calls=%async_computation.1 | async-start | bytes 786432 | tf_op jit(solution)/shard_map/all_to_all | solution.py:53
  13.3 1.5 fusion.79
  17.6 2.0 and_reduce_fusion
  19.7 7.6 %all-to-all-done.1 = bf16[8,256,96]{1,2,0:T(8,128)(2,1)S(1)} async-done(((bf16[8,256,96]{1,2,0:T(8,128)(2,1)}), bf16[8,256,96]{1,2,0:T(8,128)(2,1)S(1)}, u32[]{:S(2)}, u32[]{:S(2)}) %all-to-all-start.1) | async-done | bytes 393248 | tf_op jit(solution)/shard_map/all_to_all | solution.py:53
  29.2 3.7 %all-to-all-start = ((bf16[8,256,288]{1,2,0:T(8,128)(2,1)}), bf16[8,256,288]{1,2,0:T(8,128)(2,1)S(1)}, u32[]{:S(2)}, u32[]{:S(2)}) async-start(bf16[8,256,288]{1,2,0:T(8,128)(2,1)} %broadcast_in_dim.29), calls=%async_computation | async-start | bytes 2359296 | tf_op jit(solution)/shard_map/all_to_all | solution.py:53
  32.9 2.0 copy.62
  34.9 1.9 reshape_reshape.3
  36.8 1.8 fusion.11
  38.6 1.9 collective-permute-start.1
  40.5 1.3 collective-permute-done.1
  41.8 2.4 %collective-permute-start.2 = (bf16[3,64,512]{2,1,0:T(8,128)(2,1)S(1)}, bf16[3,64,512]{2,1,0:T(8,128)(2,1)S(1)}, u32[]{:S(2)}, u32[]{:S(2)}) collective-permute-start(bf16[3,64,512]{2,1,0:T(8,128)(2,1)S(1)} %maximum_select_fusion.3), channel_id=1, source_target_pairs={{0,2},{2,0},{4,6},{6,4},{8,10},{10,8},{12,14},{14,12},{1,3},{3,1},... | collective-permute-start | bytes 589832 | tf_op jit(solution)/shard_map/ppermute | solution.py:123
  44.2 6.4 %collective-permute-done.2 = bf16[3,64,512]{2,1,0:T(8,128)(2,1)S(1)} collective-permute-done((bf16[3,64,512]{2,1,0:T(8,128)(2,1)S(1)}, bf16[3,64,512]{2,1,0:T(8,128)(2,1)S(1)}, u32[]{:S(2)}, u32[]{:S(2)}) %collective-permute-start.2) | collective-permute-done | bytes 196640 | tf_op jit(solution)/shard_map/ppermute | solution.py:123
  51.1 2.2 %fusion.86 = (f32[512]{0:T(512)S(1)}, f32[512,2176]{1,0:T(8,128)S(1)}) fusion(bf16[128,128]{1,0:T(8,128)(2,1)S(1)} %bitcast.106, bf16[2048,128]{1,0:T(8,128)(2,1)} %bitcast.96, bf16[3,128,512]{2,1,0:T(8,128)(2,1)S(1)} %maximum_select_fusion, pred[512,128]{1,0:T(32,128)(4,1)S(1)} %iota_compare_fusion, pred[2176]{0:T(1024)(128)(4,1)S(1)} %pad.14.clone), kind=kOutput, calls=%fused_computation.119 | convolution fusion | flops 290782720 | bytes 5215232 | tf_op jit(solution)/shard_map/qd,kd->qk/dot_general | solution.py:29
  55.3 2.4 %collective-permute-start.3 = (f32[66,512]{1,0:T(8,128)S(1)}, f32[66,512]{1,0:T(8,128)S(1)}, u32[]{:S(2)}, u32[]{:S(2)}) collective-permute-start(f32[66,512]{1,0:T(8,128)S(1)} %pad_maximum_fusion.1), channel_id=1, source_target_pairs={{0,2},{2,0},{4,6},{6,4},{8,10},{10,8},{12,14},{14,12},{1,3},{3,1},... | collective-permute-start | bytes 405512 | tf_op jit(solution)/shard_map/ppermute | solution.py:123
  57.6 4.7 %collective-permute-done.3 = f32[66,512]{1,0:T(8,128)S(1)} collective-permute-done((f32[66,512]{1,0:T(8,128)S(1)}, f32[66,512]{1,0:T(8,128)S(1)}, u32[]{:S(2)}, u32[]{:S(2)}) %collective-permute-start.3) | collective-permute-done | bytes 135200 | tf_op jit(solution)/shard_map/ppermute | solution.py:123
  62.4 1.9 collective-permute-start.4
  64.3 1.2 collective-permute-done.4
  67.0 10.8 %all-to-all-start.2 = ((bf16[64,32,256]{2,1,0:T(8,128)(2,1)}), bf16[64,32,256]{2,1,0:T(8,128)(2,1)}, u32[]{:S(2)}, u32[]{:S(2)}) async-start(bf16[64,32,256]{2,1,0:T(8,128)(2,1)} %bitcast.25), calls=%async_computation.2 | async-start | bytes 2097152 | tf_op jit(solution)/shard_map/all_to_all | solution.py:185
  77.9 2.1 collective-permute-start
  80.9 1.8 collective-permute-done
  82.6 22.9 %all-to-all-done.2 = bf16[64,32,256]{2,1,0:T(8,128)(2,1)} async-done(((bf16[64,32,256]{2,1,0:T(8,128)(2,1)}), bf16[64,32,256]{2,1,0:T(8,128)(2,1)}, u32[]{:S(2)}, u32[]{:S(2)}) %all-to-all-start.2) | async-done | bytes 1048608 | tf_op jit(solution)/shard_map/all_to_all | solution.py:185
  105.5 1.5 fusion.14
  107.1 1.1 broadcast_in_dim.39
  108.2 6.5 %all-to-all-start.3 = ((bf16[32,64,256]{2,1,0:T(8,128)(2,1)}), bf16[32,64,256]{2,1,0:T(8,128)(2,1)S(1)}, u32[]{:S(2)}, u32[]{:S(2)}) async-start(bf16[32,64,256]{2,1,0:T(8,128)(2,1)} %broadcast_in_dim.39), calls=%async_computation.3 | async-start | bytes 2097152 | tf_op jit(solution)/shard_map/all_to_all | solution.py:195
  119.4 23.9 %all-to-all-done.3 = bf16[32,64,256]{2,1,0:T(8,128)(2,1)S(1)} async-done(((bf16[32,64,256]{2,1,0:T(8,128)(2,1)}), bf16[32,64,256]{2,1,0:T(8,128)(2,1)S(1)}, u32[]{:S(2)}, u32[]{:S(2)}) %all-to-all-start.3) | async-done | bytes 1048608 | tf_op jit(solution)/shard_map/all_to_all | solution.py:195
  143.3 1.6 bitcast_convert_fusion
  144.9 1.9 copy.69
  146.8 1.7 fusion.27
  149.9 4.2 %convolution_bitcast_fusion = f32[32,8,2048]{2,1,0:T(8,128)} fusion(bf16[2048,128]{0,1:T(8,128)(2,1)} %get-tuple-element.14, bf16[2048,128]{0,1:T(8,128)(2,1)} %get-tuple-element.12, bf16[256,2048]{1,0:T(8,128)(2,1)S(1)} %add_convert_fusion, bf16[2048,128]{0,1:T(8,128)(2,1)} %get-tuple-element.13, bf16[2048,128]{0,1:T(8,128)(2,1)} %get-tuple-element.11, ...), kind=kOutput, calls=%fused_computation.6 | convolution fusion | flops 541720576 | bytes 5243904 | tf_op jit(solution)/shard_map/rf,df->rd/dot_general | solution.py:207
  154.1 5.3 %all-to-all-start.4 = ((f32[32,8,2048]{2,1,0:T(8,128)}), f32[32,8,2048]{2,1,0:T(8,128)S(1)}, u32[]{:S(2)}, u32[]{:S(2)}) async-start(f32[32,8,2048]{2,1,0:T(8,128)} %convolution_bitcast_fusion), calls=%async_computation.4 | async-start | bytes 4194304 | tf_op jit(solution)/shard_map/all_to_all | solution.py:208
  160.1 48.7 %all-to-all-done.4 = f32[32,8,2048]{2,1,0:T(8,128)S(1)} async-done(((f32[32,8,2048]{2,1,0:T(8,128)}), f32[32,8,2048]{2,1,0:T(8,128)S(1)}, u32[]{:S(2)}, u32[]{:S(2)}) %all-to-all-start.4) | async-done | bytes 2097184 | tf_op jit(solution)/shard_map/all_to_all | solution.py:208
  (89 shorter events, 17.5 us)
Async XLA Ops:
  0.6 12.6 %copy-start.2 = (bf16[1,1,2048,2,128]{4,3,2,1,0:T(2,128)(2,1)S(1)}, bf16[1,1,2048,2,128]{4,3,2,1,0:T(2,128)(2,1)}, u32[]{:S(2)}) copy-start(bf16[1,1,2048,2,128]{4,3,2,1,0:T(2,128)(2,1)} %param.15) | copy-start | bytes 3145732
  2.3 25.0 %all-to-all-start.1 = ((bf16[8,256,96]{1,2,0:T(8,128)(2,1)}), bf16[8,256,96]{1,2,0:T(8,128)(2,1)S(1)}, u32[]{:S(2)}, u32[]{:S(2)}) async-start(bf16[8,256,96]{1,2,0:T(8,128)(2,1)} %broadcast_in_dim.31), calls=%async_computation.1 | async-start | bytes 786432 | tf_op jit(solution)/shard_map/all_to_all | solution.py:53
  14.8 1.8 copy-start.12
  14.8 1.9 copy-start.7
  14.8 1.9 copy-start.8
  14.8 2.2 %copy-start.15 = (s32[1,2]{1,0:T(1,128)S(1)}, s32[1,2]{1,0:T(1,128)}, u32[]{:S(2)}) copy-start(s32[1,2]{1,0:T(1,128)} %param.18) | copy-start | bytes 28
  27.3 0.7 copy-start.3
  29.2 7.6 %copy-start = (bf16[1,512,2048]{2,1,0:T(8,128)(2,1)S(1)}, bf16[1,512,2048]{2,1,0:T(8,128)(2,1)}, u32[]{:S(2)}) copy-start(bf16[1,512,2048]{2,1,0:T(8,128)(2,1)} %param.14) | copy-start | bytes 6291460
  29.2 7.6 %copy-start.16 = (f32[3,32]{1,0:T(4,128)S(1)}, f32[3,32]{1,0:T(4,128)}, u32[]{:S(2)}) copy-start(f32[3,32]{1,0:T(4,128)} %param.20) | copy-start | bytes 1156
  29.2 36.7 %all-to-all-start = ((bf16[8,256,288]{1,2,0:T(8,128)(2,1)}), bf16[8,256,288]{1,2,0:T(8,128)(2,1)S(1)}, u32[]{:S(2)}, u32[]{:S(2)}) async-start(bf16[8,256,288]{1,2,0:T(8,128)(2,1)} %broadcast_in_dim.29), calls=%async_computation | async-start | bytes 2359296 | tf_op jit(solution)/shard_map/all_to_all | solution.py:53
  38.6 12.2 %copy-start.4 = (bf16[3,32,512]{2,1,0:T(8,128)(2,1)}, bf16[3,32,512]{2,1,0:T(8,128)(2,1)S(1)}, u32[]{:S(2)}) copy-start(bf16[3,32,512]{2,1,0:T(8,128)(2,1)S(1)} %fusion.11) | copy-start | bytes 294916
  38.6 3.2 %collective-permute-start.1 = (bf16[3,32,512]{2,1,0:T(8,128)(2,1)S(1)}, bf16[3,32,512]{2,1,0:T(8,128)(2,1)S(1)}, u32[]{:S(2)}, u32[]{:S(2)}) collective-permute-start(bf16[3,32,512]{2,1,0:T(8,128)(2,1)S(1)} %fusion.11), channel_id=1, source_target_pairs={{0,1},{1,0},{2,3},{3,2},{4,5},{5,4},{6,7},{7,6},{8,9},{9,8},{10,11... | collective-permute-start | bytes 294920 | tf_op jit(solution)/shard_map/ppermute | solution.py:122
  41.8 8.9 %collective-permute-start.2 = (bf16[3,64,512]{2,1,0:T(8,128)(2,1)S(1)}, bf16[3,64,512]{2,1,0:T(8,128)(2,1)S(1)}, u32[]{:S(2)}, u32[]{:S(2)}) collective-permute-start(bf16[3,64,512]{2,1,0:T(8,128)(2,1)S(1)} %maximum_select_fusion.3), channel_id=1, source_target_pairs={{0,2},{2,0},{4,6},{6,4},{8,10},{10,8},{12,14},{14,12},{1,3},{3,1},... | collective-permute-start | bytes 589832 | tf_op jit(solution)/shard_map/ppermute | solution.py:123
  51.1 2.2 %copy-start.6 = (bf16[1,1,2048,1,128]{4,2,3,1,0:T(8,128)(2,1)S(1)}, bf16[1,1,2048,1,128]{4,2,3,1,0:T(8,128)(2,1)}, u32[]{:S(2)}) copy-start(bf16[1,1,2048,1,128]{4,2,3,1,0:T(8,128)(2,1)} %copy.77) | copy-start | bytes 1572868
  55.3 7.0 %collective-permute-start.3 = (f32[66,512]{1,0:T(8,128)S(1)}, f32[66,512]{1,0:T(8,128)S(1)}, u32[]{:S(2)}, u32[]{:S(2)}) collective-permute-start(f32[66,512]{1,0:T(8,128)S(1)} %pad_maximum_fusion.1), channel_id=1, source_target_pairs={{0,2},{2,0},{4,6},{6,4},{8,10},{10,8},{12,14},{14,12},{1,3},{3,1},... | collective-permute-start | bytes 405512 | tf_op jit(solution)/shard_map/ppermute | solution.py:123
  62.4 3.2 %collective-permute-start.4 = (f32[34,512]{1,0:T(8,128)S(1)}, f32[34,512]{1,0:T(8,128)S(1)}, u32[]{:S(2)}, u32[]{:S(2)}) collective-permute-start(f32[34,512]{1,0:T(8,128)S(1)} %pad_maximum_fusion.2), channel_id=1, source_target_pairs={{0,1},{1,0},{2,3},{3,2},{4,5},{5,4},{6,7},{7,6},{8,9},{9,8},{10,11... | collective-permute-start | bytes 208904 | tf_op jit(solution)/shard_map/ppermute | solution.py:122
  67.0 38.6 %all-to-all-start.2 = ((bf16[64,32,256]{2,1,0:T(8,128)(2,1)}), bf16[64,32,256]{2,1,0:T(8,128)(2,1)}, u32[]{:S(2)}, u32[]{:S(2)}) async-start(bf16[64,32,256]{2,1,0:T(8,128)(2,1)} %bitcast.25), calls=%async_computation.2 | async-start | bytes 2097152 | tf_op jit(solution)/shard_map/all_to_all | solution.py:185
  77.9 4.7 %collective-permute-start = (bf16[2048,288]{0,1:T(8,128)(2,1)S(1)}, bf16[2048,288]{0,1:T(8,128)(2,1)S(1)}, u32[]{:S(2)}, u32[]{:S(2)}) collective-permute-start(bf16[2048,288]{0,1:T(8,128)(2,1)S(1)} %bitcast.92), channel_id=1, source_target_pairs={{0,1},{1,0},{2,3},{3,2},{4,5},{5,4},{6,7},{7,6},{8,9},{9,8},{10,11... | collective-permute-start | bytes 3538952 | tf_op jit(solution)/shard_map/ppermute | solution.py:95
  105.5 10.6 %copy-start.13 = (f32[2,2048]{1,0:T(2,128)S(1)}, f32[2,2048]{1,0:T(2,128)}, u32[]{:S(2)}) copy-start(f32[2,2048]{1,0:T(2,128)} %param.26) | copy-start | bytes 49156
  105.5 11.2 %copy-start.14 = (f32[2,2048]{1,0:T(2,128)S(1)}, f32[2,2048]{1,0:T(2,128)}, u32[]{:S(2)}) copy-start(f32[2,2048]{1,0:T(2,128)} %param.27) | copy-start | bytes 49156
  108.2 35.1 %all-to-all-start.3 = ((bf16[32,64,256]{2,1,0:T(8,128)(2,1)}), bf16[32,64,256]{2,1,0:T(8,128)(2,1)S(1)}, u32[]{:S(2)}, u32[]{:S(2)}) async-start(bf16[32,64,256]{2,1,0:T(8,128)(2,1)} %broadcast_in_dim.39), calls=%async_computation.3 | async-start | bytes 2097152 | tf_op jit(solution)/shard_map/all_to_all | solution.py:195
  146.8 1.9 copy-start.1
  148.5 0.8 copy-start.9
  149.2 0.7 copy-start.17
  154.1 5.4 %copy-start.5 = (bf16[3,32,512]{2,1,0:T(8,128)(2,1)S(1)}, bf16[3,32,512]{2,1,0:T(8,128)(2,1)}, u32[]{:S(2)}) copy-start(bf16[3,32,512]{2,1,0:T(8,128)(2,1)} %copy-done.4) | copy-start | bytes 294916
  154.1 54.7 %all-to-all-start.4 = ((f32[32,8,2048]{2,1,0:T(8,128)}), f32[32,8,2048]{2,1,0:T(8,128)S(1)}, u32[]{:S(2)}, u32[]{:S(2)}) async-start(f32[32,8,2048]{2,1,0:T(8,128)} %convolution_bitcast_fusion), calls=%async_computation.4 | async-start | bytes 4194304 | tf_op jit(solution)/shard_map/all_to_all | solution.py:208
  159.4 49.8 %copy-start.10 = (f32[1,2048]{1,0:T(1,128)S(1)}, f32[1,2048]{1,0:T(1,128)}, u32[]{:S(2)}) copy-start(f32[1,2048]{1,0:T(1,128)} %get-tuple-element.24) | copy-start | bytes 24580
  159.4 49.8 %copy-start.11 = (f32[1,2048]{1,0:T(1,128)S(1)}, f32[1,2048]{1,0:T(1,128)}, u32[]{:S(2)}) copy-start(f32[1,2048]{1,0:T(1,128)} %get-tuple-element.26) | copy-start | bytes 24580

commit v4 on v3

--- a/solution.py
+++ b/solution.py
@@ -37,14 +37,6 @@
         "qk,kd->dq", weights.astype(jnp.bfloat16), value_rows, preferred_element_type=jnp.float32
     )
     return (numerator, row_max, row_total)
-
-
-def merge_blocks(earlier_part, later_part):
-    joined = jnp.maximum(earlier_part[1], later_part[1])
-    scale_earlier = jnp.exp(earlier_part[1] - joined)
-    scale_later = jnp.exp(later_part[1] - joined)
-    numerator = earlier_part[0] * scale_earlier[:, None] + later_part[0] * scale_later[:, None]
-    return (numerator, joined, earlier_part[2] * scale_earlier + later_part[2] * scale_later)
 
 
 def gather_rows(block):
@@ -83,7 +75,6 @@
     block_index = chip * nc + core
     group_size = nx * ny * nc
     groups = group_size // HEADS
-    low_bits = groups.bit_length() - 1
     group_index = block_index % groups
 
     rows, _, column_width = qkv_weight.shape
@@ -117,25 +108,36 @@
     ).astype(jnp.bfloat16)
     appended = qkv_columns[1:].transpose(2, 0, 1)[None]
 
-    def from_partner(value, bit_level):
-        if bit_level == 0:
-            return lax.ppermute(value, "bc", swap("bc", nc))
-        return lax.ppermute(value, "by", [(i, i ^ (1 << (bit_level - 1))) for i in range(ny)])
-
-    head_qkv = qkv_columns
-    for bit_level in range(low_bits):
-        partner = from_partner(head_qkv, bit_level)
-        upper_bit = group_index >> bit_level & 1
-        head_qkv = jnp.where(
-            upper_bit == 1,
-            jnp.concatenate([partner, head_qkv], axis=1),
-            jnp.concatenate([head_qkv, partner], axis=1),
+    quarter = query_total // groups
+    members = ny * nc
+
+    def from_member(value, k):
+        return lax.ppermute(value, ("by", "bc"), [(i, i ^ k) for i in range(members)])
+
+    own_kv = qkv_columns[1:]
+
+    def outgoing_for(target):
+        part = lax.dynamic_slice_in_dim(own_kv, target * quarter, quarter, 2)
+        return jnp.concatenate(
+            [qkv_columns[0], part.transpose(1, 0, 2).reshape(column_width, 2 * quarter)], axis=1
         )
-    queries = head_qkv[0].T
-    fresh_count = query_total // groups
+
+    sources = [outgoing_for(group_index)]
+    for k in range(1, groups):
+        sources.append(from_member(outgoing_for(group_index ^ k), k))
+    ordered = jnp.take(jnp.stack(sources), group_index ^ jnp.arange(groups), axis=0)
+    head_q = ordered[:, :, :query_total].reshape(groups * column_width, query_total)
+    head_kv = (
+        ordered[:, :, query_total:]
+        .reshape(groups, column_width, 2, quarter)
+        .transpose(2, 0, 1, 3)
+        .reshape(2, groups * column_width, quarter)
+    )
+    queries = head_q.T
+    fresh_count = quarter
+    fresh_keys = head_kv[0].T
+    fresh_values = head_kv[1].T
     fresh_start = group_index * fresh_count
-    fresh_keys = lax.dynamic_slice_in_dim(head_qkv[1], fresh_start, fresh_count, 1).T
-    fresh_values = lax.dynamic_slice_in_dim(head_qkv[2], fresh_start, fresh_count, 1).T
     cache_count = cache_entries.shape[2]
     cache_keys = cache_entries[0, 0, :, 0]
     cache_values = cache_entries[0, 0, :, 1]
@@ -158,19 +160,21 @@
         jnp.concatenate([cache_values, fresh_values], axis=0),
         jnp.concatenate([cache_visible, fresh_visible], axis=1),
     )
-    for bit_level in reversed(range(low_bits)):
-        halves = numerator.reshape(2, -1, query_total)
-        upper_bit = group_index >> bit_level & 1
-        kept_half = jnp.where(upper_bit == 1, halves[1], halves[0])
-        sent_half = jnp.where(upper_bit == 1, halves[0], halves[1])
-        sent = jnp.concatenate([sent_half, row_max[None], row_total[None]], axis=0)
-        got_back = from_partner(sent, bit_level)
-        other_sum, other_max, other_total = got_back[:-2], got_back[-2], got_back[-1]
-        joined = jnp.maximum(row_max, other_max)
-        scale_kept = jnp.exp(row_max - joined)
-        scale_other = jnp.exp(other_max - joined)
-        numerator = kept_half * scale_kept[None] + other_sum * scale_other[None]
-        row_max, row_total = joined, row_total * scale_kept + other_total * scale_other
+    def stats_for(target):
+        part = lax.dynamic_slice_in_dim(numerator, target * column_width, column_width, 0)
+        return jnp.concatenate([part, row_max[None], row_total[None]], axis=0)
+
+    pieces = [stats_for(group_index)]
+    for k in range(1, groups):
+        pieces.append(from_member(stats_for(group_index ^ k), k))
+    maxima = jnp.stack([piece[-2] for piece in pieces])
+    joined = jnp.max(maxima, axis=0)
+    scales = jnp.exp(maxima - joined[None])
+    numerator = pieces[0][:-2] * scales[0][None]
+    row_total = pieces[0][-1] * scales[0]
+    for k in range(1, groups):
+        numerator = numerator + pieces[k][:-2] * scales[k][None]
+        row_total = row_total + pieces[k][-1] * scales[k]
     context_columns = (numerator / row_total[None]).astype(jnp.bfloat16)
 
     block_rows = query_total // (group_size)

time: 211 us -> 216 us (1.024)
  waiting for transfers between devices: 118 us -> 109 us
  starting transfers between devices: 47.2 us -> 53.6 us
  matrix products: 10.7 us -> 14 us
  other arithmetic: 9.44 us -> 12.7 us
    ppermute x4 -> x6, waiting for transfers between devices: 13.6 us -> 4.36 us  [from_member(): lax.ppermute(value, ('by', 'bc'), [(i, i ^ k) for i in range(members)])]
    ppermute x4 -> x6, starting transfers between devices: 8.56 us -> 15.2 us  [from_member(): lax.ppermute(value, ('by', 'bc'), [(i, i ^ k) for i in range(members)])]
    dot_general x1, matrix products: 1.02 us -> 3.38 us  [partial_block(): jnp.einsum('qk,kd->dq', weights.astype(jnp.bfloat16), value_rows, preferr...]
  transfers between devices with their start and end apart: 10 -> 12, of which waited for: 9 -> 7; matrix products, arithmetic and copies ran while one was open for 11% -> 14% of each run, Pallas kernels for 0% -> 0%
where the time goes in v4:
time: 216 us; the launch traced here: 215 us
  waiting for transfers between devices  109 us (50%)
  starting transfers between devices  53.6 us (25%)
  local copies, waits for them, and re-layouts  23.4 us (11%)
  matrix products  14 us (6%)
  other arithmetic  12.7 us (6%)
    all_to_all x1, waiting for transfers between devices, local(): lax.all_to_all(mixed_parts.reshape(chips, block_rows, -1), PLANE, 0, 0, t...  49.4 us
    all_to_all x1, waiting for transfers between devices, local(): lax.all_to_all(spread, PLANE, 0, 0, tiled=True)  23.9 us
    all_to_all x1, waiting for transfers between devices, local(): lax.all_to_all(outgoing.reshape(group_size, column_width, core_rows), BLK...  22.9 us
    ppermute x6, starting transfers between devices, from_member(): lax.ppermute(value, ('by', 'bc'), [(i, i ^ k) for i in range(members)])  15.2 us
    all_to_all x2, starting transfers between devices, gather_rows(): lax.all_to_all(spread, 'req', 0, 0, tiled=True)  14 us
    all_to_all x1, starting transfers between devices, local(): lax.all_to_all(outgoing.reshape(group_size, column_width, core_rows), BLK...  10.7 us
    all_to_all x2, waiting for transfers between devices, gather_rows(): lax.all_to_all(spread, 'req', 0, 0, tiled=True)  6.96 us
    all_to_all x1, starting transfers between devices, local(): lax.all_to_all(spread, PLANE, 0, 0, tiled=True)  6.47 us
  transfers between devices with their start and end apart: 12, of which 7 were waited for; matrix products, arithmetic and copies ran while one was open for 14% of the time, Pallas kernels for 0%

profile of v4, /device:TPU:8, one launch (start us, length us, event | category | flops | bytes accessed | tf_op | source)
XLA Modules:
  0.0 214.7 jit_solution(11226066848944591122)
XLA Ops:
  0.6 1.7 broadcast_in_dim.44
  2.3 10.3 %all-to-all-start.1 = ((bf16[8,256,96]{1,2,0:T(8,128)(2,1)}), bf16[8,256,96]{1,2,0:T(8,128)(2,1)S(1)}, u32[]{:S(2)}, u32[]{:S(2)}) async-start(bf16[8,256,96]{1,2,0:T(8,128)(2,1)} %broadcast_in_dim.44), calls=%async_computation.1 | async-start | bytes 786432 | tf_op jit(solution)/shard_map/all_to_all | solution.py:45
  13.7 1.4 fusion.87
  15.1 1.5 fusion.80
  20.3 7.0 %all-to-all-done.1 = bf16[8,256,96]{1,2,0:T(8,128)(2,1)S(1)} async-done(((bf16[8,256,96]{1,2,0:T(8,128)(2,1)}), bf16[8,256,96]{1,2,0:T(8,128)(2,1)S(1)}, u32[]{:S(2)}, u32[]{:S(2)}) %all-to-all-start.1) | async-done | bytes 393248 | tf_op jit(solution)/shard_map/all_to_all | solution.py:45
  29.2 3.7 %all-to-all-start = ((bf16[8,256,288]{1,2,0:T(8,128)(2,1)}), bf16[8,256,288]{1,2,0:T(8,128)(2,1)S(1)}, u32[]{:S(2)}, u32[]{:S(2)}) async-start(bf16[8,256,288]{1,2,0:T(8,128)(2,1)} %broadcast_in_dim.41), calls=%async_computation | async-start | bytes 2359296 | tf_op jit(solution)/shard_map/all_to_all | solution.py:45
  32.9 2.0 copy.84
  34.9 1.9 reshape_reshape.3
  36.8 1.8 fusion.11
  39.3 1.9 collective-permute-start.1
  41.3 2.4 %collective-permute-start.2 = (bf16[32,768]{1,0:T(8,128)(2,1)S(1)}, bf16[32,768]{1,0:T(8,128)(2,1)S(1)}, u32[]{:S(2)}, u32[]{:S(2)}) collective-permute-start(bf16[32,768]{1,0:T(8,128)(2,1)S(1)} %get-tuple-element.29), channel_id=1, source_target_pairs={{0,2},{1,3},{2,0},{3,1},{4,6},{5,7},{6,4},{7,5},{8,10},{9,11},{10,... | collective-permute-start | bytes 147464 | tf_op jit(solution)/shard_map/ppermute | solution.py:115
  43.6 3.3 %collective-permute-start.3 = (bf16[32,768]{1,0:T(8,128)(2,1)S(1)}, bf16[32,768]{1,0:T(8,128)(2,1)S(1)}, u32[]{:S(2)}, u32[]{:S(2)}) collective-permute-start(bf16[32,768]{1,0:T(8,128)(2,1)S(1)} %get-tuple-element.30), channel_id=1, source_target_pairs={{0,3},{1,2},{2,1},{3,0},{4,7},{5,6},{6,5},{7,4},{8,11},{9,10},{10,... | collective-permute-start | bytes 147464 | tf_op jit(solution)/shard_map/ppermute | solution.py:115
  47.6 2.0 and_reduce_fusion
  50.8 3.0 %fusion.88 = (f32[512]{0:T(512)S(1)}, f32[512,2176]{1,0:T(8,128)}) fusion(bf16[128,512]{1,0:T(8,128)(2,1)S(1)} %bitcast.127, bf16[128,128]{1,0:T(8,128)(2,1)S(1)} %bitcast.142, bf16[2048,128]{1,0:T(8,128)(2,1)S(1)} %copy-done.6, pred[512,128]{1,0:T(32,128)(4,1)S(1)} %copy-done.7, pred[2176]{0:T(1024)(128)(4,1)S(1)} %pad.21.clone), kind=kOutput, calls=%fused_computation.144 | convolution fusion | flops 290782720 | bytes 5214336 | tf_op jit(solution)/shard_map/qd,kd->qk/dot_general | solution.py:29
  53.9 3.4 %fusion.3 = f32[128,512]{1,0:T(8,128)S(1)} fusion(f32[512,2176]{1,0:T(8,128)} %get-tuple-element.48, pred[512,128]{1,0:T(32,128)(4,1)S(1)} %copy-done.7, f32[512]{0:T(512)S(1)} %get-tuple-element.47, pred[2176]{0:T(1024)(128)(4,1)S(1)} %pad.21.clone, bf16[128,128]{1,0:T(8,128)(2,1)S(1)} %bitcast.143, bf16[2048,128]{1,0:T(8,128)(2,1)S(1)} %copy-done.5), kind=kOutput, calls=%fused_computation.8 | convolution fusion | flops 290783232 | bytes 5345408 | tf_op jit(solution)/shard_map/qk,kd->dq/dot_general | solution.py:36
  58.5 2.2 %collective-permute-start.4 = (f32[34,512]{1,0:T(8,128)S(1)}, f32[34,512]{1,0:T(8,128)S(1)}, u32[]{:S(2)}, u32[]{:S(2)}) collective-permute-start(f32[34,512]{1,0:T(8,128)S(1)} %get-tuple-element.42), channel_id=1, source_target_pairs={{0,1},{1,0},{2,3},{3,2},{4,5},{5,4},{6,7},{7,6},{8,9},{9,8},{10,11... | collective-permute-start | bytes 208904 | tf_op jit(solution)/shard_map/ppermute | solution.py:115
  60.7 3.1 %collective-permute-start.5 = (f32[34,512]{1,0:T(8,128)S(1)}, f32[34,512]{1,0:T(8,128)S(1)}, u32[]{:S(2)}, u32[]{:S(2)}) collective-permute-start(f32[34,512]{1,0:T(8,128)S(1)} %get-tuple-element.43), channel_id=1, source_target_pairs={{0,2},{1,3},{2,0},{3,1},{4,6},{5,7},{6,4},{7,5},{8,10},{9,11},{10,... | collective-permute-start | bytes 208904 | tf_op jit(solution)/shard_map/ppermute | solution.py:115
  63.8 2.3 %collective-permute-start.6 = (f32[34,512]{1,0:T(8,128)S(1)}, f32[34,512]{1,0:T(8,128)S(1)}, u32[]{:S(2)}, u32[]{:S(2)}) collective-permute-start(f32[34,512]{1,0:T(8,128)S(1)} %get-tuple-element.44), channel_id=1, source_target_pairs={{0,3},{1,2},{2,1},{3,0},{4,7},{5,6},{6,5},{7,4},{8,11},{9,10},{10,... | collective-permute-start | bytes 208904 | tf_op jit(solution)/shard_map/ppermute | solution.py:115
  67.1 3.3 %collective-permute-done.6 = f32[34,512]{1,0:T(8,128)S(1)} collective-permute-done((f32[34,512]{1,0:T(8,128)S(1)}, f32[34,512]{1,0:T(8,128)S(1)}, u32[]{:S(2)}, u32[]{:S(2)}) %collective-permute-start.6) | collective-permute-done | bytes 69664 | tf_op jit(solution)/shard_map/ppermute | solution.py:115
  71.9 10.7 %all-to-all-start.2 = ((bf16[64,32,256]{2,1,0:T(8,128)(2,1)}), bf16[64,32,256]{2,1,0:T(8,128)(2,1)}, u32[]{:S(2)}, u32[]{:S(2)}) async-start(bf16[64,32,256]{2,1,0:T(8,128)(2,1)} %bitcast.37), calls=%async_computation.2 | async-start | bytes 2097152 | tf_op jit(solution)/shard_map/all_to_all | solution.py:189
  82.8 2.1 collective-permute-start
  85.7 1.8 collective-permute-done
  87.5 22.9 %all-to-all-done.2 = bf16[64,32,256]{2,1,0:T(8,128)(2,1)} async-done(((bf16[64,32,256]{2,1,0:T(8,128)(2,1)}), bf16[64,32,256]{2,1,0:T(8,128)(2,1)}, u32[]{:S(2)}, u32[]{:S(2)}) %all-to-all-start.2) | async-done | bytes 1048608 | tf_op jit(solution)/shard_map/all_to_all | solution.py:189
  110.4 1.5 fusion.14
  113.1 6.5 %all-to-all-start.3 = ((bf16[32,64,256]{2,1,0:T(8,128)(2,1)}), bf16[32,64,256]{2,1,0:T(8,128)(2,1)S(1)}, u32[]{:S(2)}, u32[]{:S(2)}) async-start(bf16[32,64,256]{2,1,0:T(8,128)(2,1)} %broadcast_in_dim.93), calls=%async_computation.3 | async-start | bytes 2097152 | tf_op jit(solution)/shard_map/all_to_all | solution.py:199
  124.3 23.9 %all-to-all-done.3 = bf16[32,64,256]{2,1,0:T(8,128)(2,1)S(1)} async-done(((bf16[32,64,256]{2,1,0:T(8,128)(2,1)}), bf16[32,64,256]{2,1,0:T(8,128)(2,1)S(1)}, u32[]{:S(2)}, u32[]{:S(2)}) %all-to-all-start.3) | async-done | bytes 1048608 | tf_op jit(solution)/shard_map/all_to_all | solution.py:199
  148.2 1.6 bitcast_convert_fusion
  149.7 1.9 copy.96
  151.7 1.7 fusion.27
  154.8 4.2 %convolution_bitcast_fusion = f32[32,8,2048]{2,1,0:T(8,128)} fusion(bf16[2048,128]{0,1:T(8,128)(2,1)} %get-tuple-element.7, bf16[2048,128]{0,1:T(8,128)(2,1)} %get-tuple-element.5, bf16[256,2048]{1,0:T(8,128)(2,1)S(1)} %add_convert_fusion, bf16[2048,128]{0,1:T(8,128)(2,1)} %get-tuple-element.6, bf16[2048,128]{0,1:T(8,128)(2,1)} %get-tuple-element.4, ...), kind=kOutput, calls=%fused_computation.7 | convolution fusion | flops 541720576 | bytes 5243904 | tf_op jit(solution)/shard_map/rf,df->rd/dot_general | solution.py:211
  159.0 5.2 %all-to-all-start.4 = ((f32[32,8,2048]{2,1,0:T(8,128)}), f32[32,8,2048]{2,1,0:T(8,128)S(1)}, u32[]{:S(2)}, u32[]{:S(2)}) async-start(f32[32,8,2048]{2,1,0:T(8,128)} %convolution_bitcast_fusion), calls=%async_computation.4 | async-start | bytes 4194304 | tf_op jit(solution)/shard_map/all_to_all | solution.py:212
  164.2 49.4 %all-to-all-done.4 = f32[32,8,2048]{2,1,0:T(8,128)S(1)} async-done(((f32[32,8,2048]{2,1,0:T(8,128)}), f32[32,8,2048]{2,1,0:T(8,128)S(1)}, u32[]{:S(2)}, u32[]{:S(2)}) %all-to-all-start.4) | async-done | bytes 2097184 | tf_op jit(solution)/shard_map/all_to_all | solution.py:212
  (96 shorter events, 21.5 us)
Async XLA Ops:
  0.6 14.5 %copy-start.3 = (bf16[1,1,2048,2,128]{4,3,2,1,0:T(2,128)(2,1)S(1)}, bf16[1,1,2048,2,128]{4,3,2,1,0:T(2,128)(2,1)}, u32[]{:S(2)}) copy-start(bf16[1,1,2048,2,128]{4,3,2,1,0:T(2,128)(2,1)} %param.15) | copy-start | bytes 3145732
  2.3 25.0 %all-to-all-start.1 = ((bf16[8,256,96]{1,2,0:T(8,128)(2,1)}), bf16[8,256,96]{1,2,0:T(8,128)(2,1)S(1)}, u32[]{:S(2)}, u32[]{:S(2)}) async-start(bf16[8,256,96]{1,2,0:T(8,128)(2,1)} %broadcast_in_dim.44), calls=%async_computation.1 | async-start | bytes 786432 | tf_op jit(solution)/shard_map/all_to_all | solution.py:45
  15.1 1.5 copy-start.11
  27.3 0.7 copy-start.4
  29.2 7.6 %copy-start = (bf16[1,512,2048]{2,1,0:T(8,128)(2,1)S(1)}, bf16[1,512,2048]{2,1,0:T(8,128)(2,1)}, u32[]{:S(2)}) copy-start(bf16[1,512,2048]{2,1,0:T(8,128)(2,1)} %param.14) | copy-start | bytes 6291460
  29.2 7.6 %copy-start.14 = (f32[3,32]{1,0:T(4,128)S(1)}, f32[3,32]{1,0:T(4,128)}, u32[]{:S(2)}) copy-start(f32[3,32]{1,0:T(4,128)} %param.20) | copy-start | bytes 1156
  29.2 41.6 %all-to-all-start = ((bf16[8,256,288]{1,2,0:T(8,128)(2,1)}), bf16[8,256,288]{1,2,0:T(8,128)(2,1)S(1)}, u32[]{:S(2)}, u32[]{:S(2)}) async-start(bf16[8,256,288]{1,2,0:T(8,128)(2,1)} %broadcast_in_dim.41), calls=%async_computation | async-start | bytes 2359296 | tf_op jit(solution)/shard_map/all_to_all | solution.py:45
  36.8 13.9 %copy-start.7 = (pred[512,128]{1,0:T(32,128)(4,1)S(1)}, pred[512,128]{1,0:T(32,128)(4,1)}, u32[]{:S(2)}) copy-start(pred[512,128]{1,0:T(32,128)(4,1)} %iota_compare_fusion) | copy-start | bytes 196612
  38.6 12.1 %copy-start.6 = (bf16[2048,128]{1,0:T(8,128)(2,1)S(1)}, bf16[2048,128]{1,0:T(8,128)(2,1)}, u32[]{:S(2)}) copy-start(bf16[2048,128]{1,0:T(8,128)(2,1)} %get-tuple-element.53) | copy-start | bytes 1572868
  39.3 10.4 %collective-permute-start.1 = (bf16[32,768]{1,0:T(8,128)(2,1)S(1)}, bf16[32,768]{1,0:T(8,128)(2,1)S(1)}, u32[]{:S(2)}, u32[]{:S(2)}) collective-permute-start(bf16[32,768]{1,0:T(8,128)(2,1)S(1)} %get-tuple-element.28), channel_id=1, source_target_pairs={{0,1},{1,0},{2,3},{3,2},{4,5},{5,4},{6,7},{7,6},{8,9},{9,8},{10,11... | collective-permute-start | bytes 147464 | tf_op jit(solution)/shard_map/ppermute | solution.py:115
  41.3 8.5 %collective-permute-start.2 = (bf16[32,768]{1,0:T(8,128)(2,1)S(1)}, bf16[32,768]{1,0:T(8,128)(2,1)S(1)}, u32[]{:S(2)}, u32[]{:S(2)}) collective-permute-start(bf16[32,768]{1,0:T(8,128)(2,1)S(1)} %get-tuple-element.29), channel_id=1, source_target_pairs={{0,2},{1,3},{2,0},{3,1},{4,6},{5,7},{6,4},{7,5},{8,10},{9,11},{10,... | collective-permute-start | bytes 147464 | tf_op jit(solution)/shard_map/ppermute | solution.py:115
  43.6 6.1 %collective-permute-start.3 = (bf16[32,768]{1,0:T(8,128)(2,1)S(1)}, bf16[32,768]{1,0:T(8,128)(2,1)S(1)}, u32[]{:S(2)}, u32[]{:S(2)}) collective-permute-start(bf16[32,768]{1,0:T(8,128)(2,1)S(1)} %get-tuple-element.30), channel_id=1, source_target_pairs={{0,3},{1,2},{2,1},{3,0},{4,7},{5,6},{6,5},{7,4},{8,11},{9,10},{10,... | collective-permute-start | bytes 147464 | tf_op jit(solution)/shard_map/ppermute | solution.py:115
  50.7 3.2 %copy-start.5 = (bf16[2048,128]{1,0:T(8,128)(2,1)S(1)}, bf16[2048,128]{1,0:T(8,128)(2,1)}, u32[]{:S(2)}) copy-start(bf16[2048,128]{1,0:T(8,128)(2,1)} %get-tuple-element.54) | copy-start | bytes 1572868
  53.9 3.6 %copy-start.2 = (f32[512,2176]{1,0:T(8,128)S(1)}, f32[512,2176]{1,0:T(8,128)}, u32[]{:S(2)}) copy-start(f32[512,2176]{1,0:T(8,128)} %get-tuple-element.48) | copy-start | bytes 13369348
  58.5 7.6 %collective-permute-start.4 = (f32[34,512]{1,0:T(8,128)S(1)}, f32[34,512]{1,0:T(8,128)S(1)}, u32[]{:S(2)}, u32[]{:S(2)}) collective-permute-start(f32[34,512]{1,0:T(8,128)S(1)} %get-tuple-element.42), channel_id=1, source_target_pairs={{0,1},{1,0},{2,3},{3,2},{4,5},{5,4},{6,7},{7,6},{8,9},{9,8},{10,11... | collective-permute-start | bytes 208904 | tf_op jit(solution)/shard_map/ppermute | solution.py:115
  60.7 6.5 %collective-permute-start.5 = (f32[34,512]{1,0:T(8,128)S(1)}, f32[34,512]{1,0:T(8,128)S(1)}, u32[]{:S(2)}, u32[]{:S(2)}) collective-permute-start(f32[34,512]{1,0:T(8,128)S(1)} %get-tuple-element.43), channel_id=1, source_target_pairs={{0,2},{1,3},{2,0},{3,1},{4,6},{5,7},{6,4},{7,5},{8,10},{9,11},{10,... | collective-permute-start | bytes 208904 | tf_op jit(solution)/shard_map/ppermute | solution.py:115
  63.8 6.6 %collective-permute-start.6 = (f32[34,512]{1,0:T(8,128)S(1)}, f32[34,512]{1,0:T(8,128)S(1)}, u32[]{:S(2)}, u32[]{:S(2)}) collective-permute-start(f32[34,512]{1,0:T(8,128)S(1)} %get-tuple-element.44), channel_id=1, source_target_pairs={{0,3},{1,2},{2,1},{3,0},{4,7},{5,6},{6,5},{7,4},{8,11},{9,10},{10,... | collective-permute-start | bytes 208904 | tf_op jit(solution)/shard_map/ppermute | solution.py:115
  71.9 38.5 %all-to-all-start.2 = ((bf16[64,32,256]{2,1,0:T(8,128)(2,1)}), bf16[64,32,256]{2,1,0:T(8,128)(2,1)}, u32[]{:S(2)}, u32[]{:S(2)}) async-start(bf16[64,32,256]{2,1,0:T(8,128)(2,1)} %bitcast.37), calls=%async_computation.2 | async-start | bytes 2097152 | tf_op jit(solution)/shard_map/all_to_all | solution.py:189
  82.8 4.7 %collective-permute-start = (bf16[2048,288]{0,1:T(8,128)(2,1)S(1)}, bf16[2048,288]{0,1:T(8,128)(2,1)S(1)}, u32[]{:S(2)}, u32[]{:S(2)}) collective-permute-start(bf16[2048,288]{0,1:T(8,128)(2,1)S(1)} %bitcast.122), channel_id=1, source_target_pairs={{0,1},{1,0},{2,3},{3,2},{4,5},{5,4},{6,7},{7,6},{8,9},{9,8},{10,11... | collective-permute-start | bytes 3538952 | tf_op jit(solution)/shard_map/ppermute | solution.py:86
  110.4 10.6 %copy-start.12 = (f32[2,2048]{1,0:T(2,128)S(1)}, f32[2,2048]{1,0:T(2,128)}, u32[]{:S(2)}) copy-start(f32[2,2048]{1,0:T(2,128)} %param.26) | copy-start | bytes 49156
  110.4 11.2 %copy-start.13 = (f32[2,2048]{1,0:T(2,128)S(1)}, f32[2,2048]{1,0:T(2,128)}, u32[]{:S(2)}) copy-start(f32[2,2048]{1,0:T(2,128)} %param.27) | copy-start | bytes 49156
  113.1 35.1 %all-to-all-start.3 = ((bf16[32,64,256]{2,1,0:T(8,128)(2,1)}), bf16[32,64,256]{2,1,0:T(8,128)(2,1)S(1)}, u32[]{:S(2)}, u32[]{:S(2)}) async-start(bf16[32,64,256]{2,1,0:T(8,128)(2,1)} %broadcast_in_dim.93), calls=%async_computation.3 | async-start | bytes 2097152 | tf_op jit(solution)/shard_map/all_to_all | solution.py:199
  151.7 1.9 copy-start.1
  153.3 0.8 copy-start.8
  154.1 0.7 copy-start.15
  159.0 54.6 %all-to-all-start.4 = ((f32[32,8,2048]{2,1,0:T(8,128)}), f32[32,8,2048]{2,1,0:T(8,128)S(1)}, u32[]{:S(2)}, u32[]{:S(2)}) async-start(f32[32,8,2048]{2,1,0:T(8,128)} %convolution_bitcast_fusion), calls=%async_computation.4 | async-start | bytes 4194304 | tf_op jit(solution)/shard_map/all_to_all | solution.py:212
  164.2 49.9 %copy-start.9 = (f32[1,2048]{1,0:T(1,128)S(1)}, f32[1,2048]{1,0:T(1,128)}, u32[]{:S(2)}) copy-start(f32[1,2048]{1,0:T(1,128)} %get-tuple-element.34) | copy-start | bytes 24580
  164.2 49.8 %copy-start.10 = (f32[1,2048]{1,0:T(1,128)S(1)}, f32[1,2048]{1,0:T(1,128)}, u32[]{:S(2)}) copy-start(f32[1,2048]{1,0:T(1,128)} %get-tuple-element.36) | copy-start | bytes 24580

commit v5 on v3

--- a/solution.py
+++ b/solution.py
@@ -92,22 +92,23 @@
     packed = jnp.concatenate([out_weight, in_weight, down_weight], axis=1)
     full_qkv = gather_rows(qkv_flat).reshape(-1, 3, column_width)
     late = gather_rows(packed)
-    sibling = lax.ppermute(late, "bc", swap("bc", nc))
-    chip_out = core_pair(late[:, :column_width], sibling[:, :column_width], core, 1)
-    chip_in = jnp.concatenate(
-        [late[:, column_width : column_width + hidden_width], sibling[:, column_width : column_width + hidden_width]],
-        axis=1,
-    )
-    chip_down = jnp.concatenate(
-        [late[:, column_width + hidden_width :], sibling[:, column_width + hidden_width :]], axis=1
-    )
-    sibling_block = block_index ^ 1
-    chip_in_bias = jnp.concatenate(
-        [
-            lax.dynamic_slice_in_dim(in_bias, block_index * hidden_width, hidden_width),
-            lax.dynamic_slice_in_dim(in_bias, sibling_block * hidden_width, hidden_width),
-        ]
-    )
+    front = late[:, : column_width + hidden_width]
+    sibling = lax.ppermute(front, "bc", swap("bc", nc))
+    chip_out = core_pair(front[:, :column_width], sibling[:, :column_width], core, 1)
+    chip_in = core_pair(front[:, column_width:], sibling[:, column_width:], core, 1)
+    chip_in_bias = lax.dynamic_slice_in_dim(in_bias, chip * nc * hidden_width, nc * hidden_width)
+    d_model = late.shape[0]
+    quarter_width = d_model // nx
+    own_down = late[:, column_width + hidden_width :].reshape(nx, 1, quarter_width, hidden_width)
+    group_down = lax.all_to_all(
+        jnp.broadcast_to(own_down, (nx, nc, quarter_width, hidden_width)).reshape(
+            nx * nc, quarter_width, hidden_width
+        ),
+        ("bx", "bc"),
+        0,
+        0,
+        tiled=True,
+    ).reshape(nx, nc, quarter_width, hidden_width)
 
     query_total = tokens.shape[1]
     token_rows = tokens[0]
@@ -181,6 +182,7 @@
         .transpose(2, 0, 1, 3)
         .reshape(nc, column_width, core_rows)
     )
+    halves, group_down = lax.optimization_barrier((halves, group_down))
     outgoing = jnp.broadcast_to(halves[None], (chips, nc, column_width, core_rows))
     core_context = lax.all_to_all(
         outgoing.reshape(group_size, column_width, core_rows), BLK, 0, 0, tiled=True
@@ -204,10 +206,16 @@
     inner = jax.nn.gelu(
         jnp.dot(normed, chip_in, preferred_element_type=jnp.float32) + chip_in_bias, approximate=True
     ).astype(jnp.bfloat16)
-    mixed_parts = jnp.einsum("rf,df->rd", inner, chip_down, preferred_element_type=jnp.float32)
-    mixed_rows = lax.all_to_all(
-        mixed_parts.reshape(chips, block_rows, -1), PLANE, 0, 0, tiled=True
-    ).sum(axis=0)
+    group_inner = lax.all_to_all(
+        jnp.broadcast_to(inner[None], (nx,) + inner.shape), "bx", 0, 0, tiled=True
+    ).reshape(nx, core_rows, nc, hidden_width)
+    mixed_parts = jnp.einsum(
+        "xtcf,xcdf->td", group_inner, group_down, preferred_element_type=jnp.float32
+    )
+    from_chips = lax.all_to_all(
+        mixed_parts.reshape(chips, block_rows, quarter_width), PLANE, 0, 0, tiled=True
+    ).reshape(nx, ny, block_rows, quarter_width)
+    mixed_rows = from_chips.sum(axis=1).transpose(1, 0, 2).reshape(block_rows, d_model)
     own_normed = lax.dynamic_slice_in_dim(normed, chip * block_rows, block_rows, 0)
     layer_output = layer_norm(
         own_normed.astype(jnp.float32) + mixed_rows + out_biases[1], norm_gains[1], norm_biases[1]

time: 211 us -> 207 us (0.981)
  waiting for transfers between devices: 118 us -> 99.8 us
  blocking collectives: 0 us -> 11.6 us
  local copies, waits for them, and re-layouts: 22.4 us -> 25.9 us
  matrix products: 10.7 us -> 8.23 us
  starting transfers between devices: 47.2 us -> 49.5 us
    all_to_all x1 -> x2, waiting for transfers between devices: 48.7 us -> 28.1 us  [the longest x1 15.7 us: local(): lax.all_to_all(mixed_parts.reshape(chips, block_rows, quarter_width), PLA...]
    all_to_all x0 -> x1, blocking collectives: none -> 11.6 us  [local(): lax.all_to_all(jnp.broadcast_to(inner[None], (nx,) + inner.shape), 'bx',...]
    all_to_all x1 -> x2, starting transfers between devices: 5.32 us -> 9.18 us  [the longest x1 4.88 us: local(): lax.all_to_all(mixed_parts.reshape(chips, block_rows, quarter_width), PLA...]
  transfers between devices with their start and end apart: 10 -> 11, of which waited for: 9 -> 11; matrix products, arithmetic and copies ran while one was open for 11% -> 11% of each run, Pallas kernels for 0% -> 0%
where the time goes in v5:
time: 207 us; the launch traced here: 206 us
  waiting for transfers between devices  99.8 us (48%)
  starting transfers between devices  49.5 us (24%)
  local copies, waits for them, and re-layouts  25.9 us (13%)
  blocking collectives  11.6 us (6%)
  other arithmetic  8.82 us (4%)
  matrix products  8.23 us (4%)
    all_to_all x1, waiting for transfers between devices, local(): lax.all_to_all(spread, PLANE, 0, 0, tiled=True)  25.9 us
    all_to_all x1, waiting for transfers between devices, local(): lax.all_to_all(outgoing.reshape(group_size, column_width, core_rows), BLK...  21.7 us
    all_to_all x1, waiting for transfers between devices, local(): lax.all_to_all(mixed_parts.reshape(chips, block_rows, quarter_width), PLA...  15.7 us
    all_to_all x2, starting transfers between devices, gather_rows(): lax.all_to_all(spread, 'req', 0, 0, tiled=True)  14 us
    all_to_all x1, waiting for transfers between devices, local(): lax.all_to_all(jnp.broadcast_to(own_down, (nx, nc, quarter_width, hidden_...  12.4 us
    all_to_all x1, blocking collectives, local(): lax.all_to_all(jnp.broadcast_to(inner[None], (nx,) + inner.shape), 'bx',...  11.6 us
    ppermute x2, waiting for transfers between devices, from_partner(): lax.ppermute(value, 'by', [(i, i ^ 1 << bit_level - 1) for i in range(ny)])  11.1 us
    all_to_all x1, starting transfers between devices, local(): lax.all_to_all(outgoing.reshape(group_size, column_width, core_rows), BLK...  8.71 us
  transfers between devices with their start and end apart: 11, of which 11 were waited for; matrix products, arithmetic and copies ran while one was open for 11% of the time, Pallas kernels for 0%

profile of v5, /device:TPU:8, one launch (start us, length us, event | category | flops | bytes accessed | tf_op | source)
XLA Modules:
  0.0 205.6 jit_solution(5790377608738007729)
XLA Ops:
  0.6 1.7 broadcast_in_dim.35
  2.3 10.3 %all-to-all-start.1 = ((bf16[8,256,96]{1,2,0:T(8,128)(2,1)}), bf16[8,256,96]{1,2,0:T(8,128)(2,1)}, u32[]{:S(2)}, u32[]{:S(2)}) async-start(bf16[8,256,96]{1,2,0:T(8,128)(2,1)} %broadcast_in_dim.35), calls=%async_computation.1 | async-start | bytes 786432 | tf_op jit(solution)/shard_map/all_to_all | solution.py:53
  13.3 1.5 fusion.64
  17.6 2.0 and_reduce_fusion
  19.6 7.8 %all-to-all-done.1 = bf16[8,256,96]{1,2,0:T(8,128)(2,1)} async-done(((bf16[8,256,96]{1,2,0:T(8,128)(2,1)}), bf16[8,256,96]{1,2,0:T(8,128)(2,1)}, u32[]{:S(2)}, u32[]{:S(2)}) %all-to-all-start.1) | async-done | bytes 393248 | tf_op jit(solution)/shard_map/all_to_all | solution.py:53
  28.5 3.7 %all-to-all-start = ((bf16[8,256,288]{1,2,0:T(8,128)(2,1)}), bf16[8,256,288]{1,2,0:T(8,128)(2,1)S(1)}, u32[]{:S(2)}, u32[]{:S(2)}) async-start(bf16[8,256,288]{1,2,0:T(8,128)(2,1)} %broadcast_in_dim.33), calls=%async_computation | async-start | bytes 2359296 | tf_op jit(solution)/shard_map/all_to_all | solution.py:53
  32.2 2.0 copy.74
  34.2 1.9 reshape_reshape.3
  36.1 1.8 fusion.11
  37.9 1.9 collective-permute-start.1
  41.2 2.4 %collective-permute-start.2 = (bf16[3,64,512]{2,1,0:T(8,128)(2,1)S(1)}, bf16[3,64,512]{2,1,0:T(8,128)(2,1)S(1)}, u32[]{:S(2)}, u32[]{:S(2)}) collective-permute-start(bf16[3,64,512]{2,1,0:T(8,128)(2,1)S(1)} %maximum_select_fusion.9), channel_id=1, source_target_pairs={{0,2},{2,0},{4,6},{6,4},{8,10},{10,8},{12,14},{14,12},{1,3},{3,1},... | collective-permute-start | bytes 589832 | tf_op jit(solution)/shard_map/ppermute | solution.py:124
  43.6 6.4 %collective-permute-done.2 = bf16[3,64,512]{2,1,0:T(8,128)(2,1)S(1)} collective-permute-done((bf16[3,64,512]{2,1,0:T(8,128)(2,1)S(1)}, bf16[3,64,512]{2,1,0:T(8,128)(2,1)S(1)}, u32[]{:S(2)}, u32[]{:S(2)}) %collective-permute-start.2) | collective-permute-done | bytes 196640 | tf_op jit(solution)/shard_map/ppermute | solution.py:124
  50.5 2.2 %fusion.70 = (f32[512]{0:T(512)S(1)}, f32[512,2176]{1,0:T(8,128)S(1)}) fusion(bf16[128,128]{1,0:T(8,128)(2,1)S(1)} %bitcast.133, bf16[2048,128]{1,0:T(8,128)(2,1)} %bitcast.123, bf16[3,128,512]{2,1,0:T(8,128)(2,1)S(1)} %maximum_select_fusion.2, pred[512,128]{1,0:T(32,128)(4,1)S(1)} %iota_compare_fusion, pred[2176]{0:T(1024)(128)(4,1)S(1)} %pad.12.clone), kind=kOutput, calls=%fused_computation.111 | convolution fusion | flops 290782720 | bytes 5215232 | tf_op jit(solution)/shard_map/qd,kd->qk/dot_general | solution.py:29
  54.6 2.4 %collective-permute-start.3 = (f32[66,512]{1,0:T(8,128)S(1)}, f32[66,512]{1,0:T(8,128)S(1)}, u32[]{:S(2)}, u32[]{:S(2)}) collective-permute-start(f32[66,512]{1,0:T(8,128)S(1)} %pad_maximum_fusion.1), channel_id=1, source_target_pairs={{0,2},{2,0},{4,6},{6,4},{8,10},{10,8},{12,14},{14,12},{1,3},{3,1},... | collective-permute-start | bytes 405512 | tf_op jit(solution)/shard_map/ppermute | solution.py:124
  57.0 4.7 %collective-permute-done.3 = f32[66,512]{1,0:T(8,128)S(1)} collective-permute-done((f32[66,512]{1,0:T(8,128)S(1)}, f32[66,512]{1,0:T(8,128)S(1)}, u32[]{:S(2)}, u32[]{:S(2)}) %collective-permute-start.3) | collective-permute-done | bytes 135200 | tf_op jit(solution)/shard_map/ppermute | solution.py:124
  65.6 4.3 %all-to-all-start.2 = ((bf16[8,512,128]{2,1,0:T(8,128)(2,1)}), bf16[8,512,128]{2,1,0:T(8,128)(2,1)S(1)}, u32[]{:S(2)}, u32[]{:S(2)}) async-start(bf16[8,512,128]{2,1,0:T(8,128)(2,1)} %bitcast.26), calls=%async_computation.2 | async-start | bytes 2097152 | tf_op jit(solution)/shard_map/all_to_all | solution.py:103
  70.0 2.4 %collective-permute-start.4 = (f32[34,512]{1,0:T(8,128)S(1)}, f32[34,512]{1,0:T(8,128)S(1)}, u32[]{:S(2)}, u32[]{:S(2)}) collective-permute-start(f32[34,512]{1,0:T(8,128)S(1)} %pad_maximum_fusion.2), channel_id=1, source_target_pairs={{0,1},{1,0},{2,3},{3,2},{4,5},{5,4},{6,7},{7,6},{8,9},{9,8},{10,11... | collective-permute-start | bytes 208904 | tf_op jit(solution)/shard_map/ppermute | solution.py:123
  73.5 12.4 %all-to-all-done.2 = bf16[8,512,128]{2,1,0:T(8,128)(2,1)S(1)} async-done(((bf16[8,512,128]{2,1,0:T(8,128)(2,1)}), bf16[8,512,128]{2,1,0:T(8,128)(2,1)S(1)}, u32[]{:S(2)}, u32[]{:S(2)}) %all-to-all-start.2) | async-done | bytes 1048608 | tf_op jit(solution)/shard_map/all_to_all | solution.py:103
  87.2 8.7 %all-to-all-start.3 = ((bf16[64,32,256]{2,1,0:T(8,128)(2,1)}), bf16[64,32,256]{2,1,0:T(8,128)(2,1)S(1)}, u32[]{:S(2)}, u32[]{:S(2)}) async-start(bf16[64,32,256]{2,1,0:T(8,128)(2,1)} %bitcast.28), calls=%async_computation.3 | async-start | bytes 2097152 | tf_op jit(solution)/shard_map/all_to_all | solution.py:187
  96.8 2.0 collective-permute-start
  99.0 2.1 %collective-permute-done = bf16[2048,160]{0,1:T(8,128)(2,1)} collective-permute-done((bf16[2048,160]{0,1:T(8,128)(2,1)}, bf16[2048,160]{0,1:T(8,128)(2,1)}, u32[]{:S(2)}, u32[]{:S(2)}) %collective-permute-start) | collective-permute-done | bytes 655392 | tf_op jit(solution)/shard_map/ppermute | solution.py:96
  102.1 21.7 %all-to-all-done.3 = bf16[64,32,256]{2,1,0:T(8,128)(2,1)S(1)} async-done(((bf16[64,32,256]{2,1,0:T(8,128)(2,1)}), bf16[64,32,256]{2,1,0:T(8,128)(2,1)S(1)}, u32[]{:S(2)}, u32[]{:S(2)}) %all-to-all-start.3) | async-done | bytes 1048608 | tf_op jit(solution)/shard_map/all_to_all | solution.py:187
  125.2 6.5 %all-to-all-start.4 = ((bf16[32,64,256]{2,1,0:T(8,128)(2,1)}), bf16[32,64,256]{2,1,0:T(8,128)(2,1)S(1)}, u32[]{:S(2)}, u32[]{:S(2)}) async-start(bf16[32,64,256]{2,1,0:T(8,128)(2,1)} %broadcast_in_dim.44), calls=%async_computation.4 | async-start | bytes 2097152 | tf_op jit(solution)/shard_map/all_to_all | solution.py:197
  132.5 1.9 slice.148
  134.4 25.9 %all-to-all-done.4 = bf16[32,64,256]{2,1,0:T(8,128)(2,1)S(1)} async-done(((bf16[32,64,256]{2,1,0:T(8,128)(2,1)}), bf16[32,64,256]{2,1,0:T(8,128)(2,1)S(1)}, u32[]{:S(2)}, u32[]{:S(2)}) %all-to-all-start.4) | async-done | bytes 1048608 | tf_op jit(solution)/shard_map/all_to_all | solution.py:197
  160.3 1.6 bitcast_convert_fusion
  161.9 1.9 copy.82
  163.9 1.7 fusion.28
  168.3 11.6 %all_to_all.35 = bf16[4,256,256]{1,2,0:T(8,128)(2,1)S(1)} all-to-all(bf16[4,256,256]{1,2,0:T(8,128)(2,1)S(1)} %broadcast_in_dim.45), channel_id=1, replica_groups=mesh['req'=8,'bx'=4,'by'=8,'bc'=2] {'bx'}, dimensions={0} | all-to-all | bytes 1048576 | tf_op jit(solution)/shard_map/all_to_all | solution.py:209
  180.9 2.3 %convolution_bitcast_fusion = f32[32,8,512]{2,1,0:T(8,128)} fusion(bf16[256,2,128,4]{2,0,3,1:T(8,128)(2,1)} %copy.84, bf16[4,2,512,128]{3,2,1,0:T(8,128)(2,1)S(1)} %bitcast.120), kind=kOutput, calls=%fused_computation.13 | convolution fusion | flops 268435456 | bytes 2097152 | tf_op jit(solution)/shard_map/xtcf,xcdf->td/dot_general | solution.py:212
  183.2 4.9 %all-to-all-start.6 = ((f32[32,8,512]{2,1,0:T(8,128)}), f32[32,8,512]{2,1,0:T(8,128)S(1)}, u32[]{:S(2)}, u32[]{:S(2)}) async-start(f32[32,8,512]{2,1,0:T(8,128)} %convolution_bitcast_fusion), calls=%async_computation.6 | async-start | bytes 1048576 | tf_op jit(solution)/shard_map/all_to_all | solution.py:215
  188.8 15.7 %all-to-all-done.6 = f32[32,8,512]{2,1,0:T(8,128)S(1)} async-done(((f32[32,8,512]{2,1,0:T(8,128)}), f32[32,8,512]{2,1,0:T(8,128)S(1)}, u32[]{:S(2)}, u32[]{:S(2)}) %all-to-all-start.6) | async-done | bytes 524320 | tf_op jit(solution)/shard_map/all_to_all | solution.py:215
  (102 shorter events, 23.5 us)
Async XLA Ops:
  0.6 12.6 %copy-start.2 = (bf16[1,1,2048,2,128]{4,3,2,1,0:T(2,128)(2,1)S(1)}, bf16[1,1,2048,2,128]{4,3,2,1,0:T(2,128)(2,1)}, u32[]{:S(2)}) copy-start(bf16[1,1,2048,2,128]{4,3,2,1,0:T(2,128)(2,1)} %param.15) | copy-start | bytes 3145732
  2.3 25.1 %all-to-all-start.1 = ((bf16[8,256,96]{1,2,0:T(8,128)(2,1)}), bf16[8,256,96]{1,2,0:T(8,128)(2,1)}, u32[]{:S(2)}, u32[]{:S(2)}) async-start(bf16[8,256,96]{1,2,0:T(8,128)(2,1)} %broadcast_in_dim.35), calls=%async_computation.1 | async-start | bytes 786432 | tf_op jit(solution)/shard_map/all_to_all | solution.py:53
  14.8 1.8 copy-start.14
  14.8 1.9 copy-start.12
  14.8 1.9 copy-start.13
  14.8 2.2 %copy-start.18 = (s32[1,2]{1,0:T(1,128)S(1)}, s32[1,2]{1,0:T(1,128)}, u32[]{:S(2)}) copy-start(s32[1,2]{1,0:T(1,128)} %param.18) | copy-start | bytes 28
  28.5 7.6 %copy-start = (bf16[1,512,2048]{2,1,0:T(8,128)(2,1)S(1)}, bf16[1,512,2048]{2,1,0:T(8,128)(2,1)}, u32[]{:S(2)}) copy-start(bf16[1,512,2048]{2,1,0:T(8,128)(2,1)} %param.14) | copy-start | bytes 6291460
  28.5 7.6 %copy-start.19 = (f32[3,32]{1,0:T(4,128)S(1)}, f32[3,32]{1,0:T(4,128)}, u32[]{:S(2)}) copy-start(f32[3,32]{1,0:T(4,128)} %param.20) | copy-start | bytes 1156
  28.5 34.7 %all-to-all-start = ((bf16[8,256,288]{1,2,0:T(8,128)(2,1)}), bf16[8,256,288]{1,2,0:T(8,128)(2,1)S(1)}, u32[]{:S(2)}, u32[]{:S(2)}) async-start(bf16[8,256,288]{1,2,0:T(8,128)(2,1)} %broadcast_in_dim.33), calls=%async_computation | async-start | bytes 2359296 | tf_op jit(solution)/shard_map/all_to_all | solution.py:53
  37.9 12.2 %copy-start.5 = (bf16[3,32,512]{2,1,0:T(8,128)(2,1)}, bf16[3,32,512]{2,1,0:T(8,128)(2,1)S(1)}, u32[]{:S(2)}) copy-start(bf16[3,32,512]{2,1,0:T(8,128)(2,1)S(1)} %fusion.11) | copy-start | bytes 294916
  37.9 3.2 %collective-permute-start.1 = (bf16[3,32,512]{2,1,0:T(8,128)(2,1)S(1)}, bf16[3,32,512]{2,1,0:T(8,128)(2,1)S(1)}, u32[]{:S(2)}, u32[]{:S(2)}) collective-permute-start(bf16[3,32,512]{2,1,0:T(8,128)(2,1)S(1)} %fusion.11), channel_id=1, source_target_pairs={{0,1},{1,0},{2,3},{3,2},{4,5},{5,4},{6,7},{7,6},{8,9},{9,8},{10,11... | collective-permute-start | bytes 294920 | tf_op jit(solution)/shard_map/ppermute | solution.py:123
  41.2 8.9 %collective-permute-start.2 = (bf16[3,64,512]{2,1,0:T(8,128)(2,1)S(1)}, bf16[3,64,512]{2,1,0:T(8,128)(2,1)S(1)}, u32[]{:S(2)}, u32[]{:S(2)}) collective-permute-start(bf16[3,64,512]{2,1,0:T(8,128)(2,1)S(1)} %maximum_select_fusion.9), channel_id=1, source_target_pairs={{0,2},{2,0},{4,6},{6,4},{8,10},{10,8},{12,14},{14,12},{1,3},{3,1},... | collective-permute-start | bytes 589832 | tf_op jit(solution)/shard_map/ppermute | solution.py:124
  50.5 2.2 %copy-start.7 = (bf16[1,1,2048,1,128]{4,2,3,1,0:T(8,128)(2,1)S(1)}, bf16[1,1,2048,1,128]{4,2,3,1,0:T(8,128)(2,1)}, u32[]{:S(2)}) copy-start(bf16[1,1,2048,1,128]{4,2,3,1,0:T(8,128)(2,1)} %copy.100) | copy-start | bytes 1572868
  54.6 7.0 %collective-permute-start.3 = (f32[66,512]{1,0:T(8,128)S(1)}, f32[66,512]{1,0:T(8,128)S(1)}, u32[]{:S(2)}, u32[]{:S(2)}) collective-permute-start(f32[66,512]{1,0:T(8,128)S(1)} %pad_maximum_fusion.1), channel_id=1, source_target_pairs={{0,2},{2,0},{4,6},{6,4},{8,10},{10,8},{12,14},{14,12},{1,3},{3,1},... | collective-permute-start | bytes 405512 | tf_op jit(solution)/shard_map/ppermute | solution.py:124
  61.7 0.7 copy-start.10
  64.5 5.4 %copy-start.11 = (f32[66,512]{1,0:T(8,128)S(1)}, f32[66,512]{1,0:T(8,128)}, u32[]{:S(2)}) copy-start(f32[66,512]{1,0:T(8,128)} %copy-done.10) | copy-start | bytes 405508
  65.6 20.3 %all-to-all-start.2 = ((bf16[8,512,128]{2,1,0:T(8,128)(2,1)}), bf16[8,512,128]{2,1,0:T(8,128)(2,1)S(1)}, u32[]{:S(2)}, u32[]{:S(2)}) async-start(bf16[8,512,128]{2,1,0:T(8,128)(2,1)} %bitcast.26), calls=%async_computation.2 | async-start | bytes 2097152 | tf_op jit(solution)/shard_map/all_to_all | solution.py:103
  70.0 3.3 %collective-permute-start.4 = (f32[34,512]{1,0:T(8,128)S(1)}, f32[34,512]{1,0:T(8,128)S(1)}, u32[]{:S(2)}, u32[]{:S(2)}) collective-permute-start(f32[34,512]{1,0:T(8,128)S(1)} %pad_maximum_fusion.2), channel_id=1, source_target_pairs={{0,1},{1,0},{2,3},{3,2},{4,5},{5,4},{6,7},{7,6},{8,9},{9,8},{10,11... | collective-permute-start | bytes 208904 | tf_op jit(solution)/shard_map/ppermute | solution.py:123
  85.9 10.9 %copy-start.3 = (bf16[8,512,128]{2,1,0:T(8,128)(2,1)}, bf16[8,512,128]{2,1,0:T(8,128)(2,1)S(1)}, u32[]{:S(2)}) copy-start(bf16[8,512,128]{2,1,0:T(8,128)(2,1)S(1)} %all-to-all-done.2) | copy-start | bytes 3145732
  86.0 12.9 %copy-start.15 = (f32[2,2048]{1,0:T(2,128)S(1)}, f32[2,2048]{1,0:T(2,128)}, u32[]{:S(2)}) copy-start(f32[2,2048]{1,0:T(2,128)} %param.25) | copy-start | bytes 49156
  87.2 36.6 %all-to-all-start.3 = ((bf16[64,32,256]{2,1,0:T(8,128)(2,1)}), bf16[64,32,256]{2,1,0:T(8,128)(2,1)S(1)}, u32[]{:S(2)}, u32[]{:S(2)}) async-start(bf16[64,32,256]{2,1,0:T(8,128)(2,1)} %bitcast.28), calls=%async_computation.3 | async-start | bytes 2097152 | tf_op jit(solution)/shard_map/all_to_all | solution.py:187
  96.8 4.3 %collective-permute-start = (bf16[2048,160]{0,1:T(8,128)(2,1)}, bf16[2048,160]{0,1:T(8,128)(2,1)}, u32[]{:S(2)}, u32[]{:S(2)}) collective-permute-start(bf16[2048,160]{0,1:T(8,128)(2,1)} %slice.131), channel_id=1, source_target_pairs={{0,1},{1,0},{2,3},{3,2},{4,5},{5,4},{6,7},{7,6},{8,9},{9,8},{10,11... | collective-permute-start | bytes 1966088 | tf_op jit(solution)/shard_map/ppermute | solution.py:96
  123.8 8.7 %copy-start.16 = (f32[2,2048]{1,0:T(2,128)S(1)}, f32[2,2048]{1,0:T(2,128)}, u32[]{:S(2)}) copy-start(f32[2,2048]{1,0:T(2,128)} %param.26) | copy-start | bytes 49156
  123.8 8.7 %copy-start.17 = (f32[2,2048]{1,0:T(2,128)S(1)}, f32[2,2048]{1,0:T(2,128)}, u32[]{:S(2)}) copy-start(f32[2,2048]{1,0:T(2,128)} %param.27) | copy-start | bytes 49156
  125.2 35.1 %all-to-all-start.4 = ((bf16[32,64,256]{2,1,0:T(8,128)(2,1)}), bf16[32,64,256]{2,1,0:T(8,128)(2,1)S(1)}, u32[]{:S(2)}, u32[]{:S(2)}) async-start(bf16[32,64,256]{2,1,0:T(8,128)(2,1)} %broadcast_in_dim.44), calls=%async_computation.4 | async-start | bytes 2097152 | tf_op jit(solution)/shard_map/all_to_all | solution.py:197
  163.8 1.9 copy-start.1
  166.2 1.1 copy-start.8
  166.3 1.2 copy-start.9
  168.1 12.8 %copy-start.4 = (bf16[8,512,128]{2,1,0:T(8,128)(2,1)S(1)}, bf16[8,512,128]{2,1,0:T(8,128)(2,1)}, u32[]{:S(2)}) copy-start(bf16[8,512,128]{2,1,0:T(8,128)(2,1)} %copy-done.3) | copy-start | bytes 3145732
  179.9 8.2 %copy-start.6 = (bf16[3,32,512]{2,1,0:T(8,128)(2,1)S(1)}, bf16[3,32,512]{2,1,0:T(8,128)(2,1)}, u32[]{:S(2)}) copy-start(bf16[3,32,512]{2,1,0:T(8,128)(2,1)} %copy-done.5) | copy-start | bytes 294916
  183.2 21.3 %all-to-all-start.6 = ((f32[32,8,512]{2,1,0:T(8,128)}), f32[32,8,512]{2,1,0:T(8,128)S(1)}, u32[]{:S(2)}, u32[]{:S(2)}) async-start(f32[32,8,512]{2,1,0:T(8,128)} %convolution_bitcast_fusion), calls=%async_computation.6 | async-start | bytes 1048576 | tf_op jit(solution)/shard_map/all_to_all | solution.py:215

commit v6 on v5

--- a/solution.py
+++ b/solution.py
@@ -89,17 +89,11 @@
     rows, _, column_width = qkv_weight.shape
     qkv_flat = qkv_weight.reshape(rows, 3 * column_width)
     hidden_width = in_weight.shape[1]
-    packed = jnp.concatenate([out_weight, in_weight, down_weight], axis=1)
-    full_qkv = gather_rows(qkv_flat).reshape(-1, 3, column_width)
-    late = gather_rows(packed)
-    front = late[:, : column_width + hidden_width]
-    sibling = lax.ppermute(front, "bc", swap("bc", nc))
-    chip_out = core_pair(front[:, :column_width], sibling[:, :column_width], core, 1)
-    chip_in = core_pair(front[:, column_width:], sibling[:, column_width:], core, 1)
-    chip_in_bias = lax.dynamic_slice_in_dim(in_bias, chip * nc * hidden_width, nc * hidden_width)
-    d_model = late.shape[0]
+    first = gather_rows(jnp.concatenate([qkv_flat, down_weight], axis=1))
+    full_qkv = first[:, : 3 * column_width].reshape(-1, 3, column_width)
+    d_model = first.shape[0]
     quarter_width = d_model // nx
-    own_down = late[:, column_width + hidden_width :].reshape(nx, 1, quarter_width, hidden_width)
+    own_down = first[:, 3 * column_width :].reshape(nx, 1, quarter_width, hidden_width)
     group_down = lax.all_to_all(
         jnp.broadcast_to(own_down, (nx, nc, quarter_width, hidden_width)).reshape(
             nx * nc, quarter_width, hidden_width
@@ -109,6 +103,13 @@
         0,
         tiled=True,
     ).reshape(nx, nc, quarter_width, hidden_width)
+    packed = jnp.concatenate([out_weight, in_weight], axis=1)
+    packed, group_down = lax.optimization_barrier((packed, group_down))
+    front = gather_rows(packed)
+    sibling = lax.ppermute(front, "bc", swap("bc", nc))
+    chip_out = core_pair(front[:, :column_width], sibling[:, :column_width], core, 1)
+    chip_in = core_pair(front[:, column_width:], sibling[:, column_width:], core, 1)
+    chip_in_bias = lax.dynamic_slice_in_dim(in_bias, chip * nc * hidden_width, nc * hidden_width)
 
     query_total = tokens.shape[1]
     token_rows = tokens[0]
@@ -182,7 +183,6 @@
         .transpose(2, 0, 1, 3)
         .reshape(nc, column_width, core_rows)
     )
-    halves, group_down = lax.optimization_barrier((halves, group_down))
     outgoing = jnp.broadcast_to(halves[None], (chips, nc, column_width, core_rows))
     core_context = lax.all_to_all(
         outgoing.reshape(group_size, column_width, core_rows), BLK, 0, 0, tiled=True

time: 207 us -> 212 us (1.024)
  waiting for transfers between devices: 99.8 us -> 116 us
  local copies, waits for them, and re-layouts: 25.9 us -> 17.1 us
  matrix products: 8.23 us -> 5.1 us
    all_to_all x2, waiting for transfers between devices: 8.6 us -> 36.1 us  [gather_rows(): lax.all_to_all(spread, 'req', 0, 0, tiled=True)]
    ppermute x2, waiting for transfers between devices: 11.1 us -> 0.56 us  [from_partner(): lax.ppermute(value, 'by', [(i, i ^ 1 << bit_level - 1) for i in range(ny)])]
    all_to_all x1, waiting for transfers between devices: 12.4 us -> 8.68 us  [local(): lax.all_to_all(jnp.broadcast_to(own_down, (nx, nc, quarter_width, hidden_...]
  transfers between devices with their start and end apart: 11 -> 11, of which waited for: 11 -> 10; matrix products, arithmetic and copies ran while one was open for 11% -> 7% of each run, Pallas kernels for 0% -> 0%
where the time goes in v6:
time: 212 us; the launch traced here: 211 us
  waiting for transfers between devices  116 us (55%)
  starting transfers between devices  49.8 us (23%)
  local copies, waits for them, and re-layouts  17.1 us (8%)
  blocking collectives  11.6 us (5%)
  other arithmetic  9.73 us (5%)
  matrix products  5.1 us (2%)
    all_to_all x2, waiting for transfers between devices, gather_rows(): lax.all_to_all(spread, 'req', 0, 0, tiled=True)  36.1 us
    all_to_all x1, waiting for transfers between devices, local(): lax.all_to_all(spread, PLANE, 0, 0, tiled=True)  27 us
    all_to_all x1, waiting for transfers between devices, local(): lax.all_to_all(outgoing.reshape(group_size, column_width, core_rows), BLK...  23.8 us
    all_to_all x1, waiting for transfers between devices, local(): lax.all_to_all(mixed_parts.reshape(chips, block_rows, quarter_width), PLA...  15.7 us
    all_to_all x2, starting transfers between devices, gather_rows(): lax.all_to_all(spread, 'req', 0, 0, tiled=True)  13.9 us
    all_to_all x1, blocking collectives, local(): lax.all_to_all(jnp.broadcast_to(inner[None], (nx,) + inner.shape), 'bx',...  11.6 us
    all_to_all x1, starting transfers between devices, local(): lax.all_to_all(outgoing.reshape(group_size, column_width, core_rows), BLK...  8.94 us
    all_to_all x1, waiting for transfers between devices, local(): lax.all_to_all(jnp.broadcast_to(own_down, (nx, nc, quarter_width, hidden_...  8.68 us
  transfers between devices with their start and end apart: 11, of which 10 were waited for; matrix products, arithmetic and copies ran while one was open for 7% of the time, Pallas kernels for 0%

profile of v6, /device:TPU:8, one launch (start us, length us, event | category | flops | bytes accessed | tf_op | source)
XLA Modules:
  0.0 211.3 jit_solution(2469395834697824404)
XLA Ops:
  3.7 10.3 %all-to-all-start = ((bf16[8,256,224]{1,2,0:T(8,128)(2,1)}), bf16[8,256,224]{1,2,0:T(8,128)(2,1)S(1)}, u32[]{:S(2)}, u32[]{:S(2)}) async-start(bf16[8,256,224]{1,2,0:T(8,128)(2,1)} %broadcast_in_dim.33), calls=%async_computation | async-start | bytes 1835008 | tf_op jit(solution)/shard_map/all_to_all | solution.py:53
  14.7 1.5 fusion.63
  18.5 2.0 and_reduce_fusion
  20.6 19.3 %all-to-all-done = bf16[8,256,224]{1,2,0:T(8,128)(2,1)S(1)} async-done(((bf16[8,256,224]{1,2,0:T(8,128)(2,1)}), bf16[8,256,224]{1,2,0:T(8,128)(2,1)S(1)}, u32[]{:S(2)}, u32[]{:S(2)}) %all-to-all-start) | async-done | bytes 917536 | tf_op jit(solution)/shard_map/all_to_all | solution.py:53
  40.9 1.9 collective-permute-start.1
  42.8 1.3 collective-permute-done.1
  44.1 2.4 %collective-permute-start.2 = (bf16[3,64,512]{2,1,0:T(8,128)(2,1)S(1)}, bf16[3,64,512]{2,1,0:T(8,128)(2,1)S(1)}, u32[]{:S(2)}, u32[]{:S(2)}) collective-permute-start(bf16[3,64,512]{2,1,0:T(8,128)(2,1)S(1)} %maximum_select_fusion.9), channel_id=1, source_target_pairs={{0,2},{2,0},{4,6},{6,4},{8,10},{10,8},{12,14},{14,12},{1,3},{3,1},... | collective-permute-start | bytes 589832 | tf_op jit(solution)/shard_map/ppermute | solution.py:125
  46.9 1.1 broadcast_in_dim.35
  48.0 4.4 %all-to-all-start.1 = ((bf16[8,512,128]{2,1,0:T(8,128)(2,1)}), bf16[8,512,128]{2,1,0:T(8,128)(2,1)S(1)}, u32[]{:S(2)}, u32[]{:S(2)}) async-start(bf16[8,512,128]{2,1,0:T(8,128)(2,1)} %bitcast.4), calls=%async_computation.1 | async-start | bytes 2097152 | tf_op jit(solution)/shard_map/all_to_all | solution.py:97
  53.4 1.1 fusion.69
  56.5 2.9 %collective-permute-start.3 = (f32[66,512]{1,0:T(8,128)S(1)}, f32[66,512]{1,0:T(8,128)S(1)}, u32[]{:S(2)}, u32[]{:S(2)}) collective-permute-start(f32[66,512]{1,0:T(8,128)S(1)} %pad_maximum_fusion), channel_id=1, source_target_pairs={{0,2},{2,0},{4,6},{6,4},{8,10},{10,8},{12,14},{14,12},{1,3},{3,1},... | collective-permute-start | bytes 405512 | tf_op jit(solution)/shard_map/ppermute | solution.py:125
  59.7 8.7 %all-to-all-done.1 = bf16[8,512,128]{2,1,0:T(8,128)(2,1)S(1)} async-done(((bf16[8,512,128]{2,1,0:T(8,128)(2,1)}), bf16[8,512,128]{2,1,0:T(8,128)(2,1)S(1)}, u32[]{:S(2)}, u32[]{:S(2)}) %all-to-all-start.1) | async-done | bytes 1048608 | tf_op jit(solution)/shard_map/all_to_all | solution.py:97
  68.5 1.0 broadcast_in_dim.36
  69.5 3.5 %all-to-all-start.2 = ((bf16[8,256,160]{1,2,0:T(8,128)(2,1)}), bf16[8,256,160]{1,2,0:T(8,128)(2,1)S(1)}, u32[]{:S(2)}, u32[]{:S(2)}) async-start(bf16[8,256,160]{1,2,0:T(8,128)(2,1)} %broadcast_in_dim.36), calls=%async_computation.2 | async-start | bytes 1310720 | tf_op jit(solution)/shard_map/all_to_all | solution.py:53
  73.2 1.9 collective-permute-start.4
  75.1 1.2 collective-permute-done.4
  76.6 16.7 %all-to-all-done.2 = bf16[8,256,160]{1,2,0:T(8,128)(2,1)S(1)} async-done(((bf16[8,256,160]{1,2,0:T(8,128)(2,1)}), bf16[8,256,160]{1,2,0:T(8,128)(2,1)S(1)}, u32[]{:S(2)}, u32[]{:S(2)}) %all-to-all-start.2) | async-done | bytes 655392 | tf_op jit(solution)/shard_map/all_to_all | solution.py:53
  93.4 1.1 broadcast_in_dim.43
  94.5 8.9 %all-to-all-start.3 = ((bf16[64,32,256]{2,1,0:T(8,128)(2,1)}), bf16[64,32,256]{2,1,0:T(8,128)(2,1)S(1)}, u32[]{:S(2)}, u32[]{:S(2)}) async-start(bf16[64,32,256]{2,1,0:T(8,128)(2,1)} %bitcast.29), calls=%async_computation.3 | async-start | bytes 2097152 | tf_op jit(solution)/shard_map/all_to_all | solution.py:187
  103.5 2.1 collective-permute-start
  105.7 1.8 collective-permute-done
  107.5 23.8 %all-to-all-done.3 = bf16[64,32,256]{2,1,0:T(8,128)(2,1)S(1)} async-done(((bf16[64,32,256]{2,1,0:T(8,128)(2,1)}), bf16[64,32,256]{2,1,0:T(8,128)(2,1)S(1)}, u32[]{:S(2)}, u32[]{:S(2)}) %all-to-all-start.3) | async-done | bytes 1048608 | tf_op jit(solution)/shard_map/all_to_all | solution.py:187
  131.6 1.1 broadcast_in_dim.44
  132.7 6.5 %all-to-all-start.4 = ((bf16[32,64,256]{2,1,0:T(8,128)(2,1)}), bf16[32,64,256]{2,1,0:T(8,128)(2,1)S(1)}, u32[]{:S(2)}, u32[]{:S(2)}) async-start(bf16[32,64,256]{2,1,0:T(8,128)(2,1)} %broadcast_in_dim.44), calls=%async_computation.4 | async-start | bytes 2097152 | tf_op jit(solution)/shard_map/all_to_all | solution.py:197
  140.8 27.0 %all-to-all-done.4 = bf16[32,64,256]{2,1,0:T(8,128)(2,1)S(1)} async-done(((bf16[32,64,256]{2,1,0:T(8,128)(2,1)}), bf16[32,64,256]{2,1,0:T(8,128)(2,1)S(1)}, u32[]{:S(2)}, u32[]{:S(2)}) %all-to-all-start.4) | async-done | bytes 1048608 | tf_op jit(solution)/shard_map/all_to_all | solution.py:197
  167.8 1.6 bitcast_convert_fusion
  169.4 1.9 copy.97
  171.3 1.7 fusion.28
  175.7 11.6 %all_to_all.35 = bf16[4,256,256]{1,2,0:T(8,128)(2,1)S(1)} all-to-all(bf16[4,256,256]{1,2,0:T(8,128)(2,1)S(1)} %broadcast_in_dim.45), channel_id=1, replica_groups=mesh['req'=8,'bx'=4,'by'=8,'bc'=2] {'bx'}, dimensions={0} | all-to-all | bytes 1048576 | tf_op jit(solution)/shard_map/all_to_all | solution.py:209
  187.7 1.3 convolution_bitcast_fusion
  189.0 4.9 %all-to-all-start.6 = ((f32[32,8,512]{2,1,0:T(8,128)}), f32[32,8,512]{2,1,0:T(8,128)S(1)}, u32[]{:S(2)}, u32[]{:S(2)}) async-start(f32[32,8,512]{2,1,0:T(8,128)} %convolution_bitcast_fusion), calls=%async_computation.6 | async-start | bytes 1048576 | tf_op jit(solution)/shard_map/all_to_all | solution.py:215
  194.5 15.7 %all-to-all-done.6 = f32[32,8,512]{2,1,0:T(8,128)S(1)} async-done(((f32[32,8,512]{2,1,0:T(8,128)}), f32[32,8,512]{2,1,0:T(8,128)S(1)}, u32[]{:S(2)}, u32[]{:S(2)}) %all-to-all-start.6) | async-done | bytes 524320 | tf_op jit(solution)/shard_map/all_to_all | solution.py:215
  (98 shorter events, 17.1 us)
Async XLA Ops:
  0.6 14.0 %copy-start.2 = (bf16[1,1,2048,2,128]{4,3,2,1,0:T(2,128)(2,1)S(1)}, bf16[1,1,2048,2,128]{4,3,2,1,0:T(2,128)(2,1)}, u32[]{:S(2)}) copy-start(bf16[1,1,2048,2,128]{4,3,2,1,0:T(2,128)(2,1)} %param.15) | copy-start | bytes 3145732
  3.7 36.2 %all-to-all-start = ((bf16[8,256,224]{1,2,0:T(8,128)(2,1)}), bf16[8,256,224]{1,2,0:T(8,128)(2,1)S(1)}, u32[]{:S(2)}, u32[]{:S(2)}) async-start(bf16[8,256,224]{1,2,0:T(8,128)(2,1)} %broadcast_in_dim.33), calls=%async_computation | async-start | bytes 1835008 | tf_op jit(solution)/shard_map/all_to_all | solution.py:53
  16.2 1.8 copy-start.14
  17.1 23.0 %copy-start = (bf16[1,512,2048]{2,1,0:T(8,128)(2,1)S(1)}, bf16[1,512,2048]{2,1,0:T(8,128)(2,1)}, u32[]{:S(2)}) copy-start(bf16[1,512,2048]{2,1,0:T(8,128)(2,1)} %param.14) | copy-start | bytes 6291460
  17.1 23.0 %copy-start.15 = (f32[3,32]{1,0:T(4,128)S(1)}, f32[3,32]{1,0:T(4,128)}, u32[]{:S(2)}) copy-start(f32[3,32]{1,0:T(4,128)} %param.20) | copy-start | bytes 1156
  40.9 3.2 %collective-permute-start.1 = (bf16[3,32,512]{2,1,0:T(8,128)(2,1)S(1)}, bf16[3,32,512]{2,1,0:T(8,128)(2,1)S(1)}, u32[]{:S(2)}, u32[]{:S(2)}) collective-permute-start(bf16[3,32,512]{2,1,0:T(8,128)(2,1)S(1)} %fusion.11), channel_id=1, source_target_pairs={{0,1},{1,0},{2,3},{3,2},{4,5},{5,4},{6,7},{7,6},{8,9},{9,8},{10,11... | collective-permute-start | bytes 294920 | tf_op jit(solution)/shard_map/ppermute | solution.py:124
  44.1 8.9 %collective-permute-start.2 = (bf16[3,64,512]{2,1,0:T(8,128)(2,1)S(1)}, bf16[3,64,512]{2,1,0:T(8,128)(2,1)S(1)}, u32[]{:S(2)}, u32[]{:S(2)}) collective-permute-start(bf16[3,64,512]{2,1,0:T(8,128)(2,1)S(1)} %maximum_select_fusion.9), channel_id=1, source_target_pairs={{0,2},{2,0},{4,6},{6,4},{8,10},{10,8},{12,14},{14,12},{1,3},{3,1},... | collective-permute-start | bytes 589832 | tf_op jit(solution)/shard_map/ppermute | solution.py:125
  48.0 5.4 %copy-start.7 = (bf16[1,1,2048,1,128]{4,2,3,1,0:T(8,128)(2,1)S(1)}, bf16[1,1,2048,1,128]{4,2,3,1,0:T(8,128)(2,1)}, u32[]{:S(2)}) copy-start(bf16[1,1,2048,1,128]{4,2,3,1,0:T(8,128)(2,1)} %copy.115) | copy-start | bytes 1572868
  48.0 20.4 %all-to-all-start.1 = ((bf16[8,512,128]{2,1,0:T(8,128)(2,1)}), bf16[8,512,128]{2,1,0:T(8,128)(2,1)S(1)}, u32[]{:S(2)}, u32[]{:S(2)}) async-start(bf16[8,512,128]{2,1,0:T(8,128)(2,1)} %bitcast.4), calls=%async_computation.1 | async-start | bytes 2097152 | tf_op jit(solution)/shard_map/all_to_all | solution.py:97
  53.4 1.1 copy-start.6
  55.5 3.9 %copy-start.10 = (bf16[256,32]{0,1:T(8,128)(2,1)S(1)}, bf16[256,32]{0,1:T(8,128)(2,1)}, u32[]{:S(2)}) copy-start(bf16[256,32]{0,1:T(8,128)(2,1)} %param.21) | copy-start | bytes 49156
  55.6 4.0 %copy-start.9 = (bf16[256,128]{1,0:T(8,128)(2,1)S(1)}, bf16[256,128]{1,0:T(8,128)(2,1)}, u32[]{:S(2)}) copy-start(bf16[256,128]{1,0:T(8,128)(2,1)} %param.22) | copy-start | bytes 196612
  56.5 16.6 %collective-permute-start.3 = (f32[66,512]{1,0:T(8,128)S(1)}, f32[66,512]{1,0:T(8,128)S(1)}, u32[]{:S(2)}, u32[]{:S(2)}) collective-permute-start(f32[66,512]{1,0:T(8,128)S(1)} %pad_maximum_fusion), channel_id=1, source_target_pairs={{0,2},{2,0},{4,6},{6,4},{8,10},{10,8},{12,14},{14,12},{1,3},{3,1},... | collective-permute-start | bytes 405512 | tf_op jit(solution)/shard_map/ppermute | solution.py:125
  68.4 26.1 %copy-start.3 = (bf16[8,512,128]{2,1,0:T(8,128)(2,1)}, bf16[8,512,128]{2,1,0:T(8,128)(2,1)S(1)}, u32[]{:S(2)}) copy-start(bf16[8,512,128]{2,1,0:T(8,128)(2,1)S(1)} %all-to-all-done.1) | copy-start | bytes 3145732
  69.5 23.8 %all-to-all-start.2 = ((bf16[8,256,160]{1,2,0:T(8,128)(2,1)}), bf16[8,256,160]{1,2,0:T(8,128)(2,1)S(1)}, u32[]{:S(2)}, u32[]{:S(2)}) async-start(bf16[8,256,160]{1,2,0:T(8,128)(2,1)} %broadcast_in_dim.36), calls=%async_computation.2 | async-start | bytes 1310720 | tf_op jit(solution)/shard_map/all_to_all | solution.py:53
  73.2 3.2 %collective-permute-start.4 = (f32[34,512]{1,0:T(8,128)S(1)}, f32[34,512]{1,0:T(8,128)S(1)}, u32[]{:S(2)}, u32[]{:S(2)}) collective-permute-start(f32[34,512]{1,0:T(8,128)S(1)} %pad_maximum_fusion.3), channel_id=1, source_target_pairs={{0,1},{1,0},{2,3},{3,2},{4,5},{5,4},{6,7},{7,6},{8,9},{9,8},{10,11... | collective-permute-start | bytes 208904 | tf_op jit(solution)/shard_map/ppermute | solution.py:124
  76.6 28.9 %copy-start.11 = (f32[2,2048]{1,0:T(2,128)S(1)}, f32[2,2048]{1,0:T(2,128)}, u32[]{:S(2)}) copy-start(f32[2,2048]{1,0:T(2,128)} %param.25) | copy-start | bytes 49156
  94.5 36.8 %all-to-all-start.3 = ((bf16[64,32,256]{2,1,0:T(8,128)(2,1)}), bf16[64,32,256]{2,1,0:T(8,128)(2,1)S(1)}, u32[]{:S(2)}, u32[]{:S(2)}) async-start(bf16[64,32,256]{2,1,0:T(8,128)(2,1)} %bitcast.29), calls=%async_computation.3 | async-start | bytes 2097152 | tf_op jit(solution)/shard_map/all_to_all | solution.py:187
  103.5 4.0 %collective-permute-start = (bf16[2048,160]{0,1:T(8,128)(2,1)S(1)}, bf16[2048,160]{0,1:T(8,128)(2,1)S(1)}, u32[]{:S(2)}, u32[]{:S(2)}) collective-permute-start(bf16[2048,160]{0,1:T(8,128)(2,1)S(1)} %bitcast.115), channel_id=1, source_target_pairs={{0,1},{1,0},{2,3},{3,2},{4,5},{5,4},{6,7},{7,6},{8,9},{9,8},{10,11... | collective-permute-start | bytes 1966088 | tf_op jit(solution)/shard_map/ppermute | solution.py:109
  107.5 25.2 %copy-start.5 = (bf16[2048,160]{0,1:T(8,128)(2,1)}, bf16[2048,160]{0,1:T(8,128)(2,1)S(1)}, u32[]{:S(2)}) copy-start(bf16[2048,160]{0,1:T(8,128)(2,1)S(1)} %collective-permute-done) | copy-start | bytes 1966084
  131.3 8.7 %copy-start.12 = (f32[2,2048]{1,0:T(2,128)S(1)}, f32[2,2048]{1,0:T(2,128)}, u32[]{:S(2)}) copy-start(f32[2,2048]{1,0:T(2,128)} %param.26) | copy-start | bytes 49156
  131.3 8.7 %copy-start.13 = (f32[2,2048]{1,0:T(2,128)S(1)}, f32[2,2048]{1,0:T(2,128)}, u32[]{:S(2)}) copy-start(f32[2,2048]{1,0:T(2,128)} %param.27) | copy-start | bytes 49156
  132.7 35.1 %all-to-all-start.4 = ((bf16[32,64,256]{2,1,0:T(8,128)(2,1)}), bf16[32,64,256]{2,1,0:T(8,128)(2,1)S(1)}, u32[]{:S(2)}, u32[]{:S(2)}) async-start(bf16[32,64,256]{2,1,0:T(8,128)(2,1)} %broadcast_in_dim.44), calls=%async_computation.4 | async-start | bytes 2097152 | tf_op jit(solution)/shard_map/all_to_all | solution.py:197
  171.3 1.9 copy-start.1
  173.7 1.1 slice-start
  173.7 1.2 copy-start.8
  175.6 12.1 %copy-start.4 = (bf16[8,512,128]{2,1,0:T(8,128)(2,1)S(1)}, bf16[8,512,128]{2,1,0:T(8,128)(2,1)}, u32[]{:S(2)}) copy-start(bf16[8,512,128]{2,1,0:T(8,128)(2,1)} %copy-done.3) | copy-start | bytes 3145732
  189.0 21.3 %all-to-all-start.6 = ((f32[32,8,512]{2,1,0:T(8,128)}), f32[32,8,512]{2,1,0:T(8,128)S(1)}, u32[]{:S(2)}, u32[]{:S(2)}) async-start(f32[32,8,512]{2,1,0:T(8,128)} %convolution_bitcast_fusion), calls=%async_computation.6 | async-start | bytes 1048576 | tf_op jit(solution)/shard_map/all_to_all | solution.py:215

commit v7 on v5

--- a/solution.py
+++ b/solution.py
@@ -99,16 +99,10 @@
     chip_in_bias = lax.dynamic_slice_in_dim(in_bias, chip * nc * hidden_width, nc * hidden_width)
     d_model = late.shape[0]
     quarter_width = d_model // nx
-    own_down = late[:, column_width + hidden_width :].reshape(nx, 1, quarter_width, hidden_width)
-    group_down = lax.all_to_all(
-        jnp.broadcast_to(own_down, (nx, nc, quarter_width, hidden_width)).reshape(
-            nx * nc, quarter_width, hidden_width
-        ),
-        ("bx", "bc"),
-        0,
-        0,
-        tiled=True,
-    ).reshape(nx, nc, quarter_width, hidden_width)
+    own_down = late[:, column_width + hidden_width :].reshape(nx, quarter_width, hidden_width)
+    from_row = lax.all_to_all(own_down, "bx", 0, 0, tiled=True)
+    from_sibling = lax.ppermute(from_row, "bc", swap("bc", nc))
+    group_down = core_pair(from_row[:, None], from_sibling[:, None], core, 1)
 
     query_total = tokens.shape[1]
     token_rows = tokens[0]
@@ -194,17 +188,19 @@
         + column_bias[:, None]
     ).astype(jnp.bfloat16)
     spread = jnp.broadcast_to(projected_part[None], (chips,) + projected_part.shape)
-    projected = lax.all_to_all(spread, PLANE, 0, 0, tiled=True).reshape(chips * chip_width, core_rows).T
+    projected = lax.all_to_all(spread, PLANE, 0, 0, tiled=True).reshape(chips * chip_width, core_rows)
     core_tokens = lax.dynamic_index_in_dim(
         token_rows.reshape(chips, nc, block_rows, -1), core, axis=1, keepdims=False
-    ).reshape(chips * block_rows, -1)
-    normed = layer_norm(
-        core_tokens.astype(jnp.float32) + projected.astype(jnp.float32),
-        norm_gains[0],
-        norm_biases[0],
+    ).reshape(core_rows, -1)
+    residual = core_tokens.T.astype(jnp.float32) + projected.astype(jnp.float32)
+    centered = residual - jnp.mean(residual, axis=0, keepdims=True)
+    variance = jnp.mean(centered * centered, axis=0, keepdims=True)
+    normed_t = (
+        centered * lax.rsqrt(variance + 1e-06) * norm_gains[0][:, None] + norm_biases[0][:, None]
     ).astype(jnp.bfloat16)
     inner = jax.nn.gelu(
-        jnp.dot(normed, chip_in, preferred_element_type=jnp.float32) + chip_in_bias, approximate=True
+        jnp.einsum("dt,df->tf", normed_t, chip_in, preferred_element_type=jnp.float32) + chip_in_bias,
+        approximate=True,
     ).astype(jnp.bfloat16)
     group_inner = lax.all_to_all(
         jnp.broadcast_to(inner[None], (nx,) + inner.shape), "bx", 0, 0, tiled=True
@@ -216,7 +212,7 @@
         mixed_parts.reshape(chips, block_rows, quarter_width), PLANE, 0, 0, tiled=True
     ).reshape(nx, ny, block_rows, quarter_width)
     mixed_rows = from_chips.sum(axis=1).transpose(1, 0, 2).reshape(block_rows, d_model)
-    own_normed = lax.dynamic_slice_in_dim(normed, chip * block_rows, block_rows, 0)
+    own_normed = lax.dynamic_slice_in_dim(normed_t, chip * block_rows, block_rows, 1).T
     layer_output = layer_norm(
         own_normed.astype(jnp.float32) + mixed_rows + out_biases[1], norm_gains[1], norm_biases[1]
     ).astype(jnp.bfloat16)

time: 207 us -> 206 us (level)
  waiting for transfers between devices: 99.8 us -> 96 us
  other arithmetic: 8.82 us -> 11.2 us
    all_to_all x1, waiting for transfers between devices: 12.4 us -> 8.03 us  [local(): from_row = lax.all_to_all(own_down, 'bx', 0, 0, tiled=True)]
    reduce_sum x0 -> x2, other arithmetic: none -> 2.14 us  [the longest x1 1.66 us: local(): centered = residual - jnp.mean(residual, axis=0, keepdims=True)]
  transfers between devices with their start and end apart: 11 -> 12, of which waited for: 11 -> 11; matrix products, arithmetic and copies ran while one was open for 11% -> 11% of each run, Pallas kernels for 0% -> 0%
where the time goes in v7:
time: 206 us; the launch traced here: 204 us
  waiting for transfers between devices  96 us (47%)
  starting transfers between devices  51.4 us (25%)
  local copies, waits for them, and re-layouts  25.1 us (12%)
  blocking collectives  11.5 us (6%)
  other arithmetic  11.2 us (5%)
  matrix products  7.2 us (3%)
    all_to_all x1, waiting for transfers between devices, local(): lax.all_to_all(spread, PLANE, 0, 0, tiled=True)  25.9 us
    all_to_all x1, waiting for transfers between devices, local(): lax.all_to_all(outgoing.reshape(group_size, column_width, core_rows), BLK...  21.8 us
    all_to_all x1, waiting for transfers between devices, local(): lax.all_to_all(mixed_parts.reshape(chips, block_rows, quarter_width), PLA...  15.7 us
    all_to_all x2, starting transfers between devices, gather_rows(): lax.all_to_all(spread, 'req', 0, 0, tiled=True)  14 us
    all_to_all x1, blocking collectives, local(): lax.all_to_all(jnp.broadcast_to(inner[None], (nx,) + inner.shape), 'bx',...  11.5 us
    ppermute x2, waiting for transfers between devices, from_partner(): lax.ppermute(value, 'by', [(i, i ^ 1 << bit_level - 1) for i in range(ny)])  11.1 us
    all_to_all x2, waiting for transfers between devices, gather_rows(): lax.all_to_all(spread, 'req', 0, 0, tiled=True)  9.17 us
    all_to_all x1, starting transfers between devices, local(): lax.all_to_all(outgoing.reshape(group_size, column_width, core_rows), BLK...  8.71 us
  transfers between devices with their start and end apart: 12, of which 11 were waited for; matrix products, arithmetic and copies ran while one was open for 11% of the time, Pallas kernels for 0%

profile of v7, /device:TPU:8, one launch (start us, length us, event | category | flops | bytes accessed | tf_op | source)
XLA Modules:
  0.0 204.2 jit_solution(3837933407981191702)
XLA Ops:
  0.6 1.7 broadcast_in_dim.35
  2.3 10.3 %all-to-all-start.1 = ((bf16[8,256,96]{1,2,0:T(8,128)(2,1)}), bf16[8,256,96]{1,2,0:T(8,128)(2,1)S(1)}, u32[]{:S(2)}, u32[]{:S(2)}) async-start(bf16[8,256,96]{1,2,0:T(8,128)(2,1)} %broadcast_in_dim.35), calls=%async_computation.1 | async-start | bytes 786432 | tf_op jit(solution)/shard_map/all_to_all | solution.py:53
  17.6 2.0 and_reduce_fusion
  19.6 7.7 %all-to-all-done.1 = bf16[8,256,96]{1,2,0:T(8,128)(2,1)S(1)} async-done(((bf16[8,256,96]{1,2,0:T(8,128)(2,1)}), bf16[8,256,96]{1,2,0:T(8,128)(2,1)S(1)}, u32[]{:S(2)}, u32[]{:S(2)}) %all-to-all-start.1) | async-done | bytes 393248 | tf_op jit(solution)/shard_map/all_to_all | solution.py:53
  29.2 3.7 %all-to-all-start = ((bf16[8,256,288]{1,2,0:T(8,128)(2,1)}), bf16[8,256,288]{1,2,0:T(8,128)(2,1)S(1)}, u32[]{:S(2)}, u32[]{:S(2)}) async-start(bf16[8,256,288]{1,2,0:T(8,128)(2,1)} %broadcast_in_dim.33), calls=%async_computation | async-start | bytes 2359296 | tf_op jit(solution)/shard_map/all_to_all | solution.py:53
  32.9 2.0 copy.70
  34.9 1.9 reshape_reshape.3
  36.8 1.8 fusion.12
  38.6 1.9 collective-permute-start.1
  41.8 2.4 %collective-permute-start.2 = (bf16[3,64,512]{2,1,0:T(8,128)(2,1)S(1)}, bf16[3,64,512]{2,1,0:T(8,128)(2,1)S(1)}, u32[]{:S(2)}, u32[]{:S(2)}) collective-permute-start(bf16[3,64,512]{2,1,0:T(8,128)(2,1)S(1)} %maximum_select_fusion.10), channel_id=1, source_target_pairs={{0,2},{2,0},{4,6},{6,4},{8,10},{10,8},{12,14},{14,12},{1,3},{3,1},... | collective-permute-start | bytes 589832 | tf_op jit(solution)/shard_map/ppermute | solution.py:118
  44.2 6.4 %collective-permute-done.2 = bf16[3,64,512]{2,1,0:T(8,128)(2,1)S(1)} collective-permute-done((bf16[3,64,512]{2,1,0:T(8,128)(2,1)S(1)}, bf16[3,64,512]{2,1,0:T(8,128)(2,1)S(1)}, u32[]{:S(2)}, u32[]{:S(2)}) %collective-permute-start.2) | collective-permute-done | bytes 196640 | tf_op jit(solution)/shard_map/ppermute | solution.py:118
  51.1 2.2 %fusion.72 = (f32[512]{0:T(512)S(1)}, f32[512,2176]{1,0:T(8,128)S(1)}) fusion(bf16[128,128]{1,0:T(8,128)(2,1)S(1)} %bitcast.146, bf16[2048,128]{1,0:T(8,128)(2,1)} %bitcast.135, bf16[3,128,512]{2,1,0:T(8,128)(2,1)S(1)} %maximum_select_fusion.3, pred[512,128]{1,0:T(32,128)(4,1)S(1)} %iota_compare_fusion, pred[2176]{0:T(1024)(128)(4,1)S(1)} %pad.16.clone), kind=kOutput, calls=%fused_computation.114 | convolution fusion | flops 290782720 | bytes 5215232 | tf_op jit(solution)/shard_map/qd,kd->qk/dot_general | solution.py:29
  55.2 2.4 %collective-permute-start.3 = (f32[66,512]{1,0:T(8,128)S(1)}, f32[66,512]{1,0:T(8,128)S(1)}, u32[]{:S(2)}, u32[]{:S(2)}) collective-permute-start(f32[66,512]{1,0:T(8,128)S(1)} %pad_maximum_fusion.1), channel_id=1, source_target_pairs={{0,2},{2,0},{4,6},{6,4},{8,10},{10,8},{12,14},{14,12},{1,3},{3,1},... | collective-permute-start | bytes 405512 | tf_op jit(solution)/shard_map/ppermute | solution.py:118
  57.6 4.7 %collective-permute-done.3 = f32[66,512]{1,0:T(8,128)S(1)} collective-permute-done((f32[66,512]{1,0:T(8,128)S(1)}, f32[66,512]{1,0:T(8,128)S(1)}, u32[]{:S(2)}, u32[]{:S(2)}) %collective-permute-start.3) | collective-permute-done | bytes 135200 | tf_op jit(solution)/shard_map/ppermute | solution.py:118
  62.3 1.5 all-to-all-done
  65.9 4.3 %all-to-all-start.2 = ((bf16[4,512,128]{2,1,0:T(8,128)(2,1)}), bf16[4,512,128]{2,1,0:T(8,128)(2,1)S(1)}, u32[]{:S(2)}, u32[]{:S(2)}) async-start(bf16[4,512,128]{2,1,0:T(8,128)(2,1)} %bitcast.26), calls=%async_computation.2 | async-start | bytes 1048576 | tf_op jit(solution)/shard_map/all_to_all | solution.py:103
  70.2 8.0 %all-to-all-done.2 = bf16[4,512,128]{2,1,0:T(8,128)(2,1)S(1)} async-done(((bf16[4,512,128]{2,1,0:T(8,128)(2,1)}), bf16[4,512,128]{2,1,0:T(8,128)(2,1)S(1)}, u32[]{:S(2)}, u32[]{:S(2)}) %all-to-all-start.2) | async-done | bytes 524320 | tf_op jit(solution)/shard_map/all_to_all | solution.py:103
  78.3 1.9 collective-permute-start.5
  80.2 2.4 %collective-permute-start.4 = (f32[34,512]{1,0:T(8,128)S(1)}, f32[34,512]{1,0:T(8,128)S(1)}, u32[]{:S(2)}, u32[]{:S(2)}) collective-permute-start(f32[34,512]{1,0:T(8,128)S(1)} %pad_maximum_fusion.2), channel_id=1, source_target_pairs={{0,1},{1,0},{2,3},{3,2},{4,5},{5,4},{6,7},{7,6},{8,9},{9,8},{10,11... | collective-permute-start | bytes 208904 | tf_op jit(solution)/shard_map/ppermute | solution.py:117
  85.1 8.7 %all-to-all-start.3 = ((bf16[64,32,256]{2,1,0:T(8,128)(2,1)}), bf16[64,32,256]{2,1,0:T(8,128)(2,1)S(1)}, u32[]{:S(2)}, u32[]{:S(2)}) async-start(bf16[64,32,256]{2,1,0:T(8,128)(2,1)} %bitcast.29), calls=%async_computation.3 | async-start | bytes 2097152 | tf_op jit(solution)/shard_map/all_to_all | solution.py:181
  94.7 2.0 %collective-permute-start = (bf16[2048,160]{0,1:T(8,128)(2,1)}, bf16[2048,160]{0,1:T(8,128)(2,1)}, u32[]{:S(2)}, u32[]{:S(2)}) collective-permute-start(bf16[2048,160]{0,1:T(8,128)(2,1)} %slice.131), channel_id=1, source_target_pairs={{0,1},{1,0},{2,3},{3,2},{4,5},{5,4},{6,7},{7,6},{8,9},{9,8},{10,11... | collective-permute-start | bytes 1966088 | tf_op jit(solution)/shard_map/ppermute | solution.py:96
  96.9 2.1 %collective-permute-done = bf16[2048,160]{0,1:T(8,128)(2,1)} collective-permute-done((bf16[2048,160]{0,1:T(8,128)(2,1)}, bf16[2048,160]{0,1:T(8,128)(2,1)}, u32[]{:S(2)}, u32[]{:S(2)}) %collective-permute-start) | collective-permute-done | bytes 655392 | tf_op jit(solution)/shard_map/ppermute | solution.py:96
  100.0 21.8 %all-to-all-done.3 = bf16[64,32,256]{2,1,0:T(8,128)(2,1)S(1)} async-done(((bf16[64,32,256]{2,1,0:T(8,128)(2,1)}), bf16[64,32,256]{2,1,0:T(8,128)(2,1)S(1)}, u32[]{:S(2)}, u32[]{:S(2)}) %all-to-all-start.3) | async-done | bytes 1048608 | tf_op jit(solution)/shard_map/all_to_all | solution.py:181
  123.1 6.5 %all-to-all-start.4 = ((bf16[32,64,256]{2,1,0:T(8,128)(2,1)}), bf16[32,64,256]{2,1,0:T(8,128)(2,1)S(1)}, u32[]{:S(2)}, u32[]{:S(2)}) async-start(bf16[32,64,256]{2,1,0:T(8,128)(2,1)} %broadcast_in_dim.44), calls=%async_computation.4 | async-start | bytes 2097152 | tf_op jit(solution)/shard_map/all_to_all | solution.py:191
  130.4 1.9 slice.148
  132.3 25.9 %all-to-all-done.4 = bf16[32,64,256]{2,1,0:T(8,128)(2,1)S(1)} async-done(((bf16[32,64,256]{2,1,0:T(8,128)(2,1)}), bf16[32,64,256]{2,1,0:T(8,128)(2,1)S(1)}, u32[]{:S(2)}, u32[]{:S(2)}) %all-to-all-start.4) | async-done | bytes 1048608 | tf_op jit(solution)/shard_map/all_to_all | solution.py:191
  158.3 1.6 bitcast_convert_fusion
  159.8 1.9 copy.78
  161.7 1.7 fusion.29
  166.5 11.5 %all_to_all.35 = bf16[4,256,256]{1,2,0:T(8,128)(2,1)S(1)} all-to-all(bf16[4,256,256]{1,2,0:T(8,128)(2,1)S(1)} %broadcast_in_dim.45), channel_id=1, replica_groups=mesh['req'=8,'bx'=4,'by'=8,'bc'=2] {'bx'}, dimensions={0} | all-to-all | bytes 1048576 | tf_op jit(solution)/shard_map/all_to_all | solution.py:205
  179.6 4.9 %all-to-all-start.6 = ((f32[32,8,512]{2,1,0:T(8,128)}), f32[32,8,512]{2,1,0:T(8,128)S(1)}, u32[]{:S(2)}, u32[]{:S(2)}) async-start(f32[32,8,512]{2,1,0:T(8,128)} %convolution_bitcast_fusion), calls=%async_computation.6 | async-start | bytes 1048576 | tf_op jit(solution)/shard_map/all_to_all | solution.py:211
  185.1 15.7 %all-to-all-done.6 = f32[32,8,512]{2,1,0:T(8,128)S(1)} async-done(((f32[32,8,512]{2,1,0:T(8,128)}), f32[32,8,512]{2,1,0:T(8,128)S(1)}, u32[]{:S(2)}, u32[]{:S(2)}) %all-to-all-start.6) | async-done | bytes 524320 | tf_op jit(solution)/shard_map/all_to_all | solution.py:211
  (100 shorter events, 27.1 us)
Async XLA Ops:
  0.6 12.6 %copy-start.2 = (bf16[1,1,2048,2,128]{4,3,2,1,0:T(2,128)(2,1)S(1)}, bf16[1,1,2048,2,128]{4,3,2,1,0:T(2,128)(2,1)}, u32[]{:S(2)}) copy-start(bf16[1,1,2048,2,128]{4,3,2,1,0:T(2,128)(2,1)} %param.15) | copy-start | bytes 3145732
  2.3 25.0 %all-to-all-start.1 = ((bf16[8,256,96]{1,2,0:T(8,128)(2,1)}), bf16[8,256,96]{1,2,0:T(8,128)(2,1)S(1)}, u32[]{:S(2)}, u32[]{:S(2)}) async-start(bf16[8,256,96]{1,2,0:T(8,128)(2,1)} %broadcast_in_dim.35), calls=%async_computation.1 | async-start | bytes 786432 | tf_op jit(solution)/shard_map/all_to_all | solution.py:53
  14.8 1.8 copy-start.12
  14.8 1.9 copy-start.10
  14.8 1.9 copy-start.11
  14.8 2.2 %copy-start.16 = (s32[1,2]{1,0:T(1,128)S(1)}, s32[1,2]{1,0:T(1,128)}, u32[]{:S(2)}) copy-start(s32[1,2]{1,0:T(1,128)} %param.18) | copy-start | bytes 28
  27.3 0.7 copy-start.3
  29.2 7.6 %copy-start = (bf16[1,512,2048]{2,1,0:T(8,128)(2,1)S(1)}, bf16[1,512,2048]{2,1,0:T(8,128)(2,1)}, u32[]{:S(2)}) copy-start(bf16[1,512,2048]{2,1,0:T(8,128)(2,1)} %param.14) | copy-start | bytes 6291460
  29.2 7.6 %copy-start.17 = (f32[3,32]{1,0:T(4,128)S(1)}, f32[3,32]{1,0:T(4,128)}, u32[]{:S(2)}) copy-start(f32[3,32]{1,0:T(4,128)} %param.20) | copy-start | bytes 1156
  29.2 34.7 %all-to-all-start = ((bf16[8,256,288]{1,2,0:T(8,128)(2,1)}), bf16[8,256,288]{1,2,0:T(8,128)(2,1)S(1)}, u32[]{:S(2)}, u32[]{:S(2)}) async-start(bf16[8,256,288]{1,2,0:T(8,128)(2,1)} %broadcast_in_dim.33), calls=%async_computation | async-start | bytes 2359296 | tf_op jit(solution)/shard_map/all_to_all | solution.py:53
  38.6 3.2 %collective-permute-start.1 = (bf16[3,32,512]{2,1,0:T(8,128)(2,1)S(1)}, bf16[3,32,512]{2,1,0:T(8,128)(2,1)S(1)}, u32[]{:S(2)}, u32[]{:S(2)}) collective-permute-start(bf16[3,32,512]{2,1,0:T(8,128)(2,1)S(1)} %fusion.12), channel_id=1, source_target_pairs={{0,1},{1,0},{2,3},{3,2},{4,5},{5,4},{6,7},{7,6},{8,9},{9,8},{10,11... | collective-permute-start | bytes 294920 | tf_op jit(solution)/shard_map/ppermute | solution.py:117
  41.8 8.9 %collective-permute-start.2 = (bf16[3,64,512]{2,1,0:T(8,128)(2,1)S(1)}, bf16[3,64,512]{2,1,0:T(8,128)(2,1)S(1)}, u32[]{:S(2)}, u32[]{:S(2)}) collective-permute-start(bf16[3,64,512]{2,1,0:T(8,128)(2,1)S(1)} %maximum_select_fusion.10), channel_id=1, source_target_pairs={{0,2},{2,0},{4,6},{6,4},{8,10},{10,8},{12,14},{14,12},{1,3},{3,1},... | collective-permute-start | bytes 589832 | tf_op jit(solution)/shard_map/ppermute | solution.py:118
  51.1 2.2 %copy-start.5 = (bf16[1,1,2048,1,128]{4,2,3,1,0:T(8,128)(2,1)S(1)}, bf16[1,1,2048,1,128]{4,2,3,1,0:T(8,128)(2,1)}, u32[]{:S(2)}) copy-start(bf16[1,1,2048,1,128]{4,2,3,1,0:T(8,128)(2,1)} %copy.91) | copy-start | bytes 1572868
  55.2 7.0 %collective-permute-start.3 = (f32[66,512]{1,0:T(8,128)S(1)}, f32[66,512]{1,0:T(8,128)S(1)}, u32[]{:S(2)}, u32[]{:S(2)}) collective-permute-start(f32[66,512]{1,0:T(8,128)S(1)} %pad_maximum_fusion.1), channel_id=1, source_target_pairs={{0,2},{2,0},{4,6},{6,4},{8,10},{10,8},{12,14},{14,12},{1,3},{3,1},... | collective-permute-start | bytes 405512 | tf_op jit(solution)/shard_map/ppermute | solution.py:118
  62.3 1.5 copy-start.8
  64.0 6.2 %copy-start.9 = (f32[66,512]{1,0:T(8,128)S(1)}, f32[66,512]{1,0:T(8,128)}, u32[]{:S(2)}) copy-start(f32[66,512]{1,0:T(8,128)} %copy-done.8) | copy-start | bytes 405508
  65.9 12.4 %all-to-all-start.2 = ((bf16[4,512,128]{2,1,0:T(8,128)(2,1)}), bf16[4,512,128]{2,1,0:T(8,128)(2,1)S(1)}, u32[]{:S(2)}, u32[]{:S(2)}) async-start(bf16[4,512,128]{2,1,0:T(8,128)(2,1)} %bitcast.26), calls=%async_computation.2 | async-start | bytes 1048576 | tf_op jit(solution)/shard_map/all_to_all | solution.py:103
  78.3 5.4 %collective-permute-start.5 = (bf16[4,512,128]{2,1,0:T(8,128)(2,1)S(1)}, bf16[4,512,128]{2,1,0:T(8,128)(2,1)S(1)}, u32[]{:S(2)}, u32[]{:S(2)}) collective-permute-start(bf16[4,512,128]{2,1,0:T(8,128)(2,1)S(1)} %all-to-all-done.2), channel_id=1, source_target_pairs={{0,1},{1,0},{2,3},{3,2},{4,5},{5,4},{6,7},{7,6},{8,9},{9,8},{10,11... | collective-permute-start | bytes 1572872 | tf_op jit(solution)/shard_map/ppermute | solution.py:104
  80.2 3.3 %collective-permute-start.4 = (f32[34,512]{1,0:T(8,128)S(1)}, f32[34,512]{1,0:T(8,128)S(1)}, u32[]{:S(2)}, u32[]{:S(2)}) collective-permute-start(f32[34,512]{1,0:T(8,128)S(1)} %pad_maximum_fusion.2), channel_id=1, source_target_pairs={{0,1},{1,0},{2,3},{3,2},{4,5},{5,4},{6,7},{7,6},{8,9},{9,8},{10,11... | collective-permute-start | bytes 208904 | tf_op jit(solution)/shard_map/ppermute | solution.py:117
  84.0 12.8 %copy-start.13 = (f32[2,2048]{1,0:T(2,128)S(1)}, f32[2,2048]{1,0:T(2,128)}, u32[]{:S(2)}) copy-start(f32[2,2048]{1,0:T(2,128)} %param.25) | copy-start | bytes 49156
  85.1 36.6 %all-to-all-start.3 = ((bf16[64,32,256]{2,1,0:T(8,128)(2,1)}), bf16[64,32,256]{2,1,0:T(8,128)(2,1)S(1)}, u32[]{:S(2)}, u32[]{:S(2)}) async-start(bf16[64,32,256]{2,1,0:T(8,128)(2,1)} %bitcast.29), calls=%async_computation.3 | async-start | bytes 2097152 | tf_op jit(solution)/shard_map/all_to_all | solution.py:181
  94.7 4.3 %collective-permute-start = (bf16[2048,160]{0,1:T(8,128)(2,1)}, bf16[2048,160]{0,1:T(8,128)(2,1)}, u32[]{:S(2)}, u32[]{:S(2)}) collective-permute-start(bf16[2048,160]{0,1:T(8,128)(2,1)} %slice.131), channel_id=1, source_target_pairs={{0,1},{1,0},{2,3},{3,2},{4,5},{5,4},{6,7},{7,6},{8,9},{9,8},{10,11... | collective-permute-start | bytes 1966088 | tf_op jit(solution)/shard_map/ppermute | solution.py:96
  121.7 8.7 %copy-start.14 = (f32[2,2048]{1,0:T(2,128)S(1)}, f32[2,2048]{1,0:T(2,128)}, u32[]{:S(2)}) copy-start(f32[2,2048]{1,0:T(2,128)} %param.26) | copy-start | bytes 49156
  121.7 8.7 %copy-start.15 = (f32[2,2048]{1,0:T(2,128)S(1)}, f32[2,2048]{1,0:T(2,128)}, u32[]{:S(2)}) copy-start(f32[2,2048]{1,0:T(2,128)} %param.27) | copy-start | bytes 49156
  123.1 35.1 %all-to-all-start.4 = ((bf16[32,64,256]{2,1,0:T(8,128)(2,1)}), bf16[32,64,256]{2,1,0:T(8,128)(2,1)S(1)}, u32[]{:S(2)}, u32[]{:S(2)}) async-start(bf16[32,64,256]{2,1,0:T(8,128)(2,1)} %broadcast_in_dim.44), calls=%async_computation.4 | async-start | bytes 2097152 | tf_op jit(solution)/shard_map/all_to_all | solution.py:191
  161.7 1.9 copy-start.1
  164.1 1.6 copy-start.6
  164.1 1.6 copy-start.7
  164.7 1.0 copy-start.4
  179.6 21.3 %all-to-all-start.6 = ((f32[32,8,512]{2,1,0:T(8,128)}), f32[32,8,512]{2,1,0:T(8,128)S(1)}, u32[]{:S(2)}, u32[]{:S(2)}) async-start(f32[32,8,512]{2,1,0:T(8,128)} %convolution_bitcast_fusion), calls=%async_computation.6 | async-start | bytes 1048576 | tf_op jit(solution)/shard_map/all_to_all | solution.py:211

commit v8 on v7

--- a/solution.py
+++ b/solution.py
@@ -100,7 +100,17 @@
     d_model = late.shape[0]
     quarter_width = d_model // nx
     own_down = late[:, column_width + hidden_width :].reshape(nx, quarter_width, hidden_width)
-    from_row = lax.all_to_all(own_down, "bx", 0, 0, tiled=True)
+    row = lax.axis_index("bx")
+    received = [lax.dynamic_index_in_dim(own_down, row, 0, keepdims=False)]
+    for k in range(1, nx):
+        received.append(
+            lax.ppermute(
+                lax.dynamic_index_in_dim(own_down, row ^ k, 0, keepdims=False),
+                "bx",
+                [(i, i ^ k) for i in range(nx)],
+            )
+        )
+    from_row = jnp.take(jnp.stack(received), row ^ jnp.arange(nx), axis=0)
     from_sibling = lax.ppermute(from_row, "bc", swap("bc", nc))
     group_down = core_pair(from_row[:, None], from_sibling[:, None], core, 1)
 
@@ -176,7 +186,6 @@
         .transpose(2, 0, 1, 3)
         .reshape(nc, column_width, core_rows)
     )
-    halves, group_down = lax.optimization_barrier((halves, group_down))
     outgoing = jnp.broadcast_to(halves[None], (chips, nc, column_width, core_rows))
     core_context = lax.all_to_all(
         outgoing.reshape(group_size, column_width, core_rows), BLK, 0, 0, tiled=True
@@ -188,6 +197,7 @@
         + column_bias[:, None]
     ).astype(jnp.bfloat16)
     spread = jnp.broadcast_to(projected_part[None], (chips,) + projected_part.shape)
+    spread, group_down = lax.optimization_barrier((spread, group_down))
     projected = lax.all_to_all(spread, PLANE, 0, 0, tiled=True).reshape(chips * chip_width, core_rows)
     core_tokens = lax.dynamic_index_in_dim(
         token_rows.reshape(chips, nc, block_rows, -1), core, axis=1, keepdims=False

time: 206 us -> 195 us (0.947)
  waiting for transfers between devices: 96 us -> 70 us
  starting transfers between devices: 51.4 us -> 63.3 us
  other arithmetic: 11.2 us -> 13.6 us
    all_to_all x1, waiting for transfers between devices: 21.8 us -> 0.18 us  [local(): lax.all_to_all(outgoing.reshape(group_size, column_width, core_rows), BLK...]
    ppermute x0 -> x3, starting transfers between devices: none -> 9.82 us  [local(): lax.ppermute(lax.dynamic_index_in_dim(own_down, row ^ k, 0, keepdims=Fals...]
    all_to_all x1 -> x0, waiting for transfers between devices: 8.03 us -> none  [local(): from_row = lax.all_to_all(own_down, 'bx', 0, 0, tiled=True)]
    ppermute x0 -> x3, waiting for transfers between devices: none -> 5.82 us  [local(): lax.ppermute(lax.dynamic_index_in_dim(own_down, row ^ k, 0, keepdims=Fals...]
    all_to_all x1, starting transfers between devices: 6.47 us -> 12.3 us  [local(): lax.all_to_all(spread, PLANE, 0, 0, tiled=True)]
    all_to_all x1 -> x0, starting transfers between devices: 4.29 us -> none  [local(): from_row = lax.all_to_all(own_down, 'bx', 0, 0, tiled=True)]
    ppermute x1, waiting for transfers between devices: 2.14 us -> 0.01 us  [local(): sibling = lax.ppermute(front, 'bc', swap('bc', nc))]
    unnamed x39 -> x37, local copies, waits for them, and re-layouts: 3.9 us -> 4.68 us
  transfers between devices with their start and end apart: 12 -> 14, of which waited for: 11 -> 12; matrix products, arithmetic and copies ran while one was open for 11% -> 14% of each run, Pallas kernels for 0% -> 0%
where the time goes in v8:
time: 195 us; the launch traced here: 194 us
  waiting for transfers between devices  70 us (36%)
  starting transfers between devices  63.3 us (32%)
  local copies, waits for them, and re-layouts  25.8 us (13%)
  other arithmetic  13.6 us (7%)
  blocking collectives  12.1 us (6%)
  matrix products  7.19 us (4%)
    all_to_all x1, waiting for transfers between devices, local(): lax.all_to_all(spread, PLANE, 0, 0, tiled=True)  26.1 us
    all_to_all x1, waiting for transfers between devices, local(): lax.all_to_all(mixed_parts.reshape(chips, block_rows, quarter_width), PLA...  15.8 us
    all_to_all x2, starting transfers between devices, gather_rows(): lax.all_to_all(spread, 'req', 0, 0, tiled=True)  14 us
    all_to_all x1, starting transfers between devices, local(): lax.all_to_all(spread, PLANE, 0, 0, tiled=True)  12.3 us
    all_to_all x1, blocking collectives, local(): lax.all_to_all(jnp.broadcast_to(inner[None], (nx,) + inner.shape), 'bx',...  12.1 us
    ppermute x2, waiting for transfers between devices, from_partner(): lax.ppermute(value, 'by', [(i, i ^ 1 << bit_level - 1) for i in range(ny)])  11.1 us
    all_to_all x1, starting transfers between devices, local(): lax.all_to_all(outgoing.reshape(group_size, column_width, core_rows), BLK...  10.6 us
    ppermute x3, starting transfers between devices, local(): lax.ppermute(lax.dynamic_index_in_dim(own_down, row ^ k, 0, keepdims=Fals...  9.82 us
  transfers between devices with their start and end apart: 14, of which 12 were waited for; matrix products, arithmetic and copies ran while one was open for 14% of the time, Pallas kernels for 0%

profile of v8, /device:TPU:8, one launch (start us, length us, event | category | flops | bytes accessed | tf_op | source)
XLA Modules:
  0.0 193.9 jit_solution(8095715430825997491)
XLA Ops:
  0.6 1.7 broadcast_in_dim.49
  2.3 10.3 %all-to-all-start.1 = ((bf16[8,256,96]{1,2,0:T(8,128)(2,1)}), bf16[8,256,96]{1,2,0:T(8,128)(2,1)S(1)}, u32[]{:S(2)}, u32[]{:S(2)}) async-start(bf16[8,256,96]{1,2,0:T(8,128)(2,1)} %broadcast_in_dim.49), calls=%async_computation.1 | async-start | bytes 786432 | tf_op jit(solution)/shard_map/all_to_all | solution.py:53
  17.6 2.0 %and_reduce_fusion = pred[2048]{0:T(1024)(128)(4,1)S(1)} fusion(s32[1,8192]{1,0:T(1,128)} %param.16, s32[]{:T(128)S(6)} %select_n.151, s32[]{:T(128)} %bitcast.11, s32[]{:T(128)} %bitcast.10, s32[]{:T(128)} %bitcast.132, s32[]{:T(128)S(6)} %mul.153), kind=kLoop, calls=%fused_computation.88 | loop fusion | flops 12288 | bytes 10260 | tf_op jit(solution)/shard_map/and | solution.py:152
  19.6 7.7 %all-to-all-done.1 = bf16[8,256,96]{1,2,0:T(8,128)(2,1)S(1)} async-done(((bf16[8,256,96]{1,2,0:T(8,128)(2,1)}), bf16[8,256,96]{1,2,0:T(8,128)(2,1)S(1)}, u32[]{:S(2)}, u32[]{:S(2)}) %all-to-all-start.1) | async-done | bytes 393248 | tf_op jit(solution)/shard_map/all_to_all | solution.py:53
  29.2 3.7 %all-to-all-start = ((bf16[8,256,288]{1,2,0:T(8,128)(2,1)}), bf16[8,256,288]{1,2,0:T(8,128)(2,1)S(1)}, u32[]{:S(2)}, u32[]{:S(2)}) async-start(bf16[8,256,288]{1,2,0:T(8,128)(2,1)} %broadcast_in_dim.47), calls=%async_computation | async-start | bytes 2359296 | tf_op jit(solution)/shard_map/all_to_all | solution.py:53
  32.9 2.0 %copy.69 = bf16[8,256,96]{1,0,2:T(8,128)(2,1)} copy(bf16[8,256,96]{1,2,0:T(8,128)(2,1)} %copy-done.3) | data formatting | bytes 786432 | tf_op jit(solution)/shard_map/all_to_all | solution.py:53
  34.9 1.9 reshape_reshape.3
  36.8 1.8 fusion.12
  38.6 1.9 collective-permute-start.1
  41.8 2.4 %collective-permute-start.2 = (bf16[3,64,512]{2,1,0:T(8,128)(2,1)S(1)}, bf16[3,64,512]{2,1,0:T(8,128)(2,1)S(1)}, u32[]{:S(2)}, u32[]{:S(2)}) collective-permute-start(bf16[3,64,512]{2,1,0:T(8,128)(2,1)S(1)} %maximum_select_fusion.10), channel_id=1, source_target_pairs={{0,2},{2,0},{4,6},{6,4},{8,10},{10,8},{12,14},{14,12},{1,3},{3,1},... | collective-permute-start | bytes 589832 | tf_op jit(solution)/shard_map/ppermute | solution.py:128
  44.2 6.4 %collective-permute-done.2 = bf16[3,64,512]{2,1,0:T(8,128)(2,1)S(1)} collective-permute-done((bf16[3,64,512]{2,1,0:T(8,128)(2,1)S(1)}, bf16[3,64,512]{2,1,0:T(8,128)(2,1)S(1)}, u32[]{:S(2)}, u32[]{:S(2)}) %collective-permute-start.2) | collective-permute-done | bytes 196640 | tf_op jit(solution)/shard_map/ppermute | solution.py:128
  51.1 2.2 %fusion.73 = (f32[512]{0:T(512)S(1)}, f32[512,2176]{1,0:T(8,128)S(1)}) fusion(bf16[128,128]{1,0:T(8,128)(2,1)S(1)} %bitcast.161, bf16[2048,128]{1,0:T(8,128)(2,1)} %bitcast.146, bf16[3,128,512]{2,1,0:T(8,128)(2,1)S(1)} %maximum_select_fusion.3, pred[512,128]{1,0:T(32,128)(4,1)S(1)} %iota_compare_fusion, pred[2176]{0:T(1024)(128)(4,1)S(1)} %pad.20.clone), kind=kOutput, calls=%fused_computation.127 | convolution fusion | flops 290782720 | bytes 5215232 | tf_op jit(solution)/shard_map/qd,kd->qk/dot_general | solution.py:29
  55.3 2.3 %collective-permute-start.3 = (f32[66,512]{1,0:T(8,128)S(1)}, f32[66,512]{1,0:T(8,128)S(1)}, u32[]{:S(2)}, u32[]{:S(2)}) collective-permute-start(f32[66,512]{1,0:T(8,128)S(1)} %pad_maximum_fusion.2), channel_id=1, source_target_pairs={{0,2},{2,0},{4,6},{6,4},{8,10},{10,8},{12,14},{14,12},{1,3},{3,1},... | collective-permute-start | bytes 405512 | tf_op jit(solution)/shard_map/ppermute | solution.py:128
  57.6 4.7 %collective-permute-done.3 = f32[66,512]{1,0:T(8,128)S(1)} collective-permute-done((f32[66,512]{1,0:T(8,128)S(1)}, f32[66,512]{1,0:T(8,128)S(1)}, u32[]{:S(2)}, u32[]{:S(2)}) %collective-permute-start.3) | collective-permute-done | bytes 135200 | tf_op jit(solution)/shard_map/ppermute | solution.py:128
  62.4 1.9 collective-permute-start.4
  67.0 10.6 %all-to-all-start.2 = ((bf16[64,32,256]{2,1,0:T(8,128)(2,1)}), bf16[64,32,256]{2,1,0:T(8,128)(2,1)S(1)}, u32[]{:S(2)}, u32[]{:S(2)}) async-start(bf16[64,32,256]{2,1,0:T(8,128)(2,1)} %bitcast.26), calls=%async_computation.2 | async-start | bytes 2097152 | tf_op jit(solution)/shard_map/all_to_all | solution.py:190
  78.9 4.8 %collective-permute-start.7 = (bf16[512,128]{1,0:T(8,128)(2,1)S(1)}, bf16[512,128]{1,0:T(8,128)(2,1)S(1)}, u32[]{:S(2)}, u32[]{:S(2)}) collective-permute-start(bf16[512,128]{1,0:T(8,128)(2,1)S(1)} %get-tuple-element.20), channel_id=1, source_target_pairs={{0,48},{16,32},{32,16},{48,0},{1,49},{17,33},{33,17},{49,1},{2,50}... | collective-permute-start | bytes 393224 | tf_op jit(solution)/shard_map/ppermute | solution.py:107
  83.7 2.6 %collective-permute-start.6 = (bf16[512,128]{1,0:T(8,128)(2,1)S(1)}, bf16[512,128]{1,0:T(8,128)(2,1)S(1)}, u32[]{:S(2)}, u32[]{:S(2)}) collective-permute-start(bf16[512,128]{1,0:T(8,128)(2,1)S(1)} %get-tuple-element.21), channel_id=1, source_target_pairs={{0,32},{16,48},{32,0},{48,16},{1,33},{17,49},{33,1},{49,17},{2,34}... | collective-permute-start | bytes 393224 | tf_op jit(solution)/shard_map/ppermute | solution.py:107
  86.3 2.5 %collective-permute-start.5 = (bf16[512,128]{1,0:T(8,128)(2,1)S(1)}, bf16[512,128]{1,0:T(8,128)(2,1)S(1)}, u32[]{:S(2)}, u32[]{:S(2)}) collective-permute-start(bf16[512,128]{1,0:T(8,128)(2,1)S(1)} %get-tuple-element.22), channel_id=1, source_target_pairs={{0,16},{16,0},{32,48},{48,32},{1,17},{17,1},{33,49},{49,33},{2,18}... | collective-permute-start | bytes 393224 | tf_op jit(solution)/shard_map/ppermute | solution.py:107
  89.7 1.9 collective-permute-start
  92.4 3.3 %collective-permute-done.6 = bf16[512,128]{1,0:T(8,128)(2,1)S(1)} collective-permute-done((bf16[512,128]{1,0:T(8,128)(2,1)S(1)}, bf16[512,128]{1,0:T(8,128)(2,1)S(1)}, u32[]{:S(2)}, u32[]{:S(2)}) %collective-permute-start.6) | collective-permute-done | bytes 131104 | tf_op jit(solution)/shard_map/ppermute | solution.py:107
  95.7 1.7 collective-permute-done.5
  99.1 1.9 collective-permute-start.8
  106.8 12.3 %all-to-all-start.3 = ((bf16[32,64,256]{2,1,0:T(8,128)(2,1)}), bf16[32,64,256]{2,1,0:T(8,128)(2,1)S(1)}, u32[]{:S(2)}, u32[]{:S(2)}) async-start(bf16[32,64,256]{2,1,0:T(8,128)(2,1)} %broadcast_in_dim.102), calls=%async_computation.3 | async-start | bytes 2097152 | tf_op jit(solution)/shard_map/all_to_all | solution.py:201
  119.9 1.9 slice.150
  121.8 26.1 %all-to-all-done.3 = bf16[32,64,256]{2,1,0:T(8,128)(2,1)S(1)} async-done(((bf16[32,64,256]{2,1,0:T(8,128)(2,1)}), bf16[32,64,256]{2,1,0:T(8,128)(2,1)S(1)}, u32[]{:S(2)}, u32[]{:S(2)}) %all-to-all-start.3) | async-done | bytes 1048608 | tf_op jit(solution)/shard_map/all_to_all | solution.py:201
  147.9 1.6 bitcast_convert_fusion
  149.4 1.9 copy.77
  151.4 1.7 fusion.29
  156.2 12.1 %all_to_all.30 = bf16[4,256,256]{1,2,0:T(8,128)(2,1)S(1)} all-to-all(bf16[4,256,256]{1,2,0:T(8,128)(2,1)S(1)} %broadcast_in_dim.108), channel_id=1, replica_groups=mesh['req'=8,'bx'=4,'by'=8,'bc'=2] {'bx'}, dimensions={0} | all-to-all | bytes 1048576 | tf_op jit(solution)/shard_map/all_to_all | solution.py:215
  169.8 4.3 %all-to-all-start.5 = ((f32[32,8,512]{2,1,0:T(8,128)}), f32[32,8,512]{2,1,0:T(8,128)S(1)}, u32[]{:S(2)}, u32[]{:S(2)}) async-start(f32[32,8,512]{2,1,0:T(8,128)} %convolution_bitcast_fusion), calls=%async_computation.5 | async-start | bytes 1048576 | tf_op jit(solution)/shard_map/all_to_all | solution.py:221
  174.8 15.8 %all-to-all-done.5 = f32[32,8,512]{2,1,0:T(8,128)S(1)} async-done(((f32[32,8,512]{2,1,0:T(8,128)}), f32[32,8,512]{2,1,0:T(8,128)S(1)}, u32[]{:S(2)}, u32[]{:S(2)}) %all-to-all-start.5) | async-done | bytes 524320 | tf_op jit(solution)/shard_map/all_to_all | solution.py:221
  (110 shorter events, 32.4 us)
Async XLA Ops:
  0.6 12.0 %copy-start.2 = (bf16[1,1,2048,2,128]{4,3,2,1,0:T(2,128)(2,1)S(1)}, bf16[1,1,2048,2,128]{4,3,2,1,0:T(2,128)(2,1)}, u32[]{:S(2)}) copy-start(bf16[1,1,2048,2,128]{4,3,2,1,0:T(2,128)(2,1)} %param.15) | copy-start | bytes 3145732
  2.3 25.0 %all-to-all-start.1 = ((bf16[8,256,96]{1,2,0:T(8,128)(2,1)}), bf16[8,256,96]{1,2,0:T(8,128)(2,1)S(1)}, u32[]{:S(2)}, u32[]{:S(2)}) async-start(bf16[8,256,96]{1,2,0:T(8,128)(2,1)} %broadcast_in_dim.49), calls=%async_computation.1 | async-start | bytes 786432 | tf_op jit(solution)/shard_map/all_to_all | solution.py:53
  14.1 2.4 %copy-start.11 = (bf16[256,32]{0,1:T(8,128)(2,1)S(1)}, bf16[256,32]{0,1:T(8,128)(2,1)}, u32[]{:S(2)}) copy-start(bf16[256,32]{0,1:T(8,128)(2,1)} %param.21) | copy-start | bytes 49156
  14.1 2.6 %copy-start.9 = (bf16[256,128]{1,0:T(8,128)(2,1)S(1)}, bf16[256,128]{1,0:T(8,128)(2,1)}, u32[]{:S(2)}) copy-start(bf16[256,128]{1,0:T(8,128)(2,1)} %param.24) | copy-start | bytes 196612
  14.2 2.6 %copy-start.10 = (bf16[256,128]{1,0:T(8,128)(2,1)S(1)}, bf16[256,128]{1,0:T(8,128)(2,1)}, u32[]{:S(2)}) copy-start(bf16[256,128]{1,0:T(8,128)(2,1)} %param.22) | copy-start | bytes 196612
  14.2 2.8 %copy-start.15 = (s32[1,2]{1,0:T(1,128)S(1)}, s32[1,2]{1,0:T(1,128)}, u32[]{:S(2)}) copy-start(s32[1,2]{1,0:T(1,128)} %param.18) | copy-start | bytes 28
  27.3 0.7 copy-start.3
  29.2 7.6 %copy-start = (bf16[1,512,2048]{2,1,0:T(8,128)(2,1)S(1)}, bf16[1,512,2048]{2,1,0:T(8,128)(2,1)}, u32[]{:S(2)}) copy-start(bf16[1,512,2048]{2,1,0:T(8,128)(2,1)} %param.14) | copy-start | bytes 6291460
  29.2 7.6 %copy-start.16 = (f32[3,32]{1,0:T(4,128)S(1)}, f32[3,32]{1,0:T(4,128)}, u32[]{:S(2)}) copy-start(f32[3,32]{1,0:T(4,128)} %param.20) | copy-start | bytes 1156
  29.2 36.7 %all-to-all-start = ((bf16[8,256,288]{1,2,0:T(8,128)(2,1)}), bf16[8,256,288]{1,2,0:T(8,128)(2,1)S(1)}, u32[]{:S(2)}, u32[]{:S(2)}) async-start(bf16[8,256,288]{1,2,0:T(8,128)(2,1)} %broadcast_in_dim.47), calls=%async_computation | async-start | bytes 2359296 | tf_op jit(solution)/shard_map/all_to_all | solution.py:53
  38.6 3.2 %collective-permute-start.1 = (bf16[3,32,512]{2,1,0:T(8,128)(2,1)S(1)}, bf16[3,32,512]{2,1,0:T(8,128)(2,1)S(1)}, u32[]{:S(2)}, u32[]{:S(2)}) collective-permute-start(bf16[3,32,512]{2,1,0:T(8,128)(2,1)S(1)} %fusion.12), channel_id=1, source_target_pairs={{0,1},{1,0},{2,3},{3,2},{4,5},{5,4},{6,7},{7,6},{8,9},{9,8},{10,11... | collective-permute-start | bytes 294920 | tf_op jit(solution)/shard_map/ppermute | solution.py:127
  41.8 8.9 %collective-permute-start.2 = (bf16[3,64,512]{2,1,0:T(8,128)(2,1)S(1)}, bf16[3,64,512]{2,1,0:T(8,128)(2,1)S(1)}, u32[]{:S(2)}, u32[]{:S(2)}) collective-permute-start(bf16[3,64,512]{2,1,0:T(8,128)(2,1)S(1)} %maximum_select_fusion.10), channel_id=1, source_target_pairs={{0,2},{2,0},{4,6},{6,4},{8,10},{10,8},{12,14},{14,12},{1,3},{3,1},... | collective-permute-start | bytes 589832 | tf_op jit(solution)/shard_map/ppermute | solution.py:128
  51.1 2.2 %copy-start.5 = (bf16[1,1,2048,1,128]{4,2,3,1,0:T(8,128)(2,1)S(1)}, bf16[1,1,2048,1,128]{4,2,3,1,0:T(8,128)(2,1)}, u32[]{:S(2)}) copy-start(bf16[1,1,2048,1,128]{4,2,3,1,0:T(8,128)(2,1)} %copy.89) | copy-start | bytes 1572868
  55.3 7.0 %collective-permute-start.3 = (f32[66,512]{1,0:T(8,128)S(1)}, f32[66,512]{1,0:T(8,128)S(1)}, u32[]{:S(2)}, u32[]{:S(2)}) collective-permute-start(f32[66,512]{1,0:T(8,128)S(1)} %pad_maximum_fusion.2), channel_id=1, source_target_pairs={{0,2},{2,0},{4,6},{6,4},{8,10},{10,8},{12,14},{14,12},{1,3},{3,1},... | collective-permute-start | bytes 405512 | tf_op jit(solution)/shard_map/ppermute | solution.py:128
  62.4 3.2 %collective-permute-start.4 = (f32[34,512]{1,0:T(8,128)S(1)}, f32[34,512]{1,0:T(8,128)S(1)}, u32[]{:S(2)}, u32[]{:S(2)}) collective-permute-start(f32[34,512]{1,0:T(8,128)S(1)} %pad_maximum_fusion.3), channel_id=1, source_target_pairs={{0,1},{1,0},{2,3},{3,2},{4,5},{5,4},{6,7},{7,6},{8,9},{9,8},{10,11... | collective-permute-start | bytes 208904 | tf_op jit(solution)/shard_map/ppermute | solution.py:127
  67.0 38.5 %all-to-all-start.2 = ((bf16[64,32,256]{2,1,0:T(8,128)(2,1)}), bf16[64,32,256]{2,1,0:T(8,128)(2,1)S(1)}, u32[]{:S(2)}, u32[]{:S(2)}) async-start(bf16[64,32,256]{2,1,0:T(8,128)(2,1)} %bitcast.26), calls=%async_computation.2 | async-start | bytes 2097152 | tf_op jit(solution)/shard_map/all_to_all | solution.py:190
  78.9 13.5 %collective-permute-start.7 = (bf16[512,128]{1,0:T(8,128)(2,1)S(1)}, bf16[512,128]{1,0:T(8,128)(2,1)S(1)}, u32[]{:S(2)}, u32[]{:S(2)}) collective-permute-start(bf16[512,128]{1,0:T(8,128)(2,1)S(1)} %get-tuple-element.20), channel_id=1, source_target_pairs={{0,48},{16,32},{32,16},{48,0},{1,49},{17,33},{33,17},{49,1},{2,50}... | collective-permute-start | bytes 393224 | tf_op jit(solution)/shard_map/ppermute | solution.py:107
  83.7 12.0 %collective-permute-start.6 = (bf16[512,128]{1,0:T(8,128)(2,1)S(1)}, bf16[512,128]{1,0:T(8,128)(2,1)S(1)}, u32[]{:S(2)}, u32[]{:S(2)}) collective-permute-start(bf16[512,128]{1,0:T(8,128)(2,1)S(1)} %get-tuple-element.21), channel_id=1, source_target_pairs={{0,32},{16,48},{32,0},{48,16},{1,33},{17,49},{33,1},{49,17},{2,34}... | collective-permute-start | bytes 393224 | tf_op jit(solution)/shard_map/ppermute | solution.py:107
  86.3 11.1 %collective-permute-start.5 = (bf16[512,128]{1,0:T(8,128)(2,1)S(1)}, bf16[512,128]{1,0:T(8,128)(2,1)S(1)}, u32[]{:S(2)}, u32[]{:S(2)}) collective-permute-start(bf16[512,128]{1,0:T(8,128)(2,1)S(1)} %get-tuple-element.22), channel_id=1, source_target_pairs={{0,16},{16,0},{32,48},{48,32},{1,17},{17,1},{33,49},{49,33},{2,18}... | collective-permute-start | bytes 393224 | tf_op jit(solution)/shard_map/ppermute | solution.py:107
  88.8 12.2 %copy-start.12 = (f32[2,2048]{1,0:T(2,128)S(1)}, f32[2,2048]{1,0:T(2,128)}, u32[]{:S(2)}) copy-start(f32[2,2048]{1,0:T(2,128)} %param.25) | copy-start | bytes 49156
  89.7 11.5 %collective-permute-start = (bf16[2048,160]{0,1:T(8,128)(2,1)}, bf16[2048,160]{0,1:T(8,128)(2,1)}, u32[]{:S(2)}, u32[]{:S(2)}) collective-permute-start(bf16[2048,160]{0,1:T(8,128)(2,1)} %slice.133), channel_id=1, source_target_pairs={{0,1},{1,0},{2,3},{3,2},{4,5},{5,4},{6,7},{7,6},{8,9},{9,8},{10,11... | collective-permute-start | bytes 1966088 | tf_op jit(solution)/shard_map/ppermute | solution.py:96
  99.1 4.0 %collective-permute-start.8 = (bf16[4,512,128]{2,1,0:T(8,128)(2,1)}, bf16[4,512,128]{2,1,0:T(8,128)(2,1)S(1)}, u32[]{:S(2)}, u32[]{:S(2)}) collective-permute-start(bf16[4,512,128]{2,1,0:T(8,128)(2,1)} %broadcast_select_fusion), channel_id=1, source_target_pairs={{0,1},{1,0},{2,3},{3,2},{4,5},{5,4},{6,7},{7,6},{8,9},{9,8},{10,11... | collective-permute-start | bytes 1572872 | tf_op jit(solution)/shard_map/ppermute | solution.py:114
  103.1 0.8 copy-start.6
  105.4 14.5 %copy-start.13 = (f32[2,2048]{1,0:T(2,128)S(1)}, f32[2,2048]{1,0:T(2,128)}, u32[]{:S(2)}) copy-start(f32[2,2048]{1,0:T(2,128)} %param.27) | copy-start | bytes 49156
  105.4 14.5 %copy-start.14 = (f32[2,2048]{1,0:T(2,128)S(1)}, f32[2,2048]{1,0:T(2,128)}, u32[]{:S(2)}) copy-start(f32[2,2048]{1,0:T(2,128)} %param.26) | copy-start | bytes 49156
  106.8 41.0 %all-to-all-start.3 = ((bf16[32,64,256]{2,1,0:T(8,128)(2,1)}), bf16[32,64,256]{2,1,0:T(8,128)(2,1)S(1)}, u32[]{:S(2)}, u32[]{:S(2)}) async-start(bf16[32,64,256]{2,1,0:T(8,128)(2,1)} %broadcast_in_dim.102), calls=%async_computation.3 | async-start | bytes 2097152 | tf_op jit(solution)/shard_map/all_to_all | solution.py:201
  151.4 1.9 copy-start.1
  153.8 1.6 copy-start.7
  153.8 1.6 copy-start.8
  154.4 1.0 copy-start.4
  169.8 20.8 %all-to-all-start.5 = ((f32[32,8,512]{2,1,0:T(8,128)}), f32[32,8,512]{2,1,0:T(8,128)S(1)}, u32[]{:S(2)}, u32[]{:S(2)}) async-start(f32[32,8,512]{2,1,0:T(8,128)} %convolution_bitcast_fusion), calls=%async_computation.5 | async-start | bytes 1048576 | tf_op jit(solution)/shard_map/all_to_all | solution.py:221

commit v9 on v8

--- a/solution.py
+++ b/solution.py
@@ -90,7 +90,10 @@
     qkv_flat = qkv_weight.reshape(rows, 3 * column_width)
     hidden_width = in_weight.shape[1]
     packed = jnp.concatenate([out_weight, in_weight, down_weight], axis=1)
-    full_qkv = gather_rows(qkv_flat).reshape(-1, 3, column_width)
+    reqs = lax.axis_size("req")
+    qkv_blocks = lax.all_to_all(
+        jnp.broadcast_to(qkv_flat[None], (reqs,) + qkv_flat.shape), "req", 0, 0, tiled=True
+    ).reshape(reqs, rows, 3, column_width)
     late = gather_rows(packed)
     front = late[:, : column_width + hidden_width]
     sibling = lax.ppermute(front, "bc", swap("bc", nc))
@@ -117,7 +120,12 @@
     query_total = tokens.shape[1]
     token_rows = tokens[0]
     qkv_columns = (
-        jnp.einsum("td,dce->cet", token_rows, full_qkv, preferred_element_type=jnp.float32)
+        jnp.einsum(
+            "tsd,sdce->cet",
+            token_rows.reshape(query_total, reqs, rows),
+            qkv_blocks,
+            preferred_element_type=jnp.float32,
+        )
         + qkv_bias[:, :, None]
     ).astype(jnp.bfloat16)
     appended = qkv_columns[1:].transpose(2, 0, 1)[None]

time: 195 us -> 192 us (0.985)
    all_to_all x2 -> x1, starting transfers between devices: 14 us -> 3.56 us  [gather_rows(): lax.all_to_all(spread, 'req', 0, 0, tiled=True)]
    all_to_all x0 -> x1, starting transfers between devices: none -> 10.3 us  [local(): lax.all_to_all(jnp.broadcast_to(qkv_flat[None], (reqs,) + qkv_flat.shape)...]
    all_to_all x2 -> x1, waiting for transfers between devices: 7.66 us -> 1.88 us  [gather_rows(): lax.all_to_all(spread, 'req', 0, 0, tiled=True)]
    all_to_all x0 -> x1, waiting for transfers between devices: none -> 4.07 us  [local(): lax.all_to_all(jnp.broadcast_to(qkv_flat[None], (reqs,) + qkv_flat.shape)...]
    unnamed x37 -> x36, local copies, waits for them, and re-layouts: 4.68 us -> 7.63 us
    all_to_all x1 -> x0, local copies, waits for them, and re-layouts: 1.99 us -> none  [gather_rows(): lax.all_to_all(spread, 'req', 0, 0, tiled=True)]
  transfers between devices with their start and end apart: 14 -> 14, of which waited for: 12 -> 13; matrix products, arithmetic and copies ran while one was open for 14% -> 14% of each run, Pallas kernels for 0% -> 0%
where the time goes in v9:
time: 192 us; the launch traced here: 191 us
  waiting for transfers between devices  68.3 us (36%)
  starting transfers between devices  63.6 us (33%)
  local copies, waits for them, and re-layouts  24.7 us (13%)
  other arithmetic  13.5 us (7%)
  blocking collectives  11.7 us (6%)
  matrix products  7.2 us (4%)
  between operations  1.92 us (1%)
    all_to_all x1, waiting for transfers between devices, local(): lax.all_to_all(spread, PLANE, 0, 0, tiled=True)  26.1 us
    all_to_all x1, waiting for transfers between devices, local(): lax.all_to_all(mixed_parts.reshape(chips, block_rows, quarter_width), PLA...  15.8 us
    all_to_all x1, starting transfers between devices, local(): lax.all_to_all(spread, PLANE, 0, 0, tiled=True)  12.3 us
    all_to_all x1, blocking collectives, local(): lax.all_to_all(jnp.broadcast_to(inner[None], (nx,) + inner.shape), 'bx',...  11.7 us
    ppermute x2, waiting for transfers between devices, from_partner(): lax.ppermute(value, 'by', [(i, i ^ 1 << bit_level - 1) for i in range(ny)])  11.1 us
    all_to_all x1, starting transfers between devices, local(): lax.all_to_all(outgoing.reshape(group_size, column_width, core_rows), BLK...  10.6 us
    all_to_all x1, starting transfers between devices, local(): lax.all_to_all(jnp.broadcast_to(qkv_flat[None], (reqs,) + qkv_flat.shape)...  10.3 us
    ppermute x3, starting transfers between devices, local(): lax.ppermute(lax.dynamic_index_in_dim(own_down, row ^ k, 0, keepdims=Fals...  9.82 us
  transfers between devices with their start and end apart: 14, of which 13 were waited for; matrix products, arithmetic and copies ran while one was open for 14% of the time, Pallas kernels for 0%

profile of v9, /device:TPU:8, one launch (start us, length us, event | category | flops | bytes accessed | tf_op | source)
XLA Modules:
  0.0 191.1 jit_solution(8605023837623784640)
XLA Ops:
  0.6 1.6 broadcast_in_dim.49
  2.2 10.3 %all-to-all-start.1 = ((bf16[8,256,96]{1,2,0:T(8,128)(2,1)}), bf16[8,256,96]{1,2,0:T(8,128)(2,1)}, u32[]{:S(2)}, u32[]{:S(2)}) async-start(bf16[8,256,96]{1,2,0:T(8,128)(2,1)} %broadcast_in_dim.49), calls=%async_computation.1 | async-start | bytes 786432 | tf_op jit(solution)/shard_map/all_to_all | solution.py:94
  12.5 3.7 %copy.94 = bf16[64,8,8,256]{3,2,1,0:T(8,128)(2,1)} copy(bf16[64,8,8,256]{3,1,2,0:T(8,128)(2,1)} %bitcast.135) | data formatting | bytes 4194304
  21.2 2.0 %and_reduce_fusion = pred[2048]{0:T(1024)(128)(4,1)S(1)} fusion(s32[1,8192]{1,0:T(1,128)} %param.16, s32[]{:T(128)S(6)} %select_n.151, s32[]{:T(128)} %bitcast.12, s32[]{:T(128)} %bitcast.11, s32[]{:T(128)} %bitcast.134, s32[]{:T(128)S(6)} %mul.153), kind=kLoop, calls=%fused_computation.89 | loop fusion | flops 12288 | bytes 10260 | tf_op jit(solution)/shard_map/and | solution.py:160
  23.2 4.1 %all-to-all-done.1 = bf16[8,256,96]{1,2,0:T(8,128)(2,1)} async-done(((bf16[8,256,96]{1,2,0:T(8,128)(2,1)}), bf16[8,256,96]{1,2,0:T(8,128)(2,1)}, u32[]{:S(2)}, u32[]{:S(2)}) %all-to-all-start.1) | async-done | bytes 393248 | tf_op jit(solution)/shard_map/all_to_all | solution.py:94
  28.4 3.6 %all-to-all-start = ((bf16[8,256,288]{1,2,0:T(8,128)(2,1)}), bf16[8,256,288]{1,2,0:T(8,128)(2,1)S(1)}, u32[]{:S(2)}, u32[]{:S(2)}) async-start(bf16[8,256,288]{1,2,0:T(8,128)(2,1)} %broadcast_in_dim.47), calls=%async_computation | async-start | bytes 2359296 | tf_op jit(solution)/shard_map/all_to_all | solution.py:53
  32.0 1.8 fusion.15
  33.8 1.9 %collective-permute-start.1 = (bf16[3,32,512]{2,1,0:T(8,128)(2,1)S(1)}, bf16[3,32,512]{2,1,0:T(8,128)(2,1)S(1)}, u32[]{:S(2)}, u32[]{:S(2)}) collective-permute-start(bf16[3,32,512]{2,1,0:T(8,128)(2,1)S(1)} %fusion.15), channel_id=1, source_target_pairs={{0,1},{1,0},{2,3},{3,2},{4,5},{5,4},{6,7},{7,6},{8,9},{9,8},{10,11... | collective-permute-start | bytes 294920 | tf_op jit(solution)/shard_map/ppermute | solution.py:135
  37.0 2.4 %collective-permute-start.2 = (bf16[3,64,512]{2,1,0:T(8,128)(2,1)S(1)}, bf16[3,64,512]{2,1,0:T(8,128)(2,1)S(1)}, u32[]{:S(2)}, u32[]{:S(2)}) collective-permute-start(bf16[3,64,512]{2,1,0:T(8,128)(2,1)S(1)} %maximum_select_fusion.10), channel_id=1, source_target_pairs={{0,2},{2,0},{4,6},{6,4},{8,10},{10,8},{12,14},{14,12},{1,3},{3,1},... | collective-permute-start | bytes 589832 | tf_op jit(solution)/shard_map/ppermute | solution.py:136
  39.5 6.4 %collective-permute-done.2 = bf16[3,64,512]{2,1,0:T(8,128)(2,1)S(1)} collective-permute-done((bf16[3,64,512]{2,1,0:T(8,128)(2,1)S(1)}, bf16[3,64,512]{2,1,0:T(8,128)(2,1)S(1)}, u32[]{:S(2)}, u32[]{:S(2)}) %collective-permute-start.2) | collective-permute-done | bytes 196640 | tf_op jit(solution)/shard_map/ppermute | solution.py:136
  46.3 2.2 %fusion.76 = (f32[512]{0:T(512)S(1)}, f32[512,2176]{1,0:T(8,128)S(1)}) fusion(bf16[128,128]{1,0:T(8,128)(2,1)S(1)} %bitcast.165, bf16[2048,128]{1,0:T(8,128)(2,1)} %bitcast.150, bf16[3,128,512]{2,1,0:T(8,128)(2,1)S(1)} %maximum_select_fusion.3, pred[512,128]{1,0:T(32,128)(4,1)S(1)} %iota_compare_fusion, pred[2176]{0:T(1024)(128)(4,1)S(1)} %pad.20.clone), kind=kOutput, calls=%fused_computation.128 | convolution fusion | flops 290782720 | bytes 5215232 | tf_op jit(solution)/shard_map/qd,kd->qk/dot_general | solution.py:29
  50.5 2.4 %collective-permute-start.3 = (f32[66,512]{1,0:T(8,128)S(1)}, f32[66,512]{1,0:T(8,128)S(1)}, u32[]{:S(2)}, u32[]{:S(2)}) collective-permute-start(f32[66,512]{1,0:T(8,128)S(1)} %pad_maximum_fusion.2), channel_id=1, source_target_pairs={{0,2},{2,0},{4,6},{6,4},{8,10},{10,8},{12,14},{14,12},{1,3},{3,1},... | collective-permute-start | bytes 405512 | tf_op jit(solution)/shard_map/ppermute | solution.py:136
  52.9 4.6 %collective-permute-done.3 = f32[66,512]{1,0:T(8,128)S(1)} collective-permute-done((f32[66,512]{1,0:T(8,128)S(1)}, f32[66,512]{1,0:T(8,128)S(1)}, u32[]{:S(2)}, u32[]{:S(2)}) %collective-permute-start.3) | collective-permute-done | bytes 135200 | tf_op jit(solution)/shard_map/ppermute | solution.py:136
  57.6 1.9 %collective-permute-start.4 = (f32[34,512]{1,0:T(8,128)S(1)}, f32[34,512]{1,0:T(8,128)S(1)}, u32[]{:S(2)}, u32[]{:S(2)}) collective-permute-start(f32[34,512]{1,0:T(8,128)S(1)} %pad_maximum_fusion.3), channel_id=1, source_target_pairs={{0,1},{1,0},{2,3},{3,2},{4,5},{5,4},{6,7},{7,6},{8,9},{9,8},{10,11... | collective-permute-start | bytes 208904 | tf_op jit(solution)/shard_map/ppermute | solution.py:135
  61.1 1.9 all-to-all-done
  64.1 10.6 %all-to-all-start.2 = ((bf16[64,32,256]{2,1,0:T(8,128)(2,1)}), bf16[64,32,256]{2,1,0:T(8,128)(2,1)S(1)}, u32[]{:S(2)}, u32[]{:S(2)}) async-start(bf16[64,32,256]{2,1,0:T(8,128)(2,1)} %bitcast.27), calls=%async_computation.2 | async-start | bytes 2097152 | tf_op jit(solution)/shard_map/all_to_all | solution.py:198
  76.0 4.8 %collective-permute-start.7 = (bf16[512,128]{1,0:T(8,128)(2,1)S(1)}, bf16[512,128]{1,0:T(8,128)(2,1)S(1)}, u32[]{:S(2)}, u32[]{:S(2)}) collective-permute-start(bf16[512,128]{1,0:T(8,128)(2,1)S(1)} %get-tuple-element.20), channel_id=1, source_target_pairs={{0,48},{16,32},{32,16},{48,0},{1,49},{17,33},{33,17},{49,1},{2,50}... | collective-permute-start | bytes 393224 | tf_op jit(solution)/shard_map/ppermute | solution.py:110
  80.8 2.6 %collective-permute-start.6 = (bf16[512,128]{1,0:T(8,128)(2,1)S(1)}, bf16[512,128]{1,0:T(8,128)(2,1)S(1)}, u32[]{:S(2)}, u32[]{:S(2)}) collective-permute-start(bf16[512,128]{1,0:T(8,128)(2,1)S(1)} %get-tuple-element.21), channel_id=1, source_target_pairs={{0,32},{16,48},{32,0},{48,16},{1,33},{17,49},{33,1},{49,17},{2,34}... | collective-permute-start | bytes 393224 | tf_op jit(solution)/shard_map/ppermute | solution.py:110
  83.4 2.5 %collective-permute-start.5 = (bf16[512,128]{1,0:T(8,128)(2,1)S(1)}, bf16[512,128]{1,0:T(8,128)(2,1)S(1)}, u32[]{:S(2)}, u32[]{:S(2)}) collective-permute-start(bf16[512,128]{1,0:T(8,128)(2,1)S(1)} %get-tuple-element.22), channel_id=1, source_target_pairs={{0,16},{16,0},{32,48},{48,32},{1,17},{17,1},{33,49},{49,33},{2,18}... | collective-permute-start | bytes 393224 | tf_op jit(solution)/shard_map/ppermute | solution.py:110
  86.8 1.9 collective-permute-start
  89.5 3.3 %collective-permute-done.6 = bf16[512,128]{1,0:T(8,128)(2,1)S(1)} collective-permute-done((bf16[512,128]{1,0:T(8,128)(2,1)S(1)}, bf16[512,128]{1,0:T(8,128)(2,1)S(1)}, u32[]{:S(2)}, u32[]{:S(2)}) %collective-permute-start.6) | collective-permute-done | bytes 131104 | tf_op jit(solution)/shard_map/ppermute | solution.py:110
  92.8 1.7 collective-permute-done.5
  96.2 1.9 collective-permute-start.8
  103.9 12.3 %all-to-all-start.3 = ((bf16[32,64,256]{2,1,0:T(8,128)(2,1)}), bf16[32,64,256]{2,1,0:T(8,128)(2,1)S(1)}, u32[]{:S(2)}, u32[]{:S(2)}) async-start(bf16[32,64,256]{2,1,0:T(8,128)(2,1)} %broadcast_in_dim.102), calls=%async_computation.3 | async-start | bytes 2097152 | tf_op jit(solution)/shard_map/all_to_all | solution.py:209
  117.1 1.9 slice.150
  119.0 26.1 %all-to-all-done.3 = bf16[32,64,256]{2,1,0:T(8,128)(2,1)S(1)} async-done(((bf16[32,64,256]{2,1,0:T(8,128)(2,1)}), bf16[32,64,256]{2,1,0:T(8,128)(2,1)S(1)}, u32[]{:S(2)}, u32[]{:S(2)}) %all-to-all-start.3) | async-done | bytes 1048608 | tf_op jit(solution)/shard_map/all_to_all | solution.py:209
  145.0 1.6 bitcast_convert_fusion
  146.6 1.9 %copy.83 = f32[2048,256]{0,1:T(8,128)S(1)} copy(f32[2048,256]{1,0:T(8,128)} %bitcast_convert_fusion) | data formatting | bytes 4194304 | tf_op jit(solution)/shard_map/convert_element_type | solution.py:213
  148.5 1.7 fusion.32
  153.3 11.7 %all_to_all.30 = bf16[4,256,256]{1,2,0:T(8,128)(2,1)S(1)} all-to-all(bf16[4,256,256]{1,2,0:T(8,128)(2,1)S(1)} %broadcast_in_dim.108), channel_id=1, replica_groups=mesh['req'=8,'bx'=4,'by'=8,'bc'=2] {'bx'}, dimensions={0} | all-to-all | bytes 1048576 | tf_op jit(solution)/shard_map/all_to_all | solution.py:223
  166.6 4.6 %all-to-all-start.5 = ((f32[32,8,512]{2,1,0:T(8,128)}), f32[32,8,512]{2,1,0:T(8,128)S(1)}, u32[]{:S(2)}, u32[]{:S(2)}) async-start(f32[32,8,512]{2,1,0:T(8,128)} %convolution_bitcast_fusion), calls=%async_computation.5 | async-start | bytes 1048576 | tf_op jit(solution)/shard_map/all_to_all | solution.py:229
  171.9 15.8 %all-to-all-done.5 = f32[32,8,512]{2,1,0:T(8,128)S(1)} async-done(((f32[32,8,512]{2,1,0:T(8,128)}), f32[32,8,512]{2,1,0:T(8,128)S(1)}, u32[]{:S(2)}, u32[]{:S(2)}) %all-to-all-start.5) | async-done | bytes 524320 | tf_op jit(solution)/shard_map/all_to_all | solution.py:229
  (107 shorter events, 31.7 us)
Async XLA Ops:
  2.2 25.1 %all-to-all-start.1 = ((bf16[8,256,96]{1,2,0:T(8,128)(2,1)}), bf16[8,256,96]{1,2,0:T(8,128)(2,1)}, u32[]{:S(2)}, u32[]{:S(2)}) async-start(bf16[8,256,96]{1,2,0:T(8,128)(2,1)} %broadcast_in_dim.49), calls=%async_computation.1 | async-start | bytes 786432 | tf_op jit(solution)/shard_map/all_to_all | solution.py:94
  12.5 3.7 %copy-start.1 = (bf16[1,1,2048,2,128]{4,3,2,1,0:T(2,128)(2,1)S(1)}, bf16[1,1,2048,2,128]{4,3,2,1,0:T(2,128)(2,1)}, u32[]{:S(2)}) copy-start(bf16[1,1,2048,2,128]{4,3,2,1,0:T(2,128)(2,1)} %param.15) | copy-start | bytes 3145732
  17.7 2.4 %copy-start.10 = (bf16[256,32]{0,1:T(8,128)(2,1)S(1)}, bf16[256,32]{0,1:T(8,128)(2,1)}, u32[]{:S(2)}) copy-start(bf16[256,32]{0,1:T(8,128)(2,1)} %param.21) | copy-start | bytes 49156
  17.7 2.6 %copy-start.8 = (bf16[256,128]{1,0:T(8,128)(2,1)S(1)}, bf16[256,128]{1,0:T(8,128)(2,1)}, u32[]{:S(2)}) copy-start(bf16[256,128]{1,0:T(8,128)(2,1)} %param.24) | copy-start | bytes 196612
  17.7 2.6 %copy-start.9 = (bf16[256,128]{1,0:T(8,128)(2,1)S(1)}, bf16[256,128]{1,0:T(8,128)(2,1)}, u32[]{:S(2)}) copy-start(bf16[256,128]{1,0:T(8,128)(2,1)} %param.22) | copy-start | bytes 196612
  17.7 2.9 %copy-start.14 = (s32[1,2]{1,0:T(1,128)S(1)}, s32[1,2]{1,0:T(1,128)}, u32[]{:S(2)}) copy-start(s32[1,2]{1,0:T(1,128)} %param.18) | copy-start | bytes 28
  20.4 11.6 %copy-start.2 = (bf16[64,8,8,256]{3,2,1,0:T(8,128)(2,1)S(1)}, bf16[64,8,8,256]{3,2,1,0:T(8,128)(2,1)}, u32[]{:S(2)}) copy-start(bf16[64,8,8,256]{3,2,1,0:T(8,128)(2,1)} %copy.94) | copy-start | bytes 6291460
  20.4 11.6 %copy-start.15 = (f32[3,32]{1,0:T(4,128)S(1)}, f32[3,32]{1,0:T(4,128)}, u32[]{:S(2)}) copy-start(f32[3,32]{1,0:T(4,128)} %param.20) | copy-start | bytes 1156
  28.4 34.5 %all-to-all-start = ((bf16[8,256,288]{1,2,0:T(8,128)(2,1)}), bf16[8,256,288]{1,2,0:T(8,128)(2,1)S(1)}, u32[]{:S(2)}, u32[]{:S(2)}) async-start(bf16[8,256,288]{1,2,0:T(8,128)(2,1)} %broadcast_in_dim.47), calls=%async_computation | async-start | bytes 2359296 | tf_op jit(solution)/shard_map/all_to_all | solution.py:53
  33.8 3.2 %collective-permute-start.1 = (bf16[3,32,512]{2,1,0:T(8,128)(2,1)S(1)}, bf16[3,32,512]{2,1,0:T(8,128)(2,1)S(1)}, u32[]{:S(2)}, u32[]{:S(2)}) collective-permute-start(bf16[3,32,512]{2,1,0:T(8,128)(2,1)S(1)} %fusion.15), channel_id=1, source_target_pairs={{0,1},{1,0},{2,3},{3,2},{4,5},{5,4},{6,7},{7,6},{8,9},{9,8},{10,11... | collective-permute-start | bytes 294920 | tf_op jit(solution)/shard_map/ppermute | solution.py:135
  37.0 8.9 %collective-permute-start.2 = (bf16[3,64,512]{2,1,0:T(8,128)(2,1)S(1)}, bf16[3,64,512]{2,1,0:T(8,128)(2,1)S(1)}, u32[]{:S(2)}, u32[]{:S(2)}) collective-permute-start(bf16[3,64,512]{2,1,0:T(8,128)(2,1)S(1)} %maximum_select_fusion.10), channel_id=1, source_target_pairs={{0,2},{2,0},{4,6},{6,4},{8,10},{10,8},{12,14},{14,12},{1,3},{3,1},... | collective-permute-start | bytes 589832 | tf_op jit(solution)/shard_map/ppermute | solution.py:136
  46.3 2.2 %copy-start.4 = (bf16[1,1,2048,1,128]{4,2,3,1,0:T(8,128)(2,1)S(1)}, bf16[1,1,2048,1,128]{4,2,3,1,0:T(8,128)(2,1)}, u32[]{:S(2)}) copy-start(bf16[1,1,2048,1,128]{4,2,3,1,0:T(8,128)(2,1)} %copy.107) | copy-start | bytes 1572868
  50.5 7.0 %collective-permute-start.3 = (f32[66,512]{1,0:T(8,128)S(1)}, f32[66,512]{1,0:T(8,128)S(1)}, u32[]{:S(2)}, u32[]{:S(2)}) collective-permute-start(f32[66,512]{1,0:T(8,128)S(1)} %pad_maximum_fusion.2), channel_id=1, source_target_pairs={{0,2},{2,0},{4,6},{6,4},{8,10},{10,8},{12,14},{14,12},{1,3},{3,1},... | collective-permute-start | bytes 405512 | tf_op jit(solution)/shard_map/ppermute | solution.py:136
  57.6 3.2 %collective-permute-start.4 = (f32[34,512]{1,0:T(8,128)S(1)}, f32[34,512]{1,0:T(8,128)S(1)}, u32[]{:S(2)}, u32[]{:S(2)}) collective-permute-start(f32[34,512]{1,0:T(8,128)S(1)} %pad_maximum_fusion.3), channel_id=1, source_target_pairs={{0,1},{1,0},{2,3},{3,2},{4,5},{5,4},{6,7},{7,6},{8,9},{9,8},{10,11... | collective-permute-start | bytes 208904 | tf_op jit(solution)/shard_map/ppermute | solution.py:135
  64.1 38.5 %all-to-all-start.2 = ((bf16[64,32,256]{2,1,0:T(8,128)(2,1)}), bf16[64,32,256]{2,1,0:T(8,128)(2,1)S(1)}, u32[]{:S(2)}, u32[]{:S(2)}) async-start(bf16[64,32,256]{2,1,0:T(8,128)(2,1)} %bitcast.27), calls=%async_computation.2 | async-start | bytes 2097152 | tf_op jit(solution)/shard_map/all_to_all | solution.py:198
  76.0 13.5 %collective-permute-start.7 = (bf16[512,128]{1,0:T(8,128)(2,1)S(1)}, bf16[512,128]{1,0:T(8,128)(2,1)S(1)}, u32[]{:S(2)}, u32[]{:S(2)}) collective-permute-start(bf16[512,128]{1,0:T(8,128)(2,1)S(1)} %get-tuple-element.20), channel_id=1, source_target_pairs={{0,48},{16,32},{32,16},{48,0},{1,49},{17,33},{33,17},{49,1},{2,50}... | collective-permute-start | bytes 393224 | tf_op jit(solution)/shard_map/ppermute | solution.py:110
  80.8 12.0 %collective-permute-start.6 = (bf16[512,128]{1,0:T(8,128)(2,1)S(1)}, bf16[512,128]{1,0:T(8,128)(2,1)S(1)}, u32[]{:S(2)}, u32[]{:S(2)}) collective-permute-start(bf16[512,128]{1,0:T(8,128)(2,1)S(1)} %get-tuple-element.21), channel_id=1, source_target_pairs={{0,32},{16,48},{32,0},{48,16},{1,33},{17,49},{33,1},{49,17},{2,34}... | collective-permute-start | bytes 393224 | tf_op jit(solution)/shard_map/ppermute | solution.py:110
  83.4 11.1 %collective-permute-start.5 = (bf16[512,128]{1,0:T(8,128)(2,1)S(1)}, bf16[512,128]{1,0:T(8,128)(2,1)S(1)}, u32[]{:S(2)}, u32[]{:S(2)}) collective-permute-start(bf16[512,128]{1,0:T(8,128)(2,1)S(1)} %get-tuple-element.22), channel_id=1, source_target_pairs={{0,16},{16,0},{32,48},{48,32},{1,17},{17,1},{33,49},{49,33},{2,18}... | collective-permute-start | bytes 393224 | tf_op jit(solution)/shard_map/ppermute | solution.py:110
  85.9 12.2 %copy-start.11 = (f32[2,2048]{1,0:T(2,128)S(1)}, f32[2,2048]{1,0:T(2,128)}, u32[]{:S(2)}) copy-start(f32[2,2048]{1,0:T(2,128)} %param.25) | copy-start | bytes 49156
  86.8 11.5 %collective-permute-start = (bf16[2048,160]{0,1:T(8,128)(2,1)}, bf16[2048,160]{0,1:T(8,128)(2,1)}, u32[]{:S(2)}, u32[]{:S(2)}) collective-permute-start(bf16[2048,160]{0,1:T(8,128)(2,1)} %slice.133), channel_id=1, source_target_pairs={{0,1},{1,0},{2,3},{3,2},{4,5},{5,4},{6,7},{7,6},{8,9},{9,8},{10,11... | collective-permute-start | bytes 1966088 | tf_op jit(solution)/shard_map/ppermute | solution.py:99
  96.2 4.0 %collective-permute-start.8 = (bf16[4,512,128]{2,1,0:T(8,128)(2,1)}, bf16[4,512,128]{2,1,0:T(8,128)(2,1)S(1)}, u32[]{:S(2)}, u32[]{:S(2)}) collective-permute-start(bf16[4,512,128]{2,1,0:T(8,128)(2,1)} %broadcast_select_fusion), channel_id=1, source_target_pairs={{0,1},{1,0},{2,3},{3,2},{4,5},{5,4},{6,7},{7,6},{8,9},{9,8},{10,11... | collective-permute-start | bytes 1572872 | tf_op jit(solution)/shard_map/ppermute | solution.py:117
  100.2 0.8 copy-start.5
  102.5 14.5 %copy-start.12 = (f32[2,2048]{1,0:T(2,128)S(1)}, f32[2,2048]{1,0:T(2,128)}, u32[]{:S(2)}) copy-start(f32[2,2048]{1,0:T(2,128)} %param.27) | copy-start | bytes 49156
  102.5 14.5 %copy-start.13 = (f32[2,2048]{1,0:T(2,128)S(1)}, f32[2,2048]{1,0:T(2,128)}, u32[]{:S(2)}) copy-start(f32[2,2048]{1,0:T(2,128)} %param.26) | copy-start | bytes 49156
  103.9 41.1 %all-to-all-start.3 = ((bf16[32,64,256]{2,1,0:T(8,128)(2,1)}), bf16[32,64,256]{2,1,0:T(8,128)(2,1)S(1)}, u32[]{:S(2)}, u32[]{:S(2)}) async-start(bf16[32,64,256]{2,1,0:T(8,128)(2,1)} %broadcast_in_dim.102), calls=%async_computation.3 | async-start | bytes 2097152 | tf_op jit(solution)/shard_map/all_to_all | solution.py:209
  148.5 1.9 copy-start
  150.9 1.6 copy-start.6
  150.9 1.6 copy-start.7
  151.5 1.0 copy-start.3
  166.6 21.1 %all-to-all-start.5 = ((f32[32,8,512]{2,1,0:T(8,128)}), f32[32,8,512]{2,1,0:T(8,128)S(1)}, u32[]{:S(2)}, u32[]{:S(2)}) async-start(f32[32,8,512]{2,1,0:T(8,128)} %convolution_bitcast_fusion), calls=%async_computation.5 | async-start | bytes 1048576 | tf_op jit(solution)/shard_map/all_to_all | solution.py:229

commit v10 on v9

--- a/solution.py
+++ b/solution.py
@@ -194,10 +194,14 @@
         .transpose(2, 0, 1, 3)
         .reshape(nc, column_width, core_rows)
     )
-    outgoing = jnp.broadcast_to(halves[None], (chips, nc, column_width, core_rows))
-    core_context = lax.all_to_all(
-        outgoing.reshape(group_size, column_width, core_rows), BLK, 0, 0, tiled=True
-    ).reshape(group_size * column_width, core_rows)
+    mine = lax.dynamic_index_in_dim(halves, core, 0, keepdims=False)
+    theirs = lax.dynamic_index_in_dim(halves, 1 - core, 0, keepdims=False)
+    got = lax.ppermute(theirs, "bc", swap("bc", nc))
+    chip_columns = core_pair(mine, got, core, 0)
+    outgoing = jnp.broadcast_to(chip_columns[None], (chips,) + chip_columns.shape)
+    core_context = lax.all_to_all(outgoing, PLANE, 0, 0, tiled=True).reshape(
+        group_size * column_width, core_rows
+    )
     chip_width = nc * column_width
     column_bias = lax.dynamic_slice_in_dim(out_biases[0], chip * chip_width, chip_width)
     projected_part = (

time: 192 us -> 191 us (level)
  starting transfers between devices: 63.6 us -> 61.4 us
    all_to_all x1, starting transfers between devices: 12.3 us -> 8.48 us  [local(): lax.all_to_all(spread, PLANE, 0, 0, tiled=True)]
    ppermute x0 -> x1, starting transfers between devices: none -> 2.07 us  [local(): got = lax.ppermute(theirs, 'bc', swap('bc', nc))]
  transfers between devices with their start and end apart: 14 -> 15, of which waited for: 13 -> 13; matrix products, arithmetic and copies ran while one was open for 14% -> 14% of each run, Pallas kernels for 0% -> 0%
where the time goes in v10:
time: 191 us; the launch traced here: 189 us
  waiting for transfers between devices  68.3 us (36%)
  starting transfers between devices  61.4 us (32%)
  local copies, waits for them, and re-layouts  25 us (13%)
  other arithmetic  13.6 us (7%)
  blocking collectives  11.8 us (6%)
  matrix products  7.14 us (4%)
  between operations  1.93 us (1%)
    all_to_all x1, waiting for transfers between devices, local(): lax.all_to_all(spread, PLANE, 0, 0, tiled=True)  26.1 us
    all_to_all x1, waiting for transfers between devices, local(): lax.all_to_all(mixed_parts.reshape(chips, block_rows, quarter_width), PLA...  15.8 us
    all_to_all x1, blocking collectives, local(): lax.all_to_all(jnp.broadcast_to(inner[None], (nx,) + inner.shape), 'bx',...  11.8 us
    ppermute x2, waiting for transfers between devices, from_partner(): lax.ppermute(value, 'by', [(i, i ^ 1 << bit_level - 1) for i in range(ny)])  11.1 us
    all_to_all x1, starting transfers between devices, local(): lax.all_to_all(jnp.broadcast_to(qkv_flat[None], (reqs,) + qkv_flat.shape)...  10.3 us
    all_to_all x1, starting transfers between devices, local(): lax.all_to_all(outgoing, PLANE, 0, 0, tiled=True)  10.2 us
    ppermute x3, starting transfers between devices, local(): lax.ppermute(lax.dynamic_index_in_dim(own_down, row ^ k, 0, keepdims=Fals...  9.82 us
    all_to_all x1, starting transfers between devices, local(): lax.all_to_all(spread, PLANE, 0, 0, tiled=True)  8.48 us
  transfers between devices with their start and end apart: 15, of which 13 were waited for; matrix products, arithmetic and copies ran while one was open for 14% of the time, Pallas kernels for 0%

profile of v10, /device:TPU:8, one launch (start us, length us, event | category | flops | bytes accessed | tf_op | source)
XLA Modules:
  0.0 189.1 jit_solution(12605712006851320952)
XLA Ops:
  0.6 1.6 broadcast_in_dim.47
  2.2 10.3 %all-to-all-start.1 = ((bf16[8,256,96]{1,2,0:T(8,128)(2,1)}), bf16[8,256,96]{1,2,0:T(8,128)(2,1)}, u32[]{:S(2)}, u32[]{:S(2)}) async-start(bf16[8,256,96]{1,2,0:T(8,128)(2,1)} %broadcast_in_dim.47), calls=%async_computation.1 | async-start | bytes 786432 | tf_op jit(solution)/shard_map/all_to_all | solution.py:94
  12.5 3.7 %copy.99 = bf16[64,8,8,256]{3,2,1,0:T(8,128)(2,1)} copy(bf16[64,8,8,256]{3,1,2,0:T(8,128)(2,1)} %bitcast.136) | data formatting | bytes 4194304
  21.2 2.0 %and_reduce_fusion = pred[2048]{0:T(1024)(128)(4,1)S(1)} fusion(s32[1,8192]{1,0:T(1,128)} %param.16, s32[]{:T(128)S(6)} %select_n.169, s32[]{:T(128)} %bitcast.12, s32[]{:T(128)} %bitcast.11, s32[]{:T(128)} %bitcast.135, s32[]{:T(128)S(6)} %mul.153), kind=kLoop, calls=%fused_computation.90 | loop fusion | flops 12288 | bytes 10260 | tf_op jit(solution)/shard_map/and | solution.py:160
  23.2 4.1 %all-to-all-done.1 = bf16[8,256,96]{1,2,0:T(8,128)(2,1)} async-done(((bf16[8,256,96]{1,2,0:T(8,128)(2,1)}), bf16[8,256,96]{1,2,0:T(8,128)(2,1)}, u32[]{:S(2)}, u32[]{:S(2)}) %all-to-all-start.1) | async-done | bytes 393248 | tf_op jit(solution)/shard_map/all_to_all | solution.py:94
  28.4 3.6 %all-to-all-start = ((bf16[8,256,288]{1,2,0:T(8,128)(2,1)}), bf16[8,256,288]{1,2,0:T(8,128)(2,1)S(1)}, u32[]{:S(2)}, u32[]{:S(2)}) async-start(bf16[8,256,288]{1,2,0:T(8,128)(2,1)} %broadcast_in_dim.45), calls=%async_computation | async-start | bytes 2359296 | tf_op jit(solution)/shard_map/all_to_all | solution.py:53
  32.0 1.8 fusion.15
  33.8 1.9 %collective-permute-start.1 = (bf16[3,32,512]{2,1,0:T(8,128)(2,1)S(1)}, bf16[3,32,512]{2,1,0:T(8,128)(2,1)S(1)}, u32[]{:S(2)}, u32[]{:S(2)}) collective-permute-start(bf16[3,32,512]{2,1,0:T(8,128)(2,1)S(1)} %fusion.15), channel_id=1, source_target_pairs={{0,1},{1,0},{2,3},{3,2},{4,5},{5,4},{6,7},{7,6},{8,9},{9,8},{10,11... | collective-permute-start | bytes 294920 | tf_op jit(solution)/shard_map/ppermute | solution.py:135
  37.0 2.4 %collective-permute-start.2 = (bf16[3,64,512]{2,1,0:T(8,128)(2,1)S(1)}, bf16[3,64,512]{2,1,0:T(8,128)(2,1)S(1)}, u32[]{:S(2)}, u32[]{:S(2)}) collective-permute-start(bf16[3,64,512]{2,1,0:T(8,128)(2,1)S(1)} %maximum_select_fusion.10), channel_id=1, source_target_pairs={{0,2},{2,0},{4,6},{6,4},{8,10},{10,8},{12,14},{14,12},{1,3},{3,1},... | collective-permute-start | bytes 589832 | tf_op jit(solution)/shard_map/ppermute | solution.py:136
  39.5 6.4 %collective-permute-done.2 = bf16[3,64,512]{2,1,0:T(8,128)(2,1)S(1)} collective-permute-done((bf16[3,64,512]{2,1,0:T(8,128)(2,1)S(1)}, bf16[3,64,512]{2,1,0:T(8,128)(2,1)S(1)}, u32[]{:S(2)}, u32[]{:S(2)}) %collective-permute-start.2) | collective-permute-done | bytes 196640 | tf_op jit(solution)/shard_map/ppermute | solution.py:136
  46.3 2.1 %fusion.76 = (f32[512]{0:T(512)S(1)}, f32[512,2176]{1,0:T(8,128)S(1)}) fusion(bf16[128,128]{1,0:T(8,128)(2,1)S(1)} %bitcast.167, bf16[2048,128]{1,0:T(8,128)(2,1)} %bitcast.151, bf16[3,128,512]{2,1,0:T(8,128)(2,1)S(1)} %maximum_select_fusion.3, pred[512,128]{1,0:T(32,128)(4,1)S(1)} %iota_compare_fusion, pred[2176]{0:T(1024)(128)(4,1)S(1)} %pad.24.clone), kind=kOutput, calls=%fused_computation.131 | convolution fusion | flops 290782720 | bytes 5215232 | tf_op jit(solution)/shard_map/qd,kd->qk/dot_general | solution.py:29
  50.5 2.4 %collective-permute-start.3 = (f32[66,512]{1,0:T(8,128)S(1)}, f32[66,512]{1,0:T(8,128)S(1)}, u32[]{:S(2)}, u32[]{:S(2)}) collective-permute-start(f32[66,512]{1,0:T(8,128)S(1)} %pad_maximum_fusion.2), channel_id=1, source_target_pairs={{0,2},{2,0},{4,6},{6,4},{8,10},{10,8},{12,14},{14,12},{1,3},{3,1},... | collective-permute-start | bytes 405512 | tf_op jit(solution)/shard_map/ppermute | solution.py:136
  52.9 4.7 %collective-permute-done.3 = f32[66,512]{1,0:T(8,128)S(1)} collective-permute-done((f32[66,512]{1,0:T(8,128)S(1)}, f32[66,512]{1,0:T(8,128)S(1)}, u32[]{:S(2)}, u32[]{:S(2)}) %collective-permute-start.3) | collective-permute-done | bytes 135200 | tf_op jit(solution)/shard_map/ppermute | solution.py:136
  57.7 1.9 %collective-permute-start.4 = (f32[34,512]{1,0:T(8,128)S(1)}, f32[34,512]{1,0:T(8,128)S(1)}, u32[]{:S(2)}, u32[]{:S(2)}) collective-permute-start(f32[34,512]{1,0:T(8,128)S(1)} %pad_maximum_fusion.3), channel_id=1, source_target_pairs={{0,1},{1,0},{2,3},{3,2},{4,5},{5,4},{6,7},{7,6},{8,9},{9,8},{10,11... | collective-permute-start | bytes 208904 | tf_op jit(solution)/shard_map/ppermute | solution.py:135
  61.1 2.1 %collective-permute-start.5 = (bf16[32,256]{1,0:T(8,128)(2,1)S(1)}, bf16[32,256]{1,0:T(8,128)(2,1)S(1)}, u32[]{:S(2)}, u32[]{:S(2)}) collective-permute-start(bf16[32,256]{1,0:T(8,128)(2,1)S(1)} %bitcast.174), channel_id=1, source_target_pairs={{0,1},{1,0},{2,3},{3,2},{4,5},{5,4},{6,7},{7,6},{8,9},{9,8},{10,11... | collective-permute-start | bytes 49160 | tf_op jit(solution)/shard_map/ppermute | solution.py:199
  65.4 10.2 %all-to-all-start.2 = ((bf16[32,64,256]{2,1,0:T(8,128)(2,1)}), bf16[32,64,256]{2,1,0:T(8,128)(2,1)S(1)}, u32[]{:S(2)}, u32[]{:S(2)}) async-start(bf16[32,64,256]{2,1,0:T(8,128)(2,1)} %broadcast_in_dim.53), calls=%async_computation.2 | async-start | bytes 2097152 | tf_op jit(solution)/shard_map/all_to_all | solution.py:202
  76.9 4.6 %collective-permute-start.8 = (bf16[512,128]{1,0:T(8,128)(2,1)S(1)}, bf16[512,128]{1,0:T(8,128)(2,1)S(1)}, u32[]{:S(2)}, u32[]{:S(2)}) collective-permute-start(bf16[512,128]{1,0:T(8,128)(2,1)S(1)} %get-tuple-element.20), channel_id=1, source_target_pairs={{0,48},{16,32},{32,16},{48,0},{1,49},{17,33},{33,17},{49,1},{2,50}... | collective-permute-start | bytes 393224 | tf_op jit(solution)/shard_map/ppermute | solution.py:110
  81.6 2.7 %collective-permute-start.7 = (bf16[512,128]{1,0:T(8,128)(2,1)S(1)}, bf16[512,128]{1,0:T(8,128)(2,1)S(1)}, u32[]{:S(2)}, u32[]{:S(2)}) collective-permute-start(bf16[512,128]{1,0:T(8,128)(2,1)S(1)} %get-tuple-element.21), channel_id=1, source_target_pairs={{0,32},{16,48},{32,0},{48,16},{1,33},{17,49},{33,1},{49,17},{2,34}... | collective-permute-start | bytes 393224 | tf_op jit(solution)/shard_map/ppermute | solution.py:110
  84.3 2.5 %collective-permute-start.6 = (bf16[512,128]{1,0:T(8,128)(2,1)S(1)}, bf16[512,128]{1,0:T(8,128)(2,1)S(1)}, u32[]{:S(2)}, u32[]{:S(2)}) collective-permute-start(bf16[512,128]{1,0:T(8,128)(2,1)S(1)} %get-tuple-element.22), channel_id=1, source_target_pairs={{0,16},{16,0},{32,48},{48,32},{1,17},{17,1},{33,49},{49,33},{2,18}... | collective-permute-start | bytes 393224 | tf_op jit(solution)/shard_map/ppermute | solution.py:110
  87.7 1.9 %collective-permute-start = (bf16[2048,160]{0,1:T(8,128)(2,1)}, bf16[2048,160]{0,1:T(8,128)(2,1)}, u32[]{:S(2)}, u32[]{:S(2)}) collective-permute-start(bf16[2048,160]{0,1:T(8,128)(2,1)} %slice.133), channel_id=1, source_target_pairs={{0,1},{1,0},{2,3},{3,2},{4,5},{5,4},{6,7},{7,6},{8,9},{9,8},{10,11... | collective-permute-start | bytes 1966088 | tf_op jit(solution)/shard_map/ppermute | solution.py:99
  89.6 3.6 %collective-permute-done.8 = bf16[512,128]{1,0:T(8,128)(2,1)S(1)} collective-permute-done((bf16[512,128]{1,0:T(8,128)(2,1)S(1)}, bf16[512,128]{1,0:T(8,128)(2,1)S(1)}, u32[]{:S(2)}, u32[]{:S(2)}) %collective-permute-start.8) | collective-permute-done | bytes 131104 | tf_op jit(solution)/shard_map/ppermute | solution.py:110
  93.2 1.6 collective-permute-done.7
  97.4 1.9 %collective-permute-start.9 = (bf16[4,512,128]{2,1,0:T(8,128)(2,1)}, bf16[4,512,128]{2,1,0:T(8,128)(2,1)S(1)}, u32[]{:S(2)}, u32[]{:S(2)}) collective-permute-start(bf16[4,512,128]{2,1,0:T(8,128)(2,1)} %broadcast_select_fusion), channel_id=1, source_target_pairs={{0,1},{1,0},{2,3},{3,2},{4,5},{5,4},{6,7},{7,6},{8,9},{9,8},{10,11... | collective-permute-start | bytes 1572872 | tf_op jit(solution)/shard_map/ppermute | solution.py:117
  105.7 8.5 %all-to-all-start.3 = ((bf16[32,64,256]{2,1,0:T(8,128)(2,1)}), bf16[32,64,256]{2,1,0:T(8,128)(2,1)S(1)}, u32[]{:S(2)}, u32[]{:S(2)}) async-start(bf16[32,64,256]{2,1,0:T(8,128)(2,1)} %broadcast_in_dim.100), calls=%async_computation.3 | async-start | bytes 2097152 | tf_op jit(solution)/shard_map/all_to_all | solution.py:213
  115.1 1.9 slice.150
  116.9 26.1 %all-to-all-done.3 = bf16[32,64,256]{2,1,0:T(8,128)(2,1)S(1)} async-done(((bf16[32,64,256]{2,1,0:T(8,128)(2,1)}), bf16[32,64,256]{2,1,0:T(8,128)(2,1)S(1)}, u32[]{:S(2)}, u32[]{:S(2)}) %all-to-all-start.3) | async-done | bytes 1048608 | tf_op jit(solution)/shard_map/all_to_all | solution.py:213
  143.0 1.6 bitcast_convert_fusion
  144.6 1.9 %copy.88 = f32[2048,256]{0,1:T(8,128)S(1)} copy(f32[2048,256]{1,0:T(8,128)} %bitcast_convert_fusion) | data formatting | bytes 4194304 | tf_op jit(solution)/shard_map/convert_element_type | solution.py:217
  146.5 1.7 fusion.32
  151.3 11.8 %all_to_all.30 = bf16[4,256,256]{1,2,0:T(8,128)(2,1)S(1)} all-to-all(bf16[4,256,256]{1,2,0:T(8,128)(2,1)S(1)} %broadcast_in_dim.106), channel_id=1, replica_groups=mesh['req'=8,'bx'=4,'by'=8,'bc'=2] {'bx'}, dimensions={0} | all-to-all | bytes 1048576 | tf_op jit(solution)/shard_map/all_to_all | solution.py:227
  164.6 4.6 %all-to-all-start.5 = ((f32[32,8,512]{2,1,0:T(8,128)}), f32[32,8,512]{2,1,0:T(8,128)S(1)}, u32[]{:S(2)}, u32[]{:S(2)}) async-start(f32[32,8,512]{2,1,0:T(8,128)} %convolution_bitcast_fusion), calls=%async_computation.5 | async-start | bytes 1048576 | tf_op jit(solution)/shard_map/all_to_all | solution.py:233
  169.9 15.8 %all-to-all-done.5 = f32[32,8,512]{2,1,0:T(8,128)S(1)} async-done(((f32[32,8,512]{2,1,0:T(8,128)}), f32[32,8,512]{2,1,0:T(8,128)S(1)}, u32[]{:S(2)}, u32[]{:S(2)}) %all-to-all-start.5) | async-done | bytes 524320 | tf_op jit(solution)/shard_map/all_to_all | solution.py:233
  (112 shorter events, 33.5 us)
Async XLA Ops:
  2.2 25.1 %all-to-all-start.1 = ((bf16[8,256,96]{1,2,0:T(8,128)(2,1)}), bf16[8,256,96]{1,2,0:T(8,128)(2,1)}, u32[]{:S(2)}, u32[]{:S(2)}) async-start(bf16[8,256,96]{1,2,0:T(8,128)(2,1)} %broadcast_in_dim.47), calls=%async_computation.1 | async-start | bytes 786432 | tf_op jit(solution)/shard_map/all_to_all | solution.py:94
  12.5 3.7 %copy-start.1 = (bf16[1,1,2048,2,128]{4,3,2,1,0:T(2,128)(2,1)S(1)}, bf16[1,1,2048,2,128]{4,3,2,1,0:T(2,128)(2,1)}, u32[]{:S(2)}) copy-start(bf16[1,1,2048,2,128]{4,3,2,1,0:T(2,128)(2,1)} %param.15) | copy-start | bytes 3145732
  17.7 2.4 %copy-start.10 = (bf16[256,32]{0,1:T(8,128)(2,1)S(1)}, bf16[256,32]{0,1:T(8,128)(2,1)}, u32[]{:S(2)}) copy-start(bf16[256,32]{0,1:T(8,128)(2,1)} %param.21) | copy-start | bytes 49156
  17.7 2.5 %copy-start.8 = (bf16[256,128]{1,0:T(8,128)(2,1)S(1)}, bf16[256,128]{1,0:T(8,128)(2,1)}, u32[]{:S(2)}) copy-start(bf16[256,128]{1,0:T(8,128)(2,1)} %param.24) | copy-start | bytes 196612
  17.7 2.5 %copy-start.9 = (bf16[256,128]{1,0:T(8,128)(2,1)S(1)}, bf16[256,128]{1,0:T(8,128)(2,1)}, u32[]{:S(2)}) copy-start(bf16[256,128]{1,0:T(8,128)(2,1)} %param.22) | copy-start | bytes 196612
  17.8 2.8 %copy-start.14 = (s32[1,2]{1,0:T(1,128)S(1)}, s32[1,2]{1,0:T(1,128)}, u32[]{:S(2)}) copy-start(s32[1,2]{1,0:T(1,128)} %param.18) | copy-start | bytes 28
  20.4 11.6 %copy-start.2 = (bf16[64,8,8,256]{3,2,1,0:T(8,128)(2,1)S(1)}, bf16[64,8,8,256]{3,2,1,0:T(8,128)(2,1)}, u32[]{:S(2)}) copy-start(bf16[64,8,8,256]{3,2,1,0:T(8,128)(2,1)} %copy.99) | copy-start | bytes 6291460
  20.4 11.6 %copy-start.15 = (f32[3,32]{1,0:T(4,128)S(1)}, f32[3,32]{1,0:T(4,128)}, u32[]{:S(2)}) copy-start(f32[3,32]{1,0:T(4,128)} %param.20) | copy-start | bytes 1156
  28.4 35.8 %all-to-all-start = ((bf16[8,256,288]{1,2,0:T(8,128)(2,1)}), bf16[8,256,288]{1,2,0:T(8,128)(2,1)S(1)}, u32[]{:S(2)}, u32[]{:S(2)}) async-start(bf16[8,256,288]{1,2,0:T(8,128)(2,1)} %broadcast_in_dim.45), calls=%async_computation | async-start | bytes 2359296 | tf_op jit(solution)/shard_map/all_to_all | solution.py:53
  33.8 3.2 %collective-permute-start.1 = (bf16[3,32,512]{2,1,0:T(8,128)(2,1)S(1)}, bf16[3,32,512]{2,1,0:T(8,128)(2,1)S(1)}, u32[]{:S(2)}, u32[]{:S(2)}) collective-permute-start(bf16[3,32,512]{2,1,0:T(8,128)(2,1)S(1)} %fusion.15), channel_id=1, source_target_pairs={{0,1},{1,0},{2,3},{3,2},{4,5},{5,4},{6,7},{7,6},{8,9},{9,8},{10,11... | collective-permute-start | bytes 294920 | tf_op jit(solution)/shard_map/ppermute | solution.py:135
  37.0 8.9 %collective-permute-start.2 = (bf16[3,64,512]{2,1,0:T(8,128)(2,1)S(1)}, bf16[3,64,512]{2,1,0:T(8,128)(2,1)S(1)}, u32[]{:S(2)}, u32[]{:S(2)}) collective-permute-start(bf16[3,64,512]{2,1,0:T(8,128)(2,1)S(1)} %maximum_select_fusion.10), channel_id=1, source_target_pairs={{0,2},{2,0},{4,6},{6,4},{8,10},{10,8},{12,14},{14,12},{1,3},{3,1},... | collective-permute-start | bytes 589832 | tf_op jit(solution)/shard_map/ppermute | solution.py:136
  48.4 1.0 copy-start.4
  50.5 7.0 %collective-permute-start.3 = (f32[66,512]{1,0:T(8,128)S(1)}, f32[66,512]{1,0:T(8,128)S(1)}, u32[]{:S(2)}, u32[]{:S(2)}) collective-permute-start(f32[66,512]{1,0:T(8,128)S(1)} %pad_maximum_fusion.2), channel_id=1, source_target_pairs={{0,2},{2,0},{4,6},{6,4},{8,10},{10,8},{12,14},{14,12},{1,3},{3,1},... | collective-permute-start | bytes 405512 | tf_op jit(solution)/shard_map/ppermute | solution.py:136
  57.7 3.2 %collective-permute-start.4 = (f32[34,512]{1,0:T(8,128)S(1)}, f32[34,512]{1,0:T(8,128)S(1)}, u32[]{:S(2)}, u32[]{:S(2)}) collective-permute-start(f32[34,512]{1,0:T(8,128)S(1)} %pad_maximum_fusion.3), channel_id=1, source_target_pairs={{0,1},{1,0},{2,3},{3,2},{4,5},{5,4},{6,7},{7,6},{8,9},{9,8},{10,11... | collective-permute-start | bytes 208904 | tf_op jit(solution)/shard_map/ppermute | solution.py:135
  61.1 3.1 %collective-permute-start.5 = (bf16[32,256]{1,0:T(8,128)(2,1)S(1)}, bf16[32,256]{1,0:T(8,128)(2,1)S(1)}, u32[]{:S(2)}, u32[]{:S(2)}) collective-permute-start(bf16[32,256]{1,0:T(8,128)(2,1)S(1)} %bitcast.174), channel_id=1, source_target_pairs={{0,1},{1,0},{2,3},{3,2},{4,5},{5,4},{6,7},{7,6},{8,9},{9,8},{10,11... | collective-permute-start | bytes 49160 | tf_op jit(solution)/shard_map/ppermute | solution.py:199
  65.4 38.9 %all-to-all-start.2 = ((bf16[32,64,256]{2,1,0:T(8,128)(2,1)}), bf16[32,64,256]{2,1,0:T(8,128)(2,1)S(1)}, u32[]{:S(2)}, u32[]{:S(2)}) async-start(bf16[32,64,256]{2,1,0:T(8,128)(2,1)} %broadcast_in_dim.53), calls=%async_computation.2 | async-start | bytes 2097152 | tf_op jit(solution)/shard_map/all_to_all | solution.py:202
  76.9 16.3 %collective-permute-start.8 = (bf16[512,128]{1,0:T(8,128)(2,1)S(1)}, bf16[512,128]{1,0:T(8,128)(2,1)S(1)}, u32[]{:S(2)}, u32[]{:S(2)}) collective-permute-start(bf16[512,128]{1,0:T(8,128)(2,1)S(1)} %get-tuple-element.20), channel_id=1, source_target_pairs={{0,48},{16,32},{32,16},{48,0},{1,49},{17,33},{33,17},{49,1},{2,50}... | collective-permute-start | bytes 393224 | tf_op jit(solution)/shard_map/ppermute | solution.py:110
  81.6 13.2 %collective-permute-start.7 = (bf16[512,128]{1,0:T(8,128)(2,1)S(1)}, bf16[512,128]{1,0:T(8,128)(2,1)S(1)}, u32[]{:S(2)}, u32[]{:S(2)}) collective-permute-start(bf16[512,128]{1,0:T(8,128)(2,1)S(1)} %get-tuple-element.21), channel_id=1, source_target_pairs={{0,32},{16,48},{32,0},{48,16},{1,33},{17,49},{33,1},{49,17},{2,34}... | collective-permute-start | bytes 393224 | tf_op jit(solution)/shard_map/ppermute | solution.py:110
  84.3 11.4 %collective-permute-start.6 = (bf16[512,128]{1,0:T(8,128)(2,1)S(1)}, bf16[512,128]{1,0:T(8,128)(2,1)S(1)}, u32[]{:S(2)}, u32[]{:S(2)}) collective-permute-start(bf16[512,128]{1,0:T(8,128)(2,1)S(1)} %get-tuple-element.22), channel_id=1, source_target_pairs={{0,16},{16,0},{32,48},{48,32},{1,17},{17,1},{33,49},{49,33},{2,18}... | collective-permute-start | bytes 393224 | tf_op jit(solution)/shard_map/ppermute | solution.py:110
  86.8 12.5 %copy-start.11 = (f32[2,2048]{1,0:T(2,128)S(1)}, f32[2,2048]{1,0:T(2,128)}, u32[]{:S(2)}) copy-start(f32[2,2048]{1,0:T(2,128)} %param.25) | copy-start | bytes 49156
  87.7 11.8 %collective-permute-start = (bf16[2048,160]{0,1:T(8,128)(2,1)}, bf16[2048,160]{0,1:T(8,128)(2,1)}, u32[]{:S(2)}, u32[]{:S(2)}) collective-permute-start(bf16[2048,160]{0,1:T(8,128)(2,1)} %slice.133), channel_id=1, source_target_pairs={{0,1},{1,0},{2,3},{3,2},{4,5},{5,4},{6,7},{7,6},{8,9},{9,8},{10,11... | collective-permute-start | bytes 1966088 | tf_op jit(solution)/shard_map/ppermute | solution.py:99
  97.4 4.0 %collective-permute-start.9 = (bf16[4,512,128]{2,1,0:T(8,128)(2,1)}, bf16[4,512,128]{2,1,0:T(8,128)(2,1)S(1)}, u32[]{:S(2)}, u32[]{:S(2)}) collective-permute-start(bf16[4,512,128]{2,1,0:T(8,128)(2,1)} %broadcast_select_fusion), channel_id=1, source_target_pairs={{0,1},{1,0},{2,3},{3,2},{4,5},{5,4},{6,7},{7,6},{8,9},{9,8},{10,11... | collective-permute-start | bytes 1572872 | tf_op jit(solution)/shard_map/ppermute | solution.py:117
  101.4 0.8 copy-start.5
  104.3 10.7 %copy-start.12 = (f32[2,2048]{1,0:T(2,128)S(1)}, f32[2,2048]{1,0:T(2,128)}, u32[]{:S(2)}) copy-start(f32[2,2048]{1,0:T(2,128)} %param.27) | copy-start | bytes 49156
  104.3 10.7 %copy-start.13 = (f32[2,2048]{1,0:T(2,128)S(1)}, f32[2,2048]{1,0:T(2,128)}, u32[]{:S(2)}) copy-start(f32[2,2048]{1,0:T(2,128)} %param.26) | copy-start | bytes 49156
  105.7 37.3 %all-to-all-start.3 = ((bf16[32,64,256]{2,1,0:T(8,128)(2,1)}), bf16[32,64,256]{2,1,0:T(8,128)(2,1)S(1)}, u32[]{:S(2)}, u32[]{:S(2)}) async-start(bf16[32,64,256]{2,1,0:T(8,128)(2,1)} %broadcast_in_dim.100), calls=%async_computation.3 | async-start | bytes 2097152 | tf_op jit(solution)/shard_map/all_to_all | solution.py:213
  146.5 1.9 %copy-start = (bf16[1,512,2048]{2,1,0:T(8,128)(2,1)S(1)}, bf16[1,512,2048]{2,1,0:T(8,128)(2,1)}, u32[]{:S(2)}) copy-start(bf16[1,512,2048]{2,1,0:T(8,128)(2,1)} %param.14) | copy-start | bytes 6291460
  148.9 1.6 copy-start.6
  148.9 1.6 copy-start.7
  149.5 1.0 copy-start.3
  164.6 21.1 %all-to-all-start.5 = ((f32[32,8,512]{2,1,0:T(8,128)}), f32[32,8,512]{2,1,0:T(8,128)S(1)}, u32[]{:S(2)}, u32[]{:S(2)}) async-start(f32[32,8,512]{2,1,0:T(8,128)} %convolution_bitcast_fusion), calls=%async_computation.5 | async-start | bytes 1048576 | tf_op jit(solution)/shard_map/all_to_all | solution.py:233

commit v11 on v10

--- a/solution.py
+++ b/solution.py
@@ -135,15 +135,17 @@
             return lax.ppermute(value, "bc", swap("bc", nc))
         return lax.ppermute(value, "by", [(i, i ^ (1 << (bit_level - 1))) for i in range(ny)])
 
-    head_qkv = qkv_columns
-    for bit_level in range(low_bits):
-        partner = from_partner(head_qkv, bit_level)
-        upper_bit = group_index >> bit_level & 1
-        head_qkv = jnp.where(
-            upper_bit == 1,
-            jnp.concatenate([partner, head_qkv], axis=1),
-            jnp.concatenate([head_qkv, partner], axis=1),
-        )
+    upper = group_index >> 1 & 1
+    partner = from_partner(qkv_columns, 1)
+    head_qkv = jnp.where(
+        upper == 1,
+        jnp.stack([partner, qkv_columns], axis=1),
+        jnp.stack([qkv_columns, partner], axis=1),
+    )
+    partner = from_partner(head_qkv, 0)
+    head_qkv = jnp.where(
+        core == 1, jnp.stack([partner, head_qkv], axis=2), jnp.stack([head_qkv, partner], axis=2)
+    ).reshape(3, groups * column_width, query_total)
     queries = head_qkv[0].T
     fresh_count = query_total // groups
     fresh_start = group_index * fresh_count
@@ -171,19 +173,24 @@
         jnp.concatenate([cache_values, fresh_values], axis=0),
         jnp.concatenate([cache_visible, fresh_visible], axis=1),
     )
-    for bit_level in reversed(range(low_bits)):
-        halves = numerator.reshape(2, -1, query_total)
-        upper_bit = group_index >> bit_level & 1
-        kept_half = jnp.where(upper_bit == 1, halves[1], halves[0])
-        sent_half = jnp.where(upper_bit == 1, halves[0], halves[1])
+    def merge_level(kept_half, sent_half, bit_level):
         sent = jnp.concatenate([sent_half, row_max[None], row_total[None]], axis=0)
         got_back = from_partner(sent, bit_level)
         other_sum, other_max, other_total = got_back[:-2], got_back[-2], got_back[-1]
         joined = jnp.maximum(row_max, other_max)
         scale_kept = jnp.exp(row_max - joined)
         scale_other = jnp.exp(other_max - joined)
-        numerator = kept_half * scale_kept[None] + other_sum * scale_other[None]
-        row_max, row_total = joined, row_total * scale_kept + other_total * scale_other
+        merged = kept_half * scale_kept[None] + other_sum * scale_other[None]
+        return merged, joined, row_total * scale_kept + other_total * scale_other
+
+    by_bits = numerator.reshape(2, 2, column_width, query_total)
+    kept_half = jnp.where(core == 1, by_bits[:, 1], by_bits[:, 0]).reshape(2 * column_width, query_total)
+    sent_half = jnp.where(core == 1, by_bits[:, 0], by_bits[:, 1]).reshape(2 * column_width, query_total)
+    numerator, row_max, row_total = merge_level(kept_half, sent_half, 0)
+    by_bits = numerator.reshape(2, column_width, query_total)
+    kept_half = jnp.where(upper == 1, by_bits[1], by_bits[0])
+    sent_half = jnp.where(upper == 1, by_bits[0], by_bits[1])
+    numerator, row_max, row_total = merge_level(kept_half, sent_half, 1)
     context_columns = (numerator / row_total[None]).astype(jnp.bfloat16)
 
     block_rows = query_total // (group_size)

time: 191 us -> 187 us (0.979)
    all_to_all x1, waiting for transfers between devices: 4.07 us -> 8 us  [local(): lax.all_to_all(jnp.broadcast_to(qkv_flat[None], (reqs,) + qkv_flat.shape)...]
    ppermute x2, waiting for transfers between devices: 11.1 us -> 7.65 us  [from_partner(): lax.ppermute(value, 'by', [(i, i ^ 1 << bit_level - 1) for i in range(ny)])]
    unnamed x36, local copies, waits for them, and re-layouts: 7.76 us -> 5.47 us
  transfers between devices with their start and end apart: 15 -> 15, of which waited for: 13 -> 13; matrix products, arithmetic and copies ran while one was open for 14% -> 13% of each run, Pallas kernels for 0% -> 0%
where the time goes in v11:
time: 187 us; the launch traced here: 185 us
  waiting for transfers between devices  69 us (37%)
  starting transfers between devices  59.8 us (32%)
  local copies, waits for them, and re-layouts  23.6 us (13%)
  other arithmetic  12.7 us (7%)
  blocking collectives  12.1 us (6%)
  matrix products  6.1 us (3%)
  between operations  1.95 us (1%)
    all_to_all x1, waiting for transfers between devices, local(): lax.all_to_all(spread, PLANE, 0, 0, tiled=True)  26 us
    all_to_all x1, waiting for transfers between devices, local(): lax.all_to_all(mixed_parts.reshape(chips, block_rows, quarter_width), PLA...  15.8 us
    all_to_all x1, blocking collectives, local(): lax.all_to_all(jnp.broadcast_to(inner[None], (nx,) + inner.shape), 'bx',...  12.1 us
    all_to_all x1, starting transfers between devices, local(): lax.all_to_all(jnp.broadcast_to(qkv_flat[None], (reqs,) + qkv_flat.shape)...  10.3 us
    all_to_all x1, starting transfers between devices, local(): lax.all_to_all(outgoing, PLANE, 0, 0, tiled=True)  10.2 us
    ppermute x3, starting transfers between devices, local(): lax.ppermute(lax.dynamic_index_in_dim(own_down, row ^ k, 0, keepdims=Fals...  9.82 us
    all_to_all x1, waiting for transfers between devices, local(): lax.all_to_all(jnp.broadcast_to(qkv_flat[None], (reqs,) + qkv_flat.shape)...  8 us
    ppermute x2, waiting for transfers between devices, from_partner(): lax.ppermute(value, 'by', [(i, i ^ 1 << bit_level - 1) for i in range(ny)])  7.65 us
  transfers between devices with their start and end apart: 15, of which 13 were waited for; matrix products, arithmetic and copies ran while one was open for 13% of the time, Pallas kernels for 0%

profile of v11, /device:TPU:8, one launch (start us, length us, event | category | flops | bytes accessed | tf_op | source)
XLA Modules:
  0.0 185.2 jit_solution(15532845603254723736)
XLA Ops:
  0.6 1.6 broadcast_in_dim.47
  2.2 10.3 %all-to-all-start.1 = ((bf16[8,256,96]{1,2,0:T(8,128)(2,1)}), bf16[8,256,96]{1,2,0:T(8,128)(2,1)}, u32[]{:S(2)}, u32[]{:S(2)}) async-start(bf16[8,256,96]{1,2,0:T(8,128)(2,1)} %broadcast_in_dim.47), calls=%async_computation.1 | async-start | bytes 786432 | tf_op jit(solution)/shard_map/all_to_all | solution.py:94
  12.5 3.7 %copy.114 = bf16[64,8,8,256]{3,2,1,0:T(8,128)(2,1)} copy(bf16[64,8,8,256]{3,1,2,0:T(8,128)(2,1)} %bitcast.152) | data formatting | bytes 4194304
  19.3 8.0 %all-to-all-done.1 = bf16[8,256,96]{1,2,0:T(8,128)(2,1)} async-done(((bf16[8,256,96]{1,2,0:T(8,128)(2,1)}), bf16[8,256,96]{1,2,0:T(8,128)(2,1)}, u32[]{:S(2)}, u32[]{:S(2)}) %all-to-all-start.1) | async-done | bytes 393248 | tf_op jit(solution)/shard_map/all_to_all | solution.py:94
  28.4 3.6 %all-to-all-start = ((bf16[8,256,288]{1,2,0:T(8,128)(2,1)}), bf16[8,256,288]{1,2,0:T(8,128)(2,1)S(1)}, u32[]{:S(2)}, u32[]{:S(2)}) async-start(bf16[8,256,288]{1,2,0:T(8,128)(2,1)} %broadcast_in_dim.45), calls=%async_computation | async-start | bytes 2359296 | tf_op jit(solution)/shard_map/all_to_all | solution.py:53
  32.0 1.8 fusion.15
  33.8 2.5 %collective-permute-start.1 = (bf16[3,32,512]{2,1,0:T(8,128)(2,1)S(1)}, bf16[3,32,512]{2,1,0:T(8,128)(2,1)S(1)}, u32[]{:S(2)}, u32[]{:S(2)}) collective-permute-start(bf16[3,32,512]{2,1,0:T(8,128)(2,1)S(1)} %fusion.15), channel_id=1, source_target_pairs={{0,2},{2,0},{4,6},{6,4},{8,10},{10,8},{12,14},{14,12},{1,3},{3,1},... | collective-permute-start | bytes 294920 | tf_op jit(solution)/shard_map/ppermute | solution.py:136
  37.0 3.4 %collective-permute-done.1 = bf16[3,32,512]{2,1,0:T(8,128)(2,1)S(1)} collective-permute-done((bf16[3,32,512]{2,1,0:T(8,128)(2,1)S(1)}, bf16[3,32,512]{2,1,0:T(8,128)(2,1)S(1)}, u32[]{:S(2)}, u32[]{:S(2)}) %collective-permute-start.1) | collective-permute-done | bytes 98336 | tf_op jit(solution)/shard_map/ppermute | solution.py:136
  40.5 1.9 %collective-permute-start.2 = (bf16[3,2,32,512]{3,2,0,1:T(8,128)(2,1)S(1)}, bf16[3,2,32,512]{3,2,0,1:T(8,128)(2,1)S(1)}, u32[]{:S(2)}, u32[]{:S(2)}) collective-permute-start(bf16[3,2,32,512]{3,2,0,1:T(8,128)(2,1)S(1)} %maximum_select_fusion.10), channel_id=1, source_target_pairs={{0,1},{1,0},{2,3},{3,2},{4,5},{5,4},{6,7},{7,6},{8,9},{9,8},{10,11... | collective-permute-start | bytes 589832 | tf_op jit(solution)/shard_map/ppermute | solution.py:135
  43.0 2.0 %and_reduce_fusion = pred[2048]{0:T(1024)(128)(4,1)S(1)} fusion(s32[1,8192]{1,0:T(1,128)} %param.16, s32[]{:T(128)S(6)} %select_n.190, s32[]{:T(128)} %bitcast.17, s32[]{:T(128)} %bitcast.16, s32[]{:T(128)} %bitcast.151, s32[]{:T(128)S(6)} %mul.153), kind=kLoop, calls=%fused_computation.92 | loop fusion | flops 12288 | bytes 10260 | tf_op jit(solution)/shard_map/and | solution.py:162
  48.6 2.4 %collective-permute-start.3 = (f32[66,512]{1,0:T(8,128)S(1)}, f32[66,512]{1,0:T(8,128)S(1)}, u32[]{:S(2)}, u32[]{:S(2)}) collective-permute-start(f32[66,512]{1,0:T(8,128)S(1)} %pad_maximum_fusion.2), channel_id=1, source_target_pairs={{0,1},{1,0},{2,3},{3,2},{4,5},{5,4},{6,7},{7,6},{8,9},{9,8},{10,11... | collective-permute-start | bytes 405512 | tf_op jit(solution)/shard_map/ppermute | solution.py:135
  52.1 2.4 %collective-permute-start.4 = (f32[34,512]{1,0:T(8,128)S(1)}, f32[34,512]{1,0:T(8,128)S(1)}, u32[]{:S(2)}, u32[]{:S(2)}) collective-permute-start(f32[34,512]{1,0:T(8,128)S(1)} %pad_maximum_fusion.3), channel_id=1, source_target_pairs={{0,2},{2,0},{4,6},{6,4},{8,10},{10,8},{12,14},{14,12},{1,3},{3,1},... | collective-permute-start | bytes 208904 | tf_op jit(solution)/shard_map/ppermute | solution.py:136
  54.5 4.2 %collective-permute-done.4 = f32[34,512]{1,0:T(8,128)S(1)} collective-permute-done((f32[34,512]{1,0:T(8,128)S(1)}, f32[34,512]{1,0:T(8,128)S(1)}, u32[]{:S(2)}, u32[]{:S(2)}) %collective-permute-start.4) | collective-permute-done | bytes 69664 | tf_op jit(solution)/shard_map/ppermute | solution.py:136
  59.0 1.9 %collective-permute-start.5 = (bf16[32,256]{1,0:T(8,128)(2,1)S(1)}, bf16[32,256]{1,0:T(8,128)(2,1)S(1)}, u32[]{:S(2)}, u32[]{:S(2)}) collective-permute-start(bf16[32,256]{1,0:T(8,128)(2,1)S(1)} %bitcast.197), channel_id=1, source_target_pairs={{0,1},{1,0},{2,3},{3,2},{4,5},{5,4},{6,7},{7,6},{8,9},{9,8},{10,11... | collective-permute-start | bytes 49160 | tf_op jit(solution)/shard_map/ppermute | solution.py:206
  64.1 10.2 %all-to-all-start.2 = ((bf16[32,64,256]{2,1,0:T(8,128)(2,1)}), bf16[32,64,256]{2,1,0:T(8,128)(2,1)S(1)}, u32[]{:S(2)}, u32[]{:S(2)}) async-start(bf16[32,64,256]{2,1,0:T(8,128)(2,1)} %broadcast_in_dim.53), calls=%async_computation.2 | async-start | bytes 2097152 | tf_op jit(solution)/shard_map/all_to_all | solution.py:209
  75.6 4.6 %collective-permute-start.8 = (bf16[512,128]{1,0:T(8,128)(2,1)S(1)}, bf16[512,128]{1,0:T(8,128)(2,1)S(1)}, u32[]{:S(2)}, u32[]{:S(2)}) collective-permute-start(bf16[512,128]{1,0:T(8,128)(2,1)S(1)} %get-tuple-element.20), channel_id=1, source_target_pairs={{0,48},{16,32},{32,16},{48,0},{1,49},{17,33},{33,17},{49,1},{2,50}... | collective-permute-start | bytes 393224 | tf_op jit(solution)/shard_map/ppermute | solution.py:110
  80.3 2.7 %collective-permute-start.7 = (bf16[512,128]{1,0:T(8,128)(2,1)S(1)}, bf16[512,128]{1,0:T(8,128)(2,1)S(1)}, u32[]{:S(2)}, u32[]{:S(2)}) collective-permute-start(bf16[512,128]{1,0:T(8,128)(2,1)S(1)} %get-tuple-element.21), channel_id=1, source_target_pairs={{0,32},{16,48},{32,0},{48,16},{1,33},{17,49},{33,1},{49,17},{2,34}... | collective-permute-start | bytes 393224 | tf_op jit(solution)/shard_map/ppermute | solution.py:110
  83.0 2.5 %collective-permute-start.6 = (bf16[512,128]{1,0:T(8,128)(2,1)S(1)}, bf16[512,128]{1,0:T(8,128)(2,1)S(1)}, u32[]{:S(2)}, u32[]{:S(2)}) collective-permute-start(bf16[512,128]{1,0:T(8,128)(2,1)S(1)} %get-tuple-element.22), channel_id=1, source_target_pairs={{0,16},{16,0},{32,48},{48,32},{1,17},{17,1},{33,49},{49,33},{2,18}... | collective-permute-start | bytes 393224 | tf_op jit(solution)/shard_map/ppermute | solution.py:110
  86.4 1.9 %collective-permute-start = (bf16[2048,160]{0,1:T(8,128)(2,1)}, bf16[2048,160]{0,1:T(8,128)(2,1)}, u32[]{:S(2)}, u32[]{:S(2)}) collective-permute-start(bf16[2048,160]{0,1:T(8,128)(2,1)} %slice.134), channel_id=1, source_target_pairs={{0,1},{1,0},{2,3},{3,2},{4,5},{5,4},{6,7},{7,6},{8,9},{9,8},{10,11... | collective-permute-start | bytes 1966088 | tf_op jit(solution)/shard_map/ppermute | solution.py:99
  88.3 2.0 %collective-permute-done.8 = bf16[512,128]{1,0:T(8,128)(2,1)S(1)} collective-permute-done((bf16[512,128]{1,0:T(8,128)(2,1)S(1)}, bf16[512,128]{1,0:T(8,128)(2,1)S(1)}, u32[]{:S(2)}, u32[]{:S(2)}) %collective-permute-start.8) | collective-permute-done | bytes 131104 | tf_op jit(solution)/shard_map/ppermute | solution.py:110
  90.3 2.5 %collective-permute-done.7 = bf16[512,128]{1,0:T(8,128)(2,1)S(1)} collective-permute-done((bf16[512,128]{1,0:T(8,128)(2,1)S(1)}, bf16[512,128]{1,0:T(8,128)(2,1)S(1)}, u32[]{:S(2)}, u32[]{:S(2)}) %collective-permute-start.7) | collective-permute-done | bytes 131104 | tf_op jit(solution)/shard_map/ppermute | solution.py:110
  94.7 1.9 %collective-permute-start.9 = (bf16[4,512,128]{2,1,0:T(8,128)(2,1)S(1)}, bf16[4,512,128]{2,1,0:T(8,128)(2,1)}, u32[]{:S(2)}, u32[]{:S(2)}) collective-permute-start(bf16[4,512,128]{2,1,0:T(8,128)(2,1)S(1)} %broadcast_select_fusion), channel_id=1, source_target_pairs={{0,1},{1,0},{2,3},{3,2},{4,5},{5,4},{6,7},{7,6},{8,9},{9,8},{10,11... | collective-permute-start | bytes 1572872 | tf_op jit(solution)/shard_map/ppermute | solution.py:117
  100.0 2.3 %all-to-all-done.2 = bf16[32,64,256]{2,1,0:T(8,128)(2,1)S(1)} async-done(((bf16[32,64,256]{2,1,0:T(8,128)(2,1)}), bf16[32,64,256]{2,1,0:T(8,128)(2,1)S(1)}, u32[]{:S(2)}, u32[]{:S(2)}) %all-to-all-start.2) | async-done | bytes 1048608 | tf_op jit(solution)/shard_map/all_to_all | solution.py:209
  103.7 6.7 %all-to-all-start.3 = ((bf16[32,64,256]{2,1,0:T(8,128)(2,1)}), bf16[32,64,256]{2,1,0:T(8,128)(2,1)S(1)}, u32[]{:S(2)}, u32[]{:S(2)}) async-start(bf16[32,64,256]{2,1,0:T(8,128)(2,1)} %broadcast_in_dim.100), calls=%async_computation.3 | async-start | bytes 2097152 | tf_op jit(solution)/shard_map/all_to_all | solution.py:220
  111.2 1.9 %slice.151 = bf16[2048,128]{0,1:T(8,128)(2,1)} slice(bf16[2048,160]{0,1:T(8,128)(2,1)} %collective-permute-done), slice={[0:2048], [32:160]} | slice | bytes 1048576 | tf_op jit(solution)/shard_map/slice | solution.py:101
  113.1 26.0 %all-to-all-done.3 = bf16[32,64,256]{2,1,0:T(8,128)(2,1)S(1)} async-done(((bf16[32,64,256]{2,1,0:T(8,128)(2,1)}), bf16[32,64,256]{2,1,0:T(8,128)(2,1)S(1)}, u32[]{:S(2)}, u32[]{:S(2)}) %all-to-all-start.3) | async-done | bytes 1048608 | tf_op jit(solution)/shard_map/all_to_all | solution.py:220
  139.2 1.6 bitcast_convert_fusion
  140.7 1.9 %copy.99 = f32[2048,256]{0,1:T(8,128)S(1)} copy(f32[2048,256]{1,0:T(8,128)} %bitcast_convert_fusion) | data formatting | bytes 4194304 | tf_op jit(solution)/shard_map/convert_element_type | solution.py:224
  142.7 1.7 fusion.32
  147.5 12.1 %all_to_all.30 = bf16[4,256,256]{1,2,0:T(8,128)(2,1)S(1)} all-to-all(bf16[4,256,256]{1,2,0:T(8,128)(2,1)S(1)} %broadcast_in_dim.106), channel_id=1, replica_groups=mesh['req'=8,'bx'=4,'by'=8,'bc'=2] {'bx'}, dimensions={0} | all-to-all | bytes 1048576 | tf_op jit(solution)/shard_map/all_to_all | solution.py:234
  161.1 4.3 %all-to-all-start.5 = ((f32[32,8,512]{2,1,0:T(8,128)}), f32[32,8,512]{2,1,0:T(8,128)S(1)}, u32[]{:S(2)}, u32[]{:S(2)}) async-start(f32[32,8,512]{2,1,0:T(8,128)} %convolution_bitcast_fusion), calls=%async_computation.5 | async-start | bytes 1048576 | tf_op jit(solution)/shard_map/all_to_all | solution.py:240
  166.1 15.8 %all-to-all-done.5 = f32[32,8,512]{2,1,0:T(8,128)S(1)} async-done(((f32[32,8,512]{2,1,0:T(8,128)}), f32[32,8,512]{2,1,0:T(8,128)S(1)}, u32[]{:S(2)}, u32[]{:S(2)}) %all-to-all-start.5) | async-done | bytes 524320 | tf_op jit(solution)/shard_map/all_to_all | solution.py:240
  (112 shorter events, 31.0 us)
Async XLA Ops:
  2.2 25.1 %all-to-all-start.1 = ((bf16[8,256,96]{1,2,0:T(8,128)(2,1)}), bf16[8,256,96]{1,2,0:T(8,128)(2,1)}, u32[]{:S(2)}, u32[]{:S(2)}) async-start(bf16[8,256,96]{1,2,0:T(8,128)(2,1)} %broadcast_in_dim.47), calls=%async_computation.1 | async-start | bytes 786432 | tf_op jit(solution)/shard_map/all_to_all | solution.py:94
  12.5 3.7 %copy-start.1 = (bf16[1,1,2048,2,128]{4,3,2,1,0:T(2,128)(2,1)S(1)}, bf16[1,1,2048,2,128]{4,3,2,1,0:T(2,128)(2,1)}, u32[]{:S(2)}) copy-start(bf16[1,1,2048,2,128]{4,3,2,1,0:T(2,128)(2,1)} %param.15) | copy-start | bytes 3145732
  16.2 1.5 copy-start.10
  16.2 1.7 copy-start.8
  16.2 1.7 copy-start.9
  19.3 12.7 %copy-start.2 = (bf16[64,8,8,256]{3,2,1,0:T(8,128)(2,1)S(1)}, bf16[64,8,8,256]{3,2,1,0:T(8,128)(2,1)}, u32[]{:S(2)}) copy-start(bf16[64,8,8,256]{3,2,1,0:T(8,128)(2,1)} %copy.114) | copy-start | bytes 6291460
  19.3 12.7 %copy-start.15 = (f32[3,32]{1,0:T(4,128)S(1)}, f32[3,32]{1,0:T(4,128)}, u32[]{:S(2)}) copy-start(f32[3,32]{1,0:T(4,128)} %param.20) | copy-start | bytes 1156
  28.4 34.5 %all-to-all-start = ((bf16[8,256,288]{1,2,0:T(8,128)(2,1)}), bf16[8,256,288]{1,2,0:T(8,128)(2,1)S(1)}, u32[]{:S(2)}, u32[]{:S(2)}) async-start(bf16[8,256,288]{1,2,0:T(8,128)(2,1)} %broadcast_in_dim.45), calls=%async_computation | async-start | bytes 2359296 | tf_op jit(solution)/shard_map/all_to_all | solution.py:53
  32.0 10.4 %copy-start.14 = (s32[1,2]{1,0:T(1,128)S(1)}, s32[1,2]{1,0:T(1,128)}, u32[]{:S(2)}) copy-start(s32[1,2]{1,0:T(1,128)} %param.18) | copy-start | bytes 28
  33.8 11.6 %copy-start.7 = (bf16[2048,128]{1,0:T(8,128)(2,1)S(1)}, bf16[2048,128]{1,0:T(8,128)(2,1)}, u32[]{:S(2)}) copy-start(bf16[2048,128]{1,0:T(8,128)(2,1)} %get-tuple-element.42) | copy-start | bytes 1572868
  33.8 6.6 %collective-permute-start.1 = (bf16[3,32,512]{2,1,0:T(8,128)(2,1)S(1)}, bf16[3,32,512]{2,1,0:T(8,128)(2,1)S(1)}, u32[]{:S(2)}, u32[]{:S(2)}) collective-permute-start(bf16[3,32,512]{2,1,0:T(8,128)(2,1)S(1)} %fusion.15), channel_id=1, source_target_pairs={{0,2},{2,0},{4,6},{6,4},{8,10},{10,8},{12,14},{14,12},{1,3},{3,1},... | collective-permute-start | bytes 294920 | tf_op jit(solution)/shard_map/ppermute | solution.py:136
  40.5 4.6 %collective-permute-start.2 = (bf16[3,2,32,512]{3,2,0,1:T(8,128)(2,1)S(1)}, bf16[3,2,32,512]{3,2,0,1:T(8,128)(2,1)S(1)}, u32[]{:S(2)}, u32[]{:S(2)}) collective-permute-start(bf16[3,2,32,512]{3,2,0,1:T(8,128)(2,1)S(1)} %maximum_select_fusion.10), channel_id=1, source_target_pairs={{0,1},{1,0},{2,3},{3,2},{4,5},{5,4},{6,7},{7,6},{8,9},{9,8},{10,11... | collective-permute-start | bytes 589832 | tf_op jit(solution)/shard_map/ppermute | solution.py:135
  46.5 1.0 copy-start.6
  48.6 3.4 %collective-permute-start.3 = (f32[66,512]{1,0:T(8,128)S(1)}, f32[66,512]{1,0:T(8,128)S(1)}, u32[]{:S(2)}, u32[]{:S(2)}) collective-permute-start(f32[66,512]{1,0:T(8,128)S(1)} %pad_maximum_fusion.2), channel_id=1, source_target_pairs={{0,1},{1,0},{2,3},{3,2},{4,5},{5,4},{6,7},{7,6},{8,9},{9,8},{10,11... | collective-permute-start | bytes 405512 | tf_op jit(solution)/shard_map/ppermute | solution.py:135
  52.1 6.6 %collective-permute-start.4 = (f32[34,512]{1,0:T(8,128)S(1)}, f32[34,512]{1,0:T(8,128)S(1)}, u32[]{:S(2)}, u32[]{:S(2)}) collective-permute-start(f32[34,512]{1,0:T(8,128)S(1)} %pad_maximum_fusion.3), channel_id=1, source_target_pairs={{0,2},{2,0},{4,6},{6,4},{8,10},{10,8},{12,14},{14,12},{1,3},{3,1},... | collective-permute-start | bytes 208904 | tf_op jit(solution)/shard_map/ppermute | solution.py:136
  59.0 3.1 %collective-permute-start.5 = (bf16[32,256]{1,0:T(8,128)(2,1)S(1)}, bf16[32,256]{1,0:T(8,128)(2,1)S(1)}, u32[]{:S(2)}, u32[]{:S(2)}) collective-permute-start(bf16[32,256]{1,0:T(8,128)(2,1)S(1)} %bitcast.197), channel_id=1, source_target_pairs={{0,1},{1,0},{2,3},{3,2},{4,5},{5,4},{6,7},{7,6},{8,9},{9,8},{10,11... | collective-permute-start | bytes 49160 | tf_op jit(solution)/shard_map/ppermute | solution.py:206
  64.1 38.2 %all-to-all-start.2 = ((bf16[32,64,256]{2,1,0:T(8,128)(2,1)}), bf16[32,64,256]{2,1,0:T(8,128)(2,1)S(1)}, u32[]{:S(2)}, u32[]{:S(2)}) async-start(bf16[32,64,256]{2,1,0:T(8,128)(2,1)} %broadcast_in_dim.53), calls=%async_computation.2 | async-start | bytes 2097152 | tf_op jit(solution)/shard_map/all_to_all | solution.py:209
  75.6 14.7 %collective-permute-start.8 = (bf16[512,128]{1,0:T(8,128)(2,1)S(1)}, bf16[512,128]{1,0:T(8,128)(2,1)S(1)}, u32[]{:S(2)}, u32[]{:S(2)}) collective-permute-start(bf16[512,128]{1,0:T(8,128)(2,1)S(1)} %get-tuple-element.20), channel_id=1, source_target_pairs={{0,48},{16,32},{32,16},{48,0},{1,49},{17,33},{33,17},{49,1},{2,50}... | collective-permute-start | bytes 393224 | tf_op jit(solution)/shard_map/ppermute | solution.py:110
  80.3 12.5 %collective-permute-start.7 = (bf16[512,128]{1,0:T(8,128)(2,1)S(1)}, bf16[512,128]{1,0:T(8,128)(2,1)S(1)}, u32[]{:S(2)}, u32[]{:S(2)}) collective-permute-start(bf16[512,128]{1,0:T(8,128)(2,1)S(1)} %get-tuple-element.21), channel_id=1, source_target_pairs={{0,32},{16,48},{32,0},{48,16},{1,33},{17,49},{33,1},{49,17},{2,34}... | collective-permute-start | bytes 393224 | tf_op jit(solution)/shard_map/ppermute | solution.py:110
  83.0 10.8 %collective-permute-start.6 = (bf16[512,128]{1,0:T(8,128)(2,1)S(1)}, bf16[512,128]{1,0:T(8,128)(2,1)S(1)}, u32[]{:S(2)}, u32[]{:S(2)}) collective-permute-start(bf16[512,128]{1,0:T(8,128)(2,1)S(1)} %get-tuple-element.22), channel_id=1, source_target_pairs={{0,16},{16,0},{32,48},{48,32},{1,17},{17,1},{33,49},{49,33},{2,18}... | collective-permute-start | bytes 393224 | tf_op jit(solution)/shard_map/ppermute | solution.py:110
  85.5 11.1 %copy-start.11 = (f32[2,2048]{1,0:T(2,128)S(1)}, f32[2,2048]{1,0:T(2,128)}, u32[]{:S(2)}) copy-start(f32[2,2048]{1,0:T(2,128)} %param.25) | copy-start | bytes 49156
  86.4 10.4 %collective-permute-start = (bf16[2048,160]{0,1:T(8,128)(2,1)}, bf16[2048,160]{0,1:T(8,128)(2,1)}, u32[]{:S(2)}, u32[]{:S(2)}) collective-permute-start(bf16[2048,160]{0,1:T(8,128)(2,1)} %slice.134), channel_id=1, source_target_pairs={{0,1},{1,0},{2,3},{3,2},{4,5},{5,4},{6,7},{7,6},{8,9},{9,8},{10,11... | collective-permute-start | bytes 1966088 | tf_op jit(solution)/shard_map/ppermute | solution.py:99
  94.7 3.9 %collective-permute-start.9 = (bf16[4,512,128]{2,1,0:T(8,128)(2,1)S(1)}, bf16[4,512,128]{2,1,0:T(8,128)(2,1)}, u32[]{:S(2)}, u32[]{:S(2)}) collective-permute-start(bf16[4,512,128]{2,1,0:T(8,128)(2,1)S(1)} %broadcast_select_fusion), channel_id=1, source_target_pairs={{0,1},{1,0},{2,3},{3,2},{4,5},{5,4},{6,7},{7,6},{8,9},{9,8},{10,11... | collective-permute-start | bytes 1572872 | tf_op jit(solution)/shard_map/ppermute | solution.py:117
  102.3 8.9 %copy-start.12 = (f32[2,2048]{1,0:T(2,128)S(1)}, f32[2,2048]{1,0:T(2,128)}, u32[]{:S(2)}) copy-start(f32[2,2048]{1,0:T(2,128)} %param.27) | copy-start | bytes 49156
  102.3 8.9 %copy-start.13 = (f32[2,2048]{1,0:T(2,128)S(1)}, f32[2,2048]{1,0:T(2,128)}, u32[]{:S(2)}) copy-start(f32[2,2048]{1,0:T(2,128)} %param.26) | copy-start | bytes 49156
  103.7 35.4 %all-to-all-start.3 = ((bf16[32,64,256]{2,1,0:T(8,128)(2,1)}), bf16[32,64,256]{2,1,0:T(8,128)(2,1)S(1)}, u32[]{:S(2)}, u32[]{:S(2)}) async-start(bf16[32,64,256]{2,1,0:T(8,128)(2,1)} %broadcast_in_dim.100), calls=%async_computation.3 | async-start | bytes 2097152 | tf_op jit(solution)/shard_map/all_to_all | solution.py:220
  142.7 1.9 %copy-start = (bf16[1,512,2048]{2,1,0:T(8,128)(2,1)S(1)}, bf16[1,512,2048]{2,1,0:T(8,128)(2,1)}, u32[]{:S(2)}) copy-start(bf16[1,512,2048]{2,1,0:T(8,128)(2,1)} %param.14) | copy-start | bytes 6291460
  145.1 1.6 copy-start.4
  145.1 1.6 copy-start.5
  145.6 1.0 copy-start.3
  161.1 20.8 %all-to-all-start.5 = ((f32[32,8,512]{2,1,0:T(8,128)}), f32[32,8,512]{2,1,0:T(8,128)S(1)}, u32[]{:S(2)}, u32[]{:S(2)}) async-start(f32[32,8,512]{2,1,0:T(8,128)} %convolution_bitcast_fusion), calls=%async_computation.5 | async-start | bytes 1048576 | tf_op jit(solution)/shard_map/all_to_all | solution.py:240

commit v12 on v11

--- a/solution.py
+++ b/solution.py
@@ -103,20 +103,6 @@
     d_model = late.shape[0]
     quarter_width = d_model // nx
     own_down = late[:, column_width + hidden_width :].reshape(nx, quarter_width, hidden_width)
-    row = lax.axis_index("bx")
-    received = [lax.dynamic_index_in_dim(own_down, row, 0, keepdims=False)]
-    for k in range(1, nx):
-        received.append(
-            lax.ppermute(
-                lax.dynamic_index_in_dim(own_down, row ^ k, 0, keepdims=False),
-                "bx",
-                [(i, i ^ k) for i in range(nx)],
-            )
-        )
-    from_row = jnp.take(jnp.stack(received), row ^ jnp.arange(nx), axis=0)
-    from_sibling = lax.ppermute(from_row, "bc", swap("bc", nc))
-    group_down = core_pair(from_row[:, None], from_sibling[:, None], core, 1)
-
     query_total = tokens.shape[1]
     token_rows = tokens[0]
     qkv_columns = (
@@ -216,7 +202,20 @@
         + column_bias[:, None]
     ).astype(jnp.bfloat16)
     spread = jnp.broadcast_to(projected_part[None], (chips,) + projected_part.shape)
-    spread, group_down = lax.optimization_barrier((spread, group_down))
+    spread, own_down = lax.optimization_barrier((spread, own_down))
+    row = lax.axis_index("bx")
+    received = [lax.dynamic_index_in_dim(own_down, row, 0, keepdims=False)]
+    for k in range(1, nx):
+        received.append(
+            lax.ppermute(
+                lax.dynamic_index_in_dim(own_down, row ^ k, 0, keepdims=False),
+                "bx",
+                [(i, i ^ k) for i in range(nx)],
+            )
+        )
+    from_row = jnp.take(jnp.stack(received), row ^ jnp.arange(nx), axis=0)
+    from_sibling = lax.ppermute(from_row, "bc", swap("bc", nc))
+    group_down = core_pair(from_row[:, None], from_sibling[:, None], core, 1)
     projected = lax.all_to_all(spread, PLANE, 0, 0, tiled=True).reshape(chips * chip_width, core_rows)
     core_tokens = lax.dynamic_index_in_dim(
         token_rows.reshape(chips, nc, block_rows, -1), core, axis=1, keepdims=False

time: 187 us -> 190 us (1.016)
  blocking collectives: 12.1 us -> 0 us
  waiting for transfers between devices: 69 us -> 77.7 us
  starting transfers between devices: 59.8 us -> 64.9 us
    all_to_all x1, waiting for transfers between devices: 26 us -> 3.59 us  [local(): lax.all_to_all(spread, PLANE, 0, 0, tiled=True)]
    all_to_all x1, waiting for transfers between devices: 2.33 us -> 22.2 us  [local(): lax.all_to_all(outgoing, PLANE, 0, 0, tiled=True)]
    all_to_all x1 -> x0, blocking collectives: 12.1 us -> none  [local(): lax.all_to_all(jnp.broadcast_to(inner[None], (nx,) + inner.shape), 'bx',...]
    all_to_all x0 -> x1, waiting for transfers between devices: none -> 7.93 us  [local(): lax.all_to_all(jnp.broadcast_to(inner[None], (nx,) + inner.shape), 'bx',...]
    all_to_all x0 -> x1, starting transfers between devices: none -> 3.47 us  [local(): lax.all_to_all(jnp.broadcast_to(inner[None], (nx,) + inner.shape), 'bx',...]
    all_to_all x1, starting transfers between devices: 4.31 us -> 6.83 us  [local(): lax.all_to_all(mixed_parts.reshape(chips, block_rows, quarter_width), PLA...]
    ppermute x3, waiting for transfers between devices: 5.5 us -> 7.84 us  [local(): lax.ppermute(lax.dynamic_index_in_dim(own_down, row ^ k, 0, keepdims=Fals...]
    unnamed x36 -> x32, local copies, waits for them, and re-layouts: 5.47 us -> 5.28 us
  transfers between devices with their start and end apart: 15 -> 16, of which waited for: 13 -> 13; matrix products, arithmetic and copies ran while one was open for 13% -> 17% of each run, Pallas kernels for 0% -> 0%
where the time goes in v12:
time: 190 us; the launch traced here: 188 us
  waiting for transfers between devices  77.7 us (41%)
  starting transfers between devices  64.9 us (34%)
  local copies, waits for them, and re-layouts  23.9 us (13%)
  other arithmetic  12.1 us (6%)
  matrix products  7.91 us (4%)
  between operations  1.94 us (1%)
    all_to_all x1, waiting for transfers between devices, local(): lax.all_to_all(outgoing, PLANE, 0, 0, tiled=True)  22.2 us
    all_to_all x1, waiting for transfers between devices, local(): lax.all_to_all(mixed_parts.reshape(chips, block_rows, quarter_width), PLA...  16.9 us
    ppermute x3, starting transfers between devices, local(): lax.ppermute(lax.dynamic_index_in_dim(own_down, row ^ k, 0, keepdims=Fals...  10.4 us
    all_to_all x1, starting transfers between devices, local(): lax.all_to_all(jnp.broadcast_to(qkv_flat[None], (reqs,) + qkv_flat.shape)...  10.3 us
    all_to_all x1, starting transfers between devices, local(): lax.all_to_all(outgoing, PLANE, 0, 0, tiled=True)  10.2 us
    all_to_all x1, waiting for transfers between devices, local(): lax.all_to_all(jnp.broadcast_to(qkv_flat[None], (reqs,) + qkv_flat.shape)...  8.09 us
    all_to_all x1, waiting for transfers between devices, local(): lax.all_to_all(jnp.broadcast_to(inner[None], (nx,) + inner.shape), 'bx',...  7.93 us
    ppermute x3, waiting for transfers between devices, local(): lax.ppermute(lax.dynamic_index_in_dim(own_down, row ^ k, 0, keepdims=Fals...  7.84 us
  transfers between devices with their start and end apart: 16, of which 13 were waited for; matrix products, arithmetic and copies ran while one was open for 17% of the time, Pallas kernels for 0%

profile of v12, /device:TPU:8, one launch (start us, length us, event | category | flops | bytes accessed | tf_op | source)
XLA Modules:
  0.0 188.4 jit_solution(9288208323629134238)
XLA Ops:
  0.6 1.6 broadcast_in_dim.47
  2.2 10.3 %all-to-all-start.1 = ((bf16[8,256,96]{1,2,0:T(8,128)(2,1)}), bf16[8,256,96]{1,2,0:T(8,128)(2,1)S(1)}, u32[]{:S(2)}, u32[]{:S(2)}) async-start(bf16[8,256,96]{1,2,0:T(8,128)(2,1)} %broadcast_in_dim.47), calls=%async_computation.1 | async-start | bytes 786432 | tf_op jit(solution)/shard_map/all_to_all | solution.py:94
  12.5 3.7 %copy.114 = bf16[64,8,8,256]{3,2,1,0:T(8,128)(2,1)} copy(bf16[64,8,8,256]{3,1,2,0:T(8,128)(2,1)} %bitcast.152) | data formatting | bytes 4194304
  19.1 8.1 %all-to-all-done.1 = bf16[8,256,96]{1,2,0:T(8,128)(2,1)S(1)} async-done(((bf16[8,256,96]{1,2,0:T(8,128)(2,1)}), bf16[8,256,96]{1,2,0:T(8,128)(2,1)S(1)}, u32[]{:S(2)}, u32[]{:S(2)}) %all-to-all-start.1) | async-done | bytes 393248 | tf_op jit(solution)/shard_map/all_to_all | solution.py:94
  28.3 3.6 %all-to-all-start = ((bf16[8,256,288]{1,2,0:T(8,128)(2,1)}), bf16[8,256,288]{1,2,0:T(8,128)(2,1)S(1)}, u32[]{:S(2)}, u32[]{:S(2)}) async-start(bf16[8,256,288]{1,2,0:T(8,128)(2,1)} %broadcast_in_dim.45), calls=%async_computation | async-start | bytes 2359296 | tf_op jit(solution)/shard_map/all_to_all | solution.py:53
  31.9 2.4 %fusion.15 = bf16[3,32,512]{2,1,0:T(8,128)(2,1)S(1)} fusion(bf16[8,256,3,32]{1,3,2,0:T(8,128)(2,1)S(1)} %bitcast.172, bf16[512,8,256,1]{2,1,0,3:T(8,128)(2,1)} %bitcast.160, f32[3,32]{1,0:T(4,128)S(1)} %copy-done.13), kind=kOutput, calls=%fused_computation.19 | convolution fusion | flops 201424896 | bytes 2589056 | tf_op jit(solution)/shard_map/tsd,sdce->cet/dot_general | solution.py:109
  34.3 2.5 %collective-permute-start.1 = (bf16[3,32,512]{2,1,0:T(8,128)(2,1)S(1)}, bf16[3,32,512]{2,1,0:T(8,128)(2,1)S(1)}, u32[]{:S(2)}, u32[]{:S(2)}) collective-permute-start(bf16[3,32,512]{2,1,0:T(8,128)(2,1)S(1)} %fusion.15), channel_id=1, source_target_pairs={{0,2},{2,0},{4,6},{6,4},{8,10},{10,8},{12,14},{14,12},{1,3},{3,1},... | collective-permute-start | bytes 294920 | tf_op jit(solution)/shard_map/ppermute | solution.py:122
  37.6 3.4 %collective-permute-done.1 = bf16[3,32,512]{2,1,0:T(8,128)(2,1)S(1)} collective-permute-done((bf16[3,32,512]{2,1,0:T(8,128)(2,1)S(1)}, bf16[3,32,512]{2,1,0:T(8,128)(2,1)S(1)}, u32[]{:S(2)}, u32[]{:S(2)}) %collective-permute-start.1) | collective-permute-done | bytes 98336 | tf_op jit(solution)/shard_map/ppermute | solution.py:122
  41.0 1.9 %collective-permute-start.2 = (bf16[3,2,32,512]{3,2,0,1:T(8,128)(2,1)S(1)}, bf16[3,2,32,512]{3,2,0,1:T(8,128)(2,1)S(1)}, u32[]{:S(2)}, u32[]{:S(2)}) collective-permute-start(bf16[3,2,32,512]{3,2,0,1:T(8,128)(2,1)S(1)} %maximum_select_fusion.10), channel_id=1, source_target_pairs={{0,1},{1,0},{2,3},{3,2},{4,5},{5,4},{6,7},{7,6},{8,9},{9,8},{10,11... | collective-permute-start | bytes 589832 | tf_op jit(solution)/shard_map/ppermute | solution.py:121
  43.5 2.0 %and_reduce_fusion = pred[2048]{0:T(1024)(128)(4,1)S(1)} fusion(s32[1,8192]{1,0:T(1,128)} %param.16, s32[]{:T(128)S(6)} %select_n.190, s32[]{:T(128)} %bitcast.17, s32[]{:T(128)} %bitcast.16, s32[]{:T(128)} %bitcast.151, s32[]{:T(128)S(6)} %mul.153), kind=kLoop, calls=%fused_computation.98 | loop fusion | flops 12288 | bytes 10260 | tf_op jit(solution)/shard_map/and | solution.py:148
  49.0 2.4 %collective-permute-start.3 = (f32[66,512]{1,0:T(8,128)S(1)}, f32[66,512]{1,0:T(8,128)S(1)}, u32[]{:S(2)}, u32[]{:S(2)}) collective-permute-start(f32[66,512]{1,0:T(8,128)S(1)} %pad_maximum_fusion.2), channel_id=1, source_target_pairs={{0,1},{1,0},{2,3},{3,2},{4,5},{5,4},{6,7},{7,6},{8,9},{9,8},{10,11... | collective-permute-start | bytes 405512 | tf_op jit(solution)/shard_map/ppermute | solution.py:121
  52.5 2.4 %collective-permute-start.4 = (f32[34,512]{1,0:T(8,128)S(1)}, f32[34,512]{1,0:T(8,128)S(1)}, u32[]{:S(2)}, u32[]{:S(2)}) collective-permute-start(f32[34,512]{1,0:T(8,128)S(1)} %pad_maximum_fusion.3), channel_id=1, source_target_pairs={{0,2},{2,0},{4,6},{6,4},{8,10},{10,8},{12,14},{14,12},{1,3},{3,1},... | collective-permute-start | bytes 208904 | tf_op jit(solution)/shard_map/ppermute | solution.py:122
  54.9 4.2 %collective-permute-done.4 = f32[34,512]{1,0:T(8,128)S(1)} collective-permute-done((f32[34,512]{1,0:T(8,128)S(1)}, f32[34,512]{1,0:T(8,128)S(1)}, u32[]{:S(2)}, u32[]{:S(2)}) %collective-permute-start.4) | collective-permute-done | bytes 69664 | tf_op jit(solution)/shard_map/ppermute | solution.py:122
  59.4 1.9 %collective-permute-start.5 = (bf16[32,256]{1,0:T(8,128)(2,1)S(1)}, bf16[32,256]{1,0:T(8,128)(2,1)S(1)}, u32[]{:S(2)}, u32[]{:S(2)}) collective-permute-start(bf16[32,256]{1,0:T(8,128)(2,1)S(1)} %bitcast.198), channel_id=1, source_target_pairs={{0,1},{1,0},{2,3},{3,2},{4,5},{5,4},{6,7},{7,6},{8,9},{9,8},{10,11... | collective-permute-start | bytes 49160 | tf_op jit(solution)/shard_map/ppermute | solution.py:192
  64.0 10.2 %all-to-all-start.2 = ((bf16[32,64,256]{2,1,0:T(8,128)(2,1)}), bf16[32,64,256]{2,1,0:T(8,128)(2,1)S(1)}, u32[]{:S(2)}, u32[]{:S(2)}) async-start(bf16[32,64,256]{2,1,0:T(8,128)(2,1)} %broadcast_in_dim.53), calls=%async_computation.2 | async-start | bytes 2097152 | tf_op jit(solution)/shard_map/all_to_all | solution.py:195
  75.2 1.9 %collective-permute-start = (bf16[2048,160]{0,1:T(8,128)(2,1)}, bf16[2048,160]{0,1:T(8,128)(2,1)}, u32[]{:S(2)}, u32[]{:S(2)}) collective-permute-start(bf16[2048,160]{0,1:T(8,128)(2,1)} %slice.134), channel_id=1, source_target_pairs={{0,1},{1,0},{2,3},{3,2},{4,5},{5,4},{6,7},{7,6},{8,9},{9,8},{10,11... | collective-permute-start | bytes 1966088 | tf_op jit(solution)/shard_map/ppermute | solution.py:99
  80.5 22.2 %all-to-all-done.2 = bf16[32,64,256]{2,1,0:T(8,128)(2,1)S(1)} async-done(((bf16[32,64,256]{2,1,0:T(8,128)(2,1)}), bf16[32,64,256]{2,1,0:T(8,128)(2,1)S(1)}, u32[]{:S(2)}, u32[]{:S(2)}) %all-to-all-start.2) | async-done | bytes 1048608 | tf_op jit(solution)/shard_map/all_to_all | solution.py:195
  104.1 5.2 %all-to-all-start.3 = ((bf16[32,64,256]{2,1,0:T(8,128)(2,1)}), bf16[32,64,256]{2,1,0:T(8,128)(2,1)S(1)}, u32[]{:S(2)}, u32[]{:S(2)}) async-start(bf16[32,64,256]{2,1,0:T(8,128)(2,1)} %broadcast_in_dim.100), calls=%async_computation.3 | async-start | bytes 2097152 | tf_op jit(solution)/shard_map/all_to_all | solution.py:219
  109.5 3.4 %collective-permute-start.6 = (bf16[512,128]{1,0:T(8,128)(2,1)S(1)}, bf16[512,128]{1,0:T(8,128)(2,1)S(1)}, u32[]{:S(2)}, u32[]{:S(2)}) collective-permute-start(bf16[512,128]{1,0:T(8,128)(2,1)S(1)} %get-tuple-element.22), channel_id=1, source_target_pairs={{0,16},{16,0},{32,48},{48,32},{1,17},{17,1},{33,49},{49,33},{2,18}... | collective-permute-start | bytes 393224 | tf_op jit(solution)/shard_map/ppermute | solution.py:210
  112.8 4.6 %collective-permute-start.7 = (bf16[512,128]{1,0:T(8,128)(2,1)S(1)}, bf16[512,128]{1,0:T(8,128)(2,1)S(1)}, u32[]{:S(2)}, u32[]{:S(2)}) collective-permute-start(bf16[512,128]{1,0:T(8,128)(2,1)S(1)} %get-tuple-element.21), channel_id=1, source_target_pairs={{0,32},{16,48},{32,0},{48,16},{1,33},{17,49},{33,1},{49,17},{2,34}... | collective-permute-start | bytes 393224 | tf_op jit(solution)/shard_map/ppermute | solution.py:210
  117.5 2.4 %collective-permute-start.8 = (bf16[512,128]{1,0:T(8,128)(2,1)S(1)}, bf16[512,128]{1,0:T(8,128)(2,1)S(1)}, u32[]{:S(2)}, u32[]{:S(2)}) collective-permute-start(bf16[512,128]{1,0:T(8,128)(2,1)S(1)} %get-tuple-element.20), channel_id=1, source_target_pairs={{0,48},{16,32},{32,16},{48,0},{1,49},{17,33},{33,17},{49,1},{2,50}... | collective-permute-start | bytes 393224 | tf_op jit(solution)/shard_map/ppermute | solution.py:210
  122.4 4.3 %collective-permute-done.7 = bf16[512,128]{1,0:T(8,128)(2,1)S(1)} collective-permute-done((bf16[512,128]{1,0:T(8,128)(2,1)S(1)}, bf16[512,128]{1,0:T(8,128)(2,1)S(1)}, u32[]{:S(2)}, u32[]{:S(2)}) %collective-permute-start.7) | collective-permute-done | bytes 131104 | tf_op jit(solution)/shard_map/ppermute | solution.py:210
  126.7 3.5 %collective-permute-done.8 = bf16[512,128]{1,0:T(8,128)(2,1)S(1)} collective-permute-done((bf16[512,128]{1,0:T(8,128)(2,1)S(1)}, bf16[512,128]{1,0:T(8,128)(2,1)S(1)}, u32[]{:S(2)}, u32[]{:S(2)}) %collective-permute-start.8) | collective-permute-done | bytes 131104 | tf_op jit(solution)/shard_map/ppermute | solution.py:210
  131.8 1.9 %collective-permute-start.9 = (bf16[4,512,128]{2,1,0:T(8,128)(2,1)}, bf16[4,512,128]{2,1,0:T(8,128)(2,1)}, u32[]{:S(2)}, u32[]{:S(2)}) collective-permute-start(bf16[4,512,128]{2,1,0:T(8,128)(2,1)} %broadcast_select_fusion), channel_id=1, source_target_pairs={{0,1},{1,0},{2,3},{3,2},{4,5},{5,4},{6,7},{7,6},{8,9},{9,8},{10,11... | collective-permute-start | bytes 1572872 | tf_op jit(solution)/shard_map/ppermute | solution.py:217
  133.8 3.6 %all-to-all-done.3 = bf16[32,64,256]{2,1,0:T(8,128)(2,1)S(1)} async-done(((bf16[32,64,256]{2,1,0:T(8,128)(2,1)}), bf16[32,64,256]{2,1,0:T(8,128)(2,1)S(1)}, u32[]{:S(2)}, u32[]{:S(2)}) %all-to-all-start.3) | async-done | bytes 1048608 | tf_op jit(solution)/shard_map/all_to_all | solution.py:219
  138.9 1.9 %copy.99 = f32[2048,256]{0,1:T(8,128)S(1)} copy(f32[2048,256]{1,0:T(8,128)} %bitcast_convert_fusion) | data formatting | bytes 4194304 | tf_op jit(solution)/shard_map/convert_element_type | solution.py:223
  140.8 1.7 fusion.39
  146.4 3.5 %all-to-all-start.4 = ((bf16[4,256,256]{1,2,0:T(8,128)(2,1)}), bf16[4,256,256]{1,2,0:T(8,128)(2,1)S(1)}, u32[]{:S(2)}, u32[]{:S(2)}) async-start(bf16[4,256,256]{1,2,0:T(8,128)(2,1)} %broadcast_in_dim.101), calls=%async_computation.4 | async-start | bytes 1048576 | tf_op jit(solution)/shard_map/all_to_all | solution.py:233
  150.0 7.9 %all-to-all-done.4 = bf16[4,256,256]{1,2,0:T(8,128)(2,1)S(1)} async-done(((bf16[4,256,256]{1,2,0:T(8,128)(2,1)}), bf16[4,256,256]{1,2,0:T(8,128)(2,1)S(1)}, u32[]{:S(2)}, u32[]{:S(2)}) %all-to-all-start.4) | async-done | bytes 524320 | tf_op jit(solution)/shard_map/all_to_all | solution.py:233
  158.2 2.5 %convolution_bitcast_fusion = f32[32,8,512]{2,1,0:T(8,128)} fusion(bf16[4,1,512,128]{3,2,0,1:T(8,128)(2,1)} %bitcast.55, bf16[4,1,512,128]{3,2,0,1:T(8,128)(2,1)S(1)} %bitcast_select_fusion, pred[]{:T(512)S(6)} %eq.8, bf16[256,2,128,4]{2,0,3,1:T(8,128)(2,1)S(1)} %copy.101), kind=kOutput, calls=%fused_computation.15 | convolution fusion | flops 270008320 | bytes 2097153 | tf_op jit(solution)/shard_map/xtcf,xcdf->td/dot_general | solution.py:236
  160.7 6.8 %all-to-all-start.5 = ((f32[32,8,512]{2,1,0:T(8,128)}), f32[32,8,512]{2,1,0:T(8,128)S(1)}, u32[]{:S(2)}, u32[]{:S(2)}) async-start(f32[32,8,512]{2,1,0:T(8,128)} %convolution_bitcast_fusion), calls=%async_computation.5 | async-start | bytes 1048576 | tf_op jit(solution)/shard_map/all_to_all | solution.py:239
  168.2 16.9 %all-to-all-done.5 = f32[32,8,512]{2,1,0:T(8,128)S(1)} async-done(((f32[32,8,512]{2,1,0:T(8,128)}), f32[32,8,512]{2,1,0:T(8,128)S(1)}, u32[]{:S(2)}, u32[]{:S(2)}) %all-to-all-start.5) | async-done | bytes 524320 | tf_op jit(solution)/shard_map/all_to_all | solution.py:239
  (108 shorter events, 31.6 us)
Async XLA Ops:
  2.2 25.0 %all-to-all-start.1 = ((bf16[8,256,96]{1,2,0:T(8,128)(2,1)}), bf16[8,256,96]{1,2,0:T(8,128)(2,1)S(1)}, u32[]{:S(2)}, u32[]{:S(2)}) async-start(bf16[8,256,96]{1,2,0:T(8,128)(2,1)} %broadcast_in_dim.47), calls=%async_computation.1 | async-start | bytes 786432 | tf_op jit(solution)/shard_map/all_to_all | solution.py:94
  12.5 3.7 %copy-start.1 = (bf16[1,1,2048,2,128]{4,3,2,1,0:T(2,128)(2,1)S(1)}, bf16[1,1,2048,2,128]{4,3,2,1,0:T(2,128)(2,1)}, u32[]{:S(2)}) copy-start(bf16[1,1,2048,2,128]{4,3,2,1,0:T(2,128)(2,1)} %param.15) | copy-start | bytes 3145732
  16.2 1.5 copy-start.7
  16.2 1.7 copy-start.5
  16.2 1.7 copy-start.6
  19.1 12.8 %copy-start.13 = (f32[3,32]{1,0:T(4,128)S(1)}, f32[3,32]{1,0:T(4,128)}, u32[]{:S(2)}) copy-start(f32[3,32]{1,0:T(4,128)} %param.20) | copy-start | bytes 1156
  28.3 34.5 %all-to-all-start = ((bf16[8,256,288]{1,2,0:T(8,128)(2,1)}), bf16[8,256,288]{1,2,0:T(8,128)(2,1)S(1)}, u32[]{:S(2)}, u32[]{:S(2)}) async-start(bf16[8,256,288]{1,2,0:T(8,128)(2,1)} %broadcast_in_dim.45), calls=%async_computation | async-start | bytes 2359296 | tf_op jit(solution)/shard_map/all_to_all | solution.py:53
  31.9 11.0 %copy-start.11 = (s32[1,2]{1,0:T(1,128)S(1)}, s32[1,2]{1,0:T(1,128)}, u32[]{:S(2)}) copy-start(s32[1,2]{1,0:T(1,128)} %param.18) | copy-start | bytes 28
  34.3 11.6 %copy-start.4 = (bf16[2048,128]{1,0:T(8,128)(2,1)S(1)}, bf16[2048,128]{1,0:T(8,128)(2,1)}, u32[]{:S(2)}) copy-start(bf16[2048,128]{1,0:T(8,128)(2,1)} %get-tuple-element.42) | copy-start | bytes 1572868
  34.3 6.6 %collective-permute-start.1 = (bf16[3,32,512]{2,1,0:T(8,128)(2,1)S(1)}, bf16[3,32,512]{2,1,0:T(8,128)(2,1)S(1)}, u32[]{:S(2)}, u32[]{:S(2)}) collective-permute-start(bf16[3,32,512]{2,1,0:T(8,128)(2,1)S(1)} %fusion.15), channel_id=1, source_target_pairs={{0,2},{2,0},{4,6},{6,4},{8,10},{10,8},{12,14},{14,12},{1,3},{3,1},... | collective-permute-start | bytes 294920 | tf_op jit(solution)/shard_map/ppermute | solution.py:122
  41.0 4.6 %collective-permute-start.2 = (bf16[3,2,32,512]{3,2,0,1:T(8,128)(2,1)S(1)}, bf16[3,2,32,512]{3,2,0,1:T(8,128)(2,1)S(1)}, u32[]{:S(2)}, u32[]{:S(2)}) collective-permute-start(bf16[3,2,32,512]{3,2,0,1:T(8,128)(2,1)S(1)} %maximum_select_fusion.10), channel_id=1, source_target_pairs={{0,1},{1,0},{2,3},{3,2},{4,5},{5,4},{6,7},{7,6},{8,9},{9,8},{10,11... | collective-permute-start | bytes 589832 | tf_op jit(solution)/shard_map/ppermute | solution.py:121
  49.0 3.4 %collective-permute-start.3 = (f32[66,512]{1,0:T(8,128)S(1)}, f32[66,512]{1,0:T(8,128)S(1)}, u32[]{:S(2)}, u32[]{:S(2)}) collective-permute-start(f32[66,512]{1,0:T(8,128)S(1)} %pad_maximum_fusion.2), channel_id=1, source_target_pairs={{0,1},{1,0},{2,3},{3,2},{4,5},{5,4},{6,7},{7,6},{8,9},{9,8},{10,11... | collective-permute-start | bytes 405512 | tf_op jit(solution)/shard_map/ppermute | solution.py:121
  52.5 6.6 %collective-permute-start.4 = (f32[34,512]{1,0:T(8,128)S(1)}, f32[34,512]{1,0:T(8,128)S(1)}, u32[]{:S(2)}, u32[]{:S(2)}) collective-permute-start(f32[34,512]{1,0:T(8,128)S(1)} %pad_maximum_fusion.3), channel_id=1, source_target_pairs={{0,2},{2,0},{4,6},{6,4},{8,10},{10,8},{12,14},{14,12},{1,3},{3,1},... | collective-permute-start | bytes 208904 | tf_op jit(solution)/shard_map/ppermute | solution.py:122
  59.4 3.1 %collective-permute-start.5 = (bf16[32,256]{1,0:T(8,128)(2,1)S(1)}, bf16[32,256]{1,0:T(8,128)(2,1)S(1)}, u32[]{:S(2)}, u32[]{:S(2)}) collective-permute-start(bf16[32,256]{1,0:T(8,128)(2,1)S(1)} %bitcast.198), channel_id=1, source_target_pairs={{0,1},{1,0},{2,3},{3,2},{4,5},{5,4},{6,7},{7,6},{8,9},{9,8},{10,11... | collective-permute-start | bytes 49160 | tf_op jit(solution)/shard_map/ppermute | solution.py:192
  64.0 38.7 %all-to-all-start.2 = ((bf16[32,64,256]{2,1,0:T(8,128)(2,1)}), bf16[32,64,256]{2,1,0:T(8,128)(2,1)S(1)}, u32[]{:S(2)}, u32[]{:S(2)}) async-start(bf16[32,64,256]{2,1,0:T(8,128)(2,1)} %broadcast_in_dim.53), calls=%async_computation.2 | async-start | bytes 2097152 | tf_op jit(solution)/shard_map/all_to_all | solution.py:195
  74.2 3.0 %copy-start.8 = (f32[2,2048]{1,0:T(2,128)S(1)}, f32[2,2048]{1,0:T(2,128)}, u32[]{:S(2)}) copy-start(f32[2,2048]{1,0:T(2,128)} %param.25) | copy-start | bytes 49156
  75.2 4.3 %collective-permute-start = (bf16[2048,160]{0,1:T(8,128)(2,1)}, bf16[2048,160]{0,1:T(8,128)(2,1)}, u32[]{:S(2)}, u32[]{:S(2)}) collective-permute-start(bf16[2048,160]{0,1:T(8,128)(2,1)} %slice.134), channel_id=1, source_target_pairs={{0,1},{1,0},{2,3},{3,2},{4,5},{5,4},{6,7},{7,6},{8,9},{9,8},{10,11... | collective-permute-start | bytes 1966088 | tf_op jit(solution)/shard_map/ppermute | solution.py:99
  102.7 6.6 %copy-start.9 = (f32[2,2048]{1,0:T(2,128)S(1)}, f32[2,2048]{1,0:T(2,128)}, u32[]{:S(2)}) copy-start(f32[2,2048]{1,0:T(2,128)} %param.26) | copy-start | bytes 49156
  102.7 6.7 %copy-start.10 = (f32[2,2048]{1,0:T(2,128)S(1)}, f32[2,2048]{1,0:T(2,128)}, u32[]{:S(2)}) copy-start(f32[2,2048]{1,0:T(2,128)} %param.27) | copy-start | bytes 49156
  104.1 33.2 %all-to-all-start.3 = ((bf16[32,64,256]{2,1,0:T(8,128)(2,1)}), bf16[32,64,256]{2,1,0:T(8,128)(2,1)S(1)}, u32[]{:S(2)}, u32[]{:S(2)}) async-start(bf16[32,64,256]{2,1,0:T(8,128)(2,1)} %broadcast_in_dim.100), calls=%async_computation.3 | async-start | bytes 2097152 | tf_op jit(solution)/shard_map/all_to_all | solution.py:219
  109.5 12.9 %collective-permute-start.6 = (bf16[512,128]{1,0:T(8,128)(2,1)S(1)}, bf16[512,128]{1,0:T(8,128)(2,1)S(1)}, u32[]{:S(2)}, u32[]{:S(2)}) collective-permute-start(bf16[512,128]{1,0:T(8,128)(2,1)S(1)} %get-tuple-element.22), channel_id=1, source_target_pairs={{0,16},{16,0},{32,48},{48,32},{1,17},{17,1},{33,49},{49,33},{2,18}... | collective-permute-start | bytes 393224 | tf_op jit(solution)/shard_map/ppermute | solution.py:210
  112.8 13.8 %collective-permute-start.7 = (bf16[512,128]{1,0:T(8,128)(2,1)S(1)}, bf16[512,128]{1,0:T(8,128)(2,1)S(1)}, u32[]{:S(2)}, u32[]{:S(2)}) collective-permute-start(bf16[512,128]{1,0:T(8,128)(2,1)S(1)} %get-tuple-element.21), channel_id=1, source_target_pairs={{0,32},{16,48},{32,0},{48,16},{1,33},{17,49},{33,1},{49,17},{2,34}... | collective-permute-start | bytes 393224 | tf_op jit(solution)/shard_map/ppermute | solution.py:210
  117.5 12.7 %collective-permute-start.8 = (bf16[512,128]{1,0:T(8,128)(2,1)S(1)}, bf16[512,128]{1,0:T(8,128)(2,1)S(1)}, u32[]{:S(2)}, u32[]{:S(2)}) collective-permute-start(bf16[512,128]{1,0:T(8,128)(2,1)S(1)} %get-tuple-element.20), channel_id=1, source_target_pairs={{0,48},{16,32},{32,16},{48,0},{1,49},{17,33},{33,17},{49,1},{2,50}... | collective-permute-start | bytes 393224 | tf_op jit(solution)/shard_map/ppermute | solution.py:210
  131.8 26.3 %collective-permute-start.9 = (bf16[4,512,128]{2,1,0:T(8,128)(2,1)}, bf16[4,512,128]{2,1,0:T(8,128)(2,1)}, u32[]{:S(2)}, u32[]{:S(2)}) collective-permute-start(bf16[4,512,128]{2,1,0:T(8,128)(2,1)} %broadcast_select_fusion), channel_id=1, source_target_pairs={{0,1},{1,0},{2,3},{3,2},{4,5},{5,4},{6,7},{7,6},{8,9},{9,8},{10,11... | collective-permute-start | bytes 1572872 | tf_op jit(solution)/shard_map/ppermute | solution.py:217
  140.8 1.9 %copy-start = (bf16[1,512,2048]{2,1,0:T(8,128)(2,1)S(1)}, bf16[1,512,2048]{2,1,0:T(8,128)(2,1)}, u32[]{:S(2)}) copy-start(bf16[1,512,2048]{2,1,0:T(8,128)(2,1)} %param.14) | copy-start | bytes 6291460
  143.2 1.6 copy-start.3
  143.2 1.6 copy-start.12
  143.8 1.0 copy-start.2
  146.4 11.5 %all-to-all-start.4 = ((bf16[4,256,256]{1,2,0:T(8,128)(2,1)}), bf16[4,256,256]{1,2,0:T(8,128)(2,1)S(1)}, u32[]{:S(2)}, u32[]{:S(2)}) async-start(bf16[4,256,256]{1,2,0:T(8,128)(2,1)} %broadcast_in_dim.101), calls=%async_computation.4 | async-start | bytes 1048576 | tf_op jit(solution)/shard_map/all_to_all | solution.py:233
  160.7 24.3 %all-to-all-start.5 = ((f32[32,8,512]{2,1,0:T(8,128)}), f32[32,8,512]{2,1,0:T(8,128)S(1)}, u32[]{:S(2)}, u32[]{:S(2)}) async-start(f32[32,8,512]{2,1,0:T(8,128)} %convolution_bitcast_fusion), calls=%async_computation.5 | async-start | bytes 1048576 | tf_op jit(solution)/shard_map/all_to_all | solution.py:239

commit v13 on v11

--- a/solution.py
+++ b/solution.py
@@ -183,28 +183,19 @@
         merged = kept_half * scale_kept[None] + other_sum * scale_other[None]
         return merged, joined, row_total * scale_kept + other_total * scale_other
 
-    by_bits = numerator.reshape(2, 2, column_width, query_total)
-    kept_half = jnp.where(core == 1, by_bits[:, 1], by_bits[:, 0]).reshape(2 * column_width, query_total)
-    sent_half = jnp.where(core == 1, by_bits[:, 0], by_bits[:, 1]).reshape(2 * column_width, query_total)
-    numerator, row_max, row_total = merge_level(kept_half, sent_half, 0)
-    by_bits = numerator.reshape(2, column_width, query_total)
+    by_bits = numerator.reshape(2, 2 * column_width, query_total)
     kept_half = jnp.where(upper == 1, by_bits[1], by_bits[0])
     sent_half = jnp.where(upper == 1, by_bits[0], by_bits[1])
     numerator, row_max, row_total = merge_level(kept_half, sent_half, 1)
+    numerator, row_max, row_total = merge_level(numerator, numerator, 0)
     context_columns = (numerator / row_total[None]).astype(jnp.bfloat16)
 
     block_rows = query_total // (group_size)
     chips = nx * ny
     core_rows = chips * block_rows
-    halves = (
-        context_columns.reshape(column_width, chips, nc, block_rows)
-        .transpose(2, 0, 1, 3)
-        .reshape(nc, column_width, core_rows)
-    )
-    mine = lax.dynamic_index_in_dim(halves, core, 0, keepdims=False)
-    theirs = lax.dynamic_index_in_dim(halves, 1 - core, 0, keepdims=False)
-    got = lax.ppermute(theirs, "bc", swap("bc", nc))
-    chip_columns = core_pair(mine, got, core, 0)
+    chip_columns = lax.dynamic_index_in_dim(
+        context_columns.reshape(nc * column_width, chips, nc, block_rows), core, 2, keepdims=False
+    ).reshape(nc * column_width, core_rows)
     outgoing = jnp.broadcast_to(chip_columns[None], (chips,) + chip_columns.shape)
     core_context = lax.all_to_all(outgoing, PLANE, 0, 0, tiled=True).reshape(
         group_size * column_width, core_rows

time: 187 us -> 186 us (level)
    ppermute x1 -> x0, starting transfers between devices: 1.93 us -> none  [local(): got = lax.ppermute(theirs, 'bc', swap('bc', nc))]
  transfers between devices with their start and end apart: 15 -> 14, of which waited for: 13 -> 12; matrix products, arithmetic and copies ran while one was open for 13% -> 13% of each run, Pallas kernels for 0% -> 0%
where the time goes in v13:
time: 186 us; the launch traced here: 185 us
  waiting for transfers between devices  70.3 us (38%)
  starting transfers between devices  58.7 us (32%)
  local copies, waits for them, and re-layouts  23.4 us (13%)
  other arithmetic  12.7 us (7%)
  blocking collectives  11.7 us (6%)
  matrix products  6.1 us (3%)
  between operations  1.94 us (1%)
    all_to_all x1, waiting for transfers between devices, local(): lax.all_to_all(spread, PLANE, 0, 0, tiled=True)  26.1 us
    all_to_all x1, waiting for transfers between devices, local(): lax.all_to_all(mixed_parts.reshape(chips, block_rows, quarter_width), PLA...  15.8 us
    all_to_all x1, blocking collectives, local(): lax.all_to_all(jnp.broadcast_to(inner[None], (nx,) + inner.shape), 'bx',...  11.7 us
    all_to_all x1, starting transfers between devices, local(): lax.all_to_all(jnp.broadcast_to(qkv_flat[None], (reqs,) + qkv_flat.shape)...  10.3 us
    all_to_all x1, starting transfers between devices, local(): lax.all_to_all(outgoing, PLANE, 0, 0, tiled=True)  10.2 us
    ppermute x3, starting transfers between devices, local(): lax.ppermute(lax.dynamic_index_in_dim(own_down, row ^ k, 0, keepdims=Fals...  9.82 us
    ppermute x2, waiting for transfers between devices, from_partner(): lax.ppermute(value, 'by', [(i, i ^ 1 << bit_level - 1) for i in range(ny)])  9.2 us
    all_to_all x1, waiting for transfers between devices, local(): lax.all_to_all(jnp.broadcast_to(qkv_flat[None], (reqs,) + qkv_flat.shape)...  8 us
  transfers between devices with their start and end apart: 14, of which 12 were waited for; matrix products, arithmetic and copies ran while one was open for 13% of the time, Pallas kernels for 0%

profile of v13, /device:TPU:8, one launch (start us, length us, event | category | flops | bytes accessed | tf_op | source)
XLA Modules:
  0.0 184.9 jit_solution(14785565207839963756)
XLA Ops:
  0.6 1.6 broadcast_in_dim.49
  2.2 10.3 %all-to-all-start.1 = ((bf16[8,256,96]{1,2,0:T(8,128)(2,1)}), bf16[8,256,96]{1,2,0:T(8,128)(2,1)}, u32[]{:S(2)}, u32[]{:S(2)}) async-start(bf16[8,256,96]{1,2,0:T(8,128)(2,1)} %broadcast_in_dim.49), calls=%async_computation.1 | async-start | bytes 786432 | tf_op jit(solution)/shard_map/all_to_all | solution.py:94
  12.5 3.7 %copy.93 = bf16[64,8,8,256]{3,2,1,0:T(8,128)(2,1)} copy(bf16[64,8,8,256]{3,1,2,0:T(8,128)(2,1)} %bitcast.129) | data formatting | bytes 4194304
  16.2 1.5 fusion.70
  19.3 8.0 %all-to-all-done.1 = bf16[8,256,96]{1,2,0:T(8,128)(2,1)} async-done(((bf16[8,256,96]{1,2,0:T(8,128)(2,1)}), bf16[8,256,96]{1,2,0:T(8,128)(2,1)}, u32[]{:S(2)}, u32[]{:S(2)}) %all-to-all-start.1) | async-done | bytes 393248 | tf_op jit(solution)/shard_map/all_to_all | solution.py:94
  28.4 3.6 %all-to-all-start = ((bf16[8,256,288]{1,2,0:T(8,128)(2,1)}), bf16[8,256,288]{1,2,0:T(8,128)(2,1)S(1)}, u32[]{:S(2)}, u32[]{:S(2)}) async-start(bf16[8,256,288]{1,2,0:T(8,128)(2,1)} %broadcast_in_dim.47), calls=%async_computation | async-start | bytes 2359296 | tf_op jit(solution)/shard_map/all_to_all | solution.py:53
  32.0 1.8 fusion.15
  33.8 2.5 %collective-permute-start.1 = (bf16[3,32,512]{2,1,0:T(8,128)(2,1)S(1)}, bf16[3,32,512]{2,1,0:T(8,128)(2,1)S(1)}, u32[]{:S(2)}, u32[]{:S(2)}) collective-permute-start(bf16[3,32,512]{2,1,0:T(8,128)(2,1)S(1)} %fusion.15), channel_id=1, source_target_pairs={{0,2},{2,0},{4,6},{6,4},{8,10},{10,8},{12,14},{14,12},{1,3},{3,1},... | collective-permute-start | bytes 294920 | tf_op jit(solution)/shard_map/ppermute | solution.py:136
  37.0 3.4 %collective-permute-done.1 = bf16[3,32,512]{2,1,0:T(8,128)(2,1)S(1)} collective-permute-done((bf16[3,32,512]{2,1,0:T(8,128)(2,1)S(1)}, bf16[3,32,512]{2,1,0:T(8,128)(2,1)S(1)}, u32[]{:S(2)}, u32[]{:S(2)}) %collective-permute-start.1) | collective-permute-done | bytes 98336 | tf_op jit(solution)/shard_map/ppermute | solution.py:136
  40.5 1.9 %collective-permute-start.2 = (bf16[3,2,32,512]{3,2,0,1:T(8,128)(2,1)S(1)}, bf16[3,2,32,512]{3,2,0,1:T(8,128)(2,1)S(1)}, u32[]{:S(2)}, u32[]{:S(2)}) collective-permute-start(bf16[3,2,32,512]{3,2,0,1:T(8,128)(2,1)S(1)} %maximum_select_fusion.10), channel_id=1, source_target_pairs={{0,1},{1,0},{2,3},{3,2},{4,5},{5,4},{6,7},{7,6},{8,9},{9,8},{10,11... | collective-permute-start | bytes 589832 | tf_op jit(solution)/shard_map/ppermute | solution.py:135
  43.0 2.0 %and_reduce_fusion = pred[2048]{0:T(1024)(128)(4,1)S(1)} fusion(s32[1,8192]{1,0:T(1,128)} %param.16, s32[]{:T(128)S(6)} %select_n.153, s32[]{:T(128)} %bitcast.17, s32[]{:T(128)} %bitcast.16, s32[]{:T(128)} %bitcast.128, s32[]{:T(128)S(6)} %mul.153), kind=kLoop, calls=%fused_computation.86 | loop fusion | flops 12288 | bytes 10260 | tf_op jit(solution)/shard_map/and | solution.py:162
  48.5 2.4 %collective-permute-start.3 = (f32[66,512]{1,0:T(8,128)S(1)}, f32[66,512]{1,0:T(8,128)S(1)}, u32[]{:S(2)}, u32[]{:S(2)}) collective-permute-start(f32[66,512]{1,0:T(8,128)S(1)} %pad_maximum_fusion.2), channel_id=1, source_target_pairs={{0,2},{2,0},{4,6},{6,4},{8,10},{10,8},{12,14},{14,12},{1,3},{3,1},... | collective-permute-start | bytes 405512 | tf_op jit(solution)/shard_map/ppermute | solution.py:136
  50.9 5.8 %collective-permute-done.3 = f32[66,512]{1,0:T(8,128)S(1)} collective-permute-done((f32[66,512]{1,0:T(8,128)S(1)}, f32[66,512]{1,0:T(8,128)S(1)}, u32[]{:S(2)}, u32[]{:S(2)}) %collective-permute-start.3) | collective-permute-done | bytes 135200 | tf_op jit(solution)/shard_map/ppermute | solution.py:136
  56.8 1.9 %collective-permute-start.4 = (f32[66,512]{1,0:T(8,128)S(1)}, f32[66,512]{1,0:T(8,128)S(1)}, u32[]{:S(2)}, u32[]{:S(2)}) collective-permute-start(f32[66,512]{1,0:T(8,128)S(1)} %pad_maximum_fusion.3), channel_id=1, source_target_pairs={{0,1},{1,0},{2,3},{3,2},{4,5},{5,4},{6,7},{7,6},{8,9},{9,8},{10,11... | collective-permute-start | bytes 405512 | tf_op jit(solution)/shard_map/ppermute | solution.py:135
  60.3 2.6 %all-to-all-done = bf16[8,256,288]{1,2,0:T(8,128)(2,1)S(1)} async-done(((bf16[8,256,288]{1,2,0:T(8,128)(2,1)}), bf16[8,256,288]{1,2,0:T(8,128)(2,1)S(1)}, u32[]{:S(2)}, u32[]{:S(2)}) %all-to-all-start) | async-done | bytes 1179680 | tf_op jit(solution)/shard_map/all_to_all | solution.py:53
  64.1 10.2 %all-to-all-start.2 = ((bf16[32,64,256]{2,1,0:T(8,128)(2,1)}), bf16[32,64,256]{2,1,0:T(8,128)(2,1)S(1)}, u32[]{:S(2)}, u32[]{:S(2)}) async-start(bf16[32,64,256]{2,1,0:T(8,128)(2,1)} %broadcast_in_dim.101), calls=%async_computation.2 | async-start | bytes 2097152 | tf_op jit(solution)/shard_map/all_to_all | solution.py:200
  75.6 4.6 %collective-permute-start.7 = (bf16[512,128]{1,0:T(8,128)(2,1)S(1)}, bf16[512,128]{1,0:T(8,128)(2,1)S(1)}, u32[]{:S(2)}, u32[]{:S(2)}) collective-permute-start(bf16[512,128]{1,0:T(8,128)(2,1)S(1)} %get-tuple-element.20), channel_id=1, source_target_pairs={{0,48},{16,32},{32,16},{48,0},{1,49},{17,33},{33,17},{49,1},{2,50}... | collective-permute-start | bytes 393224 | tf_op jit(solution)/shard_map/ppermute | solution.py:110
  80.2 2.7 %collective-permute-start.6 = (bf16[512,128]{1,0:T(8,128)(2,1)S(1)}, bf16[512,128]{1,0:T(8,128)(2,1)S(1)}, u32[]{:S(2)}, u32[]{:S(2)}) collective-permute-start(bf16[512,128]{1,0:T(8,128)(2,1)S(1)} %get-tuple-element.21), channel_id=1, source_target_pairs={{0,32},{16,48},{32,0},{48,16},{1,33},{17,49},{33,1},{49,17},{2,34}... | collective-permute-start | bytes 393224 | tf_op jit(solution)/shard_map/ppermute | solution.py:110
  83.0 2.5 %collective-permute-start.5 = (bf16[512,128]{1,0:T(8,128)(2,1)S(1)}, bf16[512,128]{1,0:T(8,128)(2,1)S(1)}, u32[]{:S(2)}, u32[]{:S(2)}) collective-permute-start(bf16[512,128]{1,0:T(8,128)(2,1)S(1)} %get-tuple-element.22), channel_id=1, source_target_pairs={{0,16},{16,0},{32,48},{48,32},{1,17},{17,1},{33,49},{49,33},{2,18}... | collective-permute-start | bytes 393224 | tf_op jit(solution)/shard_map/ppermute | solution.py:110
  86.4 1.9 %collective-permute-start = (bf16[2048,160]{0,1:T(8,128)(2,1)}, bf16[2048,160]{0,1:T(8,128)(2,1)}, u32[]{:S(2)}, u32[]{:S(2)}) collective-permute-start(bf16[2048,160]{0,1:T(8,128)(2,1)} %slice.124), channel_id=1, source_target_pairs={{0,1},{1,0},{2,3},{3,2},{4,5},{5,4},{6,7},{7,6},{8,9},{9,8},{10,11... | collective-permute-start | bytes 1966088 | tf_op jit(solution)/shard_map/ppermute | solution.py:99
  88.3 2.4 %collective-permute-done.7 = bf16[512,128]{1,0:T(8,128)(2,1)S(1)} collective-permute-done((bf16[512,128]{1,0:T(8,128)(2,1)S(1)}, bf16[512,128]{1,0:T(8,128)(2,1)S(1)}, u32[]{:S(2)}, u32[]{:S(2)}) %collective-permute-start.7) | collective-permute-done | bytes 131104 | tf_op jit(solution)/shard_map/ppermute | solution.py:110
  93.1 1.9 %collective-permute-start.8 = (bf16[4,512,128]{2,1,0:T(8,128)(2,1)S(1)}, bf16[4,512,128]{2,1,0:T(8,128)(2,1)}, u32[]{:S(2)}, u32[]{:S(2)}) collective-permute-start(bf16[4,512,128]{2,1,0:T(8,128)(2,1)S(1)} %broadcast_select_fusion), channel_id=1, source_target_pairs={{0,1},{1,0},{2,3},{3,2},{4,5},{5,4},{6,7},{7,6},{8,9},{9,8},{10,11... | collective-permute-start | bytes 1572872 | tf_op jit(solution)/shard_map/ppermute | solution.py:117
  98.4 2.6 %all-to-all-done.2 = bf16[32,64,256]{2,1,0:T(8,128)(2,1)S(1)} async-done(((bf16[32,64,256]{2,1,0:T(8,128)(2,1)}), bf16[32,64,256]{2,1,0:T(8,128)(2,1)S(1)}, u32[]{:S(2)}, u32[]{:S(2)}) %all-to-all-start.2) | async-done | bytes 1048608 | tf_op jit(solution)/shard_map/all_to_all | solution.py:200
  102.4 7.7 %all-to-all-start.3 = ((bf16[32,64,256]{2,1,0:T(8,128)(2,1)}), bf16[32,64,256]{2,1,0:T(8,128)(2,1)S(1)}, u32[]{:S(2)}, u32[]{:S(2)}) async-start(bf16[32,64,256]{2,1,0:T(8,128)(2,1)} %broadcast_in_dim.102), calls=%async_computation.3 | async-start | bytes 2097152 | tf_op jit(solution)/shard_map/all_to_all | solution.py:211
  110.9 1.9 %slice.139 = bf16[2048,128]{0,1:T(8,128)(2,1)} slice(bf16[2048,160]{0,1:T(8,128)(2,1)} %collective-permute-done), slice={[0:2048], [32:160]} | slice | bytes 1048576 | tf_op jit(solution)/shard_map/slice | solution.py:101
  112.8 26.1 %all-to-all-done.3 = bf16[32,64,256]{2,1,0:T(8,128)(2,1)S(1)} async-done(((bf16[32,64,256]{2,1,0:T(8,128)(2,1)}), bf16[32,64,256]{2,1,0:T(8,128)(2,1)S(1)}, u32[]{:S(2)}, u32[]{:S(2)}) %all-to-all-start.3) | async-done | bytes 1048608 | tf_op jit(solution)/shard_map/all_to_all | solution.py:211
  138.8 1.6 bitcast_convert_fusion
  140.4 1.9 %copy.80 = f32[2048,256]{0,1:T(8,128)S(1)} copy(f32[2048,256]{1,0:T(8,128)} %bitcast_convert_fusion) | data formatting | bytes 4194304 | tf_op jit(solution)/shard_map/convert_element_type | solution.py:215
  142.3 1.7 fusion.32
  147.1 11.7 %all_to_all.30 = bf16[4,256,256]{1,2,0:T(8,128)(2,1)S(1)} all-to-all(bf16[4,256,256]{1,2,0:T(8,128)(2,1)S(1)} %broadcast_in_dim.108), channel_id=1, replica_groups=mesh['req'=8,'bx'=4,'by'=8,'bc'=2] {'bx'}, dimensions={0} | all-to-all | bytes 1048576 | tf_op jit(solution)/shard_map/all_to_all | solution.py:225
  160.4 4.6 %all-to-all-start.5 = ((f32[32,8,512]{2,1,0:T(8,128)}), f32[32,8,512]{2,1,0:T(8,128)S(1)}, u32[]{:S(2)}, u32[]{:S(2)}) async-start(f32[32,8,512]{2,1,0:T(8,128)} %convolution_bitcast_fusion), calls=%async_computation.5 | async-start | bytes 1048576 | tf_op jit(solution)/shard_map/all_to_all | solution.py:231
  165.7 15.8 %all-to-all-done.5 = f32[32,8,512]{2,1,0:T(8,128)S(1)} async-done(((f32[32,8,512]{2,1,0:T(8,128)}), f32[32,8,512]{2,1,0:T(8,128)S(1)}, u32[]{:S(2)}, u32[]{:S(2)}) %all-to-all-start.5) | async-done | bytes 524320 | tf_op jit(solution)/shard_map/all_to_all | solution.py:231
  (106 shorter events, 28.2 us)
Async XLA Ops:
  2.2 25.1 %all-to-all-start.1 = ((bf16[8,256,96]{1,2,0:T(8,128)(2,1)}), bf16[8,256,96]{1,2,0:T(8,128)(2,1)}, u32[]{:S(2)}, u32[]{:S(2)}) async-start(bf16[8,256,96]{1,2,0:T(8,128)(2,1)} %broadcast_in_dim.49), calls=%async_computation.1 | async-start | bytes 786432 | tf_op jit(solution)/shard_map/all_to_all | solution.py:94
  12.5 3.7 %copy-start.1 = (bf16[1,1,2048,2,128]{4,3,2,1,0:T(2,128)(2,1)S(1)}, bf16[1,1,2048,2,128]{4,3,2,1,0:T(2,128)(2,1)}, u32[]{:S(2)}) copy-start(bf16[1,1,2048,2,128]{4,3,2,1,0:T(2,128)(2,1)} %param.15) | copy-start | bytes 3145732
  16.2 1.5 copy-start.10
  16.2 1.7 copy-start.8
  16.2 1.7 copy-start.9
  19.3 12.7 %copy-start.2 = (bf16[64,8,8,256]{3,2,1,0:T(8,128)(2,1)S(1)}, bf16[64,8,8,256]{3,2,1,0:T(8,128)(2,1)}, u32[]{:S(2)}) copy-start(bf16[64,8,8,256]{3,2,1,0:T(8,128)(2,1)} %copy.93) | copy-start | bytes 6291460
  19.3 12.7 %copy-start.15 = (f32[3,32]{1,0:T(4,128)S(1)}, f32[3,32]{1,0:T(4,128)}, u32[]{:S(2)}) copy-start(f32[3,32]{1,0:T(4,128)} %param.20) | copy-start | bytes 1156
  28.4 34.5 %all-to-all-start = ((bf16[8,256,288]{1,2,0:T(8,128)(2,1)}), bf16[8,256,288]{1,2,0:T(8,128)(2,1)S(1)}, u32[]{:S(2)}, u32[]{:S(2)}) async-start(bf16[8,256,288]{1,2,0:T(8,128)(2,1)} %broadcast_in_dim.47), calls=%async_computation | async-start | bytes 2359296 | tf_op jit(solution)/shard_map/all_to_all | solution.py:53
  32.0 10.4 %copy-start.14 = (s32[1,2]{1,0:T(1,128)S(1)}, s32[1,2]{1,0:T(1,128)}, u32[]{:S(2)}) copy-start(s32[1,2]{1,0:T(1,128)} %param.18) | copy-start | bytes 28
  33.8 11.6 %copy-start.7 = (bf16[2048,128]{1,0:T(8,128)(2,1)S(1)}, bf16[2048,128]{1,0:T(8,128)(2,1)}, u32[]{:S(2)}) copy-start(bf16[2048,128]{1,0:T(8,128)(2,1)} %get-tuple-element.38) | copy-start | bytes 1572868
  33.8 6.6 %collective-permute-start.1 = (bf16[3,32,512]{2,1,0:T(8,128)(2,1)S(1)}, bf16[3,32,512]{2,1,0:T(8,128)(2,1)S(1)}, u32[]{:S(2)}, u32[]{:S(2)}) collective-permute-start(bf16[3,32,512]{2,1,0:T(8,128)(2,1)S(1)} %fusion.15), channel_id=1, source_target_pairs={{0,2},{2,0},{4,6},{6,4},{8,10},{10,8},{12,14},{14,12},{1,3},{3,1},... | collective-permute-start | bytes 294920 | tf_op jit(solution)/shard_map/ppermute | solution.py:136
  40.5 4.6 %collective-permute-start.2 = (bf16[3,2,32,512]{3,2,0,1:T(8,128)(2,1)S(1)}, bf16[3,2,32,512]{3,2,0,1:T(8,128)(2,1)S(1)}, u32[]{:S(2)}, u32[]{:S(2)}) collective-permute-start(bf16[3,2,32,512]{3,2,0,1:T(8,128)(2,1)S(1)} %maximum_select_fusion.10), channel_id=1, source_target_pairs={{0,1},{1,0},{2,3},{3,2},{4,5},{5,4},{6,7},{7,6},{8,9},{9,8},{10,11... | collective-permute-start | bytes 589832 | tf_op jit(solution)/shard_map/ppermute | solution.py:135
  45.5 1.1 copy-start.6
  48.5 8.1 %collective-permute-start.3 = (f32[66,512]{1,0:T(8,128)S(1)}, f32[66,512]{1,0:T(8,128)S(1)}, u32[]{:S(2)}, u32[]{:S(2)}) collective-permute-start(f32[66,512]{1,0:T(8,128)S(1)} %pad_maximum_fusion.2), channel_id=1, source_target_pairs={{0,2},{2,0},{4,6},{6,4},{8,10},{10,8},{12,14},{14,12},{1,3},{3,1},... | collective-permute-start | bytes 405512 | tf_op jit(solution)/shard_map/ppermute | solution.py:136
  56.8 3.3 %collective-permute-start.4 = (f32[66,512]{1,0:T(8,128)S(1)}, f32[66,512]{1,0:T(8,128)S(1)}, u32[]{:S(2)}, u32[]{:S(2)}) collective-permute-start(f32[66,512]{1,0:T(8,128)S(1)} %pad_maximum_fusion.3), channel_id=1, source_target_pairs={{0,1},{1,0},{2,3},{3,2},{4,5},{5,4},{6,7},{7,6},{8,9},{9,8},{10,11... | collective-permute-start | bytes 405512 | tf_op jit(solution)/shard_map/ppermute | solution.py:135
  64.1 36.9 %all-to-all-start.2 = ((bf16[32,64,256]{2,1,0:T(8,128)(2,1)}), bf16[32,64,256]{2,1,0:T(8,128)(2,1)S(1)}, u32[]{:S(2)}, u32[]{:S(2)}) async-start(bf16[32,64,256]{2,1,0:T(8,128)(2,1)} %broadcast_in_dim.101), calls=%async_computation.2 | async-start | bytes 2097152 | tf_op jit(solution)/shard_map/all_to_all | solution.py:200
  75.6 15.1 %collective-permute-start.7 = (bf16[512,128]{1,0:T(8,128)(2,1)S(1)}, bf16[512,128]{1,0:T(8,128)(2,1)S(1)}, u32[]{:S(2)}, u32[]{:S(2)}) collective-permute-start(bf16[512,128]{1,0:T(8,128)(2,1)S(1)} %get-tuple-element.20), channel_id=1, source_target_pairs={{0,48},{16,32},{32,16},{48,0},{1,49},{17,33},{33,17},{49,1},{2,50}... | collective-permute-start | bytes 393224 | tf_op jit(solution)/shard_map/ppermute | solution.py:110
  80.2 11.2 %collective-permute-start.6 = (bf16[512,128]{1,0:T(8,128)(2,1)S(1)}, bf16[512,128]{1,0:T(8,128)(2,1)S(1)}, u32[]{:S(2)}, u32[]{:S(2)}) collective-permute-start(bf16[512,128]{1,0:T(8,128)(2,1)S(1)} %get-tuple-element.21), channel_id=1, source_target_pairs={{0,32},{16,48},{32,0},{48,16},{1,33},{17,49},{33,1},{49,17},{2,34}... | collective-permute-start | bytes 393224 | tf_op jit(solution)/shard_map/ppermute | solution.py:110
  83.0 9.3 %collective-permute-start.5 = (bf16[512,128]{1,0:T(8,128)(2,1)S(1)}, bf16[512,128]{1,0:T(8,128)(2,1)S(1)}, u32[]{:S(2)}, u32[]{:S(2)}) collective-permute-start(bf16[512,128]{1,0:T(8,128)(2,1)S(1)} %get-tuple-element.22), channel_id=1, source_target_pairs={{0,16},{16,0},{32,48},{48,32},{1,17},{17,1},{33,49},{49,33},{2,18}... | collective-permute-start | bytes 393224 | tf_op jit(solution)/shard_map/ppermute | solution.py:110
  85.5 9.5 %copy-start.11 = (f32[2,2048]{1,0:T(2,128)S(1)}, f32[2,2048]{1,0:T(2,128)}, u32[]{:S(2)}) copy-start(f32[2,2048]{1,0:T(2,128)} %param.25) | copy-start | bytes 49156
  86.4 8.9 %collective-permute-start = (bf16[2048,160]{0,1:T(8,128)(2,1)}, bf16[2048,160]{0,1:T(8,128)(2,1)}, u32[]{:S(2)}, u32[]{:S(2)}) collective-permute-start(bf16[2048,160]{0,1:T(8,128)(2,1)} %slice.124), channel_id=1, source_target_pairs={{0,1},{1,0},{2,3},{3,2},{4,5},{5,4},{6,7},{7,6},{8,9},{9,8},{10,11... | collective-permute-start | bytes 1966088 | tf_op jit(solution)/shard_map/ppermute | solution.py:99
  93.1 3.9 %collective-permute-start.8 = (bf16[4,512,128]{2,1,0:T(8,128)(2,1)S(1)}, bf16[4,512,128]{2,1,0:T(8,128)(2,1)}, u32[]{:S(2)}, u32[]{:S(2)}) collective-permute-start(bf16[4,512,128]{2,1,0:T(8,128)(2,1)S(1)} %broadcast_select_fusion), channel_id=1, source_target_pairs={{0,1},{1,0},{2,3},{3,2},{4,5},{5,4},{6,7},{7,6},{8,9},{9,8},{10,11... | collective-permute-start | bytes 1572872 | tf_op jit(solution)/shard_map/ppermute | solution.py:117
  100.9 9.9 %copy-start.12 = (f32[2,2048]{1,0:T(2,128)S(1)}, f32[2,2048]{1,0:T(2,128)}, u32[]{:S(2)}) copy-start(f32[2,2048]{1,0:T(2,128)} %param.27) | copy-start | bytes 49156
  100.9 9.9 %copy-start.13 = (f32[2,2048]{1,0:T(2,128)S(1)}, f32[2,2048]{1,0:T(2,128)}, u32[]{:S(2)}) copy-start(f32[2,2048]{1,0:T(2,128)} %param.26) | copy-start | bytes 49156
  102.4 36.5 %all-to-all-start.3 = ((bf16[32,64,256]{2,1,0:T(8,128)(2,1)}), bf16[32,64,256]{2,1,0:T(8,128)(2,1)S(1)}, u32[]{:S(2)}, u32[]{:S(2)}) async-start(bf16[32,64,256]{2,1,0:T(8,128)(2,1)} %broadcast_in_dim.102), calls=%async_computation.3 | async-start | bytes 2097152 | tf_op jit(solution)/shard_map/all_to_all | solution.py:211
  142.3 1.9 %copy-start = (bf16[1,512,2048]{2,1,0:T(8,128)(2,1)S(1)}, bf16[1,512,2048]{2,1,0:T(8,128)(2,1)}, u32[]{:S(2)}) copy-start(bf16[1,512,2048]{2,1,0:T(8,128)(2,1)} %param.14) | copy-start | bytes 6291460
  144.7 1.6 copy-start.4
  144.7 1.6 copy-start.5
  145.3 1.0 copy-start.3
  160.4 21.1 %all-to-all-start.5 = ((f32[32,8,512]{2,1,0:T(8,128)}), f32[32,8,512]{2,1,0:T(8,128)S(1)}, u32[]{:S(2)}, u32[]{:S(2)}) async-start(f32[32,8,512]{2,1,0:T(8,128)} %convolution_bitcast_fusion), calls=%async_computation.5 | async-start | bytes 1048576 | tf_op jit(solution)/shard_map/all_to_all | solution.py:231

commit v14 on v13

--- a/solution.py
+++ b/solution.py
@@ -136,21 +136,36 @@
         return lax.ppermute(value, "by", [(i, i ^ (1 << (bit_level - 1))) for i in range(ny)])
 
     upper = group_index >> 1 & 1
-    partner = from_partner(qkv_columns, 1)
-    head_qkv = jnp.where(
-        upper == 1,
-        jnp.stack([partner, qkv_columns], axis=1),
-        jnp.stack([qkv_columns, partner], axis=1),
-    )
-    partner = from_partner(head_qkv, 0)
-    head_qkv = jnp.where(
-        core == 1, jnp.stack([partner, head_qkv], axis=2), jnp.stack([head_qkv, partner], axis=2)
-    ).reshape(3, groups * column_width, query_total)
-    queries = head_qkv[0].T
-    fresh_count = query_total // groups
+    quarter = query_total // groups
+    chip_tokens = 2 * quarter
+
+    def packed(q_part, kv_part):
+        kv_flat = jnp.swapaxes(kv_part, -3, -2)
+        kv_flat = kv_flat.reshape(kv_flat.shape[:-2] + (-1,))
+        return jnp.concatenate([q_part, kv_flat], axis=-1)
+
+    own_kv = qkv_columns[1:]
+    got = from_partner(
+        packed(qkv_columns[0], lax.dynamic_slice_in_dim(own_kv, (1 - upper) * chip_tokens, chip_tokens, 2)), 1
+    )
+    mine_kv = lax.dynamic_slice_in_dim(own_kv, upper * chip_tokens, chip_tokens, 2)
+    got_kv = jnp.swapaxes(got[:, query_total:].reshape(column_width, 2, chip_tokens), 0, 1)
+    q2 = jnp.where(
+        upper == 1, jnp.stack([got[:, :query_total], qkv_columns[0]]), jnp.stack([qkv_columns[0], got[:, :query_total]])
+    )
+    kv2 = jnp.where(upper == 1, jnp.stack([got_kv, mine_kv]), jnp.stack([mine_kv, got_kv]))
+    got = from_partner(packed(q2, lax.dynamic_slice_in_dim(kv2, (1 - core) * quarter, quarter, 3)), 0)
+    sibling_q = got[:, :, :query_total]
+    sibling_kv = jnp.swapaxes(got[:, :, query_total:].reshape(2, column_width, 2, quarter), 1, 2)
+    mine_kv = lax.dynamic_slice_in_dim(kv2, core * quarter, quarter, 3)
+    q4 = jnp.where(core == 1, jnp.stack([sibling_q, q2], 1), jnp.stack([q2, sibling_q], 1))
+    kv4 = jnp.where(core == 1, jnp.stack([sibling_kv, mine_kv], 1), jnp.stack([mine_kv, sibling_kv], 1))
+    queries = q4.reshape(groups * column_width, query_total).T
+    head_kv = kv4.transpose(2, 0, 1, 3, 4).reshape(2, groups * column_width, quarter)
+    fresh_count = quarter
+    fresh_keys = head_kv[0].T
+    fresh_values = head_kv[1].T
     fresh_start = group_index * fresh_count
-    fresh_keys = lax.dynamic_slice_in_dim(head_qkv[1], fresh_start, fresh_count, 1).T
-    fresh_values = lax.dynamic_slice_in_dim(head_qkv[2], fresh_start, fresh_count, 1).T
     cache_count = cache_entries.shape[2]
     cache_keys = cache_entries[0, 0, :, 0]
     cache_values = cache_entries[0, 0, :, 1]

time: 186 us -> 186 us (level)
    ppermute x2, waiting for transfers between devices: 9.2 us -> 6.59 us  [from_partner(): lax.ppermute(value, 'by', [(i, i ^ 1 << bit_level - 1) for i in range(ny)])]
    unnamed x36 -> x34, local copies, waits for them, and re-layouts: 5.32 us -> 5.12 us
  transfers between devices with their start and end apart: 14 -> 14, of which waited for: 12 -> 13; matrix products, arithmetic and copies ran while one was open for 13% -> 13% of each run, Pallas kernels for 0% -> 0%
where the time goes in v14:
time: 186 us; the launch traced here: 185 us
  waiting for transfers between devices  70.3 us (38%)
  starting transfers between devices  58.6 us (32%)
  local copies, waits for them, and re-layouts  23.5 us (13%)
  other arithmetic  12.7 us (7%)
  blocking collectives  11.7 us (6%)
  matrix products  6.1 us (3%)
  between operations  2 us (1%)
    all_to_all x1, waiting for transfers between devices, local(): lax.all_to_all(spread, PLANE, 0, 0, tiled=True)  26.1 us
    all_to_all x1, waiting for transfers between devices, local(): lax.all_to_all(mixed_parts.reshape(chips, block_rows, quarter_width), PLA...  16.4 us
    all_to_all x1, blocking collectives, local(): lax.all_to_all(jnp.broadcast_to(inner[None], (nx,) + inner.shape), 'bx',...  11.7 us
    all_to_all x1, starting transfers between devices, local(): lax.all_to_all(jnp.broadcast_to(qkv_flat[None], (reqs,) + qkv_flat.shape)...  10.3 us
    all_to_all x1, starting transfers between devices, local(): lax.all_to_all(outgoing, PLANE, 0, 0, tiled=True)  10.2 us
    ppermute x3, starting transfers between devices, local(): lax.ppermute(lax.dynamic_index_in_dim(own_down, row ^ k, 0, keepdims=Fals...  9.82 us
    all_to_all x1, starting transfers between devices, local(): lax.all_to_all(spread, PLANE, 0, 0, tiled=True)  7.7 us
    all_to_all x1, waiting for transfers between devices, local(): lax.all_to_all(jnp.broadcast_to(qkv_flat[None], (reqs,) + qkv_flat.shape)...  7.29 us
  transfers between devices with their start and end apart: 14, of which 13 were waited for; matrix products, arithmetic and copies ran while one was open for 13% of the time, Pallas kernels for 0%

profile of v14, /device:TPU:8, one launch (start us, length us, event | category | flops | bytes accessed | tf_op | source)
XLA Modules:
  0.0 184.9 jit_solution(17393759440956643132)
XLA Ops:
  0.6 1.6 broadcast_in_dim.49
  2.2 10.3 %all-to-all-start.1 = ((bf16[8,256,96]{1,2,0:T(8,128)(2,1)}), bf16[8,256,96]{1,2,0:T(8,128)(2,1)}, u32[]{:S(2)}, u32[]{:S(2)}) async-start(bf16[8,256,96]{1,2,0:T(8,128)(2,1)} %broadcast_in_dim.49), calls=%async_computation.1 | async-start | bytes 786432 | tf_op jit(solution)/shard_map/all_to_all | solution.py:94
  12.5 3.7 %copy.130 = bf16[64,8,8,256]{3,2,1,0:T(8,128)(2,1)} copy(bf16[64,8,8,256]{3,1,2,0:T(8,128)(2,1)} %bitcast.168) | data formatting | bytes 4194304
  16.2 1.5 fusion.71
  20.0 7.3 %all-to-all-done.1 = bf16[8,256,96]{1,2,0:T(8,128)(2,1)} async-done(((bf16[8,256,96]{1,2,0:T(8,128)(2,1)}), bf16[8,256,96]{1,2,0:T(8,128)(2,1)}, u32[]{:S(2)}, u32[]{:S(2)}) %all-to-all-start.1) | async-done | bytes 393248 | tf_op jit(solution)/shard_map/all_to_all | solution.py:94
  28.4 3.6 %all-to-all-start = ((bf16[8,256,288]{1,2,0:T(8,128)(2,1)}), bf16[8,256,288]{1,2,0:T(8,128)(2,1)S(1)}, u32[]{:S(2)}, u32[]{:S(2)}) async-start(bf16[8,256,288]{1,2,0:T(8,128)(2,1)} %broadcast_in_dim.47), calls=%async_computation | async-start | bytes 2359296 | tf_op jit(solution)/shard_map/all_to_all | solution.py:53
  32.0 1.8 fusion.15
  34.5 2.4 %collective-permute-start.1 = (bf16[32,1024]{1,0:T(8,128)(2,1)S(1)}, bf16[32,1024]{1,0:T(8,128)(2,1)S(1)}, u32[]{:S(2)}, u32[]{:S(2)}) collective-permute-start(bf16[32,1024]{1,0:T(8,128)(2,1)S(1)} %pad_maximum_fusion.5), channel_id=1, source_target_pairs={{0,2},{2,0},{4,6},{6,4},{8,10},{10,8},{12,14},{14,12},{1,3},{3,1},... | collective-permute-start | bytes 196616 | tf_op jit(solution)/shard_map/ppermute | solution.py:136
  37.5 2.0 %and_reduce_fusion = pred[2048]{0:T(1024)(128)(4,1)S(1)} fusion(s32[1,8192]{1,0:T(1,128)} %param.16, s32[]{:T(128)S(6)} %select_n.184, s32[]{:T(128)} %bitcast.25, s32[]{:T(128)} %bitcast.24, s32[]{:T(128)} %bitcast.167, s32[]{:T(128)S(6)} %mul.168), kind=kLoop, calls=%fused_computation.99 | loop fusion | flops 12288 | bytes 10260 | tf_op jit(solution)/shard_map/and | solution.py:177
  40.8 1.9 %collective-permute-start.2 = (bf16[2,32,768]{2,1,0:T(8,128)(2,1)S(1)}, bf16[2,32,768]{2,1,0:T(8,128)(2,1)S(1)}, u32[]{:S(2)}, u32[]{:S(2)}) collective-permute-start(bf16[2,32,768]{2,1,0:T(8,128)(2,1)S(1)} %pad_maximum_fusion.4), channel_id=1, source_target_pairs={{0,1},{1,0},{2,3},{3,2},{4,5},{5,4},{6,7},{7,6},{8,9},{9,8},{10,11... | collective-permute-start | bytes 294920 | tf_op jit(solution)/shard_map/ppermute | solution.py:135
  47.4 2.4 %collective-permute-start.3 = (f32[66,512]{1,0:T(8,128)S(1)}, f32[66,512]{1,0:T(8,128)S(1)}, u32[]{:S(2)}, u32[]{:S(2)}) collective-permute-start(f32[66,512]{1,0:T(8,128)S(1)} %pad_maximum_fusion.2), channel_id=1, source_target_pairs={{0,2},{2,0},{4,6},{6,4},{8,10},{10,8},{12,14},{14,12},{1,3},{3,1},... | collective-permute-start | bytes 405512 | tf_op jit(solution)/shard_map/ppermute | solution.py:136
  49.8 5.4 %collective-permute-done.3 = f32[66,512]{1,0:T(8,128)S(1)} collective-permute-done((f32[66,512]{1,0:T(8,128)S(1)}, f32[66,512]{1,0:T(8,128)S(1)}, u32[]{:S(2)}, u32[]{:S(2)}) %collective-permute-start.3) | collective-permute-done | bytes 135200 | tf_op jit(solution)/shard_map/ppermute | solution.py:136
  55.3 1.9 %collective-permute-start.4 = (f32[66,512]{1,0:T(8,128)S(1)}, f32[66,512]{1,0:T(8,128)S(1)}, u32[]{:S(2)}, u32[]{:S(2)}) collective-permute-start(f32[66,512]{1,0:T(8,128)S(1)} %pad_maximum_fusion.3), channel_id=1, source_target_pairs={{0,1},{1,0},{2,3},{3,2},{4,5},{5,4},{6,7},{7,6},{8,9},{9,8},{10,11... | collective-permute-start | bytes 405512 | tf_op jit(solution)/shard_map/ppermute | solution.py:135
  58.8 4.1 %all-to-all-done = bf16[8,256,288]{1,2,0:T(8,128)(2,1)S(1)} async-done(((bf16[8,256,288]{1,2,0:T(8,128)(2,1)}), bf16[8,256,288]{1,2,0:T(8,128)(2,1)S(1)}, u32[]{:S(2)}, u32[]{:S(2)}) %all-to-all-start) | async-done | bytes 1179680 | tf_op jit(solution)/shard_map/all_to_all | solution.py:53
  64.1 10.2 %all-to-all-start.2 = ((bf16[32,64,256]{2,1,0:T(8,128)(2,1)}), bf16[32,64,256]{2,1,0:T(8,128)(2,1)S(1)}, u32[]{:S(2)}, u32[]{:S(2)}) async-start(bf16[32,64,256]{2,1,0:T(8,128)(2,1)} %broadcast_in_dim.101), calls=%async_computation.2 | async-start | bytes 2097152 | tf_op jit(solution)/shard_map/all_to_all | solution.py:215
  75.6 4.6 %collective-permute-start.7 = (bf16[512,128]{1,0:T(8,128)(2,1)S(1)}, bf16[512,128]{1,0:T(8,128)(2,1)S(1)}, u32[]{:S(2)}, u32[]{:S(2)}) collective-permute-start(bf16[512,128]{1,0:T(8,128)(2,1)S(1)} %get-tuple-element.20), channel_id=1, source_target_pairs={{0,48},{16,32},{32,16},{48,0},{1,49},{17,33},{33,17},{49,1},{2,50}... | collective-permute-start | bytes 393224 | tf_op jit(solution)/shard_map/ppermute | solution.py:110
  80.3 2.7 %collective-permute-start.6 = (bf16[512,128]{1,0:T(8,128)(2,1)S(1)}, bf16[512,128]{1,0:T(8,128)(2,1)S(1)}, u32[]{:S(2)}, u32[]{:S(2)}) collective-permute-start(bf16[512,128]{1,0:T(8,128)(2,1)S(1)} %get-tuple-element.21), channel_id=1, source_target_pairs={{0,32},{16,48},{32,0},{48,16},{1,33},{17,49},{33,1},{49,17},{2,34}... | collective-permute-start | bytes 393224 | tf_op jit(solution)/shard_map/ppermute | solution.py:110
  83.0 2.5 %collective-permute-start.5 = (bf16[512,128]{1,0:T(8,128)(2,1)S(1)}, bf16[512,128]{1,0:T(8,128)(2,1)S(1)}, u32[]{:S(2)}, u32[]{:S(2)}) collective-permute-start(bf16[512,128]{1,0:T(8,128)(2,1)S(1)} %get-tuple-element.22), channel_id=1, source_target_pairs={{0,16},{16,0},{32,48},{48,32},{1,17},{17,1},{33,49},{49,33},{2,18}... | collective-permute-start | bytes 393224 | tf_op jit(solution)/shard_map/ppermute | solution.py:110
  86.4 1.9 %collective-permute-start = (bf16[2048,160]{0,1:T(8,128)(2,1)}, bf16[2048,160]{0,1:T(8,128)(2,1)}, u32[]{:S(2)}, u32[]{:S(2)}) collective-permute-start(bf16[2048,160]{0,1:T(8,128)(2,1)} %slice.143), channel_id=1, source_target_pairs={{0,1},{1,0},{2,3},{3,2},{4,5},{5,4},{6,7},{7,6},{8,9},{9,8},{10,11... | collective-permute-start | bytes 1966088 | tf_op jit(solution)/shard_map/ppermute | solution.py:99
  88.3 2.4 %collective-permute-done.7 = bf16[512,128]{1,0:T(8,128)(2,1)S(1)} collective-permute-done((bf16[512,128]{1,0:T(8,128)(2,1)S(1)}, bf16[512,128]{1,0:T(8,128)(2,1)S(1)}, u32[]{:S(2)}, u32[]{:S(2)}) %collective-permute-start.7) | collective-permute-done | bytes 131104 | tf_op jit(solution)/shard_map/ppermute | solution.py:110
  93.1 1.9 %collective-permute-start.8 = (bf16[4,512,128]{2,1,0:T(8,128)(2,1)S(1)}, bf16[4,512,128]{2,1,0:T(8,128)(2,1)}, u32[]{:S(2)}, u32[]{:S(2)}) collective-permute-start(bf16[4,512,128]{2,1,0:T(8,128)(2,1)S(1)} %broadcast_select_fusion), channel_id=1, source_target_pairs={{0,1},{1,0},{2,3},{3,2},{4,5},{5,4},{6,7},{7,6},{8,9},{9,8},{10,11... | collective-permute-start | bytes 1572872 | tf_op jit(solution)/shard_map/ppermute | solution.py:117
  98.4 2.6 %all-to-all-done.2 = bf16[32,64,256]{2,1,0:T(8,128)(2,1)S(1)} async-done(((bf16[32,64,256]{2,1,0:T(8,128)(2,1)}), bf16[32,64,256]{2,1,0:T(8,128)(2,1)S(1)}, u32[]{:S(2)}, u32[]{:S(2)}) %all-to-all-start.2) | async-done | bytes 1048608 | tf_op jit(solution)/shard_map/all_to_all | solution.py:215
  102.4 7.7 %all-to-all-start.3 = ((bf16[32,64,256]{2,1,0:T(8,128)(2,1)}), bf16[32,64,256]{2,1,0:T(8,128)(2,1)S(1)}, u32[]{:S(2)}, u32[]{:S(2)}) async-start(bf16[32,64,256]{2,1,0:T(8,128)(2,1)} %broadcast_in_dim.102), calls=%async_computation.3 | async-start | bytes 2097152 | tf_op jit(solution)/shard_map/all_to_all | solution.py:226
  110.9 1.9 %slice.163 = bf16[2048,128]{0,1:T(8,128)(2,1)} slice(bf16[2048,160]{0,1:T(8,128)(2,1)} %collective-permute-done), slice={[0:2048], [32:160]} | slice | bytes 1048576 | tf_op jit(solution)/shard_map/slice | solution.py:101
  112.8 26.1 %all-to-all-done.3 = bf16[32,64,256]{2,1,0:T(8,128)(2,1)S(1)} async-done(((bf16[32,64,256]{2,1,0:T(8,128)(2,1)}), bf16[32,64,256]{2,1,0:T(8,128)(2,1)S(1)}, u32[]{:S(2)}, u32[]{:S(2)}) %all-to-all-start.3) | async-done | bytes 1048608 | tf_op jit(solution)/shard_map/all_to_all | solution.py:226
  138.9 1.6 bitcast_convert_fusion
  140.5 1.9 %copy.115 = f32[2048,256]{0,1:T(8,128)S(1)} copy(f32[2048,256]{1,0:T(8,128)} %bitcast_convert_fusion) | data formatting | bytes 4194304 | tf_op jit(solution)/shard_map/convert_element_type | solution.py:230
  142.4 1.7 fusion.32
  147.2 11.7 %all_to_all.30 = bf16[4,256,256]{1,2,0:T(8,128)(2,1)S(1)} all-to-all(bf16[4,256,256]{1,2,0:T(8,128)(2,1)S(1)} %broadcast_in_dim.108), channel_id=1, replica_groups=mesh['req'=8,'bx'=4,'by'=8,'bc'=2] {'bx'}, dimensions={0} | all-to-all | bytes 1048576 | tf_op jit(solution)/shard_map/all_to_all | solution.py:240
  160.5 4.6 %all-to-all-start.5 = ((f32[32,8,512]{2,1,0:T(8,128)}), f32[32,8,512]{2,1,0:T(8,128)S(1)}, u32[]{:S(2)}, u32[]{:S(2)}) async-start(f32[32,8,512]{2,1,0:T(8,128)} %convolution_bitcast_fusion), calls=%async_computation.5 | async-start | bytes 1048576 | tf_op jit(solution)/shard_map/all_to_all | solution.py:246
  165.1 16.4 %all-to-all-done.5 = f32[32,8,512]{2,1,0:T(8,128)S(1)} async-done(((f32[32,8,512]{2,1,0:T(8,128)}), f32[32,8,512]{2,1,0:T(8,128)S(1)}, u32[]{:S(2)}, u32[]{:S(2)}) %all-to-all-start.5) | async-done | bytes 524320 | tf_op jit(solution)/shard_map/all_to_all | solution.py:246
  183.5 1.5 fusion.54
  (120 shorter events, 29.2 us)
Async XLA Ops:
  2.2 25.1 %all-to-all-start.1 = ((bf16[8,256,96]{1,2,0:T(8,128)(2,1)}), bf16[8,256,96]{1,2,0:T(8,128)(2,1)}, u32[]{:S(2)}, u32[]{:S(2)}) async-start(bf16[8,256,96]{1,2,0:T(8,128)(2,1)} %broadcast_in_dim.49), calls=%async_computation.1 | async-start | bytes 786432 | tf_op jit(solution)/shard_map/all_to_all | solution.py:94
  12.5 3.7 %copy-start.1 = (bf16[1,1,2048,2,128]{4,3,2,1,0:T(2,128)(2,1)S(1)}, bf16[1,1,2048,2,128]{4,3,2,1,0:T(2,128)(2,1)}, u32[]{:S(2)}) copy-start(bf16[1,1,2048,2,128]{4,3,2,1,0:T(2,128)(2,1)} %param.15) | copy-start | bytes 3145732
  16.2 2.2 %copy-start.10 = (bf16[256,32]{0,1:T(8,128)(2,1)S(1)}, bf16[256,32]{0,1:T(8,128)(2,1)}, u32[]{:S(2)}) copy-start(bf16[256,32]{0,1:T(8,128)(2,1)} %param.21) | copy-start | bytes 49156
  16.2 2.3 %copy-start.8 = (bf16[256,128]{1,0:T(8,128)(2,1)S(1)}, bf16[256,128]{1,0:T(8,128)(2,1)}, u32[]{:S(2)}) copy-start(bf16[256,128]{1,0:T(8,128)(2,1)} %param.24) | copy-start | bytes 196612
  16.2 2.3 %copy-start.9 = (bf16[256,128]{1,0:T(8,128)(2,1)S(1)}, bf16[256,128]{1,0:T(8,128)(2,1)}, u32[]{:S(2)}) copy-start(bf16[256,128]{1,0:T(8,128)(2,1)} %param.22) | copy-start | bytes 196612
  20.0 12.0 %copy-start.2 = (bf16[64,8,8,256]{3,2,1,0:T(8,128)(2,1)S(1)}, bf16[64,8,8,256]{3,2,1,0:T(8,128)(2,1)}, u32[]{:S(2)}) copy-start(bf16[64,8,8,256]{3,2,1,0:T(8,128)(2,1)} %copy.130) | copy-start | bytes 6291460
  20.0 12.0 %copy-start.15 = (f32[3,32]{1,0:T(4,128)S(1)}, f32[3,32]{1,0:T(4,128)}, u32[]{:S(2)}) copy-start(f32[3,32]{1,0:T(4,128)} %param.20) | copy-start | bytes 1156
  28.4 34.5 %all-to-all-start = ((bf16[8,256,288]{1,2,0:T(8,128)(2,1)}), bf16[8,256,288]{1,2,0:T(8,128)(2,1)S(1)}, u32[]{:S(2)}, u32[]{:S(2)}) async-start(bf16[8,256,288]{1,2,0:T(8,128)(2,1)} %broadcast_in_dim.47), calls=%async_computation | async-start | bytes 2359296 | tf_op jit(solution)/shard_map/all_to_all | solution.py:53
  32.0 4.9 %copy-start.14 = (s32[1,2]{1,0:T(1,128)S(1)}, s32[1,2]{1,0:T(1,128)}, u32[]{:S(2)}) copy-start(s32[1,2]{1,0:T(1,128)} %param.18) | copy-start | bytes 28
  33.8 10.5 %copy-start.7 = (bf16[2048,128]{1,0:T(8,128)(2,1)S(1)}, bf16[2048,128]{1,0:T(8,128)(2,1)}, u32[]{:S(2)}) copy-start(bf16[2048,128]{1,0:T(8,128)(2,1)} %get-tuple-element.47) | copy-start | bytes 1572868
  34.5 6.2 %collective-permute-start.1 = (bf16[32,1024]{1,0:T(8,128)(2,1)S(1)}, bf16[32,1024]{1,0:T(8,128)(2,1)S(1)}, u32[]{:S(2)}, u32[]{:S(2)}) collective-permute-start(bf16[32,1024]{1,0:T(8,128)(2,1)S(1)} %pad_maximum_fusion.5), channel_id=1, source_target_pairs={{0,2},{2,0},{4,6},{6,4},{8,10},{10,8},{12,14},{14,12},{1,3},{3,1},... | collective-permute-start | bytes 196616 | tf_op jit(solution)/shard_map/ppermute | solution.py:136
  40.8 3.2 %collective-permute-start.2 = (bf16[2,32,768]{2,1,0:T(8,128)(2,1)S(1)}, bf16[2,32,768]{2,1,0:T(8,128)(2,1)S(1)}, u32[]{:S(2)}, u32[]{:S(2)}) collective-permute-start(bf16[2,32,768]{2,1,0:T(8,128)(2,1)S(1)} %pad_maximum_fusion.4), channel_id=1, source_target_pairs={{0,1},{1,0},{2,3},{3,2},{4,5},{5,4},{6,7},{7,6},{8,9},{9,8},{10,11... | collective-permute-start | bytes 294920 | tf_op jit(solution)/shard_map/ppermute | solution.py:135
  44.3 1.1 copy-start.6
  47.4 7.8 %collective-permute-start.3 = (f32[66,512]{1,0:T(8,128)S(1)}, f32[66,512]{1,0:T(8,128)S(1)}, u32[]{:S(2)}, u32[]{:S(2)}) collective-permute-start(f32[66,512]{1,0:T(8,128)S(1)} %pad_maximum_fusion.2), channel_id=1, source_target_pairs={{0,2},{2,0},{4,6},{6,4},{8,10},{10,8},{12,14},{14,12},{1,3},{3,1},... | collective-permute-start | bytes 405512 | tf_op jit(solution)/shard_map/ppermute | solution.py:136
  55.3 3.3 %collective-permute-start.4 = (f32[66,512]{1,0:T(8,128)S(1)}, f32[66,512]{1,0:T(8,128)S(1)}, u32[]{:S(2)}, u32[]{:S(2)}) collective-permute-start(f32[66,512]{1,0:T(8,128)S(1)} %pad_maximum_fusion.3), channel_id=1, source_target_pairs={{0,1},{1,0},{2,3},{3,2},{4,5},{5,4},{6,7},{7,6},{8,9},{9,8},{10,11... | collective-permute-start | bytes 405512 | tf_op jit(solution)/shard_map/ppermute | solution.py:135
  64.1 36.9 %all-to-all-start.2 = ((bf16[32,64,256]{2,1,0:T(8,128)(2,1)}), bf16[32,64,256]{2,1,0:T(8,128)(2,1)S(1)}, u32[]{:S(2)}, u32[]{:S(2)}) async-start(bf16[32,64,256]{2,1,0:T(8,128)(2,1)} %broadcast_in_dim.101), calls=%async_computation.2 | async-start | bytes 2097152 | tf_op jit(solution)/shard_map/all_to_all | solution.py:215
  75.6 15.1 %collective-permute-start.7 = (bf16[512,128]{1,0:T(8,128)(2,1)S(1)}, bf16[512,128]{1,0:T(8,128)(2,1)S(1)}, u32[]{:S(2)}, u32[]{:S(2)}) collective-permute-start(bf16[512,128]{1,0:T(8,128)(2,1)S(1)} %get-tuple-element.20), channel_id=1, source_target_pairs={{0,48},{16,32},{32,16},{48,0},{1,49},{17,33},{33,17},{49,1},{2,50}... | collective-permute-start | bytes 393224 | tf_op jit(solution)/shard_map/ppermute | solution.py:110
  80.3 11.2 %collective-permute-start.6 = (bf16[512,128]{1,0:T(8,128)(2,1)S(1)}, bf16[512,128]{1,0:T(8,128)(2,1)S(1)}, u32[]{:S(2)}, u32[]{:S(2)}) collective-permute-start(bf16[512,128]{1,0:T(8,128)(2,1)S(1)} %get-tuple-element.21), channel_id=1, source_target_pairs={{0,32},{16,48},{32,0},{48,16},{1,33},{17,49},{33,1},{49,17},{2,34}... | collective-permute-start | bytes 393224 | tf_op jit(solution)/shard_map/ppermute | solution.py:110
  83.0 9.3 %collective-permute-start.5 = (bf16[512,128]{1,0:T(8,128)(2,1)S(1)}, bf16[512,128]{1,0:T(8,128)(2,1)S(1)}, u32[]{:S(2)}, u32[]{:S(2)}) collective-permute-start(bf16[512,128]{1,0:T(8,128)(2,1)S(1)} %get-tuple-element.22), channel_id=1, source_target_pairs={{0,16},{16,0},{32,48},{48,32},{1,17},{17,1},{33,49},{49,33},{2,18}... | collective-permute-start | bytes 393224 | tf_op jit(solution)/shard_map/ppermute | solution.py:110
  85.5 9.5 %copy-start.11 = (f32[2,2048]{1,0:T(2,128)S(1)}, f32[2,2048]{1,0:T(2,128)}, u32[]{:S(2)}) copy-start(f32[2,2048]{1,0:T(2,128)} %param.25) | copy-start | bytes 49156
  86.4 8.9 %collective-permute-start = (bf16[2048,160]{0,1:T(8,128)(2,1)}, bf16[2048,160]{0,1:T(8,128)(2,1)}, u32[]{:S(2)}, u32[]{:S(2)}) collective-permute-start(bf16[2048,160]{0,1:T(8,128)(2,1)} %slice.143), channel_id=1, source_target_pairs={{0,1},{1,0},{2,3},{3,2},{4,5},{5,4},{6,7},{7,6},{8,9},{9,8},{10,11... | collective-permute-start | bytes 1966088 | tf_op jit(solution)/shard_map/ppermute | solution.py:99
  93.1 3.9 %collective-permute-start.8 = (bf16[4,512,128]{2,1,0:T(8,128)(2,1)S(1)}, bf16[4,512,128]{2,1,0:T(8,128)(2,1)}, u32[]{:S(2)}, u32[]{:S(2)}) collective-permute-start(bf16[4,512,128]{2,1,0:T(8,128)(2,1)S(1)} %broadcast_select_fusion), channel_id=1, source_target_pairs={{0,1},{1,0},{2,3},{3,2},{4,5},{5,4},{6,7},{7,6},{8,9},{9,8},{10,11... | collective-permute-start | bytes 1572872 | tf_op jit(solution)/shard_map/ppermute | solution.py:117
  101.0 9.9 %copy-start.12 = (f32[2,2048]{1,0:T(2,128)S(1)}, f32[2,2048]{1,0:T(2,128)}, u32[]{:S(2)}) copy-start(f32[2,2048]{1,0:T(2,128)} %param.27) | copy-start | bytes 49156
  101.0 9.9 %copy-start.13 = (f32[2,2048]{1,0:T(2,128)S(1)}, f32[2,2048]{1,0:T(2,128)}, u32[]{:S(2)}) copy-start(f32[2,2048]{1,0:T(2,128)} %param.26) | copy-start | bytes 49156
  102.4 36.5 %all-to-all-start.3 = ((bf16[32,64,256]{2,1,0:T(8,128)(2,1)}), bf16[32,64,256]{2,1,0:T(8,128)(2,1)S(1)}, u32[]{:S(2)}, u32[]{:S(2)}) async-start(bf16[32,64,256]{2,1,0:T(8,128)(2,1)} %broadcast_in_dim.102), calls=%async_computation.3 | async-start | bytes 2097152 | tf_op jit(solution)/shard_map/all_to_all | solution.py:226
  142.4 1.9 %copy-start = (bf16[1,512,2048]{2,1,0:T(8,128)(2,1)S(1)}, bf16[1,512,2048]{2,1,0:T(8,128)(2,1)}, u32[]{:S(2)}) copy-start(bf16[1,512,2048]{2,1,0:T(8,128)(2,1)} %param.14) | copy-start | bytes 6291460
  144.8 1.6 copy-start.4
  144.8 1.6 copy-start.5
  145.4 1.0 copy-start.3
  160.5 21.1 %all-to-all-start.5 = ((f32[32,8,512]{2,1,0:T(8,128)}), f32[32,8,512]{2,1,0:T(8,128)S(1)}, u32[]{:S(2)}, u32[]{:S(2)}) async-start(f32[32,8,512]{2,1,0:T(8,128)} %convolution_bitcast_fusion), calls=%async_computation.5 | async-start | bytes 1048576 | tf_op jit(solution)/shard_map/all_to_all | solution.py:246

commit v15 on v13

--- a/solution.py
+++ b/solution.py
@@ -212,14 +212,13 @@
     core_tokens = lax.dynamic_index_in_dim(
         token_rows.reshape(chips, nc, block_rows, -1), core, axis=1, keepdims=False
     ).reshape(core_rows, -1)
-    residual = core_tokens.T.astype(jnp.float32) + projected.astype(jnp.float32)
-    centered = residual - jnp.mean(residual, axis=0, keepdims=True)
-    variance = jnp.mean(centered * centered, axis=0, keepdims=True)
-    normed_t = (
-        centered * lax.rsqrt(variance + 1e-06) * norm_gains[0][:, None] + norm_biases[0][:, None]
+    normed = layer_norm(
+        core_tokens.astype(jnp.float32) + projected.T.astype(jnp.float32),
+        norm_gains[0],
+        norm_biases[0],
     ).astype(jnp.bfloat16)
     inner = jax.nn.gelu(
-        jnp.einsum("dt,df->tf", normed_t, chip_in, preferred_element_type=jnp.float32) + chip_in_bias,
+        jnp.dot(normed, chip_in, preferred_element_type=jnp.float32) + chip_in_bias,
         approximate=True,
     ).astype(jnp.bfloat16)
     group_inner = lax.all_to_all(
@@ -232,7 +231,7 @@
         mixed_parts.reshape(chips, block_rows, quarter_width), PLANE, 0, 0, tiled=True
     ).reshape(nx, ny, block_rows, quarter_width)
     mixed_rows = from_chips.sum(axis=1).transpose(1, 0, 2).reshape(block_rows, d_model)
-    own_normed = lax.dynamic_slice_in_dim(normed_t, chip * block_rows, block_rows, 1).T
+    own_normed = lax.dynamic_slice_in_dim(normed, chip * block_rows, block_rows, 0)
     layer_output = layer_norm(
         own_normed.astype(jnp.float32) + mixed_rows + out_biases[1], norm_gains[1], norm_biases[1]
     ).astype(jnp.bfloat16)

time: 186 us -> 186 us (level)
    reduce_sum x2 -> x0, other arithmetic: 2.14 us -> none  [the longest x1 1.66 us: local(): centered = residual - jnp.mean(residual, axis=0, keepdims=True)]
where the time goes in v15:
time: 186 us; the launch traced here: 185 us
  waiting for transfers between devices  70.3 us (38%)
  starting transfers between devices  58.7 us (32%)
  local copies, waits for them, and re-layouts  23.4 us (13%)
  other arithmetic  12.7 us (7%)
  blocking collectives  11.7 us (6%)
  matrix products  6.1 us (3%)
  between operations  1.94 us (1%)
    all_to_all x1, waiting for transfers between devices, local(): lax.all_to_all(spread, PLANE, 0, 0, tiled=True)  26.1 us
    all_to_all x1, waiting for transfers between devices, local(): lax.all_to_all(mixed_parts.reshape(chips, block_rows, quarter_width), PLA...  15.8 us
    all_to_all x1, blocking collectives, local(): lax.all_to_all(jnp.broadcast_to(inner[None], (nx,) + inner.shape), 'bx',...  11.7 us
    all_to_all x1, starting transfers between devices, local(): lax.all_to_all(jnp.broadcast_to(qkv_flat[None], (reqs,) + qkv_flat.shape)...  10.3 us
    all_to_all x1, starting transfers between devices, local(): lax.all_to_all(outgoing, PLANE, 0, 0, tiled=True)  10.2 us
    ppermute x3, starting transfers between devices, local(): lax.ppermute(lax.dynamic_index_in_dim(own_down, row ^ k, 0, keepdims=Fals...  9.82 us
    ppermute x2, waiting for transfers between devices, from_partner(): lax.ppermute(value, 'by', [(i, i ^ 1 << bit_level - 1) for i in range(ny)])  9.2 us
    all_to_all x1, waiting for transfers between devices, local(): lax.all_to_all(jnp.broadcast_to(qkv_flat[None], (reqs,) + qkv_flat.shape)...  8 us
  transfers between devices with their start and end apart: 14, of which 12 were waited for; matrix products, arithmetic and copies ran while one was open for 13% of the time, Pallas kernels for 0%

profile of v15, /device:TPU:8, one launch (start us, length us, event | category | flops | bytes accessed | tf_op | source)
XLA Modules:
  0.0 184.9 jit_solution(14785565207839963756)
XLA Ops:
  0.6 1.6 broadcast_in_dim.49
  2.2 10.3 %all-to-all-start.1 = ((bf16[8,256,96]{1,2,0:T(8,128)(2,1)}), bf16[8,256,96]{1,2,0:T(8,128)(2,1)}, u32[]{:S(2)}, u32[]{:S(2)}) async-start(bf16[8,256,96]{1,2,0:T(8,128)(2,1)} %broadcast_in_dim.49), calls=%async_computation.1 | async-start | bytes 786432 | tf_op jit(solution)/shard_map/all_to_all | solution.py:94
  12.5 3.7 %copy.93 = bf16[64,8,8,256]{3,2,1,0:T(8,128)(2,1)} copy(bf16[64,8,8,256]{3,1,2,0:T(8,128)(2,1)} %bitcast.117) | data formatting | bytes 4194304
  16.2 1.5 fusion.68
  19.3 8.0 %all-to-all-done.1 = bf16[8,256,96]{1,2,0:T(8,128)(2,1)} async-done(((bf16[8,256,96]{1,2,0:T(8,128)(2,1)}), bf16[8,256,96]{1,2,0:T(8,128)(2,1)}, u32[]{:S(2)}, u32[]{:S(2)}) %all-to-all-start.1) | async-done | bytes 393248 | tf_op jit(solution)/shard_map/all_to_all | solution.py:94
  28.4 3.6 %all-to-all-start = ((bf16[8,256,288]{1,2,0:T(8,128)(2,1)}), bf16[8,256,288]{1,2,0:T(8,128)(2,1)S(1)}, u32[]{:S(2)}, u32[]{:S(2)}) async-start(bf16[8,256,288]{1,2,0:T(8,128)(2,1)} %broadcast_in_dim.47), calls=%async_computation | async-start | bytes 2359296 | tf_op jit(solution)/shard_map/all_to_all | solution.py:53
  32.0 1.8 fusion.14
  33.8 2.5 %collective-permute-start.1 = (bf16[3,32,512]{2,1,0:T(8,128)(2,1)S(1)}, bf16[3,32,512]{2,1,0:T(8,128)(2,1)S(1)}, u32[]{:S(2)}, u32[]{:S(2)}) collective-permute-start(bf16[3,32,512]{2,1,0:T(8,128)(2,1)S(1)} %fusion.14), channel_id=1, source_target_pairs={{0,2},{2,0},{4,6},{6,4},{8,10},{10,8},{12,14},{14,12},{1,3},{3,1},... | collective-permute-start | bytes 294920 | tf_op jit(solution)/shard_map/ppermute | solution.py:136
  37.0 3.4 %collective-permute-done.1 = bf16[3,32,512]{2,1,0:T(8,128)(2,1)S(1)} collective-permute-done((bf16[3,32,512]{2,1,0:T(8,128)(2,1)S(1)}, bf16[3,32,512]{2,1,0:T(8,128)(2,1)S(1)}, u32[]{:S(2)}, u32[]{:S(2)}) %collective-permute-start.1) | collective-permute-done | bytes 98336 | tf_op jit(solution)/shard_map/ppermute | solution.py:136
  40.5 1.9 %collective-permute-start.2 = (bf16[3,2,32,512]{3,2,0,1:T(8,128)(2,1)S(1)}, bf16[3,2,32,512]{3,2,0,1:T(8,128)(2,1)S(1)}, u32[]{:S(2)}, u32[]{:S(2)}) collective-permute-start(bf16[3,2,32,512]{3,2,0,1:T(8,128)(2,1)S(1)} %maximum_select_fusion.10), channel_id=1, source_target_pairs={{0,1},{1,0},{2,3},{3,2},{4,5},{5,4},{6,7},{7,6},{8,9},{9,8},{10,11... | collective-permute-start | bytes 589832 | tf_op jit(solution)/shard_map/ppermute | solution.py:135
  43.0 2.0 %and_reduce_fusion = pred[2048]{0:T(1024)(128)(4,1)S(1)} fusion(s32[1,8192]{1,0:T(1,128)} %param.16, s32[]{:T(128)S(6)} %select_n.153, s32[]{:T(128)} %bitcast.16, s32[]{:T(128)} %bitcast.15, s32[]{:T(128)} %bitcast.116, s32[]{:T(128)S(6)} %mul.153), kind=kLoop, calls=%fused_computation.84 | loop fusion | flops 12288 | bytes 10260 | tf_op jit(solution)/shard_map/and | solution.py:162
  48.5 2.4 %collective-permute-start.3 = (f32[66,512]{1,0:T(8,128)S(1)}, f32[66,512]{1,0:T(8,128)S(1)}, u32[]{:S(2)}, u32[]{:S(2)}) collective-permute-start(f32[66,512]{1,0:T(8,128)S(1)} %pad_maximum_fusion.2), channel_id=1, source_target_pairs={{0,2},{2,0},{4,6},{6,4},{8,10},{10,8},{12,14},{14,12},{1,3},{3,1},... | collective-permute-start | bytes 405512 | tf_op jit(solution)/shard_map/ppermute | solution.py:136
  50.9 5.8 %collective-permute-done.3 = f32[66,512]{1,0:T(8,128)S(1)} collective-permute-done((f32[66,512]{1,0:T(8,128)S(1)}, f32[66,512]{1,0:T(8,128)S(1)}, u32[]{:S(2)}, u32[]{:S(2)}) %collective-permute-start.3) | collective-permute-done | bytes 135200 | tf_op jit(solution)/shard_map/ppermute | solution.py:136
  56.8 1.9 %collective-permute-start.4 = (f32[66,512]{1,0:T(8,128)S(1)}, f32[66,512]{1,0:T(8,128)S(1)}, u32[]{:S(2)}, u32[]{:S(2)}) collective-permute-start(f32[66,512]{1,0:T(8,128)S(1)} %pad_maximum_fusion.3), channel_id=1, source_target_pairs={{0,1},{1,0},{2,3},{3,2},{4,5},{5,4},{6,7},{7,6},{8,9},{9,8},{10,11... | collective-permute-start | bytes 405512 | tf_op jit(solution)/shard_map/ppermute | solution.py:135
  60.3 2.6 %all-to-all-done = bf16[8,256,288]{1,2,0:T(8,128)(2,1)S(1)} async-done(((bf16[8,256,288]{1,2,0:T(8,128)(2,1)}), bf16[8,256,288]{1,2,0:T(8,128)(2,1)S(1)}, u32[]{:S(2)}, u32[]{:S(2)}) %all-to-all-start) | async-done | bytes 1179680 | tf_op jit(solution)/shard_map/all_to_all | solution.py:53
  64.1 10.2 %all-to-all-start.2 = ((bf16[32,64,256]{2,1,0:T(8,128)(2,1)}), bf16[32,64,256]{2,1,0:T(8,128)(2,1)S(1)}, u32[]{:S(2)}, u32[]{:S(2)}) async-start(bf16[32,64,256]{2,1,0:T(8,128)(2,1)} %broadcast_in_dim.101), calls=%async_computation.2 | async-start | bytes 2097152 | tf_op jit(solution)/shard_map/all_to_all | solution.py:200
  75.6 4.6 %collective-permute-start.7 = (bf16[512,128]{1,0:T(8,128)(2,1)S(1)}, bf16[512,128]{1,0:T(8,128)(2,1)S(1)}, u32[]{:S(2)}, u32[]{:S(2)}) collective-permute-start(bf16[512,128]{1,0:T(8,128)(2,1)S(1)} %get-tuple-element.20), channel_id=1, source_target_pairs={{0,48},{16,32},{32,16},{48,0},{1,49},{17,33},{33,17},{49,1},{2,50}... | collective-permute-start | bytes 393224 | tf_op jit(solution)/shard_map/ppermute | solution.py:110
  80.2 2.7 %collective-permute-start.6 = (bf16[512,128]{1,0:T(8,128)(2,1)S(1)}, bf16[512,128]{1,0:T(8,128)(2,1)S(1)}, u32[]{:S(2)}, u32[]{:S(2)}) collective-permute-start(bf16[512,128]{1,0:T(8,128)(2,1)S(1)} %get-tuple-element.21), channel_id=1, source_target_pairs={{0,32},{16,48},{32,0},{48,16},{1,33},{17,49},{33,1},{49,17},{2,34}... | collective-permute-start | bytes 393224 | tf_op jit(solution)/shard_map/ppermute | solution.py:110
  83.0 2.5 %collective-permute-start.5 = (bf16[512,128]{1,0:T(8,128)(2,1)S(1)}, bf16[512,128]{1,0:T(8,128)(2,1)S(1)}, u32[]{:S(2)}, u32[]{:S(2)}) collective-permute-start(bf16[512,128]{1,0:T(8,128)(2,1)S(1)} %get-tuple-element.22), channel_id=1, source_target_pairs={{0,16},{16,0},{32,48},{48,32},{1,17},{17,1},{33,49},{49,33},{2,18}... | collective-permute-start | bytes 393224 | tf_op jit(solution)/shard_map/ppermute | solution.py:110
  86.4 1.9 %collective-permute-start = (bf16[2048,160]{0,1:T(8,128)(2,1)}, bf16[2048,160]{0,1:T(8,128)(2,1)}, u32[]{:S(2)}, u32[]{:S(2)}) collective-permute-start(bf16[2048,160]{0,1:T(8,128)(2,1)} %slice.124), channel_id=1, source_target_pairs={{0,1},{1,0},{2,3},{3,2},{4,5},{5,4},{6,7},{7,6},{8,9},{9,8},{10,11... | collective-permute-start | bytes 1966088 | tf_op jit(solution)/shard_map/ppermute | solution.py:99
  88.3 2.4 %collective-permute-done.7 = bf16[512,128]{1,0:T(8,128)(2,1)S(1)} collective-permute-done((bf16[512,128]{1,0:T(8,128)(2,1)S(1)}, bf16[512,128]{1,0:T(8,128)(2,1)S(1)}, u32[]{:S(2)}, u32[]{:S(2)}) %collective-permute-start.7) | collective-permute-done | bytes 131104 | tf_op jit(solution)/shard_map/ppermute | solution.py:110
  93.1 1.9 %collective-permute-start.8 = (bf16[4,512,128]{2,1,0:T(8,128)(2,1)S(1)}, bf16[4,512,128]{2,1,0:T(8,128)(2,1)}, u32[]{:S(2)}, u32[]{:S(2)}) collective-permute-start(bf16[4,512,128]{2,1,0:T(8,128)(2,1)S(1)} %broadcast_select_fusion), channel_id=1, source_target_pairs={{0,1},{1,0},{2,3},{3,2},{4,5},{5,4},{6,7},{7,6},{8,9},{9,8},{10,11... | collective-permute-start | bytes 1572872 | tf_op jit(solution)/shard_map/ppermute | solution.py:117
  98.4 2.6 %all-to-all-done.2 = bf16[32,64,256]{2,1,0:T(8,128)(2,1)S(1)} async-done(((bf16[32,64,256]{2,1,0:T(8,128)(2,1)}), bf16[32,64,256]{2,1,0:T(8,128)(2,1)S(1)}, u32[]{:S(2)}, u32[]{:S(2)}) %all-to-all-start.2) | async-done | bytes 1048608 | tf_op jit(solution)/shard_map/all_to_all | solution.py:200
  102.4 7.7 %all-to-all-start.3 = ((bf16[32,64,256]{2,1,0:T(8,128)(2,1)}), bf16[32,64,256]{2,1,0:T(8,128)(2,1)S(1)}, u32[]{:S(2)}, u32[]{:S(2)}) async-start(bf16[32,64,256]{2,1,0:T(8,128)(2,1)} %broadcast_in_dim.102), calls=%async_computation.3 | async-start | bytes 2097152 | tf_op jit(solution)/shard_map/all_to_all | solution.py:211
  110.9 1.9 %slice.139 = bf16[2048,128]{0,1:T(8,128)(2,1)} slice(bf16[2048,160]{0,1:T(8,128)(2,1)} %collective-permute-done), slice={[0:2048], [32:160]} | slice | bytes 1048576 | tf_op jit(solution)/shard_map/slice | solution.py:101
  112.8 26.1 %all-to-all-done.3 = bf16[32,64,256]{2,1,0:T(8,128)(2,1)S(1)} async-done(((bf16[32,64,256]{2,1,0:T(8,128)(2,1)}), bf16[32,64,256]{2,1,0:T(8,128)(2,1)S(1)}, u32[]{:S(2)}, u32[]{:S(2)}) %all-to-all-start.3) | async-done | bytes 1048608 | tf_op jit(solution)/shard_map/all_to_all | solution.py:211
  138.8 1.6 bitcast_convert_fusion
  140.4 1.9 %copy.80 = f32[2048,256]{0,1:T(8,128)S(1)} copy(f32[2048,256]{1,0:T(8,128)} %bitcast_convert_fusion) | data formatting | bytes 4194304 | tf_op jit(solution)/shard_map/convert_element_type | solution.py:216
  142.3 1.7 fusion.31
  147.1 11.7 %all_to_all.30 = bf16[4,256,256]{1,2,0:T(8,128)(2,1)S(1)} all-to-all(bf16[4,256,256]{1,2,0:T(8,128)(2,1)S(1)} %broadcast_in_dim.108), channel_id=1, replica_groups=mesh['req'=8,'bx'=4,'by'=8,'bc'=2] {'bx'}, dimensions={0} | all-to-all | bytes 1048576 | tf_op jit(solution)/shard_map/all_to_all | solution.py:224
  160.4 4.6 %all-to-all-start.5 = ((f32[32,8,512]{2,1,0:T(8,128)}), f32[32,8,512]{2,1,0:T(8,128)S(1)}, u32[]{:S(2)}, u32[]{:S(2)}) async-start(f32[32,8,512]{2,1,0:T(8,128)} %convolution_bitcast_fusion), calls=%async_computation.5 | async-start | bytes 1048576 | tf_op jit(solution)/shard_map/all_to_all | solution.py:230
  165.7 15.8 %all-to-all-done.5 = f32[32,8,512]{2,1,0:T(8,128)S(1)} async-done(((f32[32,8,512]{2,1,0:T(8,128)}), f32[32,8,512]{2,1,0:T(8,128)S(1)}, u32[]{:S(2)}, u32[]{:S(2)}) %all-to-all-start.5) | async-done | bytes 524320 | tf_op jit(solution)/shard_map/all_to_all | solution.py:230
  (106 shorter events, 28.2 us)
Async XLA Ops:
  2.2 25.1 %all-to-all-start.1 = ((bf16[8,256,96]{1,2,0:T(8,128)(2,1)}), bf16[8,256,96]{1,2,0:T(8,128)(2,1)}, u32[]{:S(2)}, u32[]{:S(2)}) async-start(bf16[8,256,96]{1,2,0:T(8,128)(2,1)} %broadcast_in_dim.49), calls=%async_computation.1 | async-start | bytes 786432 | tf_op jit(solution)/shard_map/all_to_all | solution.py:94
  12.5 3.7 %copy-start.1 = (bf16[1,1,2048,2,128]{4,3,2,1,0:T(2,128)(2,1)S(1)}, bf16[1,1,2048,2,128]{4,3,2,1,0:T(2,128)(2,1)}, u32[]{:S(2)}) copy-start(bf16[1,1,2048,2,128]{4,3,2,1,0:T(2,128)(2,1)} %param.15) | copy-start | bytes 3145732
  16.2 1.5 copy-start.10
  16.2 1.7 copy-start.8
  16.2 1.7 copy-start.9
  19.3 12.7 %copy-start.2 = (bf16[64,8,8,256]{3,2,1,0:T(8,128)(2,1)S(1)}, bf16[64,8,8,256]{3,2,1,0:T(8,128)(2,1)}, u32[]{:S(2)}) copy-start(bf16[64,8,8,256]{3,2,1,0:T(8,128)(2,1)} %copy.93) | copy-start | bytes 6291460
  19.3 12.7 %copy-start.15 = (f32[3,32]{1,0:T(4,128)S(1)}, f32[3,32]{1,0:T(4,128)}, u32[]{:S(2)}) copy-start(f32[3,32]{1,0:T(4,128)} %param.20) | copy-start | bytes 1156
  28.4 34.5 %all-to-all-start = ((bf16[8,256,288]{1,2,0:T(8,128)(2,1)}), bf16[8,256,288]{1,2,0:T(8,128)(2,1)S(1)}, u32[]{:S(2)}, u32[]{:S(2)}) async-start(bf16[8,256,288]{1,2,0:T(8,128)(2,1)} %broadcast_in_dim.47), calls=%async_computation | async-start | bytes 2359296 | tf_op jit(solution)/shard_map/all_to_all | solution.py:53
  32.0 10.4 %copy-start.14 = (s32[1,2]{1,0:T(1,128)S(1)}, s32[1,2]{1,0:T(1,128)}, u32[]{:S(2)}) copy-start(s32[1,2]{1,0:T(1,128)} %param.18) | copy-start | bytes 28
  33.8 11.6 %copy-start.7 = (bf16[2048,128]{1,0:T(8,128)(2,1)S(1)}, bf16[2048,128]{1,0:T(8,128)(2,1)}, u32[]{:S(2)}) copy-start(bf16[2048,128]{1,0:T(8,128)(2,1)} %get-tuple-element.38) | copy-start | bytes 1572868
  33.8 6.6 %collective-permute-start.1 = (bf16[3,32,512]{2,1,0:T(8,128)(2,1)S(1)}, bf16[3,32,512]{2,1,0:T(8,128)(2,1)S(1)}, u32[]{:S(2)}, u32[]{:S(2)}) collective-permute-start(bf16[3,32,512]{2,1,0:T(8,128)(2,1)S(1)} %fusion.14), channel_id=1, source_target_pairs={{0,2},{2,0},{4,6},{6,4},{8,10},{10,8},{12,14},{14,12},{1,3},{3,1},... | collective-permute-start | bytes 294920 | tf_op jit(solution)/shard_map/ppermute | solution.py:136
  40.5 4.6 %collective-permute-start.2 = (bf16[3,2,32,512]{3,2,0,1:T(8,128)(2,1)S(1)}, bf16[3,2,32,512]{3,2,0,1:T(8,128)(2,1)S(1)}, u32[]{:S(2)}, u32[]{:S(2)}) collective-permute-start(bf16[3,2,32,512]{3,2,0,1:T(8,128)(2,1)S(1)} %maximum_select_fusion.10), channel_id=1, source_target_pairs={{0,1},{1,0},{2,3},{3,2},{4,5},{5,4},{6,7},{7,6},{8,9},{9,8},{10,11... | collective-permute-start | bytes 589832 | tf_op jit(solution)/shard_map/ppermute | solution.py:135
  45.5 1.1 copy-start.6
  48.5 8.1 %collective-permute-start.3 = (f32[66,512]{1,0:T(8,128)S(1)}, f32[66,512]{1,0:T(8,128)S(1)}, u32[]{:S(2)}, u32[]{:S(2)}) collective-permute-start(f32[66,512]{1,0:T(8,128)S(1)} %pad_maximum_fusion.2), channel_id=1, source_target_pairs={{0,2},{2,0},{4,6},{6,4},{8,10},{10,8},{12,14},{14,12},{1,3},{3,1},... | collective-permute-start | bytes 405512 | tf_op jit(solution)/shard_map/ppermute | solution.py:136
  56.8 3.3 %collective-permute-start.4 = (f32[66,512]{1,0:T(8,128)S(1)}, f32[66,512]{1,0:T(8,128)S(1)}, u32[]{:S(2)}, u32[]{:S(2)}) collective-permute-start(f32[66,512]{1,0:T(8,128)S(1)} %pad_maximum_fusion.3), channel_id=1, source_target_pairs={{0,1},{1,0},{2,3},{3,2},{4,5},{5,4},{6,7},{7,6},{8,9},{9,8},{10,11... | collective-permute-start | bytes 405512 | tf_op jit(solution)/shard_map/ppermute | solution.py:135
  64.1 36.9 %all-to-all-start.2 = ((bf16[32,64,256]{2,1,0:T(8,128)(2,1)}), bf16[32,64,256]{2,1,0:T(8,128)(2,1)S(1)}, u32[]{:S(2)}, u32[]{:S(2)}) async-start(bf16[32,64,256]{2,1,0:T(8,128)(2,1)} %broadcast_in_dim.101), calls=%async_computation.2 | async-start | bytes 2097152 | tf_op jit(solution)/shard_map/all_to_all | solution.py:200
  75.6 15.1 %collective-permute-start.7 = (bf16[512,128]{1,0:T(8,128)(2,1)S(1)}, bf16[512,128]{1,0:T(8,128)(2,1)S(1)}, u32[]{:S(2)}, u32[]{:S(2)}) collective-permute-start(bf16[512,128]{1,0:T(8,128)(2,1)S(1)} %get-tuple-element.20), channel_id=1, source_target_pairs={{0,48},{16,32},{32,16},{48,0},{1,49},{17,33},{33,17},{49,1},{2,50}... | collective-permute-start | bytes 393224 | tf_op jit(solution)/shard_map/ppermute | solution.py:110
  80.2 11.2 %collective-permute-start.6 = (bf16[512,128]{1,0:T(8,128)(2,1)S(1)}, bf16[512,128]{1,0:T(8,128)(2,1)S(1)}, u32[]{:S(2)}, u32[]{:S(2)}) collective-permute-start(bf16[512,128]{1,0:T(8,128)(2,1)S(1)} %get-tuple-element.21), channel_id=1, source_target_pairs={{0,32},{16,48},{32,0},{48,16},{1,33},{17,49},{33,1},{49,17},{2,34}... | collective-permute-start | bytes 393224 | tf_op jit(solution)/shard_map/ppermute | solution.py:110
  83.0 9.3 %collective-permute-start.5 = (bf16[512,128]{1,0:T(8,128)(2,1)S(1)}, bf16[512,128]{1,0:T(8,128)(2,1)S(1)}, u32[]{:S(2)}, u32[]{:S(2)}) collective-permute-start(bf16[512,128]{1,0:T(8,128)(2,1)S(1)} %get-tuple-element.22), channel_id=1, source_target_pairs={{0,16},{16,0},{32,48},{48,32},{1,17},{17,1},{33,49},{49,33},{2,18}... | collective-permute-start | bytes 393224 | tf_op jit(solution)/shard_map/ppermute | solution.py:110
  85.5 9.5 %copy-start.11 = (f32[2,2048]{1,0:T(2,128)S(1)}, f32[2,2048]{1,0:T(2,128)}, u32[]{:S(2)}) copy-start(f32[2,2048]{1,0:T(2,128)} %param.25) | copy-start | bytes 49156
  86.4 8.9 %collective-permute-start = (bf16[2048,160]{0,1:T(8,128)(2,1)}, bf16[2048,160]{0,1:T(8,128)(2,1)}, u32[]{:S(2)}, u32[]{:S(2)}) collective-permute-start(bf16[2048,160]{0,1:T(8,128)(2,1)} %slice.124), channel_id=1, source_target_pairs={{0,1},{1,0},{2,3},{3,2},{4,5},{5,4},{6,7},{7,6},{8,9},{9,8},{10,11... | collective-permute-start | bytes 1966088 | tf_op jit(solution)/shard_map/ppermute | solution.py:99
  93.1 3.9 %collective-permute-start.8 = (bf16[4,512,128]{2,1,0:T(8,128)(2,1)S(1)}, bf16[4,512,128]{2,1,0:T(8,128)(2,1)}, u32[]{:S(2)}, u32[]{:S(2)}) collective-permute-start(bf16[4,512,128]{2,1,0:T(8,128)(2,1)S(1)} %broadcast_select_fusion), channel_id=1, source_target_pairs={{0,1},{1,0},{2,3},{3,2},{4,5},{5,4},{6,7},{7,6},{8,9},{9,8},{10,11... | collective-permute-start | bytes 1572872 | tf_op jit(solution)/shard_map/ppermute | solution.py:117
  100.9 9.9 %copy-start.12 = (f32[2,2048]{1,0:T(2,128)S(1)}, f32[2,2048]{1,0:T(2,128)}, u32[]{:S(2)}) copy-start(f32[2,2048]{1,0:T(2,128)} %param.27) | copy-start | bytes 49156
  100.9 9.9 %copy-start.13 = (f32[2,2048]{1,0:T(2,128)S(1)}, f32[2,2048]{1,0:T(2,128)}, u32[]{:S(2)}) copy-start(f32[2,2048]{1,0:T(2,128)} %param.26) | copy-start | bytes 49156
  102.4 36.5 %all-to-all-start.3 = ((bf16[32,64,256]{2,1,0:T(8,128)(2,1)}), bf16[32,64,256]{2,1,0:T(8,128)(2,1)S(1)}, u32[]{:S(2)}, u32[]{:S(2)}) async-start(bf16[32,64,256]{2,1,0:T(8,128)(2,1)} %broadcast_in_dim.102), calls=%async_computation.3 | async-start | bytes 2097152 | tf_op jit(solution)/shard_map/all_to_all | solution.py:211
  142.3 1.9 %copy-start = (bf16[1,512,2048]{2,1,0:T(8,128)(2,1)S(1)}, bf16[1,512,2048]{2,1,0:T(8,128)(2,1)}, u32[]{:S(2)}) copy-start(bf16[1,512,2048]{2,1,0:T(8,128)(2,1)} %param.14) | copy-start | bytes 6291460
  144.7 1.6 copy-start.4
  144.7 1.6 copy-start.5
  145.3 1.0 copy-start.3
  160.4 21.1 %all-to-all-start.5 = ((f32[32,8,512]{2,1,0:T(8,128)}), f32[32,8,512]{2,1,0:T(8,128)S(1)}, u32[]{:S(2)}, u32[]{:S(2)}) async-start(f32[32,8,512]{2,1,0:T(8,128)} %convolution_bitcast_fusion), calls=%async_computation.5 | async-start | bytes 1048576 | tf_op jit(solution)/shard_map/all_to_all | solution.py:230

commit v16 on v15

--- a/solution.py
+++ b/solution.py
@@ -213,7 +213,7 @@
         token_rows.reshape(chips, nc, block_rows, -1), core, axis=1, keepdims=False
     ).reshape(core_rows, -1)
     normed = layer_norm(
-        core_tokens.astype(jnp.float32) + projected.T.astype(jnp.float32),
+        core_tokens.astype(jnp.float32) + lax.optimization_barrier(projected.T).astype(jnp.float32),
         norm_gains[0],
         norm_biases[0],
     ).astype(jnp.bfloat16)

time: 186 us -> 184 us (0.989)
  other arithmetic: 12.7 us -> 10.5 us
    convert_element_type x1 -> x0, local copies, waits for them, and re-layouts: 1.92 us -> none  [local(): projected.T.astype(jnp.float32)]
    unnamed x36 -> x40, local copies, waits for them, and re-layouts: 5.32 us -> 6.03 us
where the time goes in v16:
time: 184 us; the launch traced here: 183 us
  waiting for transfers between devices  69.6 us (38%)
  starting transfers between devices  59.3 us (32%)
  local copies, waits for them, and re-layouts  23.7 us (13%)
  blocking collectives  11.9 us (6%)
  other arithmetic  10.5 us (6%)
  matrix products  6.11 us (3%)
  between operations  1.95 us (1%)
    all_to_all x1, waiting for transfers between devices, local(): lax.all_to_all(spread, PLANE, 0, 0, tiled=True)  25.9 us
    all_to_all x1, waiting for transfers between devices, local(): lax.all_to_all(mixed_parts.reshape(chips, block_rows, quarter_width), PLA...  15.8 us
    all_to_all x1, blocking collectives, local(): lax.all_to_all(jnp.broadcast_to(inner[None], (nx,) + inner.shape), 'bx',...  11.9 us
    all_to_all x1, starting transfers between devices, local(): lax.all_to_all(jnp.broadcast_to(qkv_flat[None], (reqs,) + qkv_flat.shape)...  10.3 us
    all_to_all x1, starting transfers between devices, local(): lax.all_to_all(outgoing, PLANE, 0, 0, tiled=True)  10.2 us
    ppermute x3, starting transfers between devices, local(): lax.ppermute(lax.dynamic_index_in_dim(own_down, row ^ k, 0, keepdims=Fals...  9.82 us
    ppermute x2, waiting for transfers between devices, from_partner(): lax.ppermute(value, 'by', [(i, i ^ 1 << bit_level - 1) for i in range(ny)])  9.21 us
    all_to_all x1, starting transfers between devices, local(): lax.all_to_all(spread, PLANE, 0, 0, tiled=True)  8.31 us
  transfers between devices with their start and end apart: 14, of which 12 were waited for; matrix products, arithmetic and copies ran while one was open for 13% of the time, Pallas kernels for 0%

profile of v16, /device:TPU:8, one launch (start us, length us, event | category | flops | bytes accessed | tf_op | source)
XLA Modules:
  0.0 183.0 jit_solution(2634047594459694641)
XLA Ops:
  0.6 1.6 broadcast_in_dim.49
  2.2 10.3 %all-to-all-start.1 = ((bf16[8,256,96]{1,2,0:T(8,128)(2,1)}), bf16[8,256,96]{1,2,0:T(8,128)(2,1)}, u32[]{:S(2)}, u32[]{:S(2)}) async-start(bf16[8,256,96]{1,2,0:T(8,128)(2,1)} %broadcast_in_dim.49), calls=%async_computation.1 | async-start | bytes 786432 | tf_op jit(solution)/shard_map/all_to_all | solution.py:94
  12.5 3.7 %copy.93 = bf16[64,8,8,256]{3,2,1,0:T(8,128)(2,1)} copy(bf16[64,8,8,256]{3,1,2,0:T(8,128)(2,1)} %bitcast.107) | data formatting | bytes 4194304
  16.2 1.5 fusion.69
  19.3 8.0 %all-to-all-done.1 = bf16[8,256,96]{1,2,0:T(8,128)(2,1)} async-done(((bf16[8,256,96]{1,2,0:T(8,128)(2,1)}), bf16[8,256,96]{1,2,0:T(8,128)(2,1)}, u32[]{:S(2)}, u32[]{:S(2)}) %all-to-all-start.1) | async-done | bytes 393248 | tf_op jit(solution)/shard_map/all_to_all | solution.py:94
  28.4 3.6 %all-to-all-start = ((bf16[8,256,288]{1,2,0:T(8,128)(2,1)}), bf16[8,256,288]{1,2,0:T(8,128)(2,1)S(1)}, u32[]{:S(2)}, u32[]{:S(2)}) async-start(bf16[8,256,288]{1,2,0:T(8,128)(2,1)} %broadcast_in_dim.47), calls=%async_computation | async-start | bytes 2359296 | tf_op jit(solution)/shard_map/all_to_all | solution.py:53
  32.0 1.8 fusion.16
  33.8 2.5 %collective-permute-start.1 = (bf16[3,32,512]{2,1,0:T(8,128)(2,1)S(1)}, bf16[3,32,512]{2,1,0:T(8,128)(2,1)S(1)}, u32[]{:S(2)}, u32[]{:S(2)}) collective-permute-start(bf16[3,32,512]{2,1,0:T(8,128)(2,1)S(1)} %fusion.16), channel_id=1, source_target_pairs={{0,2},{2,0},{4,6},{6,4},{8,10},{10,8},{12,14},{14,12},{1,3},{3,1},... | collective-permute-start | bytes 294920 | tf_op jit(solution)/shard_map/ppermute | solution.py:136
  37.0 3.4 %collective-permute-done.1 = bf16[3,32,512]{2,1,0:T(8,128)(2,1)S(1)} collective-permute-done((bf16[3,32,512]{2,1,0:T(8,128)(2,1)S(1)}, bf16[3,32,512]{2,1,0:T(8,128)(2,1)S(1)}, u32[]{:S(2)}, u32[]{:S(2)}) %collective-permute-start.1) | collective-permute-done | bytes 98336 | tf_op jit(solution)/shard_map/ppermute | solution.py:136
  40.5 1.9 %collective-permute-start.2 = (bf16[3,2,32,512]{3,2,0,1:T(8,128)(2,1)S(1)}, bf16[3,2,32,512]{3,2,0,1:T(8,128)(2,1)S(1)}, u32[]{:S(2)}, u32[]{:S(2)}) collective-permute-start(bf16[3,2,32,512]{3,2,0,1:T(8,128)(2,1)S(1)} %maximum_select_fusion.10), channel_id=1, source_target_pairs={{0,1},{1,0},{2,3},{3,2},{4,5},{5,4},{6,7},{7,6},{8,9},{9,8},{10,11... | collective-permute-start | bytes 589832 | tf_op jit(solution)/shard_map/ppermute | solution.py:135
  43.0 2.0 %and_reduce_fusion = pred[2048]{0:T(1024)(128)(4,1)S(1)} fusion(s32[1,8192]{1,0:T(1,128)} %param.16, s32[]{:T(128)S(6)} %select_n.153, s32[]{:T(128)} %bitcast.16, s32[]{:T(128)} %bitcast.15, s32[]{:T(128)} %bitcast.103, s32[]{:T(128)S(6)} %mul.153), kind=kLoop, calls=%fused_computation.84 | loop fusion | flops 12288 | bytes 10260 | tf_op jit(solution)/shard_map/and | solution.py:162
  48.5 2.4 %collective-permute-start.3 = (f32[66,512]{1,0:T(8,128)S(1)}, f32[66,512]{1,0:T(8,128)S(1)}, u32[]{:S(2)}, u32[]{:S(2)}) collective-permute-start(f32[66,512]{1,0:T(8,128)S(1)} %pad_maximum_fusion.2), channel_id=1, source_target_pairs={{0,2},{2,0},{4,6},{6,4},{8,10},{10,8},{12,14},{14,12},{1,3},{3,1},... | collective-permute-start | bytes 405512 | tf_op jit(solution)/shard_map/ppermute | solution.py:136
  50.9 5.8 %collective-permute-done.3 = f32[66,512]{1,0:T(8,128)S(1)} collective-permute-done((f32[66,512]{1,0:T(8,128)S(1)}, f32[66,512]{1,0:T(8,128)S(1)}, u32[]{:S(2)}, u32[]{:S(2)}) %collective-permute-start.3) | collective-permute-done | bytes 135200 | tf_op jit(solution)/shard_map/ppermute | solution.py:136
  56.8 1.9 %collective-permute-start.4 = (f32[66,512]{1,0:T(8,128)S(1)}, f32[66,512]{1,0:T(8,128)S(1)}, u32[]{:S(2)}, u32[]{:S(2)}) collective-permute-start(f32[66,512]{1,0:T(8,128)S(1)} %pad_maximum_fusion.3), channel_id=1, source_target_pairs={{0,1},{1,0},{2,3},{3,2},{4,5},{5,4},{6,7},{7,6},{8,9},{9,8},{10,11... | collective-permute-start | bytes 405512 | tf_op jit(solution)/shard_map/ppermute | solution.py:135
  58.7 1.3 collective-permute-done.4
  60.3 2.6 %all-to-all-done = bf16[8,256,288]{1,2,0:T(8,128)(2,1)S(1)} async-done(((bf16[8,256,288]{1,2,0:T(8,128)(2,1)}), bf16[8,256,288]{1,2,0:T(8,128)(2,1)S(1)}, u32[]{:S(2)}, u32[]{:S(2)}) %all-to-all-start) | async-done | bytes 1179680 | tf_op jit(solution)/shard_map/all_to_all | solution.py:53
  64.0 10.2 %all-to-all-start.2 = ((bf16[32,64,256]{2,1,0:T(8,128)(2,1)}), bf16[32,64,256]{2,1,0:T(8,128)(2,1)S(1)}, u32[]{:S(2)}, u32[]{:S(2)}) async-start(bf16[32,64,256]{2,1,0:T(8,128)(2,1)} %broadcast_in_dim.101), calls=%async_computation.2 | async-start | bytes 2097152 | tf_op jit(solution)/shard_map/all_to_all | solution.py:200
  75.6 4.6 %collective-permute-start.7 = (bf16[512,128]{1,0:T(8,128)(2,1)S(1)}, bf16[512,128]{1,0:T(8,128)(2,1)S(1)}, u32[]{:S(2)}, u32[]{:S(2)}) collective-permute-start(bf16[512,128]{1,0:T(8,128)(2,1)S(1)} %get-tuple-element.20), channel_id=1, source_target_pairs={{0,48},{16,32},{32,16},{48,0},{1,49},{17,33},{33,17},{49,1},{2,50}... | collective-permute-start | bytes 393224 | tf_op jit(solution)/shard_map/ppermute | solution.py:110
  80.2 2.7 %collective-permute-start.6 = (bf16[512,128]{1,0:T(8,128)(2,1)S(1)}, bf16[512,128]{1,0:T(8,128)(2,1)S(1)}, u32[]{:S(2)}, u32[]{:S(2)}) collective-permute-start(bf16[512,128]{1,0:T(8,128)(2,1)S(1)} %get-tuple-element.21), channel_id=1, source_target_pairs={{0,32},{16,48},{32,0},{48,16},{1,33},{17,49},{33,1},{49,17},{2,34}... | collective-permute-start | bytes 393224 | tf_op jit(solution)/shard_map/ppermute | solution.py:110
  82.9 2.5 %collective-permute-start.5 = (bf16[512,128]{1,0:T(8,128)(2,1)S(1)}, bf16[512,128]{1,0:T(8,128)(2,1)S(1)}, u32[]{:S(2)}, u32[]{:S(2)}) collective-permute-start(bf16[512,128]{1,0:T(8,128)(2,1)S(1)} %get-tuple-element.22), channel_id=1, source_target_pairs={{0,16},{16,0},{32,48},{48,32},{1,17},{17,1},{33,49},{49,33},{2,18}... | collective-permute-start | bytes 393224 | tf_op jit(solution)/shard_map/ppermute | solution.py:110
  86.4 1.9 %collective-permute-start = (bf16[2048,160]{0,1:T(8,128)(2,1)}, bf16[2048,160]{0,1:T(8,128)(2,1)}, u32[]{:S(2)}, u32[]{:S(2)}) collective-permute-start(bf16[2048,160]{0,1:T(8,128)(2,1)} %slice.124), channel_id=1, source_target_pairs={{0,1},{1,0},{2,3},{3,2},{4,5},{5,4},{6,7},{7,6},{8,9},{9,8},{10,11... | collective-permute-start | bytes 1966088 | tf_op jit(solution)/shard_map/ppermute | solution.py:99
  88.3 2.4 %collective-permute-done.7 = bf16[512,128]{1,0:T(8,128)(2,1)S(1)} collective-permute-done((bf16[512,128]{1,0:T(8,128)(2,1)S(1)}, bf16[512,128]{1,0:T(8,128)(2,1)S(1)}, u32[]{:S(2)}, u32[]{:S(2)}) %collective-permute-start.7) | collective-permute-done | bytes 131104 | tf_op jit(solution)/shard_map/ppermute | solution.py:110
  93.8 1.9 %collective-permute-start.8 = (bf16[4,512,128]{2,1,0:T(8,128)(2,1)}, bf16[4,512,128]{2,1,0:T(8,128)(2,1)S(1)}, u32[]{:S(2)}, u32[]{:S(2)}) collective-permute-start(bf16[4,512,128]{2,1,0:T(8,128)(2,1)} %broadcast_select_fusion), channel_id=1, source_target_pairs={{0,1},{1,0},{2,3},{3,2},{4,5},{5,4},{6,7},{7,6},{8,9},{9,8},{10,11... | collective-permute-start | bytes 1572872 | tf_op jit(solution)/shard_map/ppermute | solution.py:117
  99.0 1.9 %all-to-all-done.2 = bf16[32,64,256]{2,1,0:T(8,128)(2,1)S(1)} async-done(((bf16[32,64,256]{2,1,0:T(8,128)(2,1)}), bf16[32,64,256]{2,1,0:T(8,128)(2,1)S(1)}, u32[]{:S(2)}, u32[]{:S(2)}) %all-to-all-start.2) | async-done | bytes 1048608 | tf_op jit(solution)/shard_map/all_to_all | solution.py:200
  102.3 8.3 %all-to-all-start.3 = ((bf16[32,64,256]{2,1,0:T(8,128)(2,1)}), bf16[32,64,256]{2,1,0:T(8,128)(2,1)S(1)}, u32[]{:S(2)}, u32[]{:S(2)}) async-start(bf16[32,64,256]{2,1,0:T(8,128)(2,1)} %broadcast_in_dim.102), calls=%async_computation.3 | async-start | bytes 2097152 | tf_op jit(solution)/shard_map/all_to_all | solution.py:211
  111.6 1.9 %slice.139 = bf16[2048,128]{0,1:T(8,128)(2,1)} slice(bf16[2048,160]{0,1:T(8,128)(2,1)} %collective-permute-done), slice={[0:2048], [32:160]} | slice | bytes 1048576 | tf_op jit(solution)/shard_map/slice | solution.py:101
  113.5 25.9 %all-to-all-done.3 = bf16[32,64,256]{2,1,0:T(8,128)(2,1)S(1)} async-done(((bf16[32,64,256]{2,1,0:T(8,128)(2,1)}), bf16[32,64,256]{2,1,0:T(8,128)(2,1)S(1)}, u32[]{:S(2)}, u32[]{:S(2)}) %all-to-all-start.3) | async-done | bytes 1048608 | tf_op jit(solution)/shard_map/all_to_all | solution.py:211
  140.4 1.5 copy.80
  145.1 11.9 %all_to_all.30 = bf16[4,256,256]{1,2,0:T(8,128)(2,1)S(1)} all-to-all(bf16[4,256,256]{1,2,0:T(8,128)(2,1)S(1)} %broadcast_in_dim.108), channel_id=1, replica_groups=mesh['req'=8,'bx'=4,'by'=8,'bc'=2] {'bx'}, dimensions={0} | all-to-all | bytes 1048576 | tf_op jit(solution)/shard_map/all_to_all | solution.py:224
  158.6 4.6 %all-to-all-start.5 = ((f32[32,8,512]{2,1,0:T(8,128)}), f32[32,8,512]{2,1,0:T(8,128)S(1)}, u32[]{:S(2)}, u32[]{:S(2)}) async-start(f32[32,8,512]{2,1,0:T(8,128)} %convolution_bitcast_fusion), calls=%async_computation.5 | async-start | bytes 1048576 | tf_op jit(solution)/shard_map/all_to_all | solution.py:230
  163.9 15.8 %all-to-all-done.5 = f32[32,8,512]{2,1,0:T(8,128)S(1)} async-done(((f32[32,8,512]{2,1,0:T(8,128)}), f32[32,8,512]{2,1,0:T(8,128)S(1)}, u32[]{:S(2)}, u32[]{:S(2)}) %all-to-all-start.5) | async-done | bytes 524320 | tf_op jit(solution)/shard_map/all_to_all | solution.py:230
  181.6 1.5 fusion.52
  (109 shorter events, 27.3 us)
Async XLA Ops:
  2.2 25.1 %all-to-all-start.1 = ((bf16[8,256,96]{1,2,0:T(8,128)(2,1)}), bf16[8,256,96]{1,2,0:T(8,128)(2,1)}, u32[]{:S(2)}, u32[]{:S(2)}) async-start(bf16[8,256,96]{1,2,0:T(8,128)(2,1)} %broadcast_in_dim.49), calls=%async_computation.1 | async-start | bytes 786432 | tf_op jit(solution)/shard_map/all_to_all | solution.py:94
  12.5 3.7 %copy-start.2 = (bf16[1,1,2048,2,128]{4,3,2,1,0:T(2,128)(2,1)S(1)}, bf16[1,1,2048,2,128]{4,3,2,1,0:T(2,128)(2,1)}, u32[]{:S(2)}) copy-start(bf16[1,1,2048,2,128]{4,3,2,1,0:T(2,128)(2,1)} %param.15) | copy-start | bytes 3145732
  16.2 1.5 copy-start.12
  16.2 1.7 copy-start.10
  16.2 1.7 copy-start.11
  19.3 12.7 %copy-start.4 = (bf16[64,8,8,256]{3,2,1,0:T(8,128)(2,1)S(1)}, bf16[64,8,8,256]{3,2,1,0:T(8,128)(2,1)}, u32[]{:S(2)}) copy-start(bf16[64,8,8,256]{3,2,1,0:T(8,128)(2,1)} %copy.93) | copy-start | bytes 6291460
  19.3 12.7 %copy-start.17 = (f32[3,32]{1,0:T(4,128)S(1)}, f32[3,32]{1,0:T(4,128)}, u32[]{:S(2)}) copy-start(f32[3,32]{1,0:T(4,128)} %param.20) | copy-start | bytes 1156
  28.4 34.5 %all-to-all-start = ((bf16[8,256,288]{1,2,0:T(8,128)(2,1)}), bf16[8,256,288]{1,2,0:T(8,128)(2,1)S(1)}, u32[]{:S(2)}, u32[]{:S(2)}) async-start(bf16[8,256,288]{1,2,0:T(8,128)(2,1)} %broadcast_in_dim.47), calls=%async_computation | async-start | bytes 2359296 | tf_op jit(solution)/shard_map/all_to_all | solution.py:53
  32.0 10.4 %copy-start.16 = (s32[1,2]{1,0:T(1,128)S(1)}, s32[1,2]{1,0:T(1,128)}, u32[]{:S(2)}) copy-start(s32[1,2]{1,0:T(1,128)} %param.18) | copy-start | bytes 28
  33.8 11.6 %copy-start.9 = (bf16[2048,128]{1,0:T(8,128)(2,1)S(1)}, bf16[2048,128]{1,0:T(8,128)(2,1)}, u32[]{:S(2)}) copy-start(bf16[2048,128]{1,0:T(8,128)(2,1)} %get-tuple-element.38) | copy-start | bytes 1572868
  33.8 6.6 %collective-permute-start.1 = (bf16[3,32,512]{2,1,0:T(8,128)(2,1)S(1)}, bf16[3,32,512]{2,1,0:T(8,128)(2,1)S(1)}, u32[]{:S(2)}, u32[]{:S(2)}) collective-permute-start(bf16[3,32,512]{2,1,0:T(8,128)(2,1)S(1)} %fusion.16), channel_id=1, source_target_pairs={{0,2},{2,0},{4,6},{6,4},{8,10},{10,8},{12,14},{14,12},{1,3},{3,1},... | collective-permute-start | bytes 294920 | tf_op jit(solution)/shard_map/ppermute | solution.py:136
  40.5 4.6 %collective-permute-start.2 = (bf16[3,2,32,512]{3,2,0,1:T(8,128)(2,1)S(1)}, bf16[3,2,32,512]{3,2,0,1:T(8,128)(2,1)S(1)}, u32[]{:S(2)}, u32[]{:S(2)}) collective-permute-start(bf16[3,2,32,512]{3,2,0,1:T(8,128)(2,1)S(1)} %maximum_select_fusion.10), channel_id=1, source_target_pairs={{0,1},{1,0},{2,3},{3,2},{4,5},{5,4},{6,7},{7,6},{8,9},{9,8},{10,11... | collective-permute-start | bytes 589832 | tf_op jit(solution)/shard_map/ppermute | solution.py:135
  45.5 1.1 copy-start.8
  48.5 8.1 %collective-permute-start.3 = (f32[66,512]{1,0:T(8,128)S(1)}, f32[66,512]{1,0:T(8,128)S(1)}, u32[]{:S(2)}, u32[]{:S(2)}) collective-permute-start(f32[66,512]{1,0:T(8,128)S(1)} %pad_maximum_fusion.2), channel_id=1, source_target_pairs={{0,2},{2,0},{4,6},{6,4},{8,10},{10,8},{12,14},{14,12},{1,3},{3,1},... | collective-permute-start | bytes 405512 | tf_op jit(solution)/shard_map/ppermute | solution.py:136
  56.8 3.3 %collective-permute-start.4 = (f32[66,512]{1,0:T(8,128)S(1)}, f32[66,512]{1,0:T(8,128)S(1)}, u32[]{:S(2)}, u32[]{:S(2)}) collective-permute-start(f32[66,512]{1,0:T(8,128)S(1)} %pad_maximum_fusion.3), channel_id=1, source_target_pairs={{0,1},{1,0},{2,3},{3,2},{4,5},{5,4},{6,7},{7,6},{8,9},{9,8},{10,11... | collective-permute-start | bytes 405512 | tf_op jit(solution)/shard_map/ppermute | solution.py:135
  64.0 36.9 %all-to-all-start.2 = ((bf16[32,64,256]{2,1,0:T(8,128)(2,1)}), bf16[32,64,256]{2,1,0:T(8,128)(2,1)S(1)}, u32[]{:S(2)}, u32[]{:S(2)}) async-start(bf16[32,64,256]{2,1,0:T(8,128)(2,1)} %broadcast_in_dim.101), calls=%async_computation.2 | async-start | bytes 2097152 | tf_op jit(solution)/shard_map/all_to_all | solution.py:200
  75.6 15.1 %collective-permute-start.7 = (bf16[512,128]{1,0:T(8,128)(2,1)S(1)}, bf16[512,128]{1,0:T(8,128)(2,1)S(1)}, u32[]{:S(2)}, u32[]{:S(2)}) collective-permute-start(bf16[512,128]{1,0:T(8,128)(2,1)S(1)} %get-tuple-element.20), channel_id=1, source_target_pairs={{0,48},{16,32},{32,16},{48,0},{1,49},{17,33},{33,17},{49,1},{2,50}... | collective-permute-start | bytes 393224 | tf_op jit(solution)/shard_map/ppermute | solution.py:110
  80.2 11.2 %collective-permute-start.6 = (bf16[512,128]{1,0:T(8,128)(2,1)S(1)}, bf16[512,128]{1,0:T(8,128)(2,1)S(1)}, u32[]{:S(2)}, u32[]{:S(2)}) collective-permute-start(bf16[512,128]{1,0:T(8,128)(2,1)S(1)} %get-tuple-element.21), channel_id=1, source_target_pairs={{0,32},{16,48},{32,0},{48,16},{1,33},{17,49},{33,1},{49,17},{2,34}... | collective-permute-start | bytes 393224 | tf_op jit(solution)/shard_map/ppermute | solution.py:110
  82.9 9.3 %collective-permute-start.5 = (bf16[512,128]{1,0:T(8,128)(2,1)S(1)}, bf16[512,128]{1,0:T(8,128)(2,1)S(1)}, u32[]{:S(2)}, u32[]{:S(2)}) collective-permute-start(bf16[512,128]{1,0:T(8,128)(2,1)S(1)} %get-tuple-element.22), channel_id=1, source_target_pairs={{0,16},{16,0},{32,48},{48,32},{1,17},{17,1},{33,49},{49,33},{2,18}... | collective-permute-start | bytes 393224 | tf_op jit(solution)/shard_map/ppermute | solution.py:110
  85.4 10.3 %copy-start.13 = (f32[2,2048]{1,0:T(2,128)S(1)}, f32[2,2048]{1,0:T(2,128)}, u32[]{:S(2)}) copy-start(f32[2,2048]{1,0:T(2,128)} %param.25) | copy-start | bytes 49156
  86.4 9.7 %collective-permute-start = (bf16[2048,160]{0,1:T(8,128)(2,1)}, bf16[2048,160]{0,1:T(8,128)(2,1)}, u32[]{:S(2)}, u32[]{:S(2)}) collective-permute-start(bf16[2048,160]{0,1:T(8,128)(2,1)} %slice.124), channel_id=1, source_target_pairs={{0,1},{1,0},{2,3},{3,2},{4,5},{5,4},{6,7},{7,6},{8,9},{9,8},{10,11... | collective-permute-start | bytes 1966088 | tf_op jit(solution)/shard_map/ppermute | solution.py:99
  93.8 4.0 %collective-permute-start.8 = (bf16[4,512,128]{2,1,0:T(8,128)(2,1)}, bf16[4,512,128]{2,1,0:T(8,128)(2,1)S(1)}, u32[]{:S(2)}, u32[]{:S(2)}) collective-permute-start(bf16[4,512,128]{2,1,0:T(8,128)(2,1)} %broadcast_select_fusion), channel_id=1, source_target_pairs={{0,1},{1,0},{2,3},{3,2},{4,5},{5,4},{6,7},{7,6},{8,9},{9,8},{10,11... | collective-permute-start | bytes 1572872 | tf_op jit(solution)/shard_map/ppermute | solution.py:117
  100.9 10.6 %copy-start.14 = (f32[2,2048]{1,0:T(2,128)S(1)}, f32[2,2048]{1,0:T(2,128)}, u32[]{:S(2)}) copy-start(f32[2,2048]{1,0:T(2,128)} %param.27) | copy-start | bytes 49156
  100.9 10.7 %copy-start.15 = (f32[2,2048]{1,0:T(2,128)S(1)}, f32[2,2048]{1,0:T(2,128)}, u32[]{:S(2)}) copy-start(f32[2,2048]{1,0:T(2,128)} %param.26) | copy-start | bytes 49156
  102.3 37.1 %all-to-all-start.3 = ((bf16[32,64,256]{2,1,0:T(8,128)(2,1)}), bf16[32,64,256]{2,1,0:T(8,128)(2,1)S(1)}, u32[]{:S(2)}, u32[]{:S(2)}) async-start(bf16[32,64,256]{2,1,0:T(8,128)(2,1)} %broadcast_in_dim.102), calls=%async_computation.3 | async-start | bytes 2097152 | tf_op jit(solution)/shard_map/all_to_all | solution.py:211
  110.6 31.2 %copy-start = (bf16[1,512,2048]{2,1,0:T(8,128)(2,1)S(1)}, bf16[1,512,2048]{2,1,0:T(8,128)(2,1)}, u32[]{:S(2)}) copy-start(bf16[1,512,2048]{2,1,0:T(8,128)(2,1)} %param.14) | copy-start | bytes 6291460
  139.4 1.0 copy-start.3
  142.8 1.6 copy-start.6
  142.8 1.5 copy-start.7
  143.3 1.0 copy-start.5
  145.0 12.3 %copy-start.1 = (bf16[4,2,512,128]{3,2,0,1:T(8,128)(2,1)S(1)}, bf16[4,2,512,128]{3,2,0,1:T(8,128)(2,1)}, u32[]{:S(2)}) copy-start(bf16[4,2,512,128]{3,2,0,1:T(8,128)(2,1)} %maximum_select_fusion) | copy-start | bytes 3145732
  158.6 21.1 %all-to-all-start.5 = ((f32[32,8,512]{2,1,0:T(8,128)}), f32[32,8,512]{2,1,0:T(8,128)S(1)}, u32[]{:S(2)}, u32[]{:S(2)}) async-start(f32[32,8,512]{2,1,0:T(8,128)} %convolution_bitcast_fusion), calls=%async_computation.5 | async-start | bytes 1048576 | tf_op jit(solution)/shard_map/all_to_all | solution.py:230
